TPU v7x, 128 devices: a whole 4x4x4 slice. The times are simulated.
128 devices in a mesh: row: 4 (over z_lo, core), col: 8 (over y, z_hi), layer: 4 (over x).
Axes of the slice: x: 4, y: 4, z: 4 (z_hi: 2, z_lo: 2; z = z_hi * 2 + z_lo), core: 2. Of those that a mesh axis runs over, the one named last changes fastest.
Arguments:
- a_tiles: bfloat16 [4, 8, 4, 32, 128, 128], P('row', 'col', 'layer'), may hold values from 0 to 1, as said below
- a_coords: int32 [4, 8, 4, 32, 2], P('row', 'col', 'layer'), may hold values from 0 to 31, as said below
- b_tiles: bfloat16 [4, 8, 4, 32, 128, 128], P('row', 'col', 'layer'), may hold values from 0 to 1, as said below
- b_coords: int32 [4, 8, 4, 32, 2], P('row', 'col', 'layer'), may hold values from 0 to 15, as said below
- out_coords: int32 [4, 8, 4, 16, 2], P('row', 'col', 'layer'), may hold values from 0 to 15, as said below
Outputs:
- flow: float32 [4, 8, 4, 16, 128, 128], P('row', 'col', 'layer')
Inputs may be any that keep to these rules, and one draw needn't show every extreme that they name: `a_tiles`: every entry is positive. `b_tiles`: every entry is positive. `a_coords`: on one device, column 0 takes every value below 32 exactly once; column 1 is below 4. `b_coords`: on one device, column 1 takes every value below 16 exactly twice, with two different values of column 0; column 0 is below 8. `out_coords`: on one device, column 1 takes every value below 16 exactly once; column 0 is below 8.
All inputs are finite; a program needn't handle non-finite values.
Results may differ from a plain program's by a relative error of at most 0.0003.
Values may be sent and summed in bfloat16 or wider, within the bound.
No kernel may reach another device: no remote copies, remote signals or barrier semaphores. Data moves between devices by JAX's collectives and lax.ppermute only.
A program may use at most 192 MiB of HBM per device.

v0:
```python
import jax
import jax.numpy as jnp
from jax import lax
from jax.sharding import PartitionSpec as P

BLK = 4
RB = 4


def local(a_tiles, a_coords, b_tiles, b_coords, out_coords):
    tile_size = a_tiles.shape[-1]
    rows_panel = a_tiles.shape[3]
    col_count = lax.axis_size("col")
    row_count = lax.axis_size("row")
    layer_count = lax.axis_size("layer")
    a_span = BLK
    b_span = BLK * col_count // row_count
    slab_tiles = a_span * col_count
    col_tiles = out_coords.shape[3]
    graph_tiles, graph_coords = (
        lax.all_gather(b_tiles, "row", axis=0, tiled=True),
        lax.all_gather(b_coords, "row", axis=0, tiled=True),
    )
    owner_rows = jnp.arange(row_count, dtype=jnp.int32)[:, None]
    inner_rows = (owner_rows * b_span + graph_coords[:, 0, 0, :, 0]).reshape(-1)
    column_ids = graph_coords[:, 0, 0, :, 1].reshape(-1)
    flat_tiles = graph_tiles.reshape(-1, tile_size, tile_size)
    graph_panel = jnp.zeros((slab_tiles, tile_size, col_tiles, tile_size), jnp.bfloat16)
    graph_panel = graph_panel.at[inner_rows, :, column_ids, :].set(flat_tiles)
    graph_panel = graph_panel.reshape(slab_tiles, tile_size, col_tiles * tile_size)
    own_rows = a_coords[0, 0, 0, :, 0]
    own_inner = a_coords[0, 0, 0, :, 1]
    ordered = jnp.zeros_like(a_tiles[0, 0, 0]).at[own_rows].set(a_tiles[0, 0, 0])
    ordered_inner = jnp.zeros_like(own_inner).at[own_rows].set(own_inner)
    flow_all, inner_all = (
        lax.all_gather(ordered[None], "col", axis=0, tiled=True),
        lax.all_gather(ordered_inner[None], "col", axis=0, tiled=True),
    )
    slab_index = jnp.arange(col_count, dtype=jnp.int32)[:, None] * a_span + inner_all

    def row_block(step_index):
        first_row = step_index * RB
        left_block = lax.dynamic_slice_in_dim(flow_all, first_row, RB, 1)
        index_block = lax.dynamic_slice_in_dim(slab_index, first_row, RB, 1)
        right_block = graph_panel[index_block]
        return jnp.einsum(
            "prxy,pryz->rxz", left_block, right_block, preferred_element_type=jnp.float32
        )

    partial_sum = lax.map(row_block, jnp.arange(rows_panel // RB, dtype=jnp.int32))
    partial_sum = partial_sum.reshape(rows_panel, tile_size, col_tiles * tile_size)
    kept_rows = out_coords[0, 0, 0, :, 0]
    kept_cols = out_coords[0, 0, 0, :, 1]
    summed_rows = lax.psum_scatter(partial_sum, "layer", scatter_dimension=0, tiled=True)
    tile_grid = summed_rows.reshape(b_span, tile_size, col_tiles, tile_size)
    kept_tiles = tile_grid[kept_rows, :, kept_cols, :]
    squared = kept_tiles * kept_tiles
    column_part = jnp.sum(squared, axis=1)
    onehot = (jnp.arange(col_tiles, dtype=jnp.int32)[:, None] == kept_cols[None, :]).astype(
        jnp.float32
    )
    local_mass = jnp.dot(onehot, column_part, precision=lax.Precision.HIGHEST)
    column_total = lax.psum(local_mass, ("row", "layer"))
    factor = jnp.float32(row_count * layer_count * tile_size) / column_total
    flow = squared * factor[kept_cols][:, None, :]
    return flow.reshape(1, 1, 1, col_tiles, tile_size, tile_size)


def solution(mesh):
    in_specs = (
        P("row", "col", "layer", None, None, None),
        P("row", "col", "layer", None, None),
        P("row", "col", "layer", None, None, None),
        P("row", "col", "layer", None, None),
        P("row", "col", "layer", None, None),
    )
    out_specs = P("row", "col", "layer", None, None, None)
    return jax.shard_map(local, mesh=mesh, in_specs=in_specs, out_specs=out_specs, check_vma=False)
```

profile of v0, /device:TPU:0, one launch (start us, length us, event | category | flops | bytes accessed | tf_op | source)
XLA Modules:
  0.0 728.4 jit_solution(13771019656350618229)
XLA Ops:
  22.0 13.9 %all-reduce = s32[256]{0:T(256)S(1)} all-reduce(s32[256]{0:T(256)S(1)} %dynamic-update-slice), channel_id=3, replica_groups=mesh['row'=4,'col'=8,'layer'=4] {'col'}, use_global_device_ids=true, to_apply=%add | all-reduce | flops 256 | bytes 2048
  36.0 21.7 %all-gather.5.cloned.1.call-done = bf16[4,1,1,32,128,128]{5,4,3,2,1,0:T(8,128)(2,1)} async-done(((bf16[1,1,1,32,128,128]{5,4,3,2,1,0:T(8,128)(2,1)}), bf16[4,1,1,32,128,128]{5,4,3,2,1,0:T(8,128)(2,1)}) %all-gather.5.cloned.1.call-update) | async-done | bytes 4194320 | tf_op jit(solution)/shard_map/all_gather | solution.py:21
  64.0 21.0 %scatter_fusion.1 = bf16[32,128,16,128]{3,1,2,0:T(8,128)(2,1)} fusion(bf16[32,128,16,128]{3,1,2,0:T(8,128)(2,1)} %broadcast_in_dim.37, s32[128]{0:T(128)S(1)} %fusion.13, bf16[128,128,128]{2,1,0:T(8,128)(2,1)} %bitcast.51), kind=kCustom, calls=%fused_computation.5 | custom fusion | bytes 12583936 | tf_op jit(solution)/shard_map/scatter | solution.py:29
  84.9 22.6 %copy.18 = bf16[32,128,16,128]{1,3,2,0:T(8,128)(2,1)} copy(bf16[32,128,16,128]{3,1,2,0:T(8,128)(2,1)} %scatter_fusion.1) | data formatting | bytes 33554432 | tf_op jit(solution)/shard_map/scatter | solution.py:29
  107.6 22.2 %copy.20 = bf16[32,128,2048]{2,1,0:T(8,128)(2,1)} copy(bf16[32,128,2048]{1,2,0:T(8,128)(2,1)} %bitcast.48) | data formatting | bytes 33554432 | tf_op jit(solution)/shard_map/while | solution.py:50
  129.8 40.7 %all-gather.7.cloned.1.call-done = bf16[256,128,128]{2,1,0:T(8,128)(2,1)} async-done(((bf16[32,128,128]{2,1,0:T(8,128)(2,1)}), bf16[256,128,128]{2,1,0:T(8,128)(2,1)}) %all-gather.7.cloned.1.call-update) | async-done | bytes 8388624 | tf_op jit(solution)/shard_map/all_gather | solution.py:36
  170.5 226.7 %while.10 = (s32[]{:T(128)}, f32[8,4,128,2048]{2,3,1,0:T(8,128)}, s32[8]{0:T(128)S(1)}, bf16[8,32,128,128]{3,2,1,0:T(8,128)(2,1)}, s32[8,32]{1,0:T(8,128)S(1)}, ...) while((s32[]{:T(128)}, f32[8,4,128,2048]{2,3,1,0:T(8,128)}, ...), condition=%wide.region_4.5_spmd, body=%wide.region_3.4_spmd.sunk | while | flops 2147484672 | bytes 55580068 | solution.py:50
  171.9 13.1 %gather_fusion = bf16[32,128,2048]{2,1,0:T(8,128)(2,1)} fusion(bf16[32,128,2048]{2,1,0:T(8,128)(2,1)} %get-tuple-element.134, s32[1024]{0:T(1024)S(1)} %pad_clamp_fusion.3), kind=kCustom, calls=%fused_computation.clone.1 | custom fusion | bytes 33554560 | tf_op jit(solution)/shard_map/while/body/eval_jaxpr/gather | solution.py:45
  185.0 13.8 %bitcast_dynamic-update-slice_fusion.2 = f32[8,4,128,2048]{2,3,1,0:T(8,128)} fusion(f32[8,4,128,2048]{2,3,1,0:T(8,128)} %get-tuple-element.120, s32[]{:T(128)} %get-tuple-element.119, bf16[8,4,128,2048]{3,2,1,0:T(8,128)(2,1)} %bitcast.47, bf16[8,32,128,128]{3,2,1,0:T(8,128)(2,1)} %get-tuple-element.132, s32[]{:T(128)S(6)} %select_n.95), kind=kOutput, calls=%fused_computation.8.clone.1 | convolution fusion | flops 2147483648 | bytes 22020612 | tf_op jit(solution)/shard_map/while/body/eval_jaxpr/prxy,pryz->rxz/dot_general | solution.py:46
  200.2 13.1 %gather_fusion = bf16[32,128,2048]{2,1,0:T(8,128)(2,1)} fusion(bf16[32,128,2048]{2,1,0:T(8,128)(2,1)} %get-tuple-element.134, s32[1024]{0:T(1024)S(1)} %pad_clamp_fusion.3), kind=kCustom, calls=%fused_computation.clone.1 | custom fusion | bytes 33554560 | tf_op jit(solution)/shard_map/while/body/eval_jaxpr/gather | solution.py:45
  213.3 13.8 %bitcast_dynamic-update-slice_fusion.2 = f32[8,4,128,2048]{2,3,1,0:T(8,128)} fusion(f32[8,4,128,2048]{2,3,1,0:T(8,128)} %get-tuple-element.120, s32[]{:T(128)} %get-tuple-element.119, bf16[8,4,128,2048]{3,2,1,0:T(8,128)(2,1)} %bitcast.47, bf16[8,32,128,128]{3,2,1,0:T(8,128)(2,1)} %get-tuple-element.132, s32[]{:T(128)S(6)} %select_n.95), kind=kOutput, calls=%fused_computation.8.clone.1 | convolution fusion | flops 2147483648 | bytes 22020612 | tf_op jit(solution)/shard_map/while/body/eval_jaxpr/prxy,pryz->rxz/dot_general | solution.py:46
  228.5 13.1 %gather_fusion = bf16[32,128,2048]{2,1,0:T(8,128)(2,1)} fusion(bf16[32,128,2048]{2,1,0:T(8,128)(2,1)} %get-tuple-element.134, s32[1024]{0:T(1024)S(1)} %pad_clamp_fusion.3), kind=kCustom, calls=%fused_computation.clone.1 | custom fusion | bytes 33554560 | tf_op jit(solution)/shard_map/while/body/eval_jaxpr/gather | solution.py:45
  241.7 13.8 %bitcast_dynamic-update-slice_fusion.2 = f32[8,4,128,2048]{2,3,1,0:T(8,128)} fusion(f32[8,4,128,2048]{2,3,1,0:T(8,128)} %get-tuple-element.120, s32[]{:T(128)} %get-tuple-element.119, bf16[8,4,128,2048]{3,2,1,0:T(8,128)(2,1)} %bitcast.47, bf16[8,32,128,128]{3,2,1,0:T(8,128)(2,1)} %get-tuple-element.132, s32[]{:T(128)S(6)} %select_n.95), kind=kOutput, calls=%fused_computation.8.clone.1 | convolution fusion | flops 2147483648 | bytes 22020612 | tf_op jit(solution)/shard_map/while/body/eval_jaxpr/prxy,pryz->rxz/dot_general | solution.py:46
  256.9 13.1 %gather_fusion = bf16[32,128,2048]{2,1,0:T(8,128)(2,1)} fusion(bf16[32,128,2048]{2,1,0:T(8,128)(2,1)} %get-tuple-element.134, s32[1024]{0:T(1024)S(1)} %pad_clamp_fusion.3), kind=kCustom, calls=%fused_computation.clone.1 | custom fusion | bytes 33554560 | tf_op jit(solution)/shard_map/while/body/eval_jaxpr/gather | solution.py:45
  270.0 13.8 %bitcast_dynamic-update-slice_fusion.2 = f32[8,4,128,2048]{2,3,1,0:T(8,128)} fusion(f32[8,4,128,2048]{2,3,1,0:T(8,128)} %get-tuple-element.120, s32[]{:T(128)} %get-tuple-element.119, bf16[8,4,128,2048]{3,2,1,0:T(8,128)(2,1)} %bitcast.47, bf16[8,32,128,128]{3,2,1,0:T(8,128)(2,1)} %get-tuple-element.132, s32[]{:T(128)S(6)} %select_n.95), kind=kOutput, calls=%fused_computation.8.clone.1 | convolution fusion | flops 2147483648 | bytes 22020612 | tf_op jit(solution)/shard_map/while/body/eval_jaxpr/prxy,pryz->rxz/dot_general | solution.py:46
  298.4 13.8 %bitcast_dynamic-update-slice_fusion.2 = f32[8,4,128,2048]{2,3,1,0:T(8,128)} fusion(f32[8,4,128,2048]{2,3,1,0:T(8,128)} %get-tuple-element.120, s32[]{:T(128)} %get-tuple-element.119, bf16[8,4,128,2048]{3,2,1,0:T(8,128)(2,1)} %bitcast.47, bf16[8,32,128,128]{3,2,1,0:T(8,128)(2,1)} %get-tuple-element.132, s32[]{:T(128)S(6)} %select_n.95), kind=kOutput, calls=%fused_computation.8.clone.1 | convolution fusion | flops 2147483648 | bytes 22020612 | tf_op jit(solution)/shard_map/while/body/eval_jaxpr/prxy,pryz->rxz/dot_general | solution.py:46
  313.5 13.1 %gather_fusion = bf16[32,128,2048]{2,1,0:T(8,128)(2,1)} fusion(bf16[32,128,2048]{2,1,0:T(8,128)(2,1)} %get-tuple-element.134, s32[1024]{0:T(1024)S(1)} %pad_clamp_fusion.3), kind=kCustom, calls=%fused_computation.clone.1 | custom fusion | bytes 33554560 | tf_op jit(solution)/shard_map/while/body/eval_jaxpr/gather | solution.py:45
  326.7 13.8 %bitcast_dynamic-update-slice_fusion.2 = f32[8,4,128,2048]{2,3,1,0:T(8,128)} fusion(f32[8,4,128,2048]{2,3,1,0:T(8,128)} %get-tuple-element.120, s32[]{:T(128)} %get-tuple-element.119, bf16[8,4,128,2048]{3,2,1,0:T(8,128)(2,1)} %bitcast.47, bf16[8,32,128,128]{3,2,1,0:T(8,128)(2,1)} %get-tuple-element.132, s32[]{:T(128)S(6)} %select_n.95), kind=kOutput, calls=%fused_computation.8.clone.1 | convolution fusion | flops 2147483648 | bytes 22020612 | tf_op jit(solution)/shard_map/while/body/eval_jaxpr/prxy,pryz->rxz/dot_general | solution.py:46
  341.9 13.1 %gather_fusion = bf16[32,128,2048]{2,1,0:T(8,128)(2,1)} fusion(bf16[32,128,2048]{2,1,0:T(8,128)(2,1)} %get-tuple-element.134, s32[1024]{0:T(1024)S(1)} %pad_clamp_fusion.3), kind=kCustom, calls=%fused_computation.clone.1 | custom fusion | bytes 33554560 | tf_op jit(solution)/shard_map/while/body/eval_jaxpr/gather | solution.py:45
  355.0 13.8 %bitcast_dynamic-update-slice_fusion.2 = f32[8,4,128,2048]{2,3,1,0:T(8,128)} fusion(f32[8,4,128,2048]{2,3,1,0:T(8,128)} %get-tuple-element.120, s32[]{:T(128)} %get-tuple-element.119, bf16[8,4,128,2048]{3,2,1,0:T(8,128)(2,1)} %bitcast.47, bf16[8,32,128,128]{3,2,1,0:T(8,128)(2,1)} %get-tuple-element.132, s32[]{:T(128)S(6)} %select_n.95), kind=kOutput, calls=%fused_computation.8.clone.1 | convolution fusion | flops 2147483648 | bytes 22020612 | tf_op jit(solution)/shard_map/while/body/eval_jaxpr/prxy,pryz->rxz/dot_general | solution.py:46
  370.3 13.1 %gather_fusion = bf16[32,128,2048]{2,1,0:T(8,128)(2,1)} fusion(bf16[32,128,2048]{2,1,0:T(8,128)(2,1)} %get-tuple-element.134, s32[1024]{0:T(1024)S(1)} %pad_clamp_fusion.3), kind=kCustom, calls=%fused_computation.clone.1 | custom fusion | bytes 33554560 | tf_op jit(solution)/shard_map/while/body/eval_jaxpr/gather | solution.py:45
  383.4 13.8 %bitcast_dynamic-update-slice_fusion.2 = f32[8,4,128,2048]{2,3,1,0:T(8,128)} fusion(f32[8,4,128,2048]{2,3,1,0:T(8,128)} %get-tuple-element.120, s32[]{:T(128)} %get-tuple-element.119, bf16[8,4,128,2048]{3,2,1,0:T(8,128)(2,1)} %bitcast.47, bf16[8,32,128,128]{3,2,1,0:T(8,128)(2,1)} %get-tuple-element.132, s32[]{:T(128)S(6)} %select_n.95), kind=kOutput, calls=%fused_computation.8.clone.1 | convolution fusion | flops 2147483648 | bytes 22020612 | tf_op jit(solution)/shard_map/while/body/eval_jaxpr/prxy,pryz->rxz/dot_general | solution.py:46
  397.9 279.9 %reduce-scatter.2.cloned.1.call-done = f32[8,128,2048]{1,2,0:T(8,128)} async-done(((f32[32,128,2048]{1,2,0:T(8,128)}), f32[8,128,2048]{1,2,0:T(8,128)}) %reduce-scatter.2.cloned.1.call-update) | async-done | bytes 8388624 | tf_op jit(solution)/shard_map/reduce_scatter | solution.py:54
  691.1 29.0 %psum.7 = f32[16,128]{1,0:T(8,128)S(1)} all-reduce(f32[16,128]{1,0:T(8,128)S(1)} %fusion.5), channel_id=1, replica_groups=mesh['row'=4,'col'=8,'layer'=4] {'row','layer'}, use_global_device_ids=true, to_apply=%region_7.8 | all-reduce | flops 2048 | bytes 16384 | tf_op jit(solution)/shard_map/psum | solution.py:63
  (75 shorter events, 56.0 us)
Async XLA Ops:
  6.5 51.1 %all-gather.5.cloned.1.call-start = ((), (), s32[]{:S(2)}) async-start(), calls=%async_computation.1 | async-start | bytes 5242880 | tf_op jit(solution)/shard_map/all_gather | solution.py:21
  7.3 163.2 %all-gather.7.cloned.1.call-start = ((), (), s32[]{:S(2)}) async-start(), calls=%async_computation.3 | async-start | bytes 9437184 | tf_op jit(solution)/shard_map/all_gather | solution.py:36
  11.8 1.0 copy-start
  12.8 665.0 %reduce-scatter.2.cloned.1.call-start = ((), (), s32[]{:S(2)}) async-start(), calls=%async_computation.2 | async-start | bytes 41943040 | tf_op jit(solution)/shard_map/reduce_scatter | solution.py:54
  397.2 0.7 copy-start.1
Sparse Core Ops, SparseCore 0:
  9.0 48.6 all-gather.4
  60.0 110.3 all-gather.6
  397.3 280.3 reduce-scatter.1
where the time goes:
time: 731 us; the launch traced here: 728 us
  waiting for transfers between devices  343 us (47%)
  local copies, waits for them, and re-layouts  205 us (28%)
  matrix products  111 us (15%)
  blocking collectives  48.2 us (7%)
  between operations  13.8 us (2%)
    reduce_scatter x1, waiting for transfers between devices, local(): lax.psum_scatter(partial_sum, 'layer', scatter_dimension=0, tiled=True)  280 us
    dot_general x8, matrix products, row_block(): jnp.einsum('prxy,pryz->rxz', left_block, right_block, preferred_element_t...  110 us
    gather x8, local copies, waits for them, and re-layouts, row_block(): right_block = graph_panel[index_block]  105 us
    scatter x2, local copies, waits for them, and re-layouts, local(): graph_panel = graph_panel.at[inner_rows, :, column_ids, :].set(flat_tiles)  43.6 us
    all_gather x1, waiting for transfers between devices, local(): lax.all_gather(ordered[None], 'col', axis=0, tiled=True)  40.7 us
    psum x1, blocking collectives, local(): column_total = lax.psum(local_mass, ('row', 'layer'))  29 us
    while x1, local copies, waits for them, and re-layouts, local(): lax.map(row_block, jnp.arange(rows_panel // RB, dtype=jnp.int32))  22.2 us
    all_gather x1, waiting for transfers between devices, local(): lax.all_gather(b_tiles, 'row', axis=0, tiled=True)  21.7 us
  transfers between devices with their start and end apart: 3, of which 3 were waited for; matrix products, arithmetic and copies ran while one was open for 11% of the time, Pallas kernels for 0%

commit v1 on v0

v1 whole, which is shorter than its diff:
```python
import functools

import jax
import jax.numpy as jnp
from jax import lax
from jax.experimental import pallas as pl
from jax.experimental.pallas import tpu as pltpu
from jax.sharding import PartitionSpec as P

KA = 4


def kept_partial_kernel(midx_ref, gidx_ref, flow_ref, graph_ref, out_ref, *, n_out, n_grp):
    tile = out_ref.shape[-1]

    def body(t, carry):
        out_ref[t] = jnp.zeros((tile, tile), jnp.float32)
        for c in range(n_grp):
            g = gidx_ref[t * n_grp + c]

            @pl.when(g >= 0)
            def _():
                left = flow_ref[midx_ref[t * n_grp + c]]
                right = graph_ref[g]
                out_ref[t] += jnp.dot(left, right, preferred_element_type=jnp.float32)

        return carry

    lax.fori_loop(0, n_out, body, 0)


def kept_partials(midx, gidx, flow_flat, graph_flat, n_out, n_grp):
    tile = flow_flat.shape[-1]
    kernel = functools.partial(kept_partial_kernel, n_out=n_out, n_grp=n_grp)
    return pl.pallas_call(
        kernel,
        out_shape=jax.ShapeDtypeStruct((n_out, tile, tile), jnp.float32),
        in_specs=[
            pl.BlockSpec(memory_space=pltpu.SMEM),
            pl.BlockSpec(memory_space=pltpu.SMEM),
            pl.BlockSpec(memory_space=pltpu.VMEM),
            pl.BlockSpec(memory_space=pltpu.VMEM),
        ],
        out_specs=pl.BlockSpec(memory_space=pltpu.VMEM),
    )(midx, gidx, flow_flat, graph_flat)


def local(a_tiles, a_coords, b_tiles, b_coords, out_coords):
    tile_size = a_tiles.shape[-1]
    rows_panel = a_tiles.shape[3]
    col_count = lax.axis_size("col")
    row_count = lax.axis_size("row")
    layer_count = lax.axis_size("layer")
    a_span = KA
    b_span = KA * col_count // row_count
    quarter = rows_panel // layer_count
    col_tiles = out_coords.shape[3]
    n_b = b_tiles.shape[3]

    graph_tiles = lax.all_gather(b_tiles[0, 0, 0], "row", axis=0, tiled=True)
    graph_coords = lax.all_gather(b_coords[0, 0, 0][None], "row", axis=0, tiled=True)
    flow_tiles = lax.all_gather(a_tiles[0, 0, 0], "col", axis=0, tiled=True)
    flow_coords = lax.all_gather(a_coords[0, 0, 0][None], "col", axis=0, tiled=True)
    kept_all = lax.all_gather(out_coords[0, 0, 0][None], "layer", axis=0, tiled=True)

    n_out = layer_count * col_tiles
    kept_row = (jnp.arange(layer_count, dtype=jnp.int32)[:, None] * quarter + kept_all[:, :, 0]).reshape(n_out)
    kept_col = kept_all[:, :, 1].reshape(n_out)

    a_rows = flow_coords[:, :, 0]
    a_inner = flow_coords[:, :, 1]
    match_a = a_rows[None, :, :] == kept_row[:, None, None]
    slot_a = jnp.argmax(match_a, axis=2).astype(jnp.int32)
    grp = jnp.arange(col_count, dtype=jnp.int32)
    midx = grp[None, :] * rows_panel + slot_a
    inner = jnp.take_along_axis(a_inner[None, :, :], slot_a[:, :, None], axis=2)[:, :, 0]
    k_layer = grp[None, :] * a_span + inner
    b_owner = k_layer // b_span
    b_row = k_layer % b_span
    owner_coords = graph_coords[b_owner]
    match_b = (owner_coords[..., 0] == b_row[..., None]) & (owner_coords[..., 1] == kept_col[:, None, None])
    slot_b = jnp.argmax(match_b, axis=2).astype(jnp.int32)
    gidx = jnp.where(jnp.any(match_b, axis=2), b_owner * n_b + slot_b, -1)

    flow_flat = flow_tiles.reshape(-1, tile_size, tile_size)
    graph_flat = graph_tiles.reshape(-1, tile_size, tile_size)
    partial_sum = kept_partials(
        midx.reshape(-1), gidx.reshape(-1).astype(jnp.int32), flow_flat, graph_flat, n_out, col_count
    )
    kept_tiles = lax.psum_scatter(partial_sum, "layer", scatter_dimension=0, tiled=True)

    kept_cols = out_coords[0, 0, 0, :, 1]
    squared = kept_tiles * kept_tiles
    column_part = jnp.sum(squared, axis=1)
    local_mass = jnp.zeros_like(column_part).at[kept_cols].set(column_part)
    column_total = lax.psum(local_mass, ("row", "layer"))
    factor = jnp.float32(row_count * layer_count * tile_size) / column_total
    flow = squared * factor[kept_cols][:, None, :]
    return flow.reshape(1, 1, 1, col_tiles, tile_size, tile_size)


def solution(mesh):
    in_specs = (
        P("row", "col", "layer", None, None, None),
        P("row", "col", "layer", None, None),
        P("row", "col", "layer", None, None, None),
        P("row", "col", "layer", None, None),
        P("row", "col", "layer", None, None),
    )
    out_specs = P("row", "col", "layer", None, None, None)
    return jax.shard_map(local, mesh=mesh, in_specs=in_specs, out_specs=out_specs, check_vma=False)
```

time: 731 us -> 283 us (0.39)
  local copies, waits for them, and re-layouts: 205 us -> 8.88 us
  waiting for transfers between devices: 343 us -> 156 us
  matrix products: 111 us -> 0 us
  Pallas kernels: 0 us -> 26.9 us
  blocking collectives: 48.2 us -> 68.8 us
    reduce_scatter x1, waiting for transfers between devices: 280 us -> 45 us  [local(): lax.psum_scatter(partial_sum, 'layer', scatter_dimension=0, tiled=True)]
    dot_general x9 -> x0, matrix products: 111 us -> none  [the longest x8 110 us: row_block(): jnp.einsum('prxy,pryz->rxz', left_block, right_block, preferred_element_t...]
    gather x9 -> x6, local copies, waits for them, and re-layouts: 109 us -> 5.03 us  [the longest x5 2.96 us: local(): jnp.take_along_axis(a_inner[None, :, :], slot_a[:, :, None], axis=2)]
    all_gather x2, waiting for transfers between devices: 62.4 us -> 110 us  [the longest x1 110 us: local(): flow_tiles = lax.all_gather(a_tiles[0, 0, 0], 'col', axis=0, tiled=True)]
    scatter x4 -> x1, local copies, waits for them, and re-layouts: 47.9 us -> 0.62 us  [local(): local_mass = jnp.zeros_like(column_part).at[kept_cols].set(column_part)]
    all_gather x1 -> x3, blocking collectives: 5.32 us -> 39.8 us  [the longest x1 24.8 us: local(): lax.all_gather(a_coords[0, 0, 0][None], 'col', axis=0, tiled=True)]
    pallas_call x0 -> x1, Pallas kernels: none -> 26.9 us  [kept_partials(): pl.pallas_call(kernel, out_shape=jax.ShapeDtypeStruct((n_out, tile, tile)...]
    while x1 -> x0, local copies, waits for them, and re-layouts: 22.2 us -> none  [local(): lax.map(row_block, jnp.arange(rows_panel // RB, dtype=jnp.int32))]
  transfers between devices with their start and end apart: 3 -> 3, of which waited for: 3 -> 2; matrix products, arithmetic and copies ran while one was open for 11% -> 5% of each run, Pallas kernels for 0% -> 0%
where the time goes in v1:
time: 283 us
  waiting for transfers between devices  156 us (55%)
  blocking collectives  68.8 us (24%)
  Pallas kernels  26.9 us (10%)
  between operations  13.2 us (5%)
  local copies, waits for them, and re-layouts  8.88 us (3%)
  other arithmetic  8.73 us (3%)
    all_gather x1, waiting for transfers between devices, local(): flow_tiles = lax.all_gather(a_tiles[0, 0, 0], 'col', axis=0, tiled=True)  110 us
    reduce_scatter x1, waiting for transfers between devices, local(): lax.psum_scatter(partial_sum, 'layer', scatter_dimension=0, tiled=True)  45 us
    psum x1, blocking collectives, local(): column_total = lax.psum(local_mass, ('row', 'layer'))  29 us
    pallas_call x1, Pallas kernels, kept_partials(): pl.pallas_call(kernel, out_shape=jax.ShapeDtypeStruct((n_out, tile, tile)...  26.9 us
    all_gather x1, blocking collectives, local(): lax.all_gather(a_coords[0, 0, 0][None], 'col', axis=0, tiled=True)  24.8 us
    all_gather x1, blocking collectives, local(): lax.all_gather(out_coords[0, 0, 0][None], 'layer', axis=0, tiled=True)  9.96 us
  transfers between devices with their start and end apart: 3, of which 2 were waited for; matrix products, arithmetic and copies ran while one was open for 5% of the time, Pallas kernels for 0%

profile of v1, /device:TPU:0, one launch (start us, length us, event | category | flops | bytes accessed | tf_op | source)
XLA Modules:
  0.0 282.8 jit_solution(5400643437784938691)
XLA Ops:
  6.5 0.7 all-gather.10.cloned.1.call-update
  7.3 0.7 all-gather.8.cloned.1.call-update
  8.1 24.8 %all-gather = s32[8,1,1,32,2]{3,4,2,1,0:T(2,128)S(1)} all-gather(s32[1,1,1,32,2]{3,4,2,1,0:T(2,128)} %param.6), channel_id=2, replica_groups=mesh['row'=4,'col'=8,'layer'=4] {'col'}, dimensions={0}, use_global_device_ids=true | all-gather | bytes 2304 | tf_op jit(solution)/shard_map/all_gather | solution.py:63
  32.8 10.0 %all-gather.1 = s32[4,1,1,16,2]{3,4,2,1,0:T(2,128)S(1)} all-gather(s32[1,1,1,16,2]{3,4,2,1,0:T(2,128)} %param.9), channel_id=3, replica_groups=mesh['row'=4,'col'=8,'layer'=4] {'layer'}, dimensions={0}, use_global_device_ids=true | all-gather | bytes 640 | tf_op jit(solution)/shard_map/all_gather | solution.py:64
  43.0 0.7 iota_reduce_fusion.1
  43.8 0.1 copy.33
  43.9 0.1 reshape.112
  44.0 2.6 gather_fusion.2
  47.0 0.1 reshape.96
  47.2 5.1 %all-gather.2 = s32[4,1,1,32,2]{3,4,2,1,0:T(2,128)S(1)} all-gather(s32[1,1,1,32,2]{3,4,2,1,0:T(2,128)S(1)} %copy-done), channel_id=4, replica_groups=mesh['row'=4,'col'=8,'layer'=4] {'row'}, dimensions={0}, use_global_device_ids=true | all-gather | bytes 1280 | tf_op jit(solution)/shard_map/all_gather | solution.py:61
  52.3 2.1 gather_fusion
  54.4 0.4 fusion.10
  54.8 1.3 fusion.9
  56.1 2.9 %iota_reduce_fusion = (pred[64,8]{1,0:T(8,128)(4,1)}, s32[64,8]{1,0:T(8,128)S(1)}) fusion(pred[64,8,32]{2,1,0:T(8,128)(4,1)S(1)} %get-tuple-element.10), kind=kLoop, calls=%fused_computation.6 | loop fusion | flops 111104 | bytes 18944 | tf_op jit(solution)/shard_map/local/reduce | solution.py:73
  59.2 0.7 reshape.92.gidx_ref
  60.0 0.7 reshape.90.midx_ref
  60.7 109.7 %all-gather.8.cloned.1.call-done = bf16[1,1,1,256,128,128]{5,4,2,1,0,3:T(8,128)(2,1)} async-done(((bf16[1,1,1,32,128,128]{5,4,2,1,0,3:T(8,128)(2,1)}), bf16[1,1,1,256,128,128]{5,4,2,1,0,3:T(8,128)(2,1)}) %all-gather.8.cloned.1.call-update) | async-done | bytes 8388624 | tf_op jit(solution)/shard_map/all_gather | solution.py:62
  170.4 26.9 %shard_map.55 = f32[64,128,128]{2,1,0:T(8,128)} custom-call(s32[512]{0:T(512)} %reshape.90.midx_ref, s32[512]{0:T(512)} %reshape.92.gidx_ref, bf16[256,128,128]{2,1,0:T(8,128)(2,1)} %bitcast.40, bf16[128,128,128]{2,1,0:T(8,128)(2,1)} %bitcast.41), custom_call_target="tpu_custom_call" | custom-call | tf_op jit(solution)/shard_map/pallas_call | solution.py:35
  197.4 45.0 %reduce-scatter.2.cloned.1.call-done = f32[16,128,128]{2,1,0:T(8,128)} async-done(((f32[64,128,128]{2,1,0:T(8,128)}), f32[16,128,128]{2,1,0:T(8,128)}) %reduce-scatter.2.cloned.1.call-update) | async-done | bytes 1048592 | tf_op jit(solution)/shard_map/reduce_scatter | solution.py:90
  242.4 1.3 multiply_reduce_fusion
  243.7 0.6 scatter_custom_fusion
  244.3 29.0 %psum.7 = f32[16,128]{1,0:T(8,128)S(1)} all-reduce(f32[16,128]{1,0:T(8,128)S(1)} %scatter_custom_fusion), channel_id=1, replica_groups=mesh['row'=4,'col'=8,'layer'=4] {'row','layer'}, use_global_device_ids=true, to_apply=%region_6.7 | all-reduce | flops 2048 | bytes 16384 | tf_op jit(solution)/shard_map/psum | solution.py:96
  273.4 0.6 gather_fusion.1
  273.9 2.3 multiply_bitcast_fusion
  (39 shorter events, 1.2 us)
Async XLA Ops:
  6.5 54.2 %all-gather.10.cloned.1.call-start = ((), (), s32[]{:S(2)}) async-start(), calls=%async_computation.3 | async-start | bytes 5242880 | tf_op jit(solution)/shard_map/all_gather | solution.py:60
  7.3 163.1 %all-gather.8.cloned.1.call-start = ((), (), s32[]{:S(2)}) async-start(), calls=%async_computation.2 | async-start | bytes 9437184 | tf_op jit(solution)/shard_map/all_gather | solution.py:62
  8.0 234.4 %reduce-scatter.2.cloned.1.call-start = ((), (), s32[]{:S(2)}) async-start(), calls=%async_computation.1 | async-start | bytes 5242880 | tf_op jit(solution)/shard_map/reduce_scatter | solution.py:90
  43.9 3.3 %copy-start = (s32[1,1,1,32,2]{3,4,2,1,0:T(2,128)S(1)}, s32[1,1,1,32,2]{3,4,2,1,0:T(2,128)}, u32[]{:S(2)}) copy-start(s32[1,1,1,32,2]{3,4,2,1,0:T(2,128)} %param.8) | copy-start | bytes 772
  170.4 27.0 %copy-start.1 = (s32[1,1,1,16,2]{3,4,2,1,0:T(2,128)S(1)}, s32[1,1,1,16,2]{3,4,2,1,0:T(2,128)}, u32[]{:S(2)}) copy-start(s32[1,1,1,16,2]{3,4,2,1,0:T(2,128)} %param.9) | copy-start | bytes 388
Sparse Core Ops, SparseCore 0:
  9.0 48.6 all-gather.9
  60.0 110.3 all-gather.7
  197.5 44.8 reduce-scatter.1

commit v2 on v1

--- a/solution.py
+++ b/solution.py
@@ -45,6 +45,14 @@
     )(midx, gidx, flow_flat, graph_flat)
 
 
+def butterfly_sum(x, axis, n):
+    d = 1
+    while d < n:
+        x = x + lax.ppermute(x, axis, [(i, i ^ d) for i in range(n)])
+        d *= 2
+    return x
+
+
 def local(a_tiles, a_coords, b_tiles, b_coords, out_coords):
     tile_size = a_tiles.shape[-1]
     rows_panel = a_tiles.shape[3]
@@ -57,7 +65,12 @@
     col_tiles = out_coords.shape[3]
     n_b = b_tiles.shape[3]
 
-    graph_tiles = lax.all_gather(b_tiles[0, 0, 0], "row", axis=0, tiled=True)
+    my_row = lax.axis_index("row")
+    graph_parts = [b_tiles[0, 0, 0]] + [
+        lax.ppermute(b_tiles[0, 0, 0], "row", [(i, (i + s) % row_count) for i in range(row_count)])
+        for s in range(1, row_count)
+    ]
+    graph_tiles = jnp.concatenate(graph_parts, axis=0)
     graph_coords = lax.all_gather(b_coords[0, 0, 0][None], "row", axis=0, tiled=True)
     flow_tiles = lax.all_gather(a_tiles[0, 0, 0], "col", axis=0, tiled=True)
     flow_coords = lax.all_gather(a_coords[0, 0, 0][None], "col", axis=0, tiled=True)
@@ -80,7 +93,8 @@
     owner_coords = graph_coords[b_owner]
     match_b = (owner_coords[..., 0] == b_row[..., None]) & (owner_coords[..., 1] == kept_col[:, None, None])
     slot_b = jnp.argmax(match_b, axis=2).astype(jnp.int32)
-    gidx = jnp.where(jnp.any(match_b, axis=2), b_owner * n_b + slot_b, -1)
+    b_part = (my_row - b_owner) % row_count
+    gidx = jnp.where(jnp.any(match_b, axis=2), b_part * n_b + slot_b, -1)
 
     flow_flat = flow_tiles.reshape(-1, tile_size, tile_size)
     graph_flat = graph_tiles.reshape(-1, tile_size, tile_size)
@@ -93,7 +107,7 @@
     squared = kept_tiles * kept_tiles
     column_part = jnp.sum(squared, axis=1)
     local_mass = jnp.zeros_like(column_part).at[kept_cols].set(column_part)
-    column_total = lax.psum(local_mass, ("row", "layer"))
+    column_total = butterfly_sum(butterfly_sum(local_mass, "row", row_count), "layer", layer_count)
     factor = jnp.float32(row_count * layer_count * tile_size) / column_total
     flow = squared * factor[kept_cols][:, None, :]
     return flow.reshape(1, 1, 1, col_tiles, tile_size, tile_size)

time: 283 us -> 231 us (0.82)
  waiting for transfers between devices: 156 us -> 73.6 us
  blocking collectives: 68.8 us -> 88.5 us
  starting transfers between devices: 0.08 us -> 6.92 us
  other arithmetic: 8.73 us -> 12.9 us
    all_gather x1, waiting for transfers between devices: 110 us -> 17.9 us  [local(): flow_tiles = lax.all_gather(a_tiles[0, 0, 0], 'col', axis=0, tiled=True)]
    all_gather x1, blocking collectives: 24.8 us -> 73.4 us  [local(): lax.all_gather(a_coords[0, 0, 0][None], 'col', axis=0, tiled=True)]
    psum x1 -> x0, blocking collectives: 29 us -> none  [local(): column_total = lax.psum(local_mass, ('row', 'layer'))]
    ppermute x0 -> x7, waiting for transfers between devices: none -> 10.4 us  [the longest x4 10.3 us: butterfly_sum(): x = x + lax.ppermute(x, axis, [(i, i ^ d) for i in range(n)])]
    ppermute x0 -> x7, starting transfers between devices: none -> 6.88 us  [the longest x3 3.53 us: local(): lax.ppermute(b_tiles[0, 0, 0], 'row', [(i, (i + s) % row_count) for i in...]
    concatenate x0 -> x1, other arithmetic: none -> 4.15 us  [local(): graph_tiles = jnp.concatenate(graph_parts, axis=0)]
  transfers between devices with their start and end apart: 3 -> 9, of which waited for: 2 -> 6; matrix products, arithmetic and copies ran while one was open for 5% -> 7% of each run, Pallas kernels for 0% -> 0%
where the time goes in v2:
time: 231 us
  blocking collectives  88.5 us (38%)
  waiting for transfers between devices  73.6 us (32%)
  Pallas kernels  26.3 us (11%)
  between operations  13.5 us (6%)
  other arithmetic  12.9 us (6%)
  local copies, waits for them, and re-layouts  9.54 us (4%)
  starting transfers between devices  6.92 us (3%)
    all_gather x1, blocking collectives, local(): lax.all_gather(a_coords[0, 0, 0][None], 'col', axis=0, tiled=True)  73.4 us
    reduce_scatter x1, waiting for transfers between devices, local(): lax.psum_scatter(partial_sum, 'layer', scatter_dimension=0, tiled=True)  44.6 us
    pallas_call x1, Pallas kernels, kept_partials(): pl.pallas_call(kernel, out_shape=jax.ShapeDtypeStruct((n_out, tile, tile)...  26.3 us
    all_gather x1, waiting for transfers between devices, local(): flow_tiles = lax.all_gather(a_tiles[0, 0, 0], 'col', axis=0, tiled=True)  17.9 us
    ppermute x4, waiting for transfers between devices, butterfly_sum(): x = x + lax.ppermute(x, axis, [(i, i ^ d) for i in range(n)])  10.3 us
    all_gather x1, blocking collectives, local(): lax.all_gather(out_coords[0, 0, 0][None], 'layer', axis=0, tiled=True)  10 us
    all_gather x1, blocking collectives, local(): lax.all_gather(b_coords[0, 0, 0][None], 'row', axis=0, tiled=True)  5.06 us
  transfers between devices with their start and end apart: 9, of which 6 were waited for; matrix products, arithmetic and copies ran while one was open for 7% of the time, Pallas kernels for 0%

profile of v2, /device:TPU:0, one launch (start us, length us, event | category | flops | bytes accessed | tf_op | source)
XLA Modules:
  0.0 231.3 jit_solution(3919857341761460753)
XLA Ops:
  6.5 0.7 all-gather.6.cloned.1.call-update
  7.4 2.1 collective-permute-start.1
  9.5 1.4 collective-permute-start.2
  10.8 73.4 %all-gather = s32[8,1,1,32,2]{3,4,2,1,0:T(2,128)S(1)} all-gather(s32[1,1,1,32,2]{3,4,2,1,0:T(2,128)} %param.6), channel_id=2, replica_groups=mesh['row'=4,'col'=8,'layer'=4] {'col'}, dimensions={0}, use_global_device_ids=true | all-gather | bytes 2304 | tf_op jit(solution)/shard_map/all_gather | solution.py:76
  84.3 10.0 %all-gather.1 = s32[4,1,1,16,2]{3,4,2,1,0:T(2,128)S(1)} all-gather(s32[1,1,1,16,2]{3,4,2,1,0:T(2,128)} %param.9), channel_id=3, replica_groups=mesh['row'=4,'col'=8,'layer'=4] {'layer'}, dimensions={0}, use_global_device_ids=true | all-gather | bytes 640 | tf_op jit(solution)/shard_map/all_gather | solution.py:77
  94.6 0.7 iota_reduce_fusion.1
  95.5 2.6 %gather_fusion.2 = s32[512]{0:T(512)S(1)} fusion(s32[8,32]{1,0:T(8,128)S(1)} %get-tuple-element.15, s32[512]{0:T(512)S(1)} %reshape.112), kind=kCustom, calls=%fused_computation.2 | custom fusion | bytes 8192 | tf_op jit(solution)/shard_map/jit(take_along_axis)/gather | solution.py:89
  98.8 5.1 %all-gather.2 = s32[4,1,1,32,2]{3,4,2,1,0:T(2,128)S(1)} all-gather(s32[1,1,1,32,2]{3,4,2,1,0:T(2,128)S(1)} %copy-done.1), channel_id=4, replica_groups=mesh['row'=4,'col'=8,'layer'=4] {'row'}, dimensions={0}, use_global_device_ids=true | all-gather | bytes 1280 | tf_op jit(solution)/shard_map/all_gather | solution.py:74
  103.8 2.1 gather_fusion
  106.3 1.3 fusion.13
  107.7 2.9 %iota_reduce_fusion = (pred[64,8]{1,0:T(8,128)(4,1)}, s32[64,8]{1,0:T(8,128)S(1)}) fusion(pred[64,8,32]{2,1,0:T(8,128)(4,1)S(1)} %get-tuple-element.10), kind=kLoop, calls=%fused_computation.7 | loop fusion | flops 111104 | bytes 18944 | tf_op jit(solution)/shard_map/local/reduce | solution.py:86
  110.8 0.7 reshape.92.gidx_ref
  112.3 4.2 %pad_maximum_fusion.graph_ref = bf16[128,128,128]{2,1,0:T(8,128)(2,1)} fusion(bf16[32,128,128]{2,1,0:T(8,128)(2,1)} %collective-permute-done.2, bf16[32,128,128]{2,1,0:T(8,128)(2,1)} %collective-permute-done.1, bf16[32,128,128]{2,1,0:T(8,128)(2,1)S(1)} %collective-permute-done, bf16[32,128,128]{2,1,0:T(8,128)(2,1)S(1)} %bitcast.46), kind=kLoop, calls=%fused_computation.4 | loop fusion | flops 6291456 | bytes 8388608 | tf_op jit(solution)/shard_map/concatenate | solution.py:73
  116.4 17.9 %all-gather.6.cloned.1.call-done = bf16[1,1,1,256,128,128]{5,4,2,1,0,3:T(8,128)(2,1)} async-done(((bf16[1,1,1,32,128,128]{5,4,2,1,0,3:T(8,128)(2,1)}), bf16[1,1,1,256,128,128]{5,4,2,1,0,3:T(8,128)(2,1)}) %all-gather.6.cloned.1.call-update) | async-done | bytes 8388624 | tf_op jit(solution)/shard_map/all_gather | solution.py:75
  134.3 26.3 %shard_map.55 = f32[64,128,128]{2,1,0:T(8,128)} custom-call(s32[512]{0:T(512)} %reshape.90.midx_ref, s32[512]{0:T(512)} %reshape.92.gidx_ref, bf16[256,128,128]{2,1,0:T(8,128)(2,1)} %bitcast.39, bf16[128,128,128]{2,1,0:T(8,128)(2,1)} %pad_maximum_fusion.graph_ref), custom_call_target="tpu_custom_call" | custom-call | tf_op jit(solution)/shard_map/pallas_call | solution.py:35
  161.3 44.6 %reduce-scatter.2.cloned.1.call-done = f32[16,128,128]{2,1,0:T(8,128)} async-done(((f32[64,128,128]{2,1,0:T(8,128)}), f32[16,128,128]{2,1,0:T(8,128)}) %reduce-scatter.2.cloned.1.call-update) | async-done | bytes 1048592 | tf_op jit(solution)/shard_map/reduce_scatter | solution.py:104
  205.9 1.3 multiply_reduce_fusion
  208.0 1.2 collective-permute-done.3
  209.1 1.6 collective-permute-start.4
  210.7 2.1 collective-permute-done.4
  213.0 3.4 %collective-permute-done.5 = f32[16,128]{1,0:T(8,128)S(1)} collective-permute-done((f32[16,128]{1,0:T(8,128)S(1)}, f32[16,128]{1,0:T(8,128)S(1)}, u32[]{:S(2)}, u32[]{:S(2)}) %collective-permute-start.5) | collective-permute-done | bytes 8224 | tf_op jit(solution)/shard_map/ppermute | solution.py:51
  216.5 1.5 collective-permute-start.6
  217.9 3.7 %collective-permute-done.6 = f32[16,128]{1,0:T(8,128)S(1)} collective-permute-done((f32[16,128]{1,0:T(8,128)S(1)}, f32[16,128]{1,0:T(8,128)S(1)}, u32[]{:S(2)}, u32[]{:S(2)}) %collective-permute-start.6) | collective-permute-done | bytes 8224 | tf_op jit(solution)/shard_map/ppermute | solution.py:51
  222.2 2.3 %multiply_bitcast_fusion = f32[1,1,1,16,128,128]{5,4,3,2,1,0:T(8,128)} fusion(f32[16,128,128]{2,1,0:T(8,128)} %reduce-scatter.2.cloned.1.call-done, f32[16,128]{1,0:T(8,128)S(1)} %gather_fusion.1), kind=kLoop, calls=%fused_computation.5 | loop fusion | flops 524288 | bytes 2105344 | tf_op jit(solution)/shard_map/reshape | solution.py:113
  (55 shorter events, 4.8 us)
Async XLA Ops:
  6.5 127.8 %all-gather.6.cloned.1.call-start = ((), (), s32[]{:S(2)}) async-start(), calls=%async_computation.2 | async-start | bytes 9437184 | tf_op jit(solution)/shard_map/all_gather | solution.py:75
  7.3 198.7 %reduce-scatter.2.cloned.1.call-start = ((), (), s32[]{:S(2)}) async-start(), calls=%async_computation.1 | async-start | bytes 5242880 | tf_op jit(solution)/shard_map/reduce_scatter | solution.py:104
  7.3 105.0 %collective-permute-start = (bf16[32,128,128]{2,1,0:T(8,128)(2,1)}, bf16[32,128,128]{2,1,0:T(8,128)(2,1)S(1)}, u32[]{:S(2)}, u32[]{:S(2)}) collective-permute-start(bf16[32,128,128]{2,1,0:T(8,128)(2,1)} %bitcast.43), channel_id=1, source_target_pairs={{0,32},{32,64},{64,96},{96,0},{1,33},{33,65},{65,97},{97,1},{2,34}... | collective-permute-start | bytes 3145736 | tf_op jit(solution)/shard_map/ppermute | solution.py:70
  7.4 104.9 %collective-permute-start.1 = (bf16[32,128,128]{2,1,0:T(8,128)(2,1)}, bf16[32,128,128]{2,1,0:T(8,128)(2,1)}, u32[]{:S(2)}, u32[]{:S(2)}) collective-permute-start(bf16[32,128,128]{2,1,0:T(8,128)(2,1)} %bitcast.44), channel_id=1, source_target_pairs={{0,64},{32,96},{64,0},{96,32},{1,65},{33,97},{65,1},{97,33},{2,66}... | collective-permute-start | bytes 3145736 | tf_op jit(solution)/shard_map/ppermute | solution.py:70
  9.5 102.8 %collective-permute-start.2 = (bf16[32,128,128]{2,1,0:T(8,128)(2,1)}, bf16[32,128,128]{2,1,0:T(8,128)(2,1)}, u32[]{:S(2)}, u32[]{:S(2)}) collective-permute-start(bf16[32,128,128]{2,1,0:T(8,128)(2,1)} %bitcast.45), channel_id=1, source_target_pairs={{0,96},{32,0},{64,32},{96,64},{1,97},{33,1},{65,33},{97,65},{2,98}... | collective-permute-start | bytes 3145736 | tf_op jit(solution)/shard_map/ppermute | solution.py:70
  95.5 3.3 %copy-start.1 = (s32[1,1,1,32,2]{3,4,2,1,0:T(2,128)S(1)}, s32[1,1,1,32,2]{3,4,2,1,0:T(2,128)}, u32[]{:S(2)}) copy-start(s32[1,1,1,32,2]{3,4,2,1,0:T(2,128)} %param.8) | copy-start | bytes 772
  103.8 8.4 %copy-start = (bf16[1,1,1,32,128,128]{5,4,3,2,1,0:T(8,128)(2,1)S(1)}, bf16[1,1,1,32,128,128]{5,4,3,2,1,0:T(8,128)(2,1)}, u32[]{:S(2)}) copy-start(bf16[1,1,1,32,128,128]{5,4,3,2,1,0:T(8,128)(2,1)} %param.7) | copy-start | bytes 3145732
  160.6 0.7 copy-start.2
  207.9 1.3 collective-permute-start.3
  209.1 3.7 %collective-permute-start.4 = (f32[16,128]{1,0:T(8,128)S(1)}, f32[16,128]{1,0:T(8,128)S(1)}, u32[]{:S(2)}, u32[]{:S(2)}) collective-permute-start(f32[16,128]{1,0:T(8,128)S(1)} %add.99), channel_id=1, source_target_pairs={{0,64},{32,96},{64,0},{96,32},{1,65},{33,97},{65,1},{97,33},{2,66}... | collective-permute-start | bytes 24584 | tf_op jit(solution)/shard_map/ppermute | solution.py:51
  212.8 3.7 %collective-permute-start.5 = (f32[16,128]{1,0:T(8,128)S(1)}, f32[16,128]{1,0:T(8,128)S(1)}, u32[]{:S(2)}, u32[]{:S(2)}) collective-permute-start(f32[16,128]{1,0:T(8,128)S(1)} %add.100), channel_id=1, source_target_pairs={{0,1},{1,0},{2,3},{3,2},{4,5},{5,4},{6,7},{7,6},{8,9},{9,8},{10,11... | collective-permute-start | bytes 24584 | tf_op jit(solution)/shard_map/ppermute | solution.py:51
  216.5 5.2 %collective-permute-start.6 = (f32[16,128]{1,0:T(8,128)S(1)}, f32[16,128]{1,0:T(8,128)S(1)}, u32[]{:S(2)}, u32[]{:S(2)}) collective-permute-start(f32[16,128]{1,0:T(8,128)S(1)} %add.101), channel_id=1, source_target_pairs={{0,2},{1,3},{2,0},{3,1},{4,6},{5,7},{6,4},{7,5},{8,10},{9,11},{10,... | collective-permute-start | bytes 24584 | tf_op jit(solution)/shard_map/ppermute | solution.py:51
Sparse Core Ops, SparseCore 0:
  9.7 124.5 all-gather.5
  160.8 45.1 reduce-scatter.1

commit v3 on v2

v3 whole, which is shorter than its diff:
```python
import functools

import jax
import jax.numpy as jnp
from jax import lax
from jax.experimental import pallas as pl
from jax.experimental.pallas import tpu as pltpu
from jax.sharding import PartitionSpec as P

KA = 4
PAD = 16


def kept_partial_kernel(mrow_ref, grow_ref, flow_ref, graph_ref, out_ref, *, n_out, n_grp, m_stride):
    tile = out_ref.shape[-1]

    def body(t, carry):
        out_ref[t] = jnp.zeros((tile, tile), jnp.float32)
        m_off = mrow_ref[t]
        for c in range(n_grp):
            g_off = grow_ref[t * n_grp + c]

            @pl.when(g_off >= 0)
            def _():
                left = flow_ref[pl.ds(pl.multiple_of(c * m_stride + m_off, PAD), tile), :]
                right = graph_ref[pl.ds(pl.multiple_of(g_off, PAD), tile), :]
                out_ref[t] += jnp.dot(left, right, preferred_element_type=jnp.float32)

        return carry

    lax.fori_loop(0, n_out, body, 0)


def kept_partials(mrow, grow, flow_flat, graph_flat, n_out, n_grp, m_stride):
    tile = flow_flat.shape[-1]
    kernel = functools.partial(kept_partial_kernel, n_out=n_out, n_grp=n_grp, m_stride=m_stride)
    return pl.pallas_call(
        kernel,
        out_shape=jax.ShapeDtypeStruct((n_out, tile, tile), jnp.float32),
        in_specs=[
            pl.BlockSpec(memory_space=pltpu.SMEM),
            pl.BlockSpec(memory_space=pltpu.SMEM),
            pl.BlockSpec(memory_space=pltpu.VMEM),
            pl.BlockSpec(memory_space=pltpu.VMEM),
        ],
        out_specs=pl.BlockSpec(memory_space=pltpu.VMEM),
        cost_estimate=pl.CostEstimate(
            flops=2 * n_out * n_grp * tile**3,
            transcendentals=0,
            bytes_accessed=2 * (flow_flat.size + graph_flat.size) + 4 * n_out * tile * tile,
        ),
    )(mrow, grow, flow_flat, graph_flat)


def butterfly_sum(x, axis, n):
    d = 1
    while d < n:
        x = x + lax.ppermute(x, axis, [(i, i ^ d) for i in range(n)])
        d *= 2
    return x


def shifted(x, axis, n):
    return [x] + [lax.ppermute(x, axis, [(i, (i + s) % n) for i in range(n)]) for s in range(1, n)]


def pack_rows(tiles, rows):
    tile = tiles.shape[-1]
    extra = jnp.zeros((PAD, tile), jnp.bfloat16)
    extra = extra.at[: rows.shape[0], : rows.shape[1]].set(rows.astype(jnp.bfloat16))
    return jnp.concatenate([tiles.reshape(-1, tile), extra], axis=0)


def local(a_tiles, a_coords, b_tiles, b_coords, out_coords):
    tile = a_tiles.shape[-1]
    rows_panel = a_tiles.shape[3]
    col_count = lax.axis_size("col")
    row_count = lax.axis_size("row")
    layer_count = lax.axis_size("layer")
    b_span = KA * col_count // row_count
    quarter = rows_panel // layer_count
    col_tiles = out_coords.shape[3]
    n_b = b_tiles.shape[3]
    my_row = lax.axis_index("row")
    my_layer = lax.axis_index("layer")

    graph_parts = shifted(pack_rows(b_tiles[0, 0, 0], b_coords[0, 0, 0].T), "row", row_count)
    g_stride = n_b * tile + PAD
    graph_flat = jnp.concatenate(graph_parts, axis=0)
    graph_coords = jnp.stack([p[n_b * tile : n_b * tile + 2, :n_b] for p in graph_parts]).astype(jnp.int32)
    kept_parts = jnp.stack(shifted(out_coords[0, 0, 0], "layer", layer_count))

    a_rows = a_coords[0, 0, 0, :, 0]
    a_inner = a_coords[0, 0, 0, :, 1]
    row_ids = jnp.arange(rows_panel, dtype=jnp.int32)
    slot_of_row = jnp.argmax(a_rows[None, :] == row_ids[:, None], axis=1).astype(jnp.int32)
    grp = jnp.arange(col_count, dtype=jnp.int32)
    m_stride = quarter * tile + PAD

    total = None
    for s in range(1, layer_count + 1):
        q = (my_layer + s) % layer_count
        slots = lax.dynamic_slice_in_dim(slot_of_row, q * quarter, quarter)
        packed = pack_rows(a_tiles[0, 0, 0][slots], a_inner[slots][None, :])
        flow_all = lax.all_gather(packed, "col", axis=0, tiled=False)
        inner_all = flow_all[:, quarter * tile, :quarter].astype(jnp.int32)
        kept_q = kept_parts[(my_layer - q) % layer_count]
        kept_r = kept_q[:, 0]
        kept_c = kept_q[:, 1]
        inner = inner_all[:, kept_r].T
        k_layer = grp[None, :] * KA + inner
        b_owner = k_layer // b_span
        b_row = k_layer % b_span
        b_part = (my_row - b_owner) % row_count
        owner_coords = graph_coords[b_part]
        match_b = (owner_coords[:, :, 0, :] == b_row[..., None]) & (owner_coords[:, :, 1, :] == kept_c[:, None, None])
        slot_b = jnp.argmax(match_b, axis=2).astype(jnp.int32)
        grow = jnp.where(jnp.any(match_b, axis=2), b_part * g_stride + slot_b * tile, -1)
        partial = kept_partials(
            (kept_r * tile).astype(jnp.int32),
            grow.reshape(-1).astype(jnp.int32),
            flow_all.reshape(-1, tile),
            graph_flat,
            col_tiles,
            col_count,
            m_stride,
        )
        if s < layer_count:
            partial = lax.ppermute(partial, "layer", [(i, (i + s) % layer_count) for i in range(layer_count)])
        total = partial if total is None else total + partial

    kept_cols = out_coords[0, 0, 0, :, 1]
    squared = total * total
    column_part = jnp.sum(squared, axis=1)
    local_mass = jnp.zeros_like(column_part).at[kept_cols].set(column_part)
    column_total = butterfly_sum(butterfly_sum(local_mass, "row", row_count), "layer", layer_count)
    factor = jnp.float32(row_count * layer_count * tile) / column_total
    flow = squared * factor[kept_cols][:, None, :]
    return flow.reshape(1, 1, 1, col_tiles, tile, tile)


def solution(mesh):
    in_specs = (
        P("row", "col", "layer", None, None, None),
        P("row", "col", "layer", None, None),
        P("row", "col", "layer", None, None, None),
        P("row", "col", "layer", None, None),
        P("row", "col", "layer", None, None),
    )
    out_specs = P("row", "col", "layer", None, None, None)
    return jax.shard_map(local, mesh=mesh, in_specs=in_specs, out_specs=out_specs, check_vma=False)
```

time: 231 us -> 359 us (1.55)
  waiting for transfers between devices: 73.6 us -> 256 us
  blocking collectives: 88.5 us -> 0 us
  local copies, waits for them, and re-layouts: 9.54 us -> 24.4 us
  Pallas kernels: 26.3 us -> 36.6 us
  other arithmetic: 12.9 us -> 17.2 us
  starting transfers between devices: 6.92 us -> 10.9 us
    all_gather x1 -> x4, waiting for transfers between devices: 17.9 us -> 160 us  [local(): flow_all = lax.all_gather(packed, 'col', axis=0, tiled=False)]
    all_gather x3 -> x0, blocking collectives: 88.5 us -> none  [the longest x1 73.4 us: local(): lax.all_gather(a_coords[0, 0, 0][None], 'col', axis=0, tiled=True)]
    ppermute x3 -> x9, waiting for transfers between devices: 0.01 us -> 82.9 us  [the longest x6 56.3 us: shifted(): lax.ppermute(x, axis, [(i, (i + s) % n) for i in range(n)])]
    reduce_scatter x1 -> x0, waiting for transfers between devices: 44.6 us -> none  [local(): lax.psum_scatter(partial_sum, 'layer', scatter_dimension=0, tiled=True)]
    pallas_call x1 -> x4, Pallas kernels: 26.3 us -> 36.6 us  [kept_partials(): pl.pallas_call(kernel, out_shape=jax.ShapeDtypeStruct((n_out, tile, tile)...]
    ppermute x3 -> x9, starting transfers between devices: 3.53 us -> 10.7 us  [the longest x6 6.81 us: shifted(): lax.ppermute(x, axis, [(i, (i + s) % n) for i in range(n)])]
    gather x6 -> x16, local copies, waits for them, and re-layouts: 5.03 us -> 10.2 us  [the longest x8 4.97 us: local(): packed = pack_rows(a_tiles[0, 0, 0][slots], a_inner[slots][None, :])]
    unnamed x7 -> x14, local copies, waits for them, and re-layouts: 0.66 us -> 4.83 us
  transfers between devices with their start and end apart: 9 -> 17, of which waited for: 6 -> 11; matrix products, arithmetic and copies ran while one was open for 7% -> 5% of each run, Pallas kernels for 0% -> 8%
where the time goes in v3:
time: 359 us
  waiting for transfers between devices  256 us (71%)
  Pallas kernels  36.6 us (10%)
  local copies, waits for them, and re-layouts  24.4 us (7%)
  other arithmetic  17.2 us (5%)
  between operations  13.6 us (4%)
  starting transfers between devices  10.9 us (3%)
    all_gather x4, waiting for transfers between devices, local(): flow_all = lax.all_gather(packed, 'col', axis=0, tiled=False)  160 us
    ppermute x6, waiting for transfers between devices, shifted(): lax.ppermute(x, axis, [(i, (i + s) % n) for i in range(n)])  56.3 us
    pallas_call x4, Pallas kernels, kept_partials(): pl.pallas_call(kernel, out_shape=jax.ShapeDtypeStruct((n_out, tile, tile)...  36.6 us
    ppermute x3, waiting for transfers between devices, local(): lax.ppermute(partial, 'layer', [(i, (i + s) % layer_count) for i in range...  26.6 us
    ppermute x4, waiting for transfers between devices, butterfly_sum(): x = x + lax.ppermute(x, axis, [(i, i ^ d) for i in range(n)])  13.6 us
  transfers between devices with their start and end apart: 17, of which 11 were waited for; matrix products, arithmetic and copies ran while one was open for 5% of the time, Pallas kernels for 8%

profile of v3, /device:TPU:0, one launch (start us, length us, event | category | flops | bytes accessed | tf_op | source)
XLA Modules:
  0.0 358.7 jit_solution(12519269480949657298)
XLA Ops:
  14.3 2.9 collective-permute-start.2
  22.2 1.4 collective-permute-start.4
  28.3 22.7 %collective-permute-done.5 = bf16[4112,128]{1,0:T(8,128)(2,1)S(1)} collective-permute-done((bf16[4112,128]{1,0:T(8,128)(2,1)}, bf16[4112,128]{1,0:T(8,128)(2,1)S(1)}, u32[]{:S(2)}, u32[]{:S(2)}) %collective-permute-start.5) | collective-permute-done | bytes 1052704 | tf_op jit(solution)/shard_map/ppermute | solution.py:64
  51.0 33.6 %collective-permute-done.4 = bf16[4112,128]{1,0:T(8,128)(2,1)S(1)} collective-permute-done((bf16[4112,128]{1,0:T(8,128)(2,1)}, bf16[4112,128]{1,0:T(8,128)(2,1)S(1)}, u32[]{:S(2)}, u32[]{:S(2)}) %collective-permute-start.4) | collective-permute-done | bytes 1052704 | tf_op jit(solution)/shard_map/ppermute | solution.py:64
  88.6 48.9 %all-gather.11.cloned.1.call-done.flow_ref = bf16[8320,128]{1,0:T(8,128)(2,1)} async-done(((bf16[1040,128]{1,0:T(8,128)(2,1)}), bf16[8320,128]{1,0:T(8,128)(2,1)}) %all-gather.11.cloned.1.call-update) | async-done | bytes 2129936 | tf_op jit(solution)/shard_map/all_gather | solution.py:105
  138.3 55.4 %all-gather.15.cloned.1.call-done.flow_ref = bf16[8320,128]{1,0:T(8,128)(2,1)} async-done(((bf16[1040,128]{1,0:T(8,128)(2,1)}), bf16[8320,128]{1,0:T(8,128)(2,1)}) %all-gather.15.cloned.1.call-update) | async-done | bytes 2129936 | tf_op jit(solution)/shard_map/all_gather | solution.py:105
  194.5 55.2 %all-gather.9.cloned.1.call-done.flow_ref = bf16[8320,128]{1,0:T(8,128)(2,1)} async-done(((bf16[1040,128]{1,0:T(8,128)(2,1)}), bf16[8320,128]{1,0:T(8,128)(2,1)}) %all-gather.9.cloned.1.call-update) | async-done | bytes 2129936 | tf_op jit(solution)/shard_map/all_gather | solution.py:105
  252.5 1.2 iota_reduce_fusion.3
  256.3 1.2 iota_reduce_fusion.2
  259.5 1.2 iota_reduce_fusion.1
  262.2 1.2 iota_reduce_fusion
  264.0 9.2 %shard_map.57 = f32[16,128,128]{2,1,0:T(8,128)} custom-call(s32[16]{0:T(128)} %get-tuple-element.113.mrow_ref, s32[128]{0:T(128)} %reshape.285.grow_ref, bf16[8320,128]{1,0:T(8,128)(2,1)} %all-gather.13.cloned.1.call-done.flow_ref, bf16[16448,128]{1,0:T(8,128)(2,1)} %constant_dynamic-update-slice_fusion.graph_ref), custom_call_target="tpu_custom_call" | custom-call | flops 536870912 | bytes 7389184 | tf_op jit(solution)/shard_map/pallas_call | solution.py:37
  273.3 1.7 collective-permute-start.8
  275.5 8.2 %shard_map.55 = f32[16,128,128]{2,1,0:T(8,128)} custom-call(s32[16]{0:T(128)} %get-tuple-element.110.mrow_ref, s32[128]{0:T(128)} %reshape.279.grow_ref, bf16[8320,128]{1,0:T(8,128)(2,1)} %all-gather.9.cloned.1.call-done.flow_ref, bf16[16448,128]{1,0:T(8,128)(2,1)} %constant_dynamic-update-slice_fusion.graph_ref), custom_call_target="tpu_custom_call" | custom-call | flops 536870912 | bytes 7389184 | tf_op jit(solution)/shard_map/pallas_call | solution.py:37
  284.8 9.6 %shard_map.56 = f32[16,128,128]{2,1,0:T(8,128)} custom-call(s32[16]{0:T(128)} %get-tuple-element.107.mrow_ref, s32[128]{0:T(128)} %reshape.282.grow_ref, bf16[8320,128]{1,0:T(8,128)(2,1)} %all-gather.11.cloned.1.call-done.flow_ref, bf16[16448,128]{1,0:T(8,128)(2,1)} %constant_dynamic-update-slice_fusion.graph_ref), custom_call_target="tpu_custom_call" | custom-call | flops 536870912 | bytes 7389184 | tf_op jit(solution)/shard_map/pallas_call | solution.py:37
  294.4 1.7 collective-permute-start.7
  296.7 9.6 %shard_map.58 = f32[16,128,128]{2,1,0:T(8,128)} custom-call(s32[16]{0:T(128)} %get-tuple-element.116.mrow_ref, s32[128]{0:T(128)} %reshape.288.grow_ref, bf16[8320,128]{1,0:T(8,128)(2,1)} %all-gather.15.cloned.1.call-done.flow_ref, bf16[16448,128]{1,0:T(8,128)(2,1)} %constant_dynamic-update-slice_fusion.graph_ref), custom_call_target="tpu_custom_call" | custom-call | flops 536870912 | bytes 7389184 | tf_op jit(solution)/shard_map/pallas_call | solution.py:37
  306.3 13.8 %collective-permute-done.8 = f32[16,128,128]{2,1,0:T(8,128)S(1)} collective-permute-done((f32[16,128,128]{2,1,0:T(8,128)}, f32[16,128,128]{2,1,0:T(8,128)S(1)}, u32[]{:S(2)}, u32[]{:S(2)}) %collective-permute-start.8) | collective-permute-done | bytes 1048608 | tf_op jit(solution)/shard_map/ppermute | solution.py:129
  320.1 12.8 %collective-permute-done.6 = f32[16,128,128]{2,1,0:T(8,128)S(1)} collective-permute-done((f32[16,128,128]{2,1,0:T(8,128)}, f32[16,128,128]{2,1,0:T(8,128)S(1)}, u32[]{:S(2)}, u32[]{:S(2)}) %collective-permute-start.6) | collective-permute-done | bytes 1048608 | tf_op jit(solution)/shard_map/ppermute | solution.py:129
  333.9 2.2 fusion.35
  336.9 1.2 collective-permute-done.9
  338.0 3.6 %collective-permute-done.10 = f32[16,128]{1,0:T(8,128)S(1)} collective-permute-done((f32[16,128]{1,0:T(8,128)S(1)}, f32[16,128]{1,0:T(8,128)S(1)}, u32[]{:S(2)}, u32[]{:S(2)}) %collective-permute-start.10) | collective-permute-done | bytes 8224 | tf_op jit(solution)/shard_map/ppermute | solution.py:58
  341.7 3.6 %collective-permute-done.11 = f32[16,128]{1,0:T(8,128)S(1)} collective-permute-done((f32[16,128]{1,0:T(8,128)S(1)}, f32[16,128]{1,0:T(8,128)S(1)}, u32[]{:S(2)}, u32[]{:S(2)}) %collective-permute-start.11) | collective-permute-done | bytes 8224 | tf_op jit(solution)/shard_map/ppermute | solution.py:58
  345.3 5.1 %collective-permute-done.12 = f32[16,128]{1,0:T(8,128)S(1)} collective-permute-done((f32[16,128]{1,0:T(8,128)S(1)}, f32[16,128]{1,0:T(8,128)S(1)}, u32[]{:S(2)}, u32[]{:S(2)}) %collective-permute-start.12) | collective-permute-done | bytes 8224 | tf_op jit(solution)/shard_map/ppermute | solution.py:58
  (127 shorter events, 37.6 us)
Async XLA Ops:
  6.5 2.2 copy-start
  6.5 81.3 %all-gather.13.cloned.1.call-start = ((), (), s32[]{:S(2)}) async-start(), calls=%async_computation.2 | async-start | bytes 2396160 | tf_op jit(solution)/shard_map/all_gather | solution.py:105
  9.3 5.0 %copy-start.4 = (s32[1,1,1,16,2]{3,4,2,1,0:T(2,128)S(1)}, s32[1,1,1,16,2]{3,4,2,1,0:T(2,128)}, u32[]{:S(2)}) copy-start(s32[1,1,1,16,2]{3,4,2,1,0:T(2,128)} %param.19) | copy-start | bytes 388
  9.3 9.6 %copy-start.3 = (s32[1,1,1,32,2]{3,4,2,1,0:T(2,128)S(1)}, s32[1,1,1,32,2]{3,4,2,1,0:T(2,128)}, u32[]{:S(2)}) copy-start(s32[1,1,1,32,2]{3,4,2,1,0:T(2,128)} %param.18) | copy-start | bytes 772
  10.1 8.9 %copy-start.1 = (bf16[1,1,1,32,128,128]{5,4,3,2,1,0:T(8,128)(2,1)S(1)}, bf16[1,1,1,32,128,128]{5,4,3,2,1,0:T(8,128)(2,1)}, u32[]{:S(2)}) copy-start(bf16[1,1,1,32,128,128]{5,4,3,2,1,0:T(8,128)(2,1)} %param.17) | copy-start | bytes 3145732
  10.1 127.4 %all-gather.11.cloned.1.call-start = ((), (), s32[]{:S(2)}) async-start(), calls=%async_computation.1 | async-start | bytes 2396160 | tf_op jit(solution)/shard_map/all_gather | solution.py:105
  12.2 181.5 %all-gather.15.cloned.1.call-start = ((), (), s32[]{:S(2)}) async-start(), calls=%async_computation.3 | async-start | bytes 2396160 | tf_op jit(solution)/shard_map/all_gather | solution.py:105
  14.3 235.5 %all-gather.9.cloned.1.call-start = ((), (), s32[]{:S(2)}) async-start(), calls=%async_computation | async-start | bytes 2396160 | tf_op jit(solution)/shard_map/all_gather | solution.py:105
  14.3 11.4 %collective-permute-start.2 = (s32[16,2]{0,1:T(2,128)S(1)}, s32[16,2]{0,1:T(2,128)S(1)}, u32[]{:S(2)}, u32[]{:S(2)}) collective-permute-start(s32[16,2]{0,1:T(2,128)S(1)} %bitcast.144), channel_id=1, source_target_pairs={{0,3},{1,0},{2,1},{3,2},{4,7},{5,4},{6,5},{7,6},{8,11},{9,8},{10,9... | collective-permute-start | bytes 392 | tf_op jit(solution)/shard_map/ppermute | solution.py:64
  17.2 8.8 %collective-permute-start.1 = (s32[16,2]{0,1:T(2,128)S(1)}, s32[16,2]{0,1:T(2,128)S(1)}, u32[]{:S(2)}, u32[]{:S(2)}) collective-permute-start(s32[16,2]{0,1:T(2,128)S(1)} %bitcast.145), channel_id=1, source_target_pairs={{0,2},{1,3},{2,0},{3,1},{4,6},{5,7},{6,4},{7,5},{8,10},{9,11},{10,... | collective-permute-start | bytes 392 | tf_op jit(solution)/shard_map/ppermute | solution.py:64
  18.0 8.0 %collective-permute-start = (s32[16,2]{0,1:T(2,128)S(1)}, s32[16,2]{0,1:T(2,128)S(1)}, u32[]{:S(2)}, u32[]{:S(2)}) collective-permute-start(s32[16,2]{0,1:T(2,128)S(1)} %bitcast.146), channel_id=1, source_target_pairs={{0,1},{1,2},{2,3},{3,0},{4,5},{5,6},{6,7},{7,4},{8,9},{9,10},{10,1... | collective-permute-start | bytes 392 | tf_op jit(solution)/shard_map/ppermute | solution.py:64
  21.7 29.3 %collective-permute-start.5 = (bf16[4112,128]{1,0:T(8,128)(2,1)}, bf16[4112,128]{1,0:T(8,128)(2,1)S(1)}, u32[]{:S(2)}, u32[]{:S(2)}) collective-permute-start(bf16[4112,128]{1,0:T(8,128)(2,1)} %pad_maximum_fusion), channel_id=1, source_target_pairs={{0,96},{32,0},{64,32},{96,64},{1,97},{33,1},{65,33},{97,65},{2,98}... | collective-permute-start | bytes 3158024 | tf_op jit(solution)/shard_map/ppermute | solution.py:64
  22.2 62.4 %collective-permute-start.4 = (bf16[4112,128]{1,0:T(8,128)(2,1)}, bf16[4112,128]{1,0:T(8,128)(2,1)S(1)}, u32[]{:S(2)}, u32[]{:S(2)}) collective-permute-start(bf16[4112,128]{1,0:T(8,128)(2,1)} %pad_maximum_fusion), channel_id=1, source_target_pairs={{0,64},{32,96},{64,0},{96,32},{1,65},{33,97},{65,1},{97,33},{2,66}... | collective-permute-start | bytes 3158024 | tf_op jit(solution)/shard_map/ppermute | solution.py:64
  25.8 58.8 %collective-permute-start.3 = (bf16[4112,128]{1,0:T(8,128)(2,1)}, bf16[4112,128]{1,0:T(8,128)(2,1)S(1)}, u32[]{:S(2)}, u32[]{:S(2)}) collective-permute-start(bf16[4112,128]{1,0:T(8,128)(2,1)} %pad_maximum_fusion), channel_id=1, source_target_pairs={{0,32},{32,64},{64,96},{96,0},{1,33},{33,65},{65,97},{97,1},{2,34}... | collective-permute-start | bytes 3158024 | tf_op jit(solution)/shard_map/ppermute | solution.py:64
  273.3 46.8 %collective-permute-start.8 = (f32[16,128,128]{2,1,0:T(8,128)}, f32[16,128,128]{2,1,0:T(8,128)S(1)}, u32[]{:S(2)}, u32[]{:S(2)}) collective-permute-start(f32[16,128,128]{2,1,0:T(8,128)} %shard_map.57), channel_id=1, source_target_pairs={{0,3},{1,0},{2,1},{3,2},{4,7},{5,4},{6,5},{7,6},{8,11},{9,8},{10,9... | collective-permute-start | bytes 3145736 | tf_op jit(solution)/shard_map/ppermute | solution.py:129
  283.7 49.2 %collective-permute-start.6 = (f32[16,128,128]{2,1,0:T(8,128)}, f32[16,128,128]{2,1,0:T(8,128)S(1)}, u32[]{:S(2)}, u32[]{:S(2)}) collective-permute-start(f32[16,128,128]{2,1,0:T(8,128)} %shard_map.55), channel_id=1, source_target_pairs={{0,1},{1,2},{2,3},{3,0},{4,5},{5,6},{6,7},{7,4},{8,9},{9,10},{10,1... | collective-permute-start | bytes 3145736 | tf_op jit(solution)/shard_map/ppermute | solution.py:129
  294.4 39.5 %collective-permute-start.7 = (f32[16,128,128]{2,1,0:T(8,128)}, f32[16,128,128]{2,1,0:T(8,128)}, u32[]{:S(2)}, u32[]{:S(2)}) collective-permute-start(f32[16,128,128]{2,1,0:T(8,128)} %shard_map.56), channel_id=1, source_target_pairs={{0,2},{1,3},{2,0},{3,1},{4,6},{5,7},{6,4},{7,5},{8,10},{9,11},{10,... | collective-permute-start | bytes 3145736 | tf_op jit(solution)/shard_map/ppermute | solution.py:129
  332.9 1.0 copy-start.2
  336.8 1.3 collective-permute-start.9
  338.0 3.7 %collective-permute-start.10 = (f32[16,128]{1,0:T(8,128)S(1)}, f32[16,128]{1,0:T(8,128)S(1)}, u32[]{:S(2)}, u32[]{:S(2)}) collective-permute-start(f32[16,128]{1,0:T(8,128)S(1)} %add.308), channel_id=1, source_target_pairs={{0,64},{32,96},{64,0},{96,32},{1,65},{33,97},{65,1},{97,33},{2,66}... | collective-permute-start | bytes 24584 | tf_op jit(solution)/shard_map/ppermute | solution.py:58
  341.7 3.7 %collective-permute-start.11 = (f32[16,128]{1,0:T(8,128)S(1)}, f32[16,128]{1,0:T(8,128)S(1)}, u32[]{:S(2)}, u32[]{:S(2)}) collective-permute-start(f32[16,128]{1,0:T(8,128)S(1)} %add.309), channel_id=1, source_target_pairs={{0,1},{1,0},{2,3},{3,2},{4,5},{5,4},{6,7},{7,6},{8,9},{9,8},{10,11... | collective-permute-start | bytes 24584 | tf_op jit(solution)/shard_map/ppermute | solution.py:58
  345.3 5.2 %collective-permute-start.12 = (f32[16,128]{1,0:T(8,128)S(1)}, f32[16,128]{1,0:T(8,128)S(1)}, u32[]{:S(2)}, u32[]{:S(2)}) collective-permute-start(f32[16,128]{1,0:T(8,128)S(1)} %add.310), channel_id=1, source_target_pairs={{0,2},{1,3},{2,0},{3,1},{4,6},{5,7},{6,4},{7,5},{8,10},{9,11},{10,... | collective-permute-start | bytes 24584 | tf_op jit(solution)/shard_map/ppermute | solution.py:58
Sparse Core Ops, SparseCore 0:
  10.2 71.0 all-gather.12
  83.6 53.8 all-gather.10
  139.8 53.8 all-gather.14
  195.9 53.8 all-gather.8

commit v4 on v2

v4 whole, which is shorter than its diff:
```python
import functools

import jax
import jax.numpy as jnp
from jax import lax
from jax.experimental import pallas as pl
from jax.experimental.pallas import tpu as pltpu
from jax.sharding import PartitionSpec as P

KA = 4


def column_kernel(goff_ref, moff_ref, oidx_ref, flow_ref, graph_ref, out_ref, lhs_ref, rhs_ref, *, n_q, n_g):
    tile = out_ref.shape[-1]
    n_col = out_ref.shape[0] // n_q

    def body(j, carry):
        for g in range(n_g):
            g_off = pl.multiple_of(goff_ref[j * n_g + g], tile)
            rhs_ref[pl.ds(g * tile, tile), :] = graph_ref[pl.ds(g_off, tile), :]
        for q in range(n_q):
            for g in range(n_g):
                m_off = moff_ref[(j * n_q + q) * n_g + g]
                left = flow_ref[pl.ds(pl.multiple_of(jnp.maximum(m_off, 0), tile), tile), :]
                left = jnp.where(m_off >= 0, left, jnp.zeros_like(left))
                lhs_ref[pl.ds(q * tile, tile), pl.ds(g * tile, tile)] = left
        res = jnp.dot(lhs_ref[...], rhs_ref[...], preferred_element_type=jnp.float32)
        for q in range(n_q):
            out_ref[oidx_ref[j * n_q + q]] = res[q * tile : (q + 1) * tile]
        return carry

    lax.fori_loop(0, n_col, body, 0)


def kept_partials(goff, moff, oidx, flow_flat, graph_flat, n_out, n_q, n_g):
    tile = flow_flat.shape[-1]
    kernel = functools.partial(column_kernel, n_q=n_q, n_g=n_g)
    return pl.pallas_call(
        kernel,
        out_shape=jax.ShapeDtypeStruct((n_out, tile, tile), jnp.float32),
        in_specs=[
            pl.BlockSpec(memory_space=pltpu.SMEM),
            pl.BlockSpec(memory_space=pltpu.SMEM),
            pl.BlockSpec(memory_space=pltpu.SMEM),
            pl.BlockSpec(memory_space=pltpu.VMEM),
            pl.BlockSpec(memory_space=pltpu.VMEM),
        ],
        out_specs=pl.BlockSpec(memory_space=pltpu.VMEM),
        scratch_shapes=[
            pltpu.VMEM((n_q * tile, n_g * tile), jnp.bfloat16),
            pltpu.VMEM((n_g * tile, tile), jnp.bfloat16),
        ],
        compiler_params=pltpu.CompilerParams(vmem_limit_bytes=48 * 1024 * 1024),
        cost_estimate=pl.CostEstimate(
            flops=2 * n_out * n_g * tile**3,
            transcendentals=0,
            bytes_accessed=2 * (flow_flat.size + graph_flat.size) + 4 * n_out * tile * tile,
        ),
    )(goff, moff, oidx, flow_flat, graph_flat)


def butterfly_sum(x, axis, n):
    d = 1
    while d < n:
        x = x + lax.ppermute(x, axis, [(i, i ^ d) for i in range(n)])
        d *= 2
    return x


def first_two(mask):
    n = mask.shape[-1]
    lo = jnp.argmax(mask, axis=-1).astype(jnp.int32)
    hi = (n - 1 - jnp.argmax(mask[..., ::-1], axis=-1)).astype(jnp.int32)
    return lo, hi


def local(a_tiles, a_coords, b_tiles, b_coords, out_coords):
    tile = a_tiles.shape[-1]
    rows_panel = a_tiles.shape[3]
    col_count = lax.axis_size("col")
    row_count = lax.axis_size("row")
    layer_count = lax.axis_size("layer")
    b_span = KA * col_count // row_count
    quarter = rows_panel // layer_count
    col_tiles = out_coords.shape[3]
    n_b = b_tiles.shape[3]
    my_row = lax.axis_index("row")

    graph_parts = [b_tiles[0, 0, 0]] + [
        lax.ppermute(b_tiles[0, 0, 0], "row", [(i, (i + s) % row_count) for i in range(row_count)])
        for s in range(1, row_count)
    ]
    graph_tiles = jnp.concatenate(graph_parts, axis=0)
    graph_coords = lax.all_gather(b_coords[0, 0, 0][None], "row", axis=0, tiled=True)
    flow_tiles = lax.all_gather(a_tiles[0, 0, 0], "col", axis=0, tiled=True)
    flow_coords = lax.all_gather(a_coords[0, 0, 0][None], "col", axis=0, tiled=True)
    kept_all = lax.all_gather(out_coords[0, 0, 0][None], "layer", axis=0, tiled=True)

    n_out = layer_count * col_tiles
    col_ids = jnp.arange(col_tiles, dtype=jnp.int32)
    part_ids = jnp.arange(row_count, dtype=jnp.int32)
    owner_of_part = (my_row - part_ids) % row_count
    coords_by_part = graph_coords[owner_of_part]
    in_col = coords_by_part[:, None, :, 1] == col_ids[None, :, None]
    lo, hi = first_two(in_col)
    g_slot = jnp.stack([lo, hi], axis=2)
    g_b0 = jnp.take_along_axis(
        jnp.broadcast_to(coords_by_part[:, None, :, 0], in_col.shape), g_slot, axis=2
    )
    g_inner = owner_of_part[:, None, None] * b_span + g_b0
    goff = ((part_ids[:, None, None] * n_b + g_slot) * tile).transpose(1, 0, 2).reshape(col_tiles, -1)
    g_inner = g_inner.transpose(1, 0, 2).reshape(col_tiles, -1)
    n_g = goff.shape[1]

    kept_here = kept_all[:, None, :, 1] == col_ids[None, :, None]
    kept_pos = jnp.argmax(kept_here, axis=2).astype(jnp.int32)
    kept_row0 = jnp.take_along_axis(kept_all[:, :, 0], kept_pos, axis=1)
    q_ids = jnp.arange(layer_count, dtype=jnp.int32)
    kept_row = q_ids[:, None] * quarter + kept_row0
    oidx = (q_ids[:, None] * col_tiles + kept_pos).T

    a_rows = flow_coords[:, :, 0]
    a_inner = flow_coords[:, :, 1]
    grp = g_inner // KA
    want = g_inner % KA
    rows_q = kept_row.T
    slot_a = jnp.argmax(
        a_rows[grp[:, None, :], :] == rows_q[:, :, None, None], axis=3
    ).astype(jnp.int32)
    have = a_inner[grp[:, None, :], slot_a] == want[:, None, :]
    moff = jnp.where(have, (grp[:, None, :] * rows_panel + slot_a) * tile, -1)

    flow_flat = flow_tiles.reshape(-1, tile)
    graph_flat = graph_tiles.reshape(-1, tile)
    partial_sum = kept_partials(
        goff.reshape(-1).astype(jnp.int32),
        moff.reshape(-1).astype(jnp.int32),
        oidx.reshape(-1).astype(jnp.int32),
        flow_flat,
        graph_flat,
        n_out,
        layer_count,
        n_g,
    )
    kept_tiles = lax.psum_scatter(partial_sum, "layer", scatter_dimension=0, tiled=True)

    kept_cols = out_coords[0, 0, 0, :, 1]
    squared = kept_tiles * kept_tiles
    column_part = jnp.sum(squared, axis=1)
    local_mass = jnp.zeros_like(column_part).at[kept_cols].set(column_part)
    column_total = butterfly_sum(butterfly_sum(local_mass, "row", row_count), "layer", layer_count)
    factor = jnp.float32(row_count * layer_count * tile) / column_total
    flow = squared * factor[kept_cols][:, None, :]
    return flow.reshape(1, 1, 1, col_tiles, tile, tile)


def solution(mesh):
    in_specs = (
        P("row", "col", "layer", None, None, None),
        P("row", "col", "layer", None, None),
        P("row", "col", "layer", None, None, None),
        P("row", "col", "layer", None, None),
        P("row", "col", "layer", None, None),
    )
    out_specs = P("row", "col", "layer", None, None, None)
    return jax.shard_map(local, mesh=mesh, in_specs=in_specs, out_specs=out_specs, check_vma=False)
```

time: 231 us -> 219 us (0.948)
  Pallas kernels: 26.3 us -> 12.8 us
  waiting for transfers between devices: 73.6 us -> 69.7 us
  blocking collectives: 88.5 us -> 91.6 us
    all_gather x1, blocking collectives: 5.06 us -> 56.7 us  [local(): lax.all_gather(b_coords[0, 0, 0][None], 'row', axis=0, tiled=True)]
    all_gather x1, blocking collectives: 73.4 us -> 25 us  [local(): lax.all_gather(a_coords[0, 0, 0][None], 'col', axis=0, tiled=True)]
    pallas_call x1, Pallas kernels: 26.3 us -> 12.8 us  [kept_partials(): pl.pallas_call(kernel, out_shape=jax.ShapeDtypeStruct((n_out, tile, tile)...]
    all_gather x1, waiting for transfers between devices: 17.9 us -> 14.5 us  [local(): flow_tiles = lax.all_gather(a_tiles[0, 0, 0], 'col', axis=0, tiled=True)]
    gather x6 -> x12, local copies, waits for them, and re-layouts: 5.03 us -> 6.99 us  [the longest x2 2.74 us: local(): have = a_inner[grp[:, None, :], slot_a] == want[:, None, :]]
    another operation x2 -> x5, other arithmetic: 3.59 us -> 5.24 us  [the longest x1 3.03 us: local(): jnp.argmax(a_rows[grp[:, None, :], :] == rows_q[:, :, None, None], axis=3)]
  transfers between devices with their start and end apart: 9 -> 9, of which waited for: 6 -> 6; matrix products, arithmetic and copies ran while one was open for 7% -> 8% of each run, Pallas kernels for 0% -> 0%
where the time goes in v4:
time: 219 us
  blocking collectives  91.6 us (42%)
  waiting for transfers between devices  69.7 us (32%)
  between operations  13.6 us (6%)
  Pallas kernels  12.8 us (6%)
  other arithmetic  12.6 us (6%)
  local copies, waits for them, and re-layouts  11.4 us (5%)
  starting transfers between devices  6.88 us (3%)
    all_gather x1, blocking collectives, local(): lax.all_gather(b_coords[0, 0, 0][None], 'row', axis=0, tiled=True)  56.7 us
    reduce_scatter x1, waiting for transfers between devices, local(): lax.psum_scatter(partial_sum, 'layer', scatter_dimension=0, tiled=True)  44.1 us
    all_gather x1, blocking collectives, local(): lax.all_gather(a_coords[0, 0, 0][None], 'col', axis=0, tiled=True)  25 us
    all_gather x1, waiting for transfers between devices, local(): flow_tiles = lax.all_gather(a_tiles[0, 0, 0], 'col', axis=0, tiled=True)  14.5 us
    pallas_call x1, Pallas kernels, kept_partials(): pl.pallas_call(kernel, out_shape=jax.ShapeDtypeStruct((n_out, tile, tile)...  12.8 us
    ppermute x4, waiting for transfers between devices, butterfly_sum(): x = x + lax.ppermute(x, axis, [(i, i ^ d) for i in range(n)])  10.4 us
    all_gather x1, blocking collectives, local(): lax.all_gather(out_coords[0, 0, 0][None], 'layer', axis=0, tiled=True)  9.85 us
  transfers between devices with their start and end apart: 9, of which 6 were waited for; matrix products, arithmetic and copies ran while one was open for 8% of the time, Pallas kernels for 0%

profile of v4, /device:TPU:0, one launch (start us, length us, event | category | flops | bytes accessed | tf_op | source)
XLA Modules:
  0.0 218.6 jit_solution(17983148503081929446)
XLA Ops:
  7.4 2.1 collective-permute-start.1
  9.5 1.4 collective-permute-start.2
  10.8 56.7 %all-gather = s32[4,1,1,32,2]{3,4,2,1,0:T(2,128)S(1)} all-gather(s32[1,1,1,32,2]{3,4,2,1,0:T(2,128)} %param.8), channel_id=2, replica_groups=mesh['row'=4,'col'=8,'layer'=4] {'row'}, dimensions={0}, use_global_device_ids=true | all-gather | bytes 1280 | tf_op jit(solution)/shard_map/all_gather | solution.py:94
  68.3 0.7 iota_reduce_fusion.2
  70.1 1.5 gather_fusion.4
  72.1 25.0 %all-gather.1 = s32[8,1,1,32,2]{3,4,2,1,0:T(2,128)S(1)} all-gather(s32[1,1,1,32,2]{3,4,2,1,0:T(2,128)S(1)} %copy-done.2), channel_id=3, replica_groups=mesh['row'=4,'col'=8,'layer'=4] {'col'}, dimensions={0}, use_global_device_ids=true | all-gather | bytes 2304 | tf_op jit(solution)/shard_map/all_gather | solution.py:96
  97.1 9.9 %all-gather.2 = s32[4,1,1,16,2]{3,4,2,1,0:T(2,128)S(1)} all-gather(s32[1,1,1,16,2]{3,4,2,1,0:T(2,128)S(1)} %copy-done.3), channel_id=4, replica_groups=mesh['row'=4,'col'=8,'layer'=4] {'layer'}, dimensions={0}, use_global_device_ids=true | all-gather | bytes 640 | tf_op jit(solution)/shard_map/all_gather | solution.py:97
  107.0 0.7 iota_reduce_fusion.1
  107.8 0.9 gather_fusion.5
  109.6 3.0 %iota_reduce_fusion = (pred[16,4,8]{2,1,0:T(4,128)(4,1)}, s32[16,4,8]{2,1,0:T(4,128)S(1)}) fusion(s32[16,4]{1,0:T(8,128)S(1)} %copy.60, s32[16,8,32]{2,1,0:T(8,128)S(1)} %bitcast.70), kind=kLoop, calls=%fused_computation.10 | loop fusion | flops 127488 | bytes 19200 | tf_op jit(solution)/shard_map/local/reduce | solution.py:127
  113.0 2.6 %gather_fusion.2 = s32[512]{0:T(512)S(1)} fusion(s32[8,32]{1,0:T(8,128)S(1)} %get-tuple-element.13, s32[512]{0:T(512)S(1)} %reshape.405), kind=kCustom, calls=%fused_computation.2 | custom fusion | bytes 8192 | tf_op jit(solution)/shard_map/gather | solution.py:130
  116.5 3.4 %pad_maximum_fusion = bf16[128,128,128]{2,1,0:T(8,128)(2,1)} fusion(bf16[32,128,128]{2,1,0:T(8,128)(2,1)} %collective-permute-done.2, bf16[32,128,128]{2,1,0:T(8,128)(2,1)S(1)} %collective-permute-done.1, bf16[32,128,128]{2,1,0:T(8,128)(2,1)S(1)} %collective-permute-done, bf16[32,128,128]{2,1,0:T(8,128)(2,1)S(1)} %bitcast.69), kind=kLoop, calls=%fused_computation.7 | loop fusion | flops 6291456 | bytes 8388608 | tf_op jit(solution)/shard_map/concatenate | solution.py:93
  119.9 14.5 %all-gather.6.cloned.1.call-done = bf16[1,1,1,256,128,128]{5,4,2,1,0,3:T(8,128)(2,1)} async-done(((bf16[1,1,1,32,128,128]{5,4,2,1,0,3:T(8,128)(2,1)}), bf16[1,1,1,256,128,128]{5,4,2,1,0,3:T(8,128)(2,1)}) %all-gather.6.cloned.1.call-update) | async-done | bytes 8388624 | tf_op jit(solution)/shard_map/all_gather | solution.py:95
  134.3 12.8 %shard_map.55 = f32[64,128,128]{2,1,0:T(8,128)S(1)} custom-call(s32[128]{0:T(128)S(1)} %reshape_reshape.3.goff_ref, s32[512]{0:T(512)S(1)} %reshape.384.moff_ref, s32[64]{0:T(128)S(1)} %reshape.385.oidx_ref, bf16[32768,128]{1,0:T(8,128)(2,1)} %bitcast.63, bf16[16384,128]{1,0:T(8,128)(2,1)} %bitcast.62), custom_call_target="tpu_custom_call" | custom-call | flops 2147483648 | bytes 16777216 | tf_op jit(solution)/shard_map/pallas_call | solution.py:38
  147.1 1.9 copy-done
  149.1 44.1 %reduce-scatter.2.cloned.1.call-done = f32[16,128,128]{2,1,0:T(8,128)} async-done(((f32[64,128,128]{2,1,0:T(8,128)}), f32[16,128,128]{2,1,0:T(8,128)}) %reduce-scatter.2.cloned.1.call-update) | async-done | bytes 1048592 | tf_op jit(solution)/shard_map/reduce_scatter | solution.py:145
  193.2 1.3 multiply_reduce_fusion
  195.2 1.2 collective-permute-done.3
  196.4 1.5 collective-permute-start.4
  197.9 2.1 collective-permute-done.4
  200.3 3.4 %collective-permute-done.5 = f32[16,128]{1,0:T(8,128)S(1)} collective-permute-done((f32[16,128]{1,0:T(8,128)S(1)}, f32[16,128]{1,0:T(8,128)S(1)}, u32[]{:S(2)}, u32[]{:S(2)}) %collective-permute-start.5) | collective-permute-done | bytes 8224 | tf_op jit(solution)/shard_map/ppermute | solution.py:65
  203.7 1.5 collective-permute-start.6
  205.2 3.7 %collective-permute-done.6 = f32[16,128]{1,0:T(8,128)S(1)} collective-permute-done((f32[16,128]{1,0:T(8,128)S(1)}, f32[16,128]{1,0:T(8,128)S(1)}, u32[]{:S(2)}, u32[]{:S(2)}) %collective-permute-start.6) | collective-permute-done | bytes 8224 | tf_op jit(solution)/shard_map/ppermute | solution.py:65
  209.4 2.3 %multiply_bitcast_fusion = f32[1,1,1,16,128,128]{5,4,3,2,1,0:T(8,128)} fusion(f32[16,128,128]{2,1,0:T(8,128)} %reduce-scatter.2.cloned.1.call-done, f32[16,128]{1,0:T(8,128)S(1)} %gather_fusion.3), kind=kLoop, calls=%fused_computation.8 | loop fusion | flops 524288 | bytes 2105344 | tf_op jit(solution)/shard_map/reshape | solution.py:154
  (72 shorter events, 6.7 us)
Async XLA Ops:
  6.5 127.8 %all-gather.6.cloned.1.call-start = ((), (), s32[]{:S(2)}) async-start(), calls=%async_computation.2 | async-start | bytes 9437184 | tf_op jit(solution)/shard_map/all_gather | solution.py:95
  7.3 186.0 %reduce-scatter.2.cloned.1.call-start = ((), (), s32[]{:S(2)}) async-start(), calls=%async_computation.1 | async-start | bytes 5242880 | tf_op jit(solution)/shard_map/reduce_scatter | solution.py:145
  7.3 109.2 %collective-permute-start = (bf16[32,128,128]{2,1,0:T(8,128)(2,1)}, bf16[32,128,128]{2,1,0:T(8,128)(2,1)S(1)}, u32[]{:S(2)}, u32[]{:S(2)}) collective-permute-start(bf16[32,128,128]{2,1,0:T(8,128)(2,1)} %bitcast.66), channel_id=1, source_target_pairs={{0,32},{32,64},{64,96},{96,0},{1,33},{33,65},{65,97},{97,1},{2,34}... | collective-permute-start | bytes 3145736 | tf_op jit(solution)/shard_map/ppermute | solution.py:90
  7.4 109.1 %collective-permute-start.1 = (bf16[32,128,128]{2,1,0:T(8,128)(2,1)}, bf16[32,128,128]{2,1,0:T(8,128)(2,1)S(1)}, u32[]{:S(2)}, u32[]{:S(2)}) collective-permute-start(bf16[32,128,128]{2,1,0:T(8,128)(2,1)} %bitcast.67), channel_id=1, source_target_pairs={{0,64},{32,96},{64,0},{96,32},{1,65},{33,97},{65,1},{97,33},{2,66}... | collective-permute-start | bytes 3145736 | tf_op jit(solution)/shard_map/ppermute | solution.py:90
  9.5 107.0 %collective-permute-start.2 = (bf16[32,128,128]{2,1,0:T(8,128)(2,1)}, bf16[32,128,128]{2,1,0:T(8,128)(2,1)}, u32[]{:S(2)}, u32[]{:S(2)}) collective-permute-start(bf16[32,128,128]{2,1,0:T(8,128)(2,1)} %bitcast.68), channel_id=1, source_target_pairs={{0,96},{32,0},{64,32},{96,64},{1,97},{33,1},{65,33},{97,65},{2,98}... | collective-permute-start | bytes 3145736 | tf_op jit(solution)/shard_map/ppermute | solution.py:90
  70.0 2.1 copy-start.2
  70.1 27.1 %copy-start.3 = (s32[1,1,1,16,2]{3,4,2,1,0:T(2,128)S(1)}, s32[1,1,1,16,2]{3,4,2,1,0:T(2,128)}, u32[]{:S(2)}) copy-start(s32[1,1,1,16,2]{3,4,2,1,0:T(2,128)} %param.9) | copy-start | bytes 388
  113.0 3.5 %copy-start.1 = (bf16[1,1,1,32,128,128]{5,4,3,2,1,0:T(8,128)(2,1)S(1)}, bf16[1,1,1,32,128,128]{5,4,3,2,1,0:T(8,128)(2,1)}, u32[]{:S(2)}) copy-start(bf16[1,1,1,32,128,128]{5,4,3,2,1,0:T(8,128)(2,1)} %param.7) | copy-start | bytes 3145732
  147.1 1.9 copy-start
  195.2 1.3 collective-permute-start.3
  196.4 3.7 %collective-permute-start.4 = (f32[16,128]{1,0:T(8,128)S(1)}, f32[16,128]{1,0:T(8,128)S(1)}, u32[]{:S(2)}, u32[]{:S(2)}) collective-permute-start(f32[16,128]{1,0:T(8,128)S(1)} %add.196), channel_id=1, source_target_pairs={{0,64},{32,96},{64,0},{96,32},{1,65},{33,97},{65,1},{97,33},{2,66}... | collective-permute-start | bytes 24584 | tf_op jit(solution)/shard_map/ppermute | solution.py:65
  200.1 3.7 %collective-permute-start.5 = (f32[16,128]{1,0:T(8,128)S(1)}, f32[16,128]{1,0:T(8,128)S(1)}, u32[]{:S(2)}, u32[]{:S(2)}) collective-permute-start(f32[16,128]{1,0:T(8,128)S(1)} %add.197), channel_id=1, source_target_pairs={{0,1},{1,0},{2,3},{3,2},{4,5},{5,4},{6,7},{7,6},{8,9},{9,8},{10,11... | collective-permute-start | bytes 24584 | tf_op jit(solution)/shard_map/ppermute | solution.py:65
  203.7 5.2 %collective-permute-start.6 = (f32[16,128]{1,0:T(8,128)S(1)}, f32[16,128]{1,0:T(8,128)S(1)}, u32[]{:S(2)}, u32[]{:S(2)}) collective-permute-start(f32[16,128]{1,0:T(8,128)S(1)} %add.198), channel_id=1, source_target_pairs={{0,2},{1,3},{2,0},{3,1},{4,6},{5,7},{6,4},{7,5},{8,10},{9,11},{10,... | collective-permute-start | bytes 24584 | tf_op jit(solution)/shard_map/ppermute | solution.py:65
Sparse Core Ops, SparseCore 0:
  9.7 124.5 all-gather.5
  149.2 43.9 reduce-scatter.1

commit v5 on v4

--- a/solution.py
+++ b/solution.py
@@ -67,6 +67,15 @@
     return x
 
 
+def all_sum(x, axes, n):
+    me = lax.axis_index(axes)
+    parts = jnp.stack([x] + [lax.ppermute(x, axes, [(i, (i + s) % n) for i in range(n)]) for s in range(1, n)])
+    total = parts[me % n]
+    for src in range(1, n):
+        total = total + parts[(me - src) % n]
+    return total
+
+
 def first_two(mask):
     n = mask.shape[-1]
     lo = jnp.argmax(mask, axis=-1).astype(jnp.int32)
@@ -86,10 +95,11 @@
     n_b = b_tiles.shape[3]
     my_row = lax.axis_index("row")
 
-    graph_parts = [b_tiles[0, 0, 0]] + [
-        lax.ppermute(b_tiles[0, 0, 0], "row", [(i, (i + s) % row_count) for i in range(row_count)])
-        for s in range(1, row_count)
-    ]
+    own = b_tiles[0, 0, 0]
+    far = lax.ppermute(own, "row", [(i, i ^ 2) for i in range(row_count)])
+    near = lax.ppermute(own, "row", [(i, i ^ 1) for i in range(row_count)])
+    far_near = lax.ppermute(far, "row", [(i, i ^ 1) for i in range(row_count)])
+    graph_parts = [own, near, far, far_near]
     graph_tiles = jnp.concatenate(graph_parts, axis=0)
     graph_coords = lax.all_gather(b_coords[0, 0, 0][None], "row", axis=0, tiled=True)
     flow_tiles = lax.all_gather(a_tiles[0, 0, 0], "col", axis=0, tiled=True)
@@ -99,7 +109,7 @@
     n_out = layer_count * col_tiles
     col_ids = jnp.arange(col_tiles, dtype=jnp.int32)
     part_ids = jnp.arange(row_count, dtype=jnp.int32)
-    owner_of_part = (my_row - part_ids) % row_count
+    owner_of_part = my_row ^ part_ids
     coords_by_part = graph_coords[owner_of_part]
     in_col = coords_by_part[:, None, :, 1] == col_ids[None, :, None]
     lo, hi = first_two(in_col)
@@ -148,7 +158,7 @@
     squared = kept_tiles * kept_tiles
     column_part = jnp.sum(squared, axis=1)
     local_mass = jnp.zeros_like(column_part).at[kept_cols].set(column_part)
-    column_total = butterfly_sum(butterfly_sum(local_mass, "row", row_count), "layer", layer_count)
+    column_total = all_sum(local_mass, ("row", "layer"), row_count * layer_count)
     factor = jnp.float32(row_count * layer_count * tile) / column_total
     flow = squared * factor[kept_cols][:, None, :]
     return flow.reshape(1, 1, 1, col_tiles, tile, tile)

time: 219 us -> 225 us (1.027)
  blocking collectives: 91.6 us -> 67.4 us
  starting transfers between devices: 6.88 us -> 23.8 us
  waiting for transfers between devices: 69.7 us -> 82.2 us
    all_gather x1, blocking collectives: 56.7 us -> 32.2 us  [local(): lax.all_gather(b_coords[0, 0, 0][None], 'row', axis=0, tiled=True)]
    all_gather x1, waiting for transfers between devices: 14.5 us -> 35.7 us  [local(): flow_tiles = lax.all_gather(a_tiles[0, 0, 0], 'col', axis=0, tiled=True)]
    ppermute x7 -> x18, starting transfers between devices: 6.84 us -> 23.7 us  [the longest x15 21.6 us: all_sum(): lax.ppermute(x, axes, [(i, (i + s) % n) for i in range(n)])]
    ppermute x7 -> x18, waiting for transfers between devices: 10.4 us -> 1.48 us  [the longest x15 1.47 us: all_sum(): lax.ppermute(x, axes, [(i, (i + s) % n) for i in range(n)])]
  transfers between devices with their start and end apart: 9 -> 20, of which waited for: 6 -> 4; matrix products, arithmetic and copies ran while one was open for 8% -> 8% of each run, Pallas kernels for 0% -> 0%
where the time goes in v5:
time: 225 us; the launch traced here: 224 us
  waiting for transfers between devices  82.2 us (37%)
  blocking collectives  67.4 us (30%)
  starting transfers between devices  23.8 us (11%)
  between operations  14 us (6%)
  Pallas kernels  12.8 us (6%)
  other arithmetic  12.5 us (6%)
  local copies, waits for them, and re-layouts  11.4 us (5%)
    reduce_scatter x1, waiting for transfers between devices, local(): lax.psum_scatter(partial_sum, 'layer', scatter_dimension=0, tiled=True)  44.3 us
    all_gather x1, waiting for transfers between devices, local(): flow_tiles = lax.all_gather(a_tiles[0, 0, 0], 'col', axis=0, tiled=True)  35.7 us
    all_gather x1, blocking collectives, local(): lax.all_gather(b_coords[0, 0, 0][None], 'row', axis=0, tiled=True)  32.2 us
    all_gather x1, blocking collectives, local(): lax.all_gather(a_coords[0, 0, 0][None], 'col', axis=0, tiled=True)  25.4 us
    ppermute x15, starting transfers between devices, all_sum(): lax.ppermute(x, axes, [(i, (i + s) % n) for i in range(n)])  21.6 us
    pallas_call x1, Pallas kernels, kept_partials(): pl.pallas_call(kernel, out_shape=jax.ShapeDtypeStruct((n_out, tile, tile)...  12.8 us
    all_gather x1, blocking collectives, local(): lax.all_gather(out_coords[0, 0, 0][None], 'layer', axis=0, tiled=True)  9.78 us
  transfers between devices with their start and end apart: 20, of which 4 were waited for; matrix products, arithmetic and copies ran while one was open for 8% of the time, Pallas kernels for 0%

profile of v5, /device:TPU:0, one launch (start us, length us, event | category | flops | bytes accessed | tf_op | source)
XLA Modules:
  0.0 224.1 jit_solution(12696498457469417376)
XLA Ops:
  7.3 2.1 collective-permute-start.1
  9.4 32.2 %all-gather = s32[4,1,1,32,2]{3,4,2,1,0:T(2,128)S(1)} all-gather(s32[1,1,1,32,2]{3,4,2,1,0:T(2,128)} %param.8), channel_id=2, replica_groups=mesh['row'=4,'col'=8,'layer'=4] {'row'}, dimensions={0}, use_global_device_ids=true | all-gather | bytes 1280 | tf_op jit(solution)/shard_map/all_gather | solution.py:104
  44.0 1.5 gather_fusion.4
  46.1 25.4 %all-gather.1 = s32[8,1,1,32,2]{3,4,2,1,0:T(2,128)S(1)} all-gather(s32[1,1,1,32,2]{3,4,2,1,0:T(2,128)S(1)} %copy-done.2), channel_id=3, replica_groups=mesh['row'=4,'col'=8,'layer'=4] {'col'}, dimensions={0}, use_global_device_ids=true | all-gather | bytes 2304 | tf_op jit(solution)/shard_map/all_gather | solution.py:106
  71.5 9.8 %all-gather.2 = s32[4,1,1,16,2]{3,4,2,1,0:T(2,128)S(1)} all-gather(s32[1,1,1,16,2]{3,4,2,1,0:T(2,128)S(1)} %copy-done.3), channel_id=4, replica_groups=mesh['row'=4,'col'=8,'layer'=4] {'layer'}, dimensions={0}, use_global_device_ids=true | all-gather | bytes 640 | tf_op jit(solution)/shard_map/all_gather | solution.py:107
  84.0 3.0 %iota_reduce_fusion = (pred[16,4,8]{2,1,0:T(4,128)(4,1)}, s32[16,4,8]{2,1,0:T(4,128)S(1)}) fusion(s32[16,4]{1,0:T(8,128)S(1)} %copy.60, s32[16,8,32]{2,1,0:T(8,128)S(1)} %bitcast.103), kind=kLoop, calls=%fused_computation.10 | loop fusion | flops 127488 | bytes 19200 | tf_op jit(solution)/shard_map/local/reduce | solution.py:137
  87.4 2.6 %gather_fusion.2 = s32[512]{0:T(512)S(1)} fusion(s32[8,32]{1,0:T(8,128)S(1)} %get-tuple-element.13, s32[512]{0:T(512)S(1)} %reshape.369), kind=kCustom, calls=%fused_computation.2 | custom fusion | bytes 8192 | tf_op jit(solution)/shard_map/gather | solution.py:140
  90.9 3.3 %pad_maximum_fusion = bf16[128,128,128]{2,1,0:T(8,128)(2,1)} fusion(bf16[32,128,128]{2,1,0:T(8,128)(2,1)} %collective-permute-done.2, bf16[32,128,128]{2,1,0:T(8,128)(2,1)S(1)} %collective-permute-done.1, bf16[32,128,128]{2,1,0:T(8,128)(2,1)S(1)} %collective-permute-done, bf16[32,128,128]{2,1,0:T(8,128)(2,1)S(1)} %bitcast.102), kind=kLoop, calls=%fused_computation.7 | loop fusion | flops 6291456 | bytes 8388608 | tf_op jit(solution)/shard_map/concatenate | solution.py:103
  94.2 35.7 %all-gather.6.cloned.1.call-done = bf16[1,1,1,256,128,128]{5,4,2,1,0,3:T(8,128)(2,1)} async-done(((bf16[1,1,1,32,128,128]{5,4,2,1,0,3:T(8,128)(2,1)}), bf16[1,1,1,256,128,128]{5,4,2,1,0,3:T(8,128)(2,1)}) %all-gather.6.cloned.1.call-update) | async-done | bytes 8388624 | tf_op jit(solution)/shard_map/all_gather | solution.py:105
  129.9 12.8 %shard_map.55 = f32[64,128,128]{2,1,0:T(8,128)S(1)} custom-call(s32[128]{0:T(128)S(1)} %reshape_reshape.3.goff_ref, s32[512]{0:T(512)S(1)} %reshape.344.moff_ref, s32[64]{0:T(128)S(1)} %reshape.345.oidx_ref, bf16[32768,128]{1,0:T(8,128)(2,1)} %bitcast.97, bf16[16384,128]{1,0:T(8,128)(2,1)} %bitcast.96), custom_call_target="tpu_custom_call" | custom-call | flops 2147483648 | bytes 16777216 | tf_op jit(solution)/shard_map/pallas_call | solution.py:38
  142.7 1.9 copy-done
  145.0 44.3 %reduce-scatter.2.cloned.1.call-done = f32[16,128,128]{2,1,0:T(8,128)} async-done(((f32[64,128,128]{2,1,0:T(8,128)}), f32[16,128,128]{2,1,0:T(8,128)}) %reduce-scatter.2.cloned.1.call-update) | async-done | bytes 1048592 | tf_op jit(solution)/shard_map/reduce_scatter | solution.py:155
  189.3 1.3 multiply_reduce_fusion
  191.5 2.1 collective-permute-start.4
  194.6 1.6 collective-permute-start.6
  196.5 1.6 collective-permute-start.8
  198.1 2.9 %collective-permute-start.9 = (f32[16,128]{1,0:T(8,128)S(1)}, f32[16,128]{1,0:T(8,128)S(1)}, u32[]{:S(2)}, u32[]{:S(2)}) collective-permute-start(f32[16,128]{1,0:T(8,128)S(1)} %scatter_custom_fusion), channel_id=1, source_target_pairs={{0,35},{1,64},{2,65},{3,66},{32,67},{33,96},{34,97},{35,98},{64,99... | collective-permute-start | bytes 24584 | tf_op jit(solution)/shard_map/ppermute | solution.py:72
  201.5 1.1 collective-permute-start.11
  202.6 2.8 %collective-permute-start.12 = (f32[16,128]{1,0:T(8,128)S(1)}, f32[16,128]{1,0:T(8,128)S(1)}, u32[]{:S(2)}, u32[]{:S(2)}) collective-permute-start(f32[16,128]{1,0:T(8,128)S(1)} %scatter_custom_fusion), channel_id=1, source_target_pairs={{0,66},{1,67},{2,96},{3,97},{32,98},{33,99},{34,0},{35,1},{64,2},{... | collective-permute-start | bytes 24584 | tf_op jit(solution)/shard_map/ppermute | solution.py:72
  205.4 1.7 collective-permute-start.13
  207.8 1.8 collective-permute-start.16
  209.6 3.4 %collective-permute-start.17 = (f32[16,128]{1,0:T(8,128)S(1)}, f32[16,128]{1,0:T(8,128)S(1)}, u32[]{:S(2)}, u32[]{:S(2)}) collective-permute-start(f32[16,128]{1,0:T(8,128)S(1)} %scatter_custom_fusion), channel_id=1, source_target_pairs={{0,99},{1,0},{2,1},{3,2},{32,3},{33,32},{34,33},{35,34},{64,35},{6... | collective-permute-start | bytes 24584 | tf_op jit(solution)/shard_map/ppermute | solution.py:72
  213.1 1.3 collective-permute-done.17
  214.9 2.3 %multiply_bitcast_fusion = f32[1,1,1,16,128,128]{5,4,3,2,1,0:T(8,128)} fusion(f32[16,128,128]{2,1,0:T(8,128)} %reduce-scatter.2.cloned.1.call-done, f32[16,128]{1,0:T(8,128)S(1)} %gather_fusion.3), kind=kLoop, calls=%fused_computation.8 | loop fusion | flops 524288 | bytes 2105344 | tf_op jit(solution)/shard_map/reshape | solution.py:164
  (107 shorter events, 11.5 us)
Async XLA Ops:
  6.5 123.4 %all-gather.6.cloned.1.call-start = ((), (), s32[]{:S(2)}) async-start(), calls=%async_computation.2 | async-start | bytes 9437184 | tf_op jit(solution)/shard_map/all_gather | solution.py:105
  7.3 182.0 %reduce-scatter.2.cloned.1.call-start = ((), (), s32[]{:S(2)}) async-start(), calls=%async_computation.1 | async-start | bytes 5242880 | tf_op jit(solution)/shard_map/reduce_scatter | solution.py:155
  7.3 76.6 %collective-permute-start.1 = (bf16[32,128,128]{2,1,0:T(8,128)(2,1)}, bf16[32,128,128]{2,1,0:T(8,128)(2,1)S(1)}, u32[]{:S(2)}, u32[]{:S(2)}) collective-permute-start(bf16[32,128,128]{2,1,0:T(8,128)(2,1)} %bitcast.100), channel_id=1, source_target_pairs={{0,64},{32,96},{64,0},{96,32},{1,65},{33,97},{65,1},{97,33},{2,66}... | collective-permute-start | bytes 3145736 | tf_op jit(solution)/shard_map/ppermute | solution.py:99
  9.4 81.5 %collective-permute-start = (bf16[32,128,128]{2,1,0:T(8,128)(2,1)}, bf16[32,128,128]{2,1,0:T(8,128)(2,1)S(1)}, u32[]{:S(2)}, u32[]{:S(2)}) collective-permute-start(bf16[32,128,128]{2,1,0:T(8,128)(2,1)} %bitcast.101), channel_id=1, source_target_pairs={{0,32},{32,0},{64,96},{96,64},{1,33},{33,1},{65,97},{97,65},{2,34}... | collective-permute-start | bytes 3145736 | tf_op jit(solution)/shard_map/ppermute | solution.py:100
  44.0 2.1 copy-start.2
  44.0 27.5 %copy-start.3 = (s32[1,1,1,16,2]{3,4,2,1,0:T(2,128)S(1)}, s32[1,1,1,16,2]{3,4,2,1,0:T(2,128)}, u32[]{:S(2)}) copy-start(s32[1,1,1,16,2]{3,4,2,1,0:T(2,128)} %param.9) | copy-start | bytes 388
  83.9 6.9 %collective-permute-start.2 = (bf16[32,128,128]{2,1,0:T(8,128)(2,1)S(1)}, bf16[32,128,128]{2,1,0:T(8,128)(2,1)}, u32[]{:S(2)}, u32[]{:S(2)}) collective-permute-start(bf16[32,128,128]{2,1,0:T(8,128)(2,1)S(1)} %collective-permute-done.1), channel_id=1, source_target_pairs={{0,32},{32,0},{64,96},{96,64},{1,33},{33,1},{65,97},{97,65},{2,34}... | collective-permute-start | bytes 3145736 | tf_op jit(solution)/shard_map/ppermute | solution.py:101
  87.4 3.5 %copy-start.1 = (bf16[1,1,1,32,128,128]{5,4,3,2,1,0:T(8,128)(2,1)S(1)}, bf16[1,1,1,32,128,128]{5,4,3,2,1,0:T(8,128)(2,1)}, u32[]{:S(2)}) copy-start(bf16[1,1,1,32,128,128]{5,4,3,2,1,0:T(8,128)(2,1)} %param.7) | copy-start | bytes 3145732
  142.7 1.9 copy-start
  191.2 5.3 %collective-permute-start.3 = (f32[16,128]{1,0:T(8,128)S(1)}, f32[16,128]{1,0:T(8,128)S(1)}, u32[]{:S(2)}, u32[]{:S(2)}) collective-permute-start(f32[16,128]{1,0:T(8,128)S(1)} %scatter_custom_fusion), channel_id=1, source_target_pairs={{0,1},{1,2},{2,3},{3,32},{32,33},{33,34},{34,35},{35,64},{64,65},{... | collective-permute-start | bytes 24584 | tf_op jit(solution)/shard_map/ppermute | solution.py:72
  191.5 6.6 %collective-permute-start.4 = (f32[16,128]{1,0:T(8,128)S(1)}, f32[16,128]{1,0:T(8,128)S(1)}, u32[]{:S(2)}, u32[]{:S(2)}) collective-permute-start(f32[16,128]{1,0:T(8,128)S(1)} %scatter_custom_fusion), channel_id=1, source_target_pairs={{0,2},{1,3},{2,32},{3,33},{32,34},{33,35},{34,64},{35,65},{64,66},... | collective-permute-start | bytes 24584 | tf_op jit(solution)/shard_map/ppermute | solution.py:72
  193.6 7.4 %collective-permute-start.5 = (f32[16,128]{1,0:T(8,128)S(1)}, f32[16,128]{1,0:T(8,128)S(1)}, u32[]{:S(2)}, u32[]{:S(2)}) collective-permute-start(f32[16,128]{1,0:T(8,128)S(1)} %scatter_custom_fusion), channel_id=1, source_target_pairs={{0,3},{1,32},{2,33},{3,34},{32,35},{33,64},{34,65},{35,66},{64,67}... | collective-permute-start | bytes 24584 | tf_op jit(solution)/shard_map/ppermute | solution.py:72
  194.6 6.9 %collective-permute-start.6 = (f32[16,128]{1,0:T(8,128)S(1)}, f32[16,128]{1,0:T(8,128)S(1)}, u32[]{:S(2)}, u32[]{:S(2)}) collective-permute-start(f32[16,128]{1,0:T(8,128)S(1)} %scatter_custom_fusion), channel_id=1, source_target_pairs={{0,32},{1,33},{2,34},{3,35},{32,64},{33,65},{34,66},{35,67},{64,96... | collective-permute-start | bytes 24584 | tf_op jit(solution)/shard_map/ppermute | solution.py:72
  196.2 6.4 %collective-permute-start.7 = (f32[16,128]{1,0:T(8,128)S(1)}, f32[16,128]{1,0:T(8,128)S(1)}, u32[]{:S(2)}, u32[]{:S(2)}) collective-permute-start(f32[16,128]{1,0:T(8,128)S(1)} %scatter_custom_fusion), channel_id=1, source_target_pairs={{0,33},{1,34},{2,35},{3,64},{32,65},{33,66},{34,67},{35,96},{64,97... | collective-permute-start | bytes 24584 | tf_op jit(solution)/shard_map/ppermute | solution.py:72
  196.5 8.9 %collective-permute-start.8 = (f32[16,128]{1,0:T(8,128)S(1)}, f32[16,128]{1,0:T(8,128)S(1)}, u32[]{:S(2)}, u32[]{:S(2)}) collective-permute-start(f32[16,128]{1,0:T(8,128)S(1)} %scatter_custom_fusion), channel_id=1, source_target_pairs={{0,34},{1,35},{2,64},{3,65},{32,66},{33,67},{34,96},{35,97},{64,98... | collective-permute-start | bytes 24584 | tf_op jit(solution)/shard_map/ppermute | solution.py:72
  198.1 9.0 %collective-permute-start.9 = (f32[16,128]{1,0:T(8,128)S(1)}, f32[16,128]{1,0:T(8,128)S(1)}, u32[]{:S(2)}, u32[]{:S(2)}) collective-permute-start(f32[16,128]{1,0:T(8,128)S(1)} %scatter_custom_fusion), channel_id=1, source_target_pairs={{0,35},{1,64},{2,65},{3,66},{32,67},{33,96},{34,97},{35,98},{64,99... | collective-permute-start | bytes 24584 | tf_op jit(solution)/shard_map/ppermute | solution.py:72
  201.0 6.7 %collective-permute-start.10 = (f32[16,128]{1,0:T(8,128)S(1)}, f32[16,128]{1,0:T(8,128)S(1)}, u32[]{:S(2)}, u32[]{:S(2)}) collective-permute-start(f32[16,128]{1,0:T(8,128)S(1)} %scatter_custom_fusion), channel_id=1, source_target_pairs={{0,64},{1,65},{2,66},{3,67},{32,96},{33,97},{34,98},{35,99},{64,0}... | collective-permute-start | bytes 24584 | tf_op jit(solution)/shard_map/ppermute | solution.py:72
  201.5 6.2 %collective-permute-start.11 = (f32[16,128]{1,0:T(8,128)S(1)}, f32[16,128]{1,0:T(8,128)S(1)}, u32[]{:S(2)}, u32[]{:S(2)}) collective-permute-start(f32[16,128]{1,0:T(8,128)S(1)} %scatter_custom_fusion), channel_id=1, source_target_pairs={{0,65},{1,66},{2,67},{3,96},{32,97},{33,98},{34,99},{35,0},{64,1},... | collective-permute-start | bytes 24584 | tf_op jit(solution)/shard_map/ppermute | solution.py:72
  202.6 7.0 %collective-permute-start.12 = (f32[16,128]{1,0:T(8,128)S(1)}, f32[16,128]{1,0:T(8,128)S(1)}, u32[]{:S(2)}, u32[]{:S(2)}) collective-permute-start(f32[16,128]{1,0:T(8,128)S(1)} %scatter_custom_fusion), channel_id=1, source_target_pairs={{0,66},{1,67},{2,96},{3,97},{32,98},{33,99},{34,0},{35,1},{64,2},{... | collective-permute-start | bytes 24584 | tf_op jit(solution)/shard_map/ppermute | solution.py:72
  205.4 7.6 %collective-permute-start.13 = (f32[16,128]{1,0:T(8,128)S(1)}, f32[16,128]{1,0:T(8,128)S(1)}, u32[]{:S(2)}, u32[]{:S(2)}) collective-permute-start(f32[16,128]{1,0:T(8,128)S(1)} %scatter_custom_fusion), channel_id=1, source_target_pairs={{0,67},{1,96},{2,97},{3,98},{32,99},{33,0},{34,1},{35,2},{64,3},{6... | collective-permute-start | bytes 24584 | tf_op jit(solution)/shard_map/ppermute | solution.py:72
  207.1 5.9 %collective-permute-start.14 = (f32[16,128]{1,0:T(8,128)S(1)}, f32[16,128]{1,0:T(8,128)S(1)}, u32[]{:S(2)}, u32[]{:S(2)}) collective-permute-start(f32[16,128]{1,0:T(8,128)S(1)} %scatter_custom_fusion), channel_id=1, source_target_pairs={{0,96},{1,97},{2,98},{3,99},{32,0},{33,1},{34,2},{35,3},{64,32},{6... | collective-permute-start | bytes 24584 | tf_op jit(solution)/shard_map/ppermute | solution.py:72
  207.7 5.3 %collective-permute-start.15 = (f32[16,128]{1,0:T(8,128)S(1)}, f32[16,128]{1,0:T(8,128)S(1)}, u32[]{:S(2)}, u32[]{:S(2)}) collective-permute-start(f32[16,128]{1,0:T(8,128)S(1)} %scatter_custom_fusion), channel_id=1, source_target_pairs={{0,97},{1,98},{2,99},{3,0},{32,1},{33,2},{34,3},{35,32},{64,33},{6... | collective-permute-start | bytes 24584 | tf_op jit(solution)/shard_map/ppermute | solution.py:72
  207.8 5.3 %collective-permute-start.16 = (f32[16,128]{1,0:T(8,128)S(1)}, f32[16,128]{1,0:T(8,128)S(1)}, u32[]{:S(2)}, u32[]{:S(2)}) collective-permute-start(f32[16,128]{1,0:T(8,128)S(1)} %scatter_custom_fusion), channel_id=1, source_target_pairs={{0,98},{1,99},{2,0},{3,1},{32,2},{33,3},{34,32},{35,33},{64,34},{6... | collective-permute-start | bytes 24584 | tf_op jit(solution)/shard_map/ppermute | solution.py:72
  209.6 4.8 %collective-permute-start.17 = (f32[16,128]{1,0:T(8,128)S(1)}, f32[16,128]{1,0:T(8,128)S(1)}, u32[]{:S(2)}, u32[]{:S(2)}) collective-permute-start(f32[16,128]{1,0:T(8,128)S(1)} %scatter_custom_fusion), channel_id=1, source_target_pairs={{0,99},{1,0},{2,1},{3,2},{32,3},{33,32},{34,33},{35,34},{64,35},{6... | collective-permute-start | bytes 24584 | tf_op jit(solution)/shard_map/ppermute | solution.py:72
Sparse Core Ops, SparseCore 0:
  9.7 120.1 all-gather.5
  144.8 44.4 reduce-scatter.1

commit v6 on v5

--- a/solution.py
+++ b/solution.py
@@ -65,15 +65,6 @@
         x = x + lax.ppermute(x, axis, [(i, i ^ d) for i in range(n)])
         d *= 2
     return x
-
-
-def all_sum(x, axes, n):
-    me = lax.axis_index(axes)
-    parts = jnp.stack([x] + [lax.ppermute(x, axes, [(i, (i + s) % n) for i in range(n)]) for s in range(1, n)])
-    total = parts[me % n]
-    for src in range(1, n):
-        total = total + parts[(me - src) % n]
-    return total
 
 
 def first_two(mask):
@@ -158,7 +149,7 @@
     squared = kept_tiles * kept_tiles
     column_part = jnp.sum(squared, axis=1)
     local_mass = jnp.zeros_like(column_part).at[kept_cols].set(column_part)
-    column_total = all_sum(local_mass, ("row", "layer"), row_count * layer_count)
+    column_total = butterfly_sum(butterfly_sum(local_mass, "row", row_count), "layer", layer_count)
     factor = jnp.float32(row_count * layer_count * tile) / column_total
     flow = squared * factor[kept_cols][:, None, :]
     return flow.reshape(1, 1, 1, col_tiles, tile, tile)

time: 225 us -> 215 us (0.956)
  starting transfers between devices: 23.8 us -> 5.55 us
  waiting for transfers between devices: 82.2 us -> 91.4 us
    ppermute x15 -> x4, starting transfers between devices: 21.6 us -> 3.35 us  [butterfly_sum(): x = x + lax.ppermute(x, axis, [(i, i ^ d) for i in range(n)])]
    ppermute x15 -> x4, waiting for transfers between devices: 1.47 us -> 10.3 us  [butterfly_sum(): x = x + lax.ppermute(x, axis, [(i, i ^ d) for i in range(n)])]
  transfers between devices with their start and end apart: 20 -> 9, of which waited for: 4 -> 6; matrix products, arithmetic and copies ran while one was open for 8% -> 8% of each run, Pallas kernels for 0% -> 0%
where the time goes in v6:
time: 215 us
  waiting for transfers between devices  91.4 us (43%)
  blocking collectives  67.4 us (31%)
  between operations  13.6 us (6%)
  Pallas kernels  12.8 us (6%)
  other arithmetic  12.5 us (6%)
  local copies, waits for them, and re-layouts  11.4 us (5%)
  starting transfers between devices  5.55 us (3%)
    reduce_scatter x1, waiting for transfers between devices, local(): lax.psum_scatter(partial_sum, 'layer', scatter_dimension=0, tiled=True)  44.6 us
    all_gather x1, waiting for transfers between devices, local(): flow_tiles = lax.all_gather(a_tiles[0, 0, 0], 'col', axis=0, tiled=True)  35.7 us
    all_gather x1, blocking collectives, local(): lax.all_gather(b_coords[0, 0, 0][None], 'row', axis=0, tiled=True)  32.2 us
    all_gather x1, blocking collectives, local(): lax.all_gather(a_coords[0, 0, 0][None], 'col', axis=0, tiled=True)  25.4 us
    pallas_call x1, Pallas kernels, kept_partials(): pl.pallas_call(kernel, out_shape=jax.ShapeDtypeStruct((n_out, tile, tile)...  12.8 us
    ppermute x4, waiting for transfers between devices, butterfly_sum(): x = x + lax.ppermute(x, axis, [(i, i ^ d) for i in range(n)])  10.3 us
    all_gather x1, blocking collectives, local(): lax.all_gather(out_coords[0, 0, 0][None], 'layer', axis=0, tiled=True)  9.78 us
  transfers between devices with their start and end apart: 9, of which 6 were waited for; matrix products, arithmetic and copies ran while one was open for 8% of the time, Pallas kernels for 0%

profile of v6, /device:TPU:0, one launch (start us, length us, event | category | flops | bytes accessed | tf_op | source)
XLA Modules:
  0.0 214.7 jit_solution(17342494750588258546)
XLA Ops:
  7.3 2.1 collective-permute-start.1
  9.4 32.2 %all-gather = s32[4,1,1,32,2]{3,4,2,1,0:T(2,128)S(1)} all-gather(s32[1,1,1,32,2]{3,4,2,1,0:T(2,128)} %param.8), channel_id=2, replica_groups=mesh['row'=4,'col'=8,'layer'=4] {'row'}, dimensions={0}, use_global_device_ids=true | all-gather | bytes 1280 | tf_op jit(solution)/shard_map/all_gather | solution.py:95
  42.3 0.7 iota_reduce_fusion.2
  43.0 0.7 iota_reduce_fusion.3
  44.0 1.5 gather_fusion.4
  46.1 25.4 %all-gather.1 = s32[8,1,1,32,2]{3,4,2,1,0:T(2,128)S(1)} all-gather(s32[1,1,1,32,2]{3,4,2,1,0:T(2,128)S(1)} %copy-done.2), channel_id=3, replica_groups=mesh['row'=4,'col'=8,'layer'=4] {'col'}, dimensions={0}, use_global_device_ids=true | all-gather | bytes 2304 | tf_op jit(solution)/shard_map/all_gather | solution.py:97
  71.5 9.8 %all-gather.2 = s32[4,1,1,16,2]{3,4,2,1,0:T(2,128)S(1)} all-gather(s32[1,1,1,16,2]{3,4,2,1,0:T(2,128)S(1)} %copy-done.3), channel_id=4, replica_groups=mesh['row'=4,'col'=8,'layer'=4] {'layer'}, dimensions={0}, use_global_device_ids=true | all-gather | bytes 640 | tf_op jit(solution)/shard_map/all_gather | solution.py:98
  81.3 0.7 iota_reduce_fusion.1
  82.1 0.9 gather_fusion.5
  84.0 3.0 %iota_reduce_fusion = (pred[16,4,8]{2,1,0:T(4,128)(4,1)}, s32[16,4,8]{2,1,0:T(4,128)S(1)}) fusion(s32[16,4]{1,0:T(8,128)S(1)} %copy.60, s32[16,8,32]{2,1,0:T(8,128)S(1)} %bitcast.69), kind=kLoop, calls=%fused_computation.10 | loop fusion | flops 127488 | bytes 19200 | tf_op jit(solution)/shard_map/local/reduce | solution.py:128
  87.4 2.6 %gather_fusion.2 = s32[512]{0:T(512)S(1)} fusion(s32[8,32]{1,0:T(8,128)S(1)} %get-tuple-element.13, s32[512]{0:T(512)S(1)} %reshape.361), kind=kCustom, calls=%fused_computation.2 | custom fusion | bytes 8192 | tf_op jit(solution)/shard_map/gather | solution.py:131
  90.9 3.3 %pad_maximum_fusion = bf16[128,128,128]{2,1,0:T(8,128)(2,1)} fusion(bf16[32,128,128]{2,1,0:T(8,128)(2,1)} %collective-permute-done.2, bf16[32,128,128]{2,1,0:T(8,128)(2,1)S(1)} %collective-permute-done.1, bf16[32,128,128]{2,1,0:T(8,128)(2,1)S(1)} %collective-permute-done, bf16[32,128,128]{2,1,0:T(8,128)(2,1)S(1)} %bitcast.68), kind=kLoop, calls=%fused_computation.7 | loop fusion | flops 6291456 | bytes 8388608 | tf_op jit(solution)/shard_map/concatenate | solution.py:94
  94.2 35.7 %all-gather.6.cloned.1.call-done = bf16[1,1,1,256,128,128]{5,4,2,1,0,3:T(8,128)(2,1)} async-done(((bf16[1,1,1,32,128,128]{5,4,2,1,0,3:T(8,128)(2,1)}), bf16[1,1,1,256,128,128]{5,4,2,1,0,3:T(8,128)(2,1)}) %all-gather.6.cloned.1.call-update) | async-done | bytes 8388624 | tf_op jit(solution)/shard_map/all_gather | solution.py:96
  129.9 12.8 %shard_map.55 = f32[64,128,128]{2,1,0:T(8,128)S(1)} custom-call(s32[128]{0:T(128)S(1)} %reshape_reshape.3.goff_ref, s32[512]{0:T(512)S(1)} %reshape.340.moff_ref, s32[64]{0:T(128)S(1)} %reshape.341.oidx_ref, bf16[32768,128]{1,0:T(8,128)(2,1)} %bitcast.63, bf16[16384,128]{1,0:T(8,128)(2,1)} %bitcast.62), custom_call_target="tpu_custom_call" | custom-call | flops 2147483648 | bytes 16777216 | tf_op jit(solution)/shard_map/pallas_call | solution.py:38
  142.7 1.9 copy-done
  144.7 44.6 %reduce-scatter.2.cloned.1.call-done = f32[16,128,128]{2,1,0:T(8,128)} async-done(((f32[64,128,128]{2,1,0:T(8,128)}), f32[16,128,128]{2,1,0:T(8,128)}) %reduce-scatter.2.cloned.1.call-update) | async-done | bytes 1048592 | tf_op jit(solution)/shard_map/reduce_scatter | solution.py:146
  189.3 1.3 multiply_reduce_fusion
  191.3 1.2 collective-permute-done.3
  192.5 1.6 collective-permute-start.4
  194.0 2.1 collective-permute-done.4
  196.4 3.4 %collective-permute-done.5 = f32[16,128]{1,0:T(8,128)S(1)} collective-permute-done((f32[16,128]{1,0:T(8,128)S(1)}, f32[16,128]{1,0:T(8,128)S(1)}, u32[]{:S(2)}, u32[]{:S(2)}) %collective-permute-start.5) | collective-permute-done | bytes 8224 | tf_op jit(solution)/shard_map/ppermute | solution.py:65
  199.8 1.5 collective-permute-start.6
  201.3 3.7 %collective-permute-done.6 = f32[16,128]{1,0:T(8,128)S(1)} collective-permute-done((f32[16,128]{1,0:T(8,128)S(1)}, f32[16,128]{1,0:T(8,128)S(1)}, u32[]{:S(2)}, u32[]{:S(2)}) %collective-permute-start.6) | collective-permute-done | bytes 8224 | tf_op jit(solution)/shard_map/ppermute | solution.py:65
  205.5 2.3 %multiply_bitcast_fusion = f32[1,1,1,16,128,128]{5,4,3,2,1,0:T(8,128)} fusion(f32[16,128,128]{2,1,0:T(8,128)} %reduce-scatter.2.cloned.1.call-done, f32[16,128]{1,0:T(8,128)S(1)} %gather_fusion.3), kind=kLoop, calls=%fused_computation.8 | loop fusion | flops 524288 | bytes 2105344 | tf_op jit(solution)/shard_map/reshape | solution.py:155
  (72 shorter events, 6.0 us)
Async XLA Ops:
  6.5 123.4 %all-gather.6.cloned.1.call-start = ((), (), s32[]{:S(2)}) async-start(), calls=%async_computation.2 | async-start | bytes 9437184 | tf_op jit(solution)/shard_map/all_gather | solution.py:96
  7.3 182.0 %reduce-scatter.2.cloned.1.call-start = ((), (), s32[]{:S(2)}) async-start(), calls=%async_computation.1 | async-start | bytes 5242880 | tf_op jit(solution)/shard_map/reduce_scatter | solution.py:146
  7.3 76.6 %collective-permute-start.1 = (bf16[32,128,128]{2,1,0:T(8,128)(2,1)}, bf16[32,128,128]{2,1,0:T(8,128)(2,1)S(1)}, u32[]{:S(2)}, u32[]{:S(2)}) collective-permute-start(bf16[32,128,128]{2,1,0:T(8,128)(2,1)} %bitcast.66), channel_id=1, source_target_pairs={{0,64},{32,96},{64,0},{96,32},{1,65},{33,97},{65,1},{97,33},{2,66}... | collective-permute-start | bytes 3145736 | tf_op jit(solution)/shard_map/ppermute | solution.py:90
  9.4 81.5 %collective-permute-start = (bf16[32,128,128]{2,1,0:T(8,128)(2,1)}, bf16[32,128,128]{2,1,0:T(8,128)(2,1)S(1)}, u32[]{:S(2)}, u32[]{:S(2)}) collective-permute-start(bf16[32,128,128]{2,1,0:T(8,128)(2,1)} %bitcast.67), channel_id=1, source_target_pairs={{0,32},{32,0},{64,96},{96,64},{1,33},{33,1},{65,97},{97,65},{2,34}... | collective-permute-start | bytes 3145736 | tf_op jit(solution)/shard_map/ppermute | solution.py:91
  44.0 2.1 copy-start.2
  44.0 27.5 %copy-start.3 = (s32[1,1,1,16,2]{3,4,2,1,0:T(2,128)S(1)}, s32[1,1,1,16,2]{3,4,2,1,0:T(2,128)}, u32[]{:S(2)}) copy-start(s32[1,1,1,16,2]{3,4,2,1,0:T(2,128)} %param.9) | copy-start | bytes 388
  83.9 6.9 %collective-permute-start.2 = (bf16[32,128,128]{2,1,0:T(8,128)(2,1)S(1)}, bf16[32,128,128]{2,1,0:T(8,128)(2,1)}, u32[]{:S(2)}, u32[]{:S(2)}) collective-permute-start(bf16[32,128,128]{2,1,0:T(8,128)(2,1)S(1)} %collective-permute-done.1), channel_id=1, source_target_pairs={{0,32},{32,0},{64,96},{96,64},{1,33},{33,1},{65,97},{97,65},{2,34}... | collective-permute-start | bytes 3145736 | tf_op jit(solution)/shard_map/ppermute | solution.py:92
  87.4 3.5 %copy-start.1 = (bf16[1,1,1,32,128,128]{5,4,3,2,1,0:T(8,128)(2,1)S(1)}, bf16[1,1,1,32,128,128]{5,4,3,2,1,0:T(8,128)(2,1)}, u32[]{:S(2)}) copy-start(bf16[1,1,1,32,128,128]{5,4,3,2,1,0:T(8,128)(2,1)} %param.7) | copy-start | bytes 3145732
  142.7 1.9 copy-start
  191.2 1.3 collective-permute-start.3
  192.5 3.7 %collective-permute-start.4 = (f32[16,128]{1,0:T(8,128)S(1)}, f32[16,128]{1,0:T(8,128)S(1)}, u32[]{:S(2)}, u32[]{:S(2)}) collective-permute-start(f32[16,128]{1,0:T(8,128)S(1)} %add.175), channel_id=1, source_target_pairs={{0,64},{32,96},{64,0},{96,32},{1,65},{33,97},{65,1},{97,33},{2,66}... | collective-permute-start | bytes 24584 | tf_op jit(solution)/shard_map/ppermute | solution.py:65
  196.1 3.7 %collective-permute-start.5 = (f32[16,128]{1,0:T(8,128)S(1)}, f32[16,128]{1,0:T(8,128)S(1)}, u32[]{:S(2)}, u32[]{:S(2)}) collective-permute-start(f32[16,128]{1,0:T(8,128)S(1)} %add.176), channel_id=1, source_target_pairs={{0,1},{1,0},{2,3},{3,2},{4,5},{5,4},{6,7},{7,6},{8,9},{9,8},{10,11... | collective-permute-start | bytes 24584 | tf_op jit(solution)/shard_map/ppermute | solution.py:65
  199.8 5.2 %collective-permute-start.6 = (f32[16,128]{1,0:T(8,128)S(1)}, f32[16,128]{1,0:T(8,128)S(1)}, u32[]{:S(2)}, u32[]{:S(2)}) collective-permute-start(f32[16,128]{1,0:T(8,128)S(1)} %add.177), channel_id=1, source_target_pairs={{0,2},{1,3},{2,0},{3,1},{4,6},{5,7},{6,4},{7,5},{8,10},{9,11},{10,... | collective-permute-start | bytes 24584 | tf_op jit(solution)/shard_map/ppermute | solution.py:65
Sparse Core Ops, SparseCore 0:
  9.7 120.1 all-gather.5
  144.8 44.4 reduce-scatter.1

commit v7 on v6

--- a/solution.py
+++ b/solution.py
@@ -143,7 +143,14 @@
         layer_count,
         n_g,
     )
-    kept_tiles = lax.psum_scatter(partial_sum, "layer", scatter_dimension=0, tiled=True)
+    my_layer = lax.axis_index("layer")
+    by_quarter = partial_sum.reshape(layer_count, col_tiles, tile, tile)
+    kept_tiles = by_quarter[my_layer]
+    for s in range(1, layer_count):
+        send = by_quarter[(my_layer + s) % layer_count]
+        kept_tiles = kept_tiles + lax.ppermute(
+            send, "layer", [(i, (i + s) % layer_count) for i in range(layer_count)]
+        )
 
     kept_cols = out_coords[0, 0, 0, :, 1]
     squared = kept_tiles * kept_tiles

time: 215 us -> 220 us (1.023)
  starting transfers between devices: 5.55 us -> 12.6 us
  waiting for transfers between devices: 91.4 us -> 89 us
    reduce_scatter x1 -> x0, waiting for transfers between devices: 44.6 us -> none  [local(): lax.psum_scatter(partial_sum, 'layer', scatter_dimension=0, tiled=True)]
    ppermute x0 -> x3, waiting for transfers between devices: none -> 43.7 us  [local(): lax.ppermute(send, 'layer', [(i, (i + s) % layer_count) for i in range(la...]
    ppermute x0 -> x3, starting transfers between devices: none -> 5.61 us  [local(): lax.ppermute(send, 'layer', [(i, (i + s) % layer_count) for i in range(la...]
  transfers between devices with their start and end apart: 9 -> 11, of which waited for: 6 -> 7; matrix products, arithmetic and copies ran while one was open for 8% -> 8% of each run, Pallas kernels for 0% -> 0%
where the time goes in v7:
time: 220 us
  waiting for transfers between devices  89 us (40%)
  blocking collectives  67.3 us (31%)
  between operations  13.6 us (6%)
  local copies, waits for them, and re-layouts  13.1 us (6%)
  Pallas kernels  12.8 us (6%)
  starting transfers between devices  12.6 us (6%)
  other arithmetic  11.9 us (5%)
    ppermute x3, waiting for transfers between devices, local(): lax.ppermute(send, 'layer', [(i, (i + s) % layer_count) for i in range(la...  43.7 us
    all_gather x1, waiting for transfers between devices, local(): flow_tiles = lax.all_gather(a_tiles[0, 0, 0], 'col', axis=0, tiled=True)  35.8 us
    all_gather x1, blocking collectives, local(): lax.all_gather(b_coords[0, 0, 0][None], 'row', axis=0, tiled=True)  32.1 us
    all_gather x1, blocking collectives, local(): lax.all_gather(a_coords[0, 0, 0][None], 'col', axis=0, tiled=True)  25.4 us
    pallas_call x1, Pallas kernels, kept_partials(): pl.pallas_call(kernel, out_shape=jax.ShapeDtypeStruct((n_out, tile, tile)...  12.8 us
    all_gather x1, blocking collectives, local(): lax.all_gather(out_coords[0, 0, 0][None], 'layer', axis=0, tiled=True)  9.78 us
    ppermute x4, waiting for transfers between devices, butterfly_sum(): x = x + lax.ppermute(x, axis, [(i, i ^ d) for i in range(n)])  8.87 us
    ppermute x3, starting transfers between devices, local(): lax.ppermute(send, 'layer', [(i, (i + s) % layer_count) for i in range(la...  5.61 us
  transfers between devices with their start and end apart: 11, of which 7 were waited for; matrix products, arithmetic and copies ran while one was open for 8% of the time, Pallas kernels for 0%

profile of v7, /device:TPU:0, one launch (start us, length us, event | category | flops | bytes accessed | tf_op | source)
XLA Modules:
  0.0 220.3 jit_solution(10561150323330249178)
XLA Ops:
  7.3 2.1 collective-permute-start.1
  9.3 32.1 %all-gather = s32[4,1,1,32,2]{3,4,2,1,0:T(2,128)S(1)} all-gather(s32[1,1,1,32,2]{3,4,2,1,0:T(2,128)} %param.8), channel_id=2, replica_groups=mesh['row'=4,'col'=8,'layer'=4] {'row'}, dimensions={0}, use_global_device_ids=true | all-gather | bytes 1280 | tf_op jit(solution)/shard_map/all_gather | solution.py:95
  44.0 1.5 gather_fusion.4
  46.0 25.4 %all-gather.1 = s32[8,1,1,32,2]{3,4,2,1,0:T(2,128)S(1)} all-gather(s32[1,1,1,32,2]{3,4,2,1,0:T(2,128)S(1)} %copy-done.2), channel_id=3, replica_groups=mesh['row'=4,'col'=8,'layer'=4] {'col'}, dimensions={0}, use_global_device_ids=true | all-gather | bytes 2304 | tf_op jit(solution)/shard_map/all_gather | solution.py:97
  71.4 9.8 %all-gather.2 = s32[4,1,1,16,2]{3,4,2,1,0:T(2,128)S(1)} all-gather(s32[1,1,1,16,2]{3,4,2,1,0:T(2,128)S(1)} %copy-done.3), channel_id=4, replica_groups=mesh['row'=4,'col'=8,'layer'=4] {'layer'}, dimensions={0}, use_global_device_ids=true | all-gather | bytes 640 | tf_op jit(solution)/shard_map/all_gather | solution.py:98
  83.9 3.0 %iota_reduce_fusion = (pred[16,4,8]{2,1,0:T(4,128)(4,1)}, s32[16,4,8]{2,1,0:T(4,128)S(1)}) fusion(s32[16,4]{1,0:T(8,128)S(1)} %copy.60, s32[16,8,32]{2,1,0:T(8,128)S(1)} %bitcast.87), kind=kLoop, calls=%fused_computation.16 | loop fusion | flops 127488 | bytes 19200 | tf_op jit(solution)/shard_map/local/reduce | solution.py:128
  87.3 2.6 %gather_fusion.2 = s32[512]{0:T(512)S(1)} fusion(s32[8,32]{1,0:T(8,128)S(1)} %get-tuple-element.18, s32[512]{0:T(512)S(1)} %reshape.365), kind=kCustom, calls=%fused_computation.2 | custom fusion | bytes 8192 | tf_op jit(solution)/shard_map/gather | solution.py:131
  90.8 3.3 %pad_maximum_fusion = bf16[128,128,128]{2,1,0:T(8,128)(2,1)} fusion(bf16[32,128,128]{2,1,0:T(8,128)(2,1)} %collective-permute-done.2, bf16[32,128,128]{2,1,0:T(8,128)(2,1)S(1)} %collective-permute-done.1, bf16[32,128,128]{2,1,0:T(8,128)(2,1)S(1)} %collective-permute-done, bf16[32,128,128]{2,1,0:T(8,128)(2,1)S(1)} %bitcast.86), kind=kLoop, calls=%fused_computation.7 | loop fusion | flops 6291456 | bytes 8388608 | tf_op jit(solution)/shard_map/concatenate | solution.py:94
  94.1 35.8 %all-gather.6.cloned.1.call-done = bf16[1,1,1,256,128,128]{5,4,2,1,0,3:T(8,128)(2,1)} async-done(((bf16[1,1,1,32,128,128]{5,4,2,1,0,3:T(8,128)(2,1)}), bf16[1,1,1,256,128,128]{5,4,2,1,0,3:T(8,128)(2,1)}) %all-gather.6.cloned.1.call-update) | async-done | bytes 8388624 | tf_op jit(solution)/shard_map/all_gather | solution.py:96
  129.9 12.8 %shard_map.55 = f32[64,128,128]{2,1,0:T(8,128)S(1)} custom-call(s32[128]{0:T(128)S(1)} %reshape_reshape.3.goff_ref, s32[512]{0:T(512)S(1)} %reshape.343.moff_ref, s32[64]{0:T(128)S(1)} %reshape.344.oidx_ref, bf16[32768,128]{1,0:T(8,128)(2,1)} %bitcast.81, bf16[16384,128]{1,0:T(8,128)(2,1)} %bitcast.80), custom_call_target="tpu_custom_call" | custom-call | flops 2147483648 | bytes 16777216 | tf_op jit(solution)/shard_map/pallas_call | solution.py:38
  142.7 1.9 copy-done
  144.6 1.7 dynamic-slice_bitcast_fusion.2
  146.3 1.5 collective-permute-start.3
  147.7 2.7 %collective-permute-start.4 = (f32[16,128,128]{2,1,0:T(8,128)}, f32[16,128,128]{2,1,0:T(8,128)S(1)}, u32[]{:S(2)}, u32[]{:S(2)}) collective-permute-start(f32[16,128,128]{2,1,0:T(8,128)} %get-tuple-element.17), channel_id=1, source_target_pairs={{0,2},{1,3},{2,0},{3,1},{4,6},{5,7},{6,4},{7,5},{8,10},{9,11},{10,... | collective-permute-start | bytes 3145736 | tf_op jit(solution)/shard_map/ppermute | solution.py:151
  150.4 1.5 collective-permute-start.5
  151.9 21.0 %collective-permute-done.3 = f32[16,128,128]{2,1,0:T(8,128)S(1)} collective-permute-done((f32[16,128,128]{2,1,0:T(8,128)}, f32[16,128,128]{2,1,0:T(8,128)S(1)}, u32[]{:S(2)}, u32[]{:S(2)}) %collective-permute-start.3) | collective-permute-done | bytes 1048608 | tf_op jit(solution)/shard_map/ppermute | solution.py:151
  172.8 22.7 %collective-permute-done.4 = f32[16,128,128]{2,1,0:T(8,128)S(1)} collective-permute-done((f32[16,128,128]{2,1,0:T(8,128)}, f32[16,128,128]{2,1,0:T(8,128)S(1)}, u32[]{:S(2)}, u32[]{:S(2)}) %collective-permute-start.4) | collective-permute-done | bytes 1048608 | tf_op jit(solution)/shard_map/ppermute | solution.py:151
  195.6 1.9 fusion.18
  198.2 1.2 collective-permute-done.6
  200.0 3.0 %collective-permute-done.7 = f32[16,128]{1,0:T(8,128)S(1)} collective-permute-done((f32[16,128]{1,0:T(8,128)S(1)}, f32[16,128]{1,0:T(8,128)S(1)}, u32[]{:S(2)}, u32[]{:S(2)}) %collective-permute-start.7) | collective-permute-done | bytes 8224 | tf_op jit(solution)/shard_map/ppermute | solution.py:65
  203.0 1.3 collective-permute-start.8
  204.3 2.4 %collective-permute-done.8 = f32[16,128]{1,0:T(8,128)S(1)} collective-permute-done((f32[16,128]{1,0:T(8,128)S(1)}, f32[16,128]{1,0:T(8,128)S(1)}, u32[]{:S(2)}, u32[]{:S(2)}) %collective-permute-start.8) | collective-permute-done | bytes 8224 | tf_op jit(solution)/shard_map/ppermute | solution.py:65
  206.7 2.8 %collective-permute-start.9 = (f32[16,128]{1,0:T(8,128)S(1)}, f32[16,128]{1,0:T(8,128)S(1)}, u32[]{:S(2)}, u32[]{:S(2)}) collective-permute-start(f32[16,128]{1,0:T(8,128)S(1)} %add.228), channel_id=1, source_target_pairs={{0,2},{1,3},{2,0},{3,1},{4,6},{5,7},{6,4},{7,5},{8,10},{9,11},{10,... | collective-permute-start | bytes 24584 | tf_op jit(solution)/shard_map/ppermute | solution.py:65
  209.5 2.4 %collective-permute-done.9 = f32[16,128]{1,0:T(8,128)S(1)} collective-permute-done((f32[16,128]{1,0:T(8,128)S(1)}, f32[16,128]{1,0:T(8,128)S(1)}, u32[]{:S(2)}, u32[]{:S(2)}) %collective-permute-start.9) | collective-permute-done | bytes 8224 | tf_op jit(solution)/shard_map/ppermute | solution.py:65
  (76 shorter events, 10.5 us)
Async XLA Ops:
  6.5 123.3 %all-gather.6.cloned.1.call-start = ((), (), s32[]{:S(2)}) async-start(), calls=%async_computation | async-start | bytes 9437184 | tf_op jit(solution)/shard_map/all_gather | solution.py:96
  7.3 76.6 %collective-permute-start.1 = (bf16[32,128,128]{2,1,0:T(8,128)(2,1)}, bf16[32,128,128]{2,1,0:T(8,128)(2,1)S(1)}, u32[]{:S(2)}, u32[]{:S(2)}) collective-permute-start(bf16[32,128,128]{2,1,0:T(8,128)(2,1)} %bitcast.84), channel_id=1, source_target_pairs={{0,64},{32,96},{64,0},{96,32},{1,65},{33,97},{65,1},{97,33},{2,66}... | collective-permute-start | bytes 3145736 | tf_op jit(solution)/shard_map/ppermute | solution.py:90
  9.3 81.4 %collective-permute-start = (bf16[32,128,128]{2,1,0:T(8,128)(2,1)}, bf16[32,128,128]{2,1,0:T(8,128)(2,1)S(1)}, u32[]{:S(2)}, u32[]{:S(2)}) collective-permute-start(bf16[32,128,128]{2,1,0:T(8,128)(2,1)} %bitcast.85), channel_id=1, source_target_pairs={{0,32},{32,0},{64,96},{96,64},{1,33},{33,1},{65,97},{97,65},{2,34}... | collective-permute-start | bytes 3145736 | tf_op jit(solution)/shard_map/ppermute | solution.py:91
  43.9 2.1 copy-start.2
  43.9 27.5 %copy-start.3 = (s32[1,1,1,16,2]{3,4,2,1,0:T(2,128)S(1)}, s32[1,1,1,16,2]{3,4,2,1,0:T(2,128)}, u32[]{:S(2)}) copy-start(s32[1,1,1,16,2]{3,4,2,1,0:T(2,128)} %param.9) | copy-start | bytes 388
  83.8 6.9 %collective-permute-start.2 = (bf16[32,128,128]{2,1,0:T(8,128)(2,1)S(1)}, bf16[32,128,128]{2,1,0:T(8,128)(2,1)}, u32[]{:S(2)}, u32[]{:S(2)}) collective-permute-start(bf16[32,128,128]{2,1,0:T(8,128)(2,1)S(1)} %collective-permute-done.1), channel_id=1, source_target_pairs={{0,32},{32,0},{64,96},{96,64},{1,33},{33,1},{65,97},{97,65},{2,34}... | collective-permute-start | bytes 3145736 | tf_op jit(solution)/shard_map/ppermute | solution.py:92
  87.3 3.5 %copy-start.1 = (bf16[1,1,1,32,128,128]{5,4,3,2,1,0:T(8,128)(2,1)S(1)}, bf16[1,1,1,32,128,128]{5,4,3,2,1,0:T(8,128)(2,1)}, u32[]{:S(2)}) copy-start(bf16[1,1,1,32,128,128]{5,4,3,2,1,0:T(8,128)(2,1)} %param.7) | copy-start | bytes 3145732
  142.7 1.9 copy-start
  146.3 26.6 %collective-permute-start.3 = (f32[16,128,128]{2,1,0:T(8,128)}, f32[16,128,128]{2,1,0:T(8,128)S(1)}, u32[]{:S(2)}, u32[]{:S(2)}) collective-permute-start(f32[16,128,128]{2,1,0:T(8,128)} %get-tuple-element.15), channel_id=1, source_target_pairs={{0,1},{1,2},{2,3},{3,0},{4,5},{5,6},{6,7},{7,4},{8,9},{9,10},{10,1... | collective-permute-start | bytes 3145736 | tf_op jit(solution)/shard_map/ppermute | solution.py:151
  147.7 47.8 %collective-permute-start.4 = (f32[16,128,128]{2,1,0:T(8,128)}, f32[16,128,128]{2,1,0:T(8,128)S(1)}, u32[]{:S(2)}, u32[]{:S(2)}) collective-permute-start(f32[16,128,128]{2,1,0:T(8,128)} %get-tuple-element.17), channel_id=1, source_target_pairs={{0,2},{1,3},{2,0},{3,1},{4,6},{5,7},{6,4},{7,5},{8,10},{9,11},{10,... | collective-permute-start | bytes 3145736 | tf_op jit(solution)/shard_map/ppermute | solution.py:151
  150.4 45.1 %collective-permute-start.5 = (f32[16,128,128]{2,1,0:T(8,128)S(1)}, f32[16,128,128]{2,1,0:T(8,128)}, u32[]{:S(2)}, u32[]{:S(2)}) collective-permute-start(f32[16,128,128]{2,1,0:T(8,128)S(1)} %get-tuple-element.16), channel_id=1, source_target_pairs={{0,3},{1,0},{2,1},{3,2},{4,7},{5,4},{6,5},{7,6},{8,11},{9,8},{10,9... | collective-permute-start | bytes 3145736 | tf_op jit(solution)/shard_map/ppermute | solution.py:151
  198.1 1.3 collective-permute-start.6
  199.3 3.7 %collective-permute-start.7 = (f32[16,128]{1,0:T(8,128)S(1)}, f32[16,128]{1,0:T(8,128)S(1)}, u32[]{:S(2)}, u32[]{:S(2)}) collective-permute-start(f32[16,128]{1,0:T(8,128)S(1)} %add.226), channel_id=1, source_target_pairs={{0,64},{32,96},{64,0},{96,32},{1,65},{33,97},{65,1},{97,33},{2,66}... | collective-permute-start | bytes 24584 | tf_op jit(solution)/shard_map/ppermute | solution.py:65
  203.0 3.7 %collective-permute-start.8 = (f32[16,128]{1,0:T(8,128)S(1)}, f32[16,128]{1,0:T(8,128)S(1)}, u32[]{:S(2)}, u32[]{:S(2)}) collective-permute-start(f32[16,128]{1,0:T(8,128)S(1)} %add.227), channel_id=1, source_target_pairs={{0,1},{1,0},{2,3},{3,2},{4,5},{5,4},{6,7},{7,6},{8,9},{9,8},{10,11... | collective-permute-start | bytes 24584 | tf_op jit(solution)/shard_map/ppermute | solution.py:65
  206.7 5.2 %collective-permute-start.9 = (f32[16,128]{1,0:T(8,128)S(1)}, f32[16,128]{1,0:T(8,128)S(1)}, u32[]{:S(2)}, u32[]{:S(2)}) collective-permute-start(f32[16,128]{1,0:T(8,128)S(1)} %add.228), channel_id=1, source_target_pairs={{0,2},{1,3},{2,0},{3,1},{4,6},{5,7},{6,4},{7,5},{8,10},{9,11},{10,... | collective-permute-start | bytes 24584 | tf_op jit(solution)/shard_map/ppermute | solution.py:65
Sparse Core Ops, SparseCore 0:
  9.7 120.1 all-gather.5

commit v8 on v6

--- a/solution.py
+++ b/solution.py
@@ -8,6 +8,7 @@
 from jax.sharding import PartitionSpec as P
 
 KA = 4
+PAD = 16
 
 
 def column_kernel(goff_ref, moff_ref, oidx_ref, flow_ref, graph_ref, out_ref, lhs_ref, rhs_ref, *, n_q, n_g):
@@ -16,12 +17,12 @@
 
     def body(j, carry):
         for g in range(n_g):
-            g_off = pl.multiple_of(goff_ref[j * n_g + g], tile)
+            g_off = pl.multiple_of(goff_ref[j * n_g + g], PAD)
             rhs_ref[pl.ds(g * tile, tile), :] = graph_ref[pl.ds(g_off, tile), :]
         for q in range(n_q):
             for g in range(n_g):
                 m_off = moff_ref[(j * n_q + q) * n_g + g]
-                left = flow_ref[pl.ds(pl.multiple_of(jnp.maximum(m_off, 0), tile), tile), :]
+                left = flow_ref[pl.ds(pl.multiple_of(jnp.maximum(m_off, 0), PAD), tile), :]
                 left = jnp.where(m_off >= 0, left, jnp.zeros_like(left))
                 lhs_ref[pl.ds(q * tile, tile), pl.ds(g * tile, tile)] = left
         res = jnp.dot(lhs_ref[...], rhs_ref[...], preferred_element_type=jnp.float32)
@@ -67,6 +68,13 @@
     return x
 
 
+def pack_rows(tiles, rows):
+    tile = tiles.shape[-1]
+    extra = jnp.zeros((PAD, tile), jnp.bfloat16)
+    extra = extra.at[: rows.shape[0], : rows.shape[1]].set(rows.astype(jnp.bfloat16))
+    return jnp.concatenate([tiles.reshape(-1, tile), extra], axis=0)
+
+
 def first_two(mask):
     n = mask.shape[-1]
     lo = jnp.argmax(mask, axis=-1).astype(jnp.int32)
@@ -85,23 +93,39 @@
     col_tiles = out_coords.shape[3]
     n_b = b_tiles.shape[3]
     my_row = lax.axis_index("row")
+    my_layer = lax.axis_index("layer")
 
-    own = b_tiles[0, 0, 0]
+    own = pack_rows(b_tiles[0, 0, 0], b_coords[0, 0, 0].T)
     far = lax.ppermute(own, "row", [(i, i ^ 2) for i in range(row_count)])
     near = lax.ppermute(own, "row", [(i, i ^ 1) for i in range(row_count)])
     far_near = lax.ppermute(far, "row", [(i, i ^ 1) for i in range(row_count)])
     graph_parts = [own, near, far, far_near]
-    graph_tiles = jnp.concatenate(graph_parts, axis=0)
-    graph_coords = lax.all_gather(b_coords[0, 0, 0][None], "row", axis=0, tiled=True)
-    flow_tiles = lax.all_gather(a_tiles[0, 0, 0], "col", axis=0, tiled=True)
-    flow_coords = lax.all_gather(a_coords[0, 0, 0][None], "col", axis=0, tiled=True)
-    kept_all = lax.all_gather(out_coords[0, 0, 0][None], "layer", axis=0, tiled=True)
+    g_stride = n_b * tile + PAD
+    graph_flat = jnp.concatenate(graph_parts, axis=0)
+    coords_by_part = jnp.stack(
+        [p[n_b * tile : n_b * tile + 2, :n_b] for p in graph_parts]
+    ).astype(jnp.int32).transpose(0, 2, 1)
+    kept_parts = jnp.stack(
+        [out_coords[0, 0, 0]]
+        + [
+            lax.ppermute(out_coords[0, 0, 0], "layer", [(i, (i + s) % layer_count) for i in range(layer_count)])
+            for s in range(1, layer_count)
+        ]
+    )
+    q_ids = jnp.arange(layer_count, dtype=jnp.int32)
+    kept_all = kept_parts[(my_layer - q_ids) % layer_count]
+    a_own = pack_rows(a_tiles[0, 0, 0], a_coords[0, 0, 0].T)
+    a_stride = a_own.shape[0]
+    flow_all = lax.all_to_all(
+        jnp.broadcast_to(a_own[None], (col_count,) + a_own.shape), "col", 0, 0, tiled=True
+    )
+    flow_coords = flow_all[:, rows_panel * tile : rows_panel * tile + 2, :rows_panel].astype(jnp.int32)
+    flow_coords = flow_coords.transpose(0, 2, 1)
 
     n_out = layer_count * col_tiles
     col_ids = jnp.arange(col_tiles, dtype=jnp.int32)
     part_ids = jnp.arange(row_count, dtype=jnp.int32)
     owner_of_part = my_row ^ part_ids
-    coords_by_part = graph_coords[owner_of_part]
     in_col = coords_by_part[:, None, :, 1] == col_ids[None, :, None]
     lo, hi = first_two(in_col)
     g_slot = jnp.stack([lo, hi], axis=2)
@@ -109,7 +133,7 @@
         jnp.broadcast_to(coords_by_part[:, None, :, 0], in_col.shape), g_slot, axis=2
     )
     g_inner = owner_of_part[:, None, None] * b_span + g_b0
-    goff = ((part_ids[:, None, None] * n_b + g_slot) * tile).transpose(1, 0, 2).reshape(col_tiles, -1)
+    goff = (part_ids[:, None, None] * g_stride + g_slot * tile).transpose(1, 0, 2).reshape(col_tiles, -1)
     g_inner = g_inner.transpose(1, 0, 2).reshape(col_tiles, -1)
     n_g = goff.shape[1]
 
@@ -129,10 +153,9 @@
         a_rows[grp[:, None, :], :] == rows_q[:, :, None, None], axis=3
     ).astype(jnp.int32)
     have = a_inner[grp[:, None, :], slot_a] == want[:, None, :]
-    moff = jnp.where(have, (grp[:, None, :] * rows_panel + slot_a) * tile, -1)
+    moff = jnp.where(have, grp[:, None, :] * a_stride + slot_a * tile, -1)
 
-    flow_flat = flow_tiles.reshape(-1, tile)
-    graph_flat = graph_tiles.reshape(-1, tile)
+    flow_flat = flow_all.reshape(-1, tile)
     partial_sum = kept_partials(
         goff.reshape(-1).astype(jnp.int32),
         moff.reshape(-1).astype(jnp.int32),

time: 215 us -> 245 us (1.14)
  waiting for transfers between devices: 91.4 us -> 167 us
  blocking collectives: 67.4 us -> 0 us
  local copies, waits for them, and re-layouts: 11.4 us -> 23.2 us
  starting transfers between devices: 5.55 us -> 16.9 us
    ppermute x1, waiting for transfers between devices: 0.01 us -> 108 us  [local(): far = lax.ppermute(own, 'row', [(i, i ^ 2) for i in range(row_count)])]
    all_gather x3 -> x0, blocking collectives: 67.4 us -> none  [the longest x1 32.2 us: local(): lax.all_gather(b_coords[0, 0, 0][None], 'row', axis=0, tiled=True)]
    all_gather x1 -> x0, waiting for transfers between devices: 35.7 us -> none  [local(): flow_tiles = lax.all_gather(a_tiles[0, 0, 0], 'col', axis=0, tiled=True)]
    all_to_all x0 -> x1, starting transfers between devices: none -> 7.91 us  [local(): lax.all_to_all(jnp.broadcast_to(a_own[None], (col_count,) + a_own.shape),...]
    unnamed x8 -> x12, local copies, waits for them, and re-layouts: 1.94 us -> 6.95 us
    ppermute x0 -> x3, starting transfers between devices: none -> 4.53 us  [local(): lax.ppermute(out_coords[0, 0, 0], 'layer', [(i, (i + s) % layer_count) fo...]
    broadcast_in_dim x0 -> x1, local copies, waits for them, and re-layouts: none -> 4.32 us  [local(): jnp.broadcast_to(a_own[None], (col_count,) + a_own.shape)]
    reduce_scatter x1, waiting for transfers between devices: 44.6 us -> 48.4 us  [local(): lax.psum_scatter(partial_sum, 'layer', scatter_dimension=0, tiled=True)]
  transfers between devices with their start and end apart: 9 -> 12, of which waited for: 6 -> 6; matrix products, arithmetic and copies ran while one was open for 8% -> 8% of each run, Pallas kernels for 0% -> 0%
where the time goes in v8:
time: 245 us
  waiting for transfers between devices  167 us (68%)
  local copies, waits for them, and re-layouts  23.2 us (9%)
  starting transfers between devices  16.9 us (7%)
  between operations  13.7 us (6%)
  Pallas kernels  12.9 us (5%)
  other arithmetic  11.3 us (5%)
    ppermute x1, waiting for transfers between devices, local(): far = lax.ppermute(own, 'row', [(i, i ^ 2) for i in range(row_count)])  108 us
    reduce_scatter x1, waiting for transfers between devices, local(): lax.psum_scatter(partial_sum, 'layer', scatter_dimension=0, tiled=True)  48.4 us
    pallas_call x1, Pallas kernels, kept_partials(): pl.pallas_call(kernel, out_shape=jax.ShapeDtypeStruct((n_out, tile, tile)...  12.9 us
    ppermute x4, waiting for transfers between devices, butterfly_sum(): x = x + lax.ppermute(x, axis, [(i, i ^ d) for i in range(n)])  10.4 us
    all_to_all x1, starting transfers between devices, local(): lax.all_to_all(jnp.broadcast_to(a_own[None], (col_count,) + a_own.shape),...  7.91 us
    unnamed x12, local copies, waits for them, and re-layouts  6.95 us
  transfers between devices with their start and end apart: 12, of which 6 were waited for; matrix products, arithmetic and copies ran while one was open for 8% of the time, Pallas kernels for 0%

profile of v8, /device:TPU:0, one launch (start us, length us, event | category | flops | bytes accessed | tf_op | source)
XLA Modules:
  0.0 244.6 jit_solution(10434378980602081232)
XLA Ops:
  6.5 2.8 %collective-permute-start.5 = (s32[16,2]{0,1:T(2,128)}, s32[16,2]{0,1:T(2,128)S(1)}, u32[]{:S(2)}, u32[]{:S(2)}) collective-permute-start(s32[16,2]{0,1:T(2,128)} %bitcast.92), channel_id=1, source_target_pairs={{0,3},{1,0},{2,1},{3,2},{4,7},{5,4},{6,5},{7,6},{8,11},{9,8},{10,9... | collective-permute-start | bytes 392 | tf_op jit(solution)/shard_map/ppermute | solution.py:111
  11.7 1.3 fusion.1
  13.0 4.3 %broadcast_in_dim.23 = bf16[8,4112,128]{2,1,0:T(8,128)(2,1)} broadcast(bf16[4112,128]{1,0:T(8,128)(2,1)S(1)} %fusion.1), dimensions={1,2} | broadcast | bytes 9474048 | tf_op jit(solution)/shard_map/broadcast_in_dim | solution.py:120
  17.4 7.9 %all-to-all-start = ((bf16[8,4112,128]{2,1,0:T(8,128)(2,1)}), bf16[8,4112,128]{2,1,0:T(8,128)(2,1)}, u32[]{:S(2)}, u32[]{:S(2)}) async-start(bf16[8,4112,128]{2,1,0:T(8,128)(2,1)} %broadcast_in_dim.23), calls=%async_computation | async-start | bytes 16842752 | tf_op jit(solution)/shard_map/all_to_all | solution.py:119
  25.4 1.0 constant_dynamic-update-slice_fusion.4
  27.1 1.1 collective-permute-start.1
  31.0 107.9 %collective-permute-done.1 = bf16[4112,128]{1,0:T(8,128)(2,1)S(1)} collective-permute-done((bf16[4112,128]{1,0:T(8,128)(2,1)S(1)}, bf16[4112,128]{1,0:T(8,128)(2,1)S(1)}, u32[]{:S(2)}, u32[]{:S(2)}) %collective-permute-start.1) | collective-permute-done | bytes 1052704 | tf_op jit(solution)/shard_map/ppermute | solution.py:99
  139.5 2.3 constant_dynamic-update-slice_fusion.2
  141.8 1.1 constant_dynamic-update-slice_fusion.1
  144.8 1.5 gather_fusion.4
  147.3 1.1 constant_dynamic-update-slice_fusion.graph_ref
  149.7 3.0 %iota_reduce_fusion = (pred[16,4,8]{2,1,0:T(4,128)(4,1)}, s32[16,4,8]{2,1,0:T(4,128)S(1)}) fusion(s32[16,4]{1,0:T(8,128)S(1)} %copy.55, s32[16,8,32]{2,1,0:T(8,128)S(1)} %bitcast.83), kind=kLoop, calls=%fused_computation.13 | loop fusion | flops 127488 | bytes 19200 | tf_op jit(solution)/shard_map/local/reduce | solution.py:152
  153.0 2.6 %gather_fusion.2 = s32[512]{0:T(512)S(1)} fusion(s32[8,32]{1,0:T(8,128)S(1)} %get-tuple-element.37, s32[512]{0:T(512)S(1)} %reshape.450), kind=kCustom, calls=%fused_computation.2 | custom fusion | bytes 8192 | tf_op jit(solution)/shard_map/gather | solution.py:155
  155.9 12.9 %shard_map.55 = f32[64,128,128]{2,1,0:T(8,128)S(1)} custom-call(s32[128]{0:T(128)S(1)} %reshape_reshape.3.goff_ref, s32[512]{0:T(512)S(1)} %reshape.430.moff_ref, s32[64]{0:T(128)S(1)} %reshape.431.oidx_ref, bf16[32896,128]{1,0:T(8,128)(2,1)} %bitcast.38.flow_ref, bf16[16448,128]{1,0:T(8,128)(2,1)} %constant_dynamic-update-slice_fusion.graph_ref), custom_call_target="tpu_custom_call" | custom-call | flops 2147483648 | bytes 16826368 | tf_op jit(solution)/shard_map/pallas_call | solution.py:39
  168.9 1.9 copy-done
  170.8 48.4 %reduce-scatter.2.cloned.1.call-done = f32[16,128,128]{2,1,0:T(8,128)} async-done(((f32[64,128,128]{2,1,0:T(8,128)}), f32[16,128,128]{2,1,0:T(8,128)}) %reduce-scatter.2.cloned.1.call-update) | async-done | bytes 1048592 | tf_op jit(solution)/shard_map/reduce_scatter | solution.py:169
  219.2 1.3 multiply_reduce_fusion
  221.2 1.2 collective-permute-done.6
  222.4 1.5 collective-permute-start.7
  223.9 2.1 collective-permute-done.7
  226.3 3.4 %collective-permute-done.8 = f32[16,128]{1,0:T(8,128)S(1)} collective-permute-done((f32[16,128]{1,0:T(8,128)S(1)}, f32[16,128]{1,0:T(8,128)S(1)}, u32[]{:S(2)}, u32[]{:S(2)}) %collective-permute-start.8) | collective-permute-done | bytes 8224 | tf_op jit(solution)/shard_map/ppermute | solution.py:66
  229.7 1.4 collective-permute-start.9
  231.1 3.7 %collective-permute-done.9 = f32[16,128]{1,0:T(8,128)S(1)} collective-permute-done((f32[16,128]{1,0:T(8,128)S(1)}, f32[16,128]{1,0:T(8,128)S(1)}, u32[]{:S(2)}, u32[]{:S(2)}) %collective-permute-start.9) | collective-permute-done | bytes 8224 | tf_op jit(solution)/shard_map/ppermute | solution.py:66
  235.4 2.3 multiply_bitcast_fusion
  (88 shorter events, 12.7 us)
Async XLA Ops:
  6.5 21.7 %collective-permute-start.5 = (s32[16,2]{0,1:T(2,128)}, s32[16,2]{0,1:T(2,128)S(1)}, u32[]{:S(2)}, u32[]{:S(2)}) collective-permute-start(s32[16,2]{0,1:T(2,128)} %bitcast.92), channel_id=1, source_target_pairs={{0,3},{1,0},{2,1},{3,2},{4,7},{5,4},{6,5},{7,6},{8,11},{9,8},{10,9... | collective-permute-start | bytes 392 | tf_op jit(solution)/shard_map/ppermute | solution.py:111
  9.4 18.9 %collective-permute-start.4 = (s32[16,2]{0,1:T(2,128)}, s32[16,2]{0,1:T(2,128)S(1)}, u32[]{:S(2)}, u32[]{:S(2)}) collective-permute-start(s32[16,2]{0,1:T(2,128)} %bitcast.93), channel_id=1, source_target_pairs={{0,2},{1,3},{2,0},{3,1},{4,6},{5,7},{6,4},{7,5},{8,10},{9,11},{10,... | collective-permute-start | bytes 392 | tf_op jit(solution)/shard_map/ppermute | solution.py:111
  10.2 18.1 %collective-permute-start.3 = (s32[16,2]{0,1:T(2,128)}, s32[16,2]{0,1:T(2,128)S(1)}, u32[]{:S(2)}, u32[]{:S(2)}) collective-permute-start(s32[16,2]{0,1:T(2,128)} %bitcast.94), channel_id=1, source_target_pairs={{0,1},{1,2},{2,3},{3,0},{4,5},{5,6},{6,7},{7,4},{8,9},{9,10},{10,1... | collective-permute-start | bytes 392 | tf_op jit(solution)/shard_map/ppermute | solution.py:111
  17.4 8.0 %copy-start.2 = (s32[1,1,1,32,2]{3,4,2,1,0:T(2,128)S(1)}, s32[1,1,1,32,2]{3,4,2,1,0:T(2,128)}, u32[]{:S(2)}) copy-start(s32[1,1,1,32,2]{3,4,2,1,0:T(2,128)} %param.12) | copy-start | bytes 772
  17.4 8.0 %copy-start.1 = (bf16[1,1,1,32,128,128]{5,4,3,2,1,0:T(8,128)(2,1)S(1)}, bf16[1,1,1,32,128,128]{5,4,3,2,1,0:T(8,128)(2,1)}, u32[]{:S(2)}) copy-start(bf16[1,1,1,32,128,128]{5,4,3,2,1,0:T(8,128)(2,1)} %param.11) | copy-start | bytes 3145732
  17.4 131.0 %all-to-all-start = ((bf16[8,4112,128]{2,1,0:T(8,128)(2,1)}), bf16[8,4112,128]{2,1,0:T(8,128)(2,1)}, u32[]{:S(2)}, u32[]{:S(2)}) async-start(bf16[8,4112,128]{2,1,0:T(8,128)(2,1)} %broadcast_in_dim.23), calls=%async_computation | async-start | bytes 16842752 | tf_op jit(solution)/shard_map/all_to_all | solution.py:119
  25.3 193.9 %reduce-scatter.2.cloned.1.call-start = ((), (), s32[]{:S(2)}) async-start(), calls=%async_computation.2 | async-start | bytes 5242880 | tf_op jit(solution)/shard_map/reduce_scatter | solution.py:169
  25.4 2.9 %copy-start.3 = (s32[1,1,1,16,2]{3,4,2,1,0:T(2,128)S(1)}, s32[1,1,1,16,2]{3,4,2,1,0:T(2,128)}, u32[]{:S(2)}) copy-start(s32[1,1,1,16,2]{3,4,2,1,0:T(2,128)} %param.13) | copy-start | bytes 388
  27.1 111.8 %collective-permute-start.1 = (bf16[4112,128]{1,0:T(8,128)(2,1)S(1)}, bf16[4112,128]{1,0:T(8,128)(2,1)S(1)}, u32[]{:S(2)}, u32[]{:S(2)}) collective-permute-start(bf16[4112,128]{1,0:T(8,128)(2,1)S(1)} %pad_maximum_fusion), channel_id=1, source_target_pairs={{0,64},{32,96},{64,0},{96,32},{1,65},{33,97},{65,1},{97,33},{2,66}... | collective-permute-start | bytes 3158024 | tf_op jit(solution)/shard_map/ppermute | solution.py:99
  28.2 110.7 %collective-permute-start = (bf16[4112,128]{1,0:T(8,128)(2,1)S(1)}, bf16[4112,128]{1,0:T(8,128)(2,1)}, u32[]{:S(2)}, u32[]{:S(2)}) collective-permute-start(bf16[4112,128]{1,0:T(8,128)(2,1)S(1)} %pad_maximum_fusion), channel_id=1, source_target_pairs={{0,32},{32,0},{64,96},{96,64},{1,33},{33,1},{65,97},{97,65},{2,34}... | collective-permute-start | bytes 3158024 | tf_op jit(solution)/shard_map/ppermute | solution.py:100
  138.9 4.0 %collective-permute-start.2 = (bf16[4112,128]{1,0:T(8,128)(2,1)S(1)}, bf16[4112,128]{1,0:T(8,128)(2,1)S(1)}, u32[]{:S(2)}, u32[]{:S(2)}) collective-permute-start(bf16[4112,128]{1,0:T(8,128)(2,1)S(1)} %collective-permute-done.1), channel_id=1, source_target_pairs={{0,32},{32,0},{64,96},{96,64},{1,33},{33,1},{65,97},{97,65},{2,34}... | collective-permute-start | bytes 3158024 | tf_op jit(solution)/shard_map/ppermute | solution.py:101
  168.8 1.9 copy-start
  221.1 1.3 collective-permute-start.6
  222.4 3.7 %collective-permute-start.7 = (f32[16,128]{1,0:T(8,128)S(1)}, f32[16,128]{1,0:T(8,128)S(1)}, u32[]{:S(2)}, u32[]{:S(2)}) collective-permute-start(f32[16,128]{1,0:T(8,128)S(1)} %add.197), channel_id=1, source_target_pairs={{0,64},{32,96},{64,0},{96,32},{1,65},{33,97},{65,1},{97,33},{2,66}... | collective-permute-start | bytes 24584 | tf_op jit(solution)/shard_map/ppermute | solution.py:66
  226.0 3.7 %collective-permute-start.8 = (f32[16,128]{1,0:T(8,128)S(1)}, f32[16,128]{1,0:T(8,128)S(1)}, u32[]{:S(2)}, u32[]{:S(2)}) collective-permute-start(f32[16,128]{1,0:T(8,128)S(1)} %add.198), channel_id=1, source_target_pairs={{0,1},{1,0},{2,3},{3,2},{4,5},{5,4},{6,7},{7,6},{8,9},{9,8},{10,11... | collective-permute-start | bytes 24584 | tf_op jit(solution)/shard_map/ppermute | solution.py:66
  229.7 5.2 %collective-permute-start.9 = (f32[16,128]{1,0:T(8,128)S(1)}, f32[16,128]{1,0:T(8,128)S(1)}, u32[]{:S(2)}, u32[]{:S(2)}) collective-permute-start(f32[16,128]{1,0:T(8,128)S(1)} %add.199), channel_id=1, source_target_pairs={{0,2},{1,3},{2,0},{3,1},{4,6},{5,7},{6,4},{7,5},{8,10},{9,11},{10,... | collective-permute-start | bytes 24584 | tf_op jit(solution)/shard_map/ppermute | solution.py:66
Sparse Core Ops, SparseCore 0:
  170.9 48.2 reduce-scatter.1

commit v9 on v6

--- a/solution.py
+++ b/solution.py
@@ -143,7 +143,10 @@
         layer_count,
         n_g,
     )
-    kept_tiles = lax.psum_scatter(partial_sum, "layer", scatter_dimension=0, tiled=True)
+    from_layers = lax.all_to_all(
+        partial_sum.reshape(layer_count, col_tiles, tile, tile), "layer", 0, 0, tiled=True
+    )
+    kept_tiles = jnp.sum(from_layers, axis=0)
 
     kept_cols = out_coords[0, 0, 0, :, 1]
     squared = kept_tiles * kept_tiles

time: 215 us -> 224 us (1.042)
  waiting for transfers between devices: 91.4 us -> 97 us
  starting transfers between devices: 5.55 us -> 8.94 us
    all_to_all x0 -> x1, waiting for transfers between devices: none -> 48.7 us  [local(): lax.all_to_all(partial_sum.reshape(layer_count, col_tiles, tile, tile), '...]
    reduce_scatter x1 -> x0, waiting for transfers between devices: 44.6 us -> none  [local(): lax.psum_scatter(partial_sum, 'layer', scatter_dimension=0, tiled=True)]
    all_to_all x0 -> x1, starting transfers between devices: none -> 4.86 us  [local(): lax.all_to_all(partial_sum.reshape(layer_count, col_tiles, tile, tile), '...]
    reduce_sum x0 -> x1, other arithmetic: none -> 2.6 us  [local(): kept_tiles = jnp.sum(from_layers, axis=0)]
    reshape x1 -> x0, other arithmetic: 2.32 us -> none  [local(): return flow.reshape(1, 1, 1, col_tiles, tile, tile)]
where the time goes in v9:
time: 224 us
  waiting for transfers between devices  97 us (43%)
  blocking collectives  67.3 us (30%)
  between operations  13.6 us (6%)
  Pallas kernels  12.8 us (6%)
  other arithmetic  12.7 us (6%)
  local copies, waits for them, and re-layouts  11.4 us (5%)
  starting transfers between devices  8.94 us (4%)
    all_to_all x1, waiting for transfers between devices, local(): lax.all_to_all(partial_sum.reshape(layer_count, col_tiles, tile, tile), '...  48.7 us
    all_gather x1, waiting for transfers between devices, local(): flow_tiles = lax.all_gather(a_tiles[0, 0, 0], 'col', axis=0, tiled=True)  35.8 us
    all_gather x1, blocking collectives, local(): lax.all_gather(b_coords[0, 0, 0][None], 'row', axis=0, tiled=True)  32.1 us
    all_gather x1, blocking collectives, local(): lax.all_gather(a_coords[0, 0, 0][None], 'col', axis=0, tiled=True)  25.4 us
    pallas_call x1, Pallas kernels, kept_partials(): pl.pallas_call(kernel, out_shape=jax.ShapeDtypeStruct((n_out, tile, tile)...  12.8 us
    ppermute x4, waiting for transfers between devices, butterfly_sum(): x = x + lax.ppermute(x, axis, [(i, i ^ d) for i in range(n)])  11.8 us
    all_gather x1, blocking collectives, local(): lax.all_gather(out_coords[0, 0, 0][None], 'layer', axis=0, tiled=True)  9.78 us
    all_to_all x1, starting transfers between devices, local(): lax.all_to_all(partial_sum.reshape(layer_count, col_tiles, tile, tile), '...  4.86 us
  transfers between devices with their start and end apart: 9, of which 6 were waited for; matrix products, arithmetic and copies ran while one was open for 8% of the time, Pallas kernels for 0%

profile of v9, /device:TPU:0, one launch (start us, length us, event | category | flops | bytes accessed | tf_op | source)
XLA Modules:
  0.0 223.8 jit_solution(2410629472258431802)
XLA Ops:
  6.5 0.7 all-gather.6.cloned.1.call-update
  7.3 2.1 collective-permute-start.1
  9.3 32.1 %all-gather = s32[4,1,1,32,2]{3,4,2,1,0:T(2,128)S(1)} all-gather(s32[1,1,1,32,2]{3,4,2,1,0:T(2,128)} %param.8), channel_id=2, replica_groups=mesh['row'=4,'col'=8,'layer'=4] {'row'}, dimensions={0}, use_global_device_ids=true | all-gather | bytes 1280 | tf_op jit(solution)/shard_map/all_gather | solution.py:95
  42.2 0.7 iota_reduce_fusion.2
  42.9 0.7 iota_reduce_fusion.3
  44.0 1.5 gather_fusion.4
  46.0 25.4 %all-gather.1 = s32[8,1,1,32,2]{3,4,2,1,0:T(2,128)S(1)} all-gather(s32[1,1,1,32,2]{3,4,2,1,0:T(2,128)S(1)} %copy-done.2), channel_id=3, replica_groups=mesh['row'=4,'col'=8,'layer'=4] {'col'}, dimensions={0}, use_global_device_ids=true | all-gather | bytes 2304 | tf_op jit(solution)/shard_map/all_gather | solution.py:97
  71.4 9.8 %all-gather.2 = s32[4,1,1,16,2]{3,4,2,1,0:T(2,128)S(1)} all-gather(s32[1,1,1,16,2]{3,4,2,1,0:T(2,128)S(1)} %copy-done.3), channel_id=4, replica_groups=mesh['row'=4,'col'=8,'layer'=4] {'layer'}, dimensions={0}, use_global_device_ids=true | all-gather | bytes 640 | tf_op jit(solution)/shard_map/all_gather | solution.py:98
  81.2 0.7 iota_reduce_fusion.1
  82.0 0.9 gather_fusion.5
  83.9 3.0 %iota_reduce_fusion = (pred[16,4,8]{2,1,0:T(4,128)(4,1)}, s32[16,4,8]{2,1,0:T(4,128)S(1)}) fusion(s32[16,4]{1,0:T(8,128)S(1)} %copy.60, s32[16,8,32]{2,1,0:T(8,128)S(1)} %bitcast.71), kind=kLoop, calls=%fused_computation.10 | loop fusion | flops 127488 | bytes 19200 | tf_op jit(solution)/shard_map/local/reduce | solution.py:128
  87.3 2.6 %gather_fusion.2 = s32[512]{0:T(512)S(1)} fusion(s32[8,32]{1,0:T(8,128)S(1)} %get-tuple-element.13, s32[512]{0:T(512)S(1)} %reshape.373), kind=kCustom, calls=%fused_computation.2 | custom fusion | bytes 8192 | tf_op jit(solution)/shard_map/gather | solution.py:131
  90.8 3.3 %pad_maximum_fusion = bf16[128,128,128]{2,1,0:T(8,128)(2,1)} fusion(bf16[32,128,128]{2,1,0:T(8,128)(2,1)} %collective-permute-done.2, bf16[32,128,128]{2,1,0:T(8,128)(2,1)S(1)} %collective-permute-done.1, bf16[32,128,128]{2,1,0:T(8,128)(2,1)S(1)} %collective-permute-done, bf16[32,128,128]{2,1,0:T(8,128)(2,1)S(1)} %bitcast.70), kind=kLoop, calls=%fused_computation.7 | loop fusion | flops 6291456 | bytes 8388608 | tf_op jit(solution)/shard_map/concatenate | solution.py:94
  94.1 35.8 %all-gather.6.cloned.1.call-done = bf16[1,1,1,256,128,128]{5,4,2,1,0,3:T(8,128)(2,1)} async-done(((bf16[1,1,1,32,128,128]{5,4,2,1,0,3:T(8,128)(2,1)}), bf16[1,1,1,256,128,128]{5,4,2,1,0,3:T(8,128)(2,1)}) %all-gather.6.cloned.1.call-update) | async-done | bytes 8388624 | tf_op jit(solution)/shard_map/all_gather | solution.py:96
  129.9 12.8 %shard_map.55 = f32[64,128,128]{2,1,0:T(8,128)S(1)} custom-call(s32[128]{0:T(128)S(1)} %reshape_reshape.3.goff_ref, s32[512]{0:T(512)S(1)} %reshape.352.moff_ref, s32[64]{0:T(128)S(1)} %reshape.353.oidx_ref, bf16[32768,128]{1,0:T(8,128)(2,1)} %bitcast.65, bf16[16384,128]{1,0:T(8,128)(2,1)} %bitcast.64), custom_call_target="tpu_custom_call" | custom-call | flops 2147483648 | bytes 16777216 | tf_op jit(solution)/shard_map/pallas_call | solution.py:38
  142.7 2.0 copy-done
  144.6 4.9 %all-to-all-start = ((f32[4,16,128,128]{3,2,1,0:T(8,128)}), f32[4,16,128,128]{3,2,1,0:T(8,128)}, u32[]{:S(2)}, u32[]{:S(2)}) async-start(f32[4,16,128,128]{3,2,1,0:T(8,128)} %bitcast.63), calls=%async_computation | async-start | bytes 8388608 | tf_op jit(solution)/shard_map/all_to_all | solution.py:146
  149.5 48.7 %all-to-all-done = f32[4,16,128,128]{3,2,1,0:T(8,128)} async-done(((f32[4,16,128,128]{3,2,1,0:T(8,128)}), f32[4,16,128,128]{3,2,1,0:T(8,128)}, u32[]{:S(2)}, u32[]{:S(2)}) %all-to-all-start) | async-done | bytes 4194336 | tf_op jit(solution)/shard_map/all_to_all | solution.py:146
  198.2 2.6 %reduce_sum.18 = f32[16,128,128]{2,1,0:T(8,128)S(1)} reduce(f32[4,16,128,128]{3,2,1,0:T(8,128)} %all-to-all-done, f32[]{:T(128)} %constant.100.clone.1), dimensions={0}, to_apply=%region_4.5 | reduce | flops 786432 | bytes 5242884 | tf_op jit(solution)/shard_map/reduce_sum | solution.py:149
  201.6 1.2 collective-permute-done.3
  203.5 3.0 %collective-permute-done.4 = f32[16,128]{1,0:T(8,128)S(1)} collective-permute-done((f32[16,128]{1,0:T(8,128)S(1)}, f32[16,128]{1,0:T(8,128)S(1)}, u32[]{:S(2)}, u32[]{:S(2)}) %collective-permute-start.4) | collective-permute-done | bytes 8224 | tf_op jit(solution)/shard_map/ppermute | solution.py:65
  207.0 3.1 %collective-permute-done.5 = f32[16,128]{1,0:T(8,128)S(1)} collective-permute-done((f32[16,128]{1,0:T(8,128)S(1)}, f32[16,128]{1,0:T(8,128)S(1)}, u32[]{:S(2)}, u32[]{:S(2)}) %collective-permute-start.5) | collective-permute-done | bytes 8224 | tf_op jit(solution)/shard_map/ppermute | solution.py:65
  210.7 4.5 %collective-permute-done.6 = f32[16,128]{1,0:T(8,128)S(1)} collective-permute-done((f32[16,128]{1,0:T(8,128)S(1)}, f32[16,128]{1,0:T(8,128)S(1)}, u32[]{:S(2)}, u32[]{:S(2)}) %collective-permute-start.6) | collective-permute-done | bytes 8224 | tf_op jit(solution)/shard_map/ppermute | solution.py:65
  215.8 1.1 bitcast_multiply_fusion
  (72 shorter events, 6.9 us)
Async XLA Ops:
  6.5 123.3 %all-gather.6.cloned.1.call-start = ((), (), s32[]{:S(2)}) async-start(), calls=%async_computation.1 | async-start | bytes 9437184 | tf_op jit(solution)/shard_map/all_gather | solution.py:96
  7.3 76.6 %collective-permute-start.1 = (bf16[32,128,128]{2,1,0:T(8,128)(2,1)}, bf16[32,128,128]{2,1,0:T(8,128)(2,1)S(1)}, u32[]{:S(2)}, u32[]{:S(2)}) collective-permute-start(bf16[32,128,128]{2,1,0:T(8,128)(2,1)} %bitcast.68), channel_id=1, source_target_pairs={{0,64},{32,96},{64,0},{96,32},{1,65},{33,97},{65,1},{97,33},{2,66}... | collective-permute-start | bytes 3145736 | tf_op jit(solution)/shard_map/ppermute | solution.py:90
  9.3 81.4 %collective-permute-start = (bf16[32,128,128]{2,1,0:T(8,128)(2,1)}, bf16[32,128,128]{2,1,0:T(8,128)(2,1)S(1)}, u32[]{:S(2)}, u32[]{:S(2)}) collective-permute-start(bf16[32,128,128]{2,1,0:T(8,128)(2,1)} %bitcast.69), channel_id=1, source_target_pairs={{0,32},{32,0},{64,96},{96,64},{1,33},{33,1},{65,97},{97,65},{2,34}... | collective-permute-start | bytes 3145736 | tf_op jit(solution)/shard_map/ppermute | solution.py:91
  43.9 2.1 copy-start.2
  43.9 27.5 %copy-start.3 = (s32[1,1,1,16,2]{3,4,2,1,0:T(2,128)S(1)}, s32[1,1,1,16,2]{3,4,2,1,0:T(2,128)}, u32[]{:S(2)}) copy-start(s32[1,1,1,16,2]{3,4,2,1,0:T(2,128)} %param.9) | copy-start | bytes 388
  83.8 6.9 %collective-permute-start.2 = (bf16[32,128,128]{2,1,0:T(8,128)(2,1)S(1)}, bf16[32,128,128]{2,1,0:T(8,128)(2,1)}, u32[]{:S(2)}, u32[]{:S(2)}) collective-permute-start(bf16[32,128,128]{2,1,0:T(8,128)(2,1)S(1)} %collective-permute-done.1), channel_id=1, source_target_pairs={{0,32},{32,0},{64,96},{96,64},{1,33},{33,1},{65,97},{97,65},{2,34}... | collective-permute-start | bytes 3145736 | tf_op jit(solution)/shard_map/ppermute | solution.py:92
  87.3 3.5 %copy-start.1 = (bf16[1,1,1,32,128,128]{5,4,3,2,1,0:T(8,128)(2,1)S(1)}, bf16[1,1,1,32,128,128]{5,4,3,2,1,0:T(8,128)(2,1)}, u32[]{:S(2)}) copy-start(bf16[1,1,1,32,128,128]{5,4,3,2,1,0:T(8,128)(2,1)} %param.7) | copy-start | bytes 3145732
  142.7 2.0 copy-start
  144.6 53.6 %all-to-all-start = ((f32[4,16,128,128]{3,2,1,0:T(8,128)}), f32[4,16,128,128]{3,2,1,0:T(8,128)}, u32[]{:S(2)}, u32[]{:S(2)}) async-start(f32[4,16,128,128]{3,2,1,0:T(8,128)} %bitcast.63), calls=%async_computation | async-start | bytes 8388608 | tf_op jit(solution)/shard_map/all_to_all | solution.py:146
  201.5 1.3 collective-permute-start.3
  202.8 3.7 %collective-permute-start.4 = (f32[16,128]{1,0:T(8,128)S(1)}, f32[16,128]{1,0:T(8,128)S(1)}, u32[]{:S(2)}, u32[]{:S(2)}) collective-permute-start(f32[16,128]{1,0:T(8,128)S(1)} %add.173), channel_id=1, source_target_pairs={{0,64},{32,96},{64,0},{96,32},{1,65},{33,97},{65,1},{97,33},{2,66}... | collective-permute-start | bytes 24584 | tf_op jit(solution)/shard_map/ppermute | solution.py:65
  206.5 3.7 %collective-permute-start.5 = (f32[16,128]{1,0:T(8,128)S(1)}, f32[16,128]{1,0:T(8,128)S(1)}, u32[]{:S(2)}, u32[]{:S(2)}) collective-permute-start(f32[16,128]{1,0:T(8,128)S(1)} %add.174), channel_id=1, source_target_pairs={{0,1},{1,0},{2,3},{3,2},{4,5},{5,4},{6,7},{7,6},{8,9},{9,8},{10,11... | collective-permute-start | bytes 24584 | tf_op jit(solution)/shard_map/ppermute | solution.py:65
  210.1 5.2 %collective-permute-start.6 = (f32[16,128]{1,0:T(8,128)S(1)}, f32[16,128]{1,0:T(8,128)S(1)}, u32[]{:S(2)}, u32[]{:S(2)}) collective-permute-start(f32[16,128]{1,0:T(8,128)S(1)} %add.175), channel_id=1, source_target_pairs={{0,2},{1,3},{2,0},{3,1},{4,6},{5,7},{6,4},{7,5},{8,10},{9,11},{10,... | collective-permute-start | bytes 24584 | tf_op jit(solution)/shard_map/ppermute | solution.py:65
Sparse Core Ops, SparseCore 0:
  9.7 120.1 all-gather.5

commit v10 on v6

--- a/solution.py
+++ b/solution.py
@@ -10,21 +10,19 @@
 KA = 4
 
 
-def column_kernel(goff_ref, moff_ref, oidx_ref, flow_ref, graph_ref, out_ref, lhs_ref, rhs_ref, *, n_q, n_g):
+def column_kernel(moff_ref, oidx_ref, flow_ref, graph_ref, out_ref, lhs_ref, *, n_q, n_g):
     tile = out_ref.shape[-1]
     n_col = out_ref.shape[0] // n_q
 
     def body(j, carry):
-        for g in range(n_g):
-            g_off = pl.multiple_of(goff_ref[j * n_g + g], tile)
-            rhs_ref[pl.ds(g * tile, tile), :] = graph_ref[pl.ds(g_off, tile), :]
         for q in range(n_q):
             for g in range(n_g):
                 m_off = moff_ref[(j * n_q + q) * n_g + g]
                 left = flow_ref[pl.ds(pl.multiple_of(jnp.maximum(m_off, 0), tile), tile), :]
                 left = jnp.where(m_off >= 0, left, jnp.zeros_like(left))
                 lhs_ref[pl.ds(q * tile, tile), pl.ds(g * tile, tile)] = left
-        res = jnp.dot(lhs_ref[...], rhs_ref[...], preferred_element_type=jnp.float32)
+        right = graph_ref[pl.ds(pl.multiple_of(j * n_g * tile, n_g * tile), n_g * tile), :]
+        res = jnp.dot(lhs_ref[...], right, preferred_element_type=jnp.float32)
         for q in range(n_q):
             out_ref[oidx_ref[j * n_q + q]] = res[q * tile : (q + 1) * tile]
         return carry
@@ -32,7 +30,7 @@
     lax.fori_loop(0, n_col, body, 0)
 
 
-def kept_partials(goff, moff, oidx, flow_flat, graph_flat, n_out, n_q, n_g):
+def kept_partials(moff, oidx, flow_flat, graph_flat, n_out, n_q, n_g):
     tile = flow_flat.shape[-1]
     kernel = functools.partial(column_kernel, n_q=n_q, n_g=n_g)
     return pl.pallas_call(
@@ -41,14 +39,12 @@
         in_specs=[
             pl.BlockSpec(memory_space=pltpu.SMEM),
             pl.BlockSpec(memory_space=pltpu.SMEM),
-            pl.BlockSpec(memory_space=pltpu.SMEM),
             pl.BlockSpec(memory_space=pltpu.VMEM),
             pl.BlockSpec(memory_space=pltpu.VMEM),
         ],
         out_specs=pl.BlockSpec(memory_space=pltpu.VMEM),
         scratch_shapes=[
             pltpu.VMEM((n_q * tile, n_g * tile), jnp.bfloat16),
-            pltpu.VMEM((n_g * tile, tile), jnp.bfloat16),
         ],
         compiler_params=pltpu.CompilerParams(vmem_limit_bytes=48 * 1024 * 1024),
         cost_estimate=pl.CostEstimate(
@@ -56,14 +52,12 @@
             transcendentals=0,
             bytes_accessed=2 * (flow_flat.size + graph_flat.size) + 4 * n_out * tile * tile,
         ),
-    )(goff, moff, oidx, flow_flat, graph_flat)
+    )(moff, oidx, flow_flat, graph_flat)
 
 
-def butterfly_sum(x, axis, n):
-    d = 1
-    while d < n:
+def butterfly_sum(x, axis, n, masks):
+    for d in masks:
         x = x + lax.ppermute(x, axis, [(i, i ^ d) for i in range(n)])
-        d *= 2
     return x
 
 
@@ -109,9 +103,9 @@
         jnp.broadcast_to(coords_by_part[:, None, :, 0], in_col.shape), g_slot, axis=2
     )
     g_inner = owner_of_part[:, None, None] * b_span + g_b0
-    goff = ((part_ids[:, None, None] * n_b + g_slot) * tile).transpose(1, 0, 2).reshape(col_tiles, -1)
+    g_tile = (part_ids[:, None, None] * n_b + g_slot).transpose(1, 0, 2).reshape(col_tiles, -1)
     g_inner = g_inner.transpose(1, 0, 2).reshape(col_tiles, -1)
-    n_g = goff.shape[1]
+    n_g = g_tile.shape[1]
 
     kept_here = kept_all[:, None, :, 1] == col_ids[None, :, None]
     kept_pos = jnp.argmax(kept_here, axis=2).astype(jnp.int32)
@@ -132,9 +126,8 @@
     moff = jnp.where(have, (grp[:, None, :] * rows_panel + slot_a) * tile, -1)
 
     flow_flat = flow_tiles.reshape(-1, tile)
-    graph_flat = graph_tiles.reshape(-1, tile)
+    graph_flat = graph_tiles[g_tile.reshape(-1)].reshape(-1, tile)
     partial_sum = kept_partials(
-        goff.reshape(-1).astype(jnp.int32),
         moff.reshape(-1).astype(jnp.int32),
         oidx.reshape(-1).astype(jnp.int32),
         flow_flat,
@@ -149,7 +142,9 @@
     squared = kept_tiles * kept_tiles
     column_part = jnp.sum(squared, axis=1)
     local_mass = jnp.zeros_like(column_part).at[kept_cols].set(column_part)
-    column_total = butterfly_sum(butterfly_sum(local_mass, "row", row_count), "layer", layer_count)
+    column_total = butterfly_sum(
+        butterfly_sum(local_mass, "row", row_count, (1, 2)), "layer", layer_count, (1, 3)
+    )
     factor = jnp.float32(row_count * layer_count * tile) / column_total
     flow = squared * factor[kept_cols][:, None, :]
     return flow.reshape(1, 1, 1, col_tiles, tile, tile)

time: 215 us -> 214 us (level)
  local copies, waits for them, and re-layouts: 11.4 us -> 16.6 us
  waiting for transfers between devices: 91.4 us -> 86.6 us
    gather x0 -> x1, local copies, waits for them, and re-layouts: none -> 5.23 us  [local(): graph_flat = graph_tiles[g_tile.reshape(-1)].reshape(-1, tile)]
    all_gather x1, waiting for transfers between devices: 35.7 us -> 30.6 us  [local(): flow_tiles = lax.all_gather(a_tiles[0, 0, 0], 'col', axis=0, tiled=True)]
  transfers between devices with their start and end apart: 9 -> 9, of which waited for: 6 -> 6; matrix products, arithmetic and copies ran while one was open for 8% -> 10% of each run, Pallas kernels for 0% -> 0%
where the time goes in v10:
time: 214 us
  waiting for transfers between devices  86.6 us (40%)
  blocking collectives  67.4 us (31%)
  local copies, waits for them, and re-layouts  16.6 us (8%)
  between operations  13.6 us (6%)
  other arithmetic  12.5 us (6%)
  Pallas kernels  12.5 us (6%)
  starting transfers between devices  4.85 us (2%)
    reduce_scatter x1, waiting for transfers between devices, local(): lax.psum_scatter(partial_sum, 'layer', scatter_dimension=0, tiled=True)  44.6 us
    all_gather x1, blocking collectives, local(): lax.all_gather(b_coords[0, 0, 0][None], 'row', axis=0, tiled=True)  32.2 us
    all_gather x1, waiting for transfers between devices, local(): flow_tiles = lax.all_gather(a_tiles[0, 0, 0], 'col', axis=0, tiled=True)  30.6 us
    all_gather x1, blocking collectives, local(): lax.all_gather(a_coords[0, 0, 0][None], 'col', axis=0, tiled=True)  25.4 us
    pallas_call x1, Pallas kernels, kept_partials(): pl.pallas_call(kernel, out_shape=jax.ShapeDtypeStruct((n_out, tile, tile)...  12.5 us
    ppermute x4, waiting for transfers between devices, butterfly_sum(): x = x + lax.ppermute(x, axis, [(i, i ^ d) for i in range(n)])  10.7 us
    all_gather x1, blocking collectives, local(): lax.all_gather(out_coords[0, 0, 0][None], 'layer', axis=0, tiled=True)  9.78 us
    gather x1, local copies, waits for them, and re-layouts, local(): graph_flat = graph_tiles[g_tile.reshape(-1)].reshape(-1, tile)  5.23 us
  transfers between devices with their start and end apart: 9, of which 6 were waited for; matrix products, arithmetic and copies ran while one was open for 10% of the time, Pallas kernels for 0%

profile of v10, /device:TPU:0, one launch (start us, length us, event | category | flops | bytes accessed | tf_op | source)
XLA Modules:
  0.0 214.1 jit_solution(8807148417831725026)
XLA Ops:
  7.3 2.1 collective-permute-start.1
  9.4 32.2 %all-gather.1 = s32[4,1,1,32,2]{3,4,2,1,0:T(2,128)S(1)} all-gather(s32[1,1,1,32,2]{3,4,2,1,0:T(2,128)} %param.8), channel_id=3, replica_groups=mesh['row'=4,'col'=8,'layer'=4] {'row'}, dimensions={0}, use_global_device_ids=true | all-gather | bytes 1280 | tf_op jit(solution)/shard_map/all_gather | solution.py:89
  42.3 0.7 iota_reduce_fusion.2
  44.0 1.5 gather_fusion.5
  46.1 25.4 %all-gather = s32[8,1,1,32,2]{3,4,2,1,0:T(2,128)S(1)} all-gather(s32[1,1,1,32,2]{3,4,2,1,0:T(2,128)S(1)} %copy-done.2), channel_id=2, replica_groups=mesh['row'=4,'col'=8,'layer'=4] {'col'}, dimensions={0}, use_global_device_ids=true | all-gather | bytes 2304 | tf_op jit(solution)/shard_map/all_gather | solution.py:91
  71.5 9.8 %all-gather.2 = s32[4,1,1,16,2]{3,4,2,1,0:T(2,128)S(1)} all-gather(s32[1,1,1,16,2]{3,4,2,1,0:T(2,128)S(1)} %copy-done.3), channel_id=4, replica_groups=mesh['row'=4,'col'=8,'layer'=4] {'layer'}, dimensions={0}, use_global_device_ids=true | all-gather | bytes 640 | tf_op jit(solution)/shard_map/all_gather | solution.py:92
  81.3 0.7 iota_reduce_fusion.1
  82.1 0.9 gather_fusion.6
  83.9 3.0 %iota_reduce_fusion = (pred[16,4,8]{2,1,0:T(4,128)(4,1)}, s32[16,4,8]{2,1,0:T(4,128)S(1)}) fusion(s32[16,4]{1,0:T(8,128)S(1)} %copy.59, s32[16,8,32]{2,1,0:T(8,128)S(1)} %bitcast.71), kind=kLoop, calls=%fused_computation.11 | loop fusion | flops 127488 | bytes 19200 | tf_op jit(solution)/shard_map/local/reduce | solution.py:122
  87.3 2.6 %gather_fusion.2 = s32[512]{0:T(512)S(1)} fusion(s32[8,32]{1,0:T(8,128)S(1)} %get-tuple-element.13, s32[512]{0:T(512)S(1)} %reshape.389), kind=kCustom, calls=%fused_computation.2 | custom fusion | bytes 8192 | tf_op jit(solution)/shard_map/gather | solution.py:125
  90.8 3.3 %pad_maximum_fusion = bf16[128,128,128]{2,1,0:T(8,128)(2,1)} fusion(bf16[32,128,128]{2,1,0:T(8,128)(2,1)} %collective-permute-done.2, bf16[32,128,128]{2,1,0:T(8,128)(2,1)S(1)} %collective-permute-done.1, bf16[32,128,128]{2,1,0:T(8,128)(2,1)S(1)} %collective-permute-done, bf16[32,128,128]{2,1,0:T(8,128)(2,1)S(1)} %bitcast.70), kind=kLoop, calls=%fused_computation.8 | loop fusion | flops 6291456 | bytes 8388608 | tf_op jit(solution)/shard_map/concatenate | solution.py:88
  94.1 5.2 %gather_fusion.3 = bf16[128,128,128]{2,1,0:T(8,128)(2,1)} fusion(bf16[128,128,128]{2,1,0:T(8,128)(2,1)} %pad_maximum_fusion, s32[1024]{0:T(1024)S(1)} %pad_clamp_fusion.1), kind=kCustom, calls=%fused_computation.3 | custom fusion | bytes 8389120 | tf_op jit(solution)/shard_map/gather | solution.py:129
  99.3 30.6 %all-gather.6.cloned.1.call-done = bf16[1,1,1,256,128,128]{5,4,2,1,0,3:T(8,128)(2,1)} async-done(((bf16[1,1,1,32,128,128]{5,4,2,1,0,3:T(8,128)(2,1)}), bf16[1,1,1,256,128,128]{5,4,2,1,0,3:T(8,128)(2,1)}) %all-gather.6.cloned.1.call-update) | async-done | bytes 8388624 | tf_op jit(solution)/shard_map/all_gather | solution.py:90
  129.9 12.5 %shard_map.55 = f32[64,128,128]{2,1,0:T(8,128)S(1)} custom-call(s32[512]{0:T(512)S(1)} %reshape.368.moff_ref, s32[64]{0:T(128)S(1)} %reshape.369.oidx_ref, bf16[32768,128]{1,0:T(8,128)(2,1)} %bitcast.65, bf16[16384,128]{1,0:T(8,128)(2,1)} %bitcast.64), custom_call_target="tpu_custom_call" | custom-call | flops 2147483648 | bytes 16777216 | tf_op jit(solution)/shard_map/pallas_call | solution.py:36
  142.4 1.9 copy-done
  144.4 44.6 %reduce-scatter.2.cloned.1.call-done = f32[16,128,128]{2,1,0:T(8,128)} async-done(((f32[64,128,128]{2,1,0:T(8,128)}), f32[16,128,128]{2,1,0:T(8,128)}) %reduce-scatter.2.cloned.1.call-update) | async-done | bytes 1048592 | tf_op jit(solution)/shard_map/reduce_scatter | solution.py:139
  189.0 1.3 multiply_reduce_fusion
  191.0 1.2 collective-permute-done.3
  192.2 1.6 collective-permute-start.4
  193.8 2.1 collective-permute-done.4
  196.1 3.4 %collective-permute-done.5 = f32[16,128]{1,0:T(8,128)S(1)} collective-permute-done((f32[16,128]{1,0:T(8,128)S(1)}, f32[16,128]{1,0:T(8,128)S(1)}, u32[]{:S(2)}, u32[]{:S(2)}) %collective-permute-start.5) | collective-permute-done | bytes 8224 | tf_op jit(solution)/shard_map/ppermute | solution.py:60
  199.5 0.8 collective-permute-start.6
  200.4 4.0 %collective-permute-done.6 = f32[16,128]{1,0:T(8,128)S(1)} collective-permute-done((f32[16,128]{1,0:T(8,128)S(1)}, f32[16,128]{1,0:T(8,128)S(1)}, u32[]{:S(2)}, u32[]{:S(2)}) %collective-permute-start.6) | collective-permute-done | bytes 8224 | tf_op jit(solution)/shard_map/ppermute | solution.py:60
  204.9 2.3 %multiply_bitcast_fusion = f32[1,1,1,16,128,128]{5,4,3,2,1,0:T(8,128)} fusion(f32[16,128,128]{2,1,0:T(8,128)} %reduce-scatter.2.cloned.1.call-done, f32[16,128]{1,0:T(8,128)S(1)} %gather_fusion.4), kind=kLoop, calls=%fused_computation.9 | loop fusion | flops 524288 | bytes 2105344 | tf_op jit(solution)/shard_map/reshape | solution.py:150
  (75 shorter events, 6.6 us)
Async XLA Ops:
  6.5 123.4 %all-gather.6.cloned.1.call-start = ((), (), s32[]{:S(2)}) async-start(), calls=%async_computation.2 | async-start | bytes 9437184 | tf_op jit(solution)/shard_map/all_gather | solution.py:90
  7.3 181.7 %reduce-scatter.2.cloned.1.call-start = ((), (), s32[]{:S(2)}) async-start(), calls=%async_computation.1 | async-start | bytes 5242880 | tf_op jit(solution)/shard_map/reduce_scatter | solution.py:139
  7.3 79.6 %collective-permute-start.1 = (bf16[32,128,128]{2,1,0:T(8,128)(2,1)}, bf16[32,128,128]{2,1,0:T(8,128)(2,1)S(1)}, u32[]{:S(2)}, u32[]{:S(2)}) collective-permute-start(bf16[32,128,128]{2,1,0:T(8,128)(2,1)} %bitcast.68), channel_id=1, source_target_pairs={{0,64},{32,96},{64,0},{96,32},{1,65},{33,97},{65,1},{97,33},{2,66}... | collective-permute-start | bytes 3145736 | tf_op jit(solution)/shard_map/ppermute | solution.py:84
  9.4 81.4 %collective-permute-start = (bf16[32,128,128]{2,1,0:T(8,128)(2,1)}, bf16[32,128,128]{2,1,0:T(8,128)(2,1)S(1)}, u32[]{:S(2)}, u32[]{:S(2)}) collective-permute-start(bf16[32,128,128]{2,1,0:T(8,128)(2,1)} %bitcast.69), channel_id=1, source_target_pairs={{0,32},{32,0},{64,96},{96,64},{1,33},{33,1},{65,97},{97,65},{2,34}... | collective-permute-start | bytes 3145736 | tf_op jit(solution)/shard_map/ppermute | solution.py:85
  44.0 2.1 copy-start.2
  44.0 27.5 %copy-start.3 = (s32[1,1,1,16,2]{3,4,2,1,0:T(2,128)S(1)}, s32[1,1,1,16,2]{3,4,2,1,0:T(2,128)}, u32[]{:S(2)}) copy-start(s32[1,1,1,16,2]{3,4,2,1,0:T(2,128)} %param.9) | copy-start | bytes 388
  86.9 3.8 %collective-permute-start.2 = (bf16[32,128,128]{2,1,0:T(8,128)(2,1)S(1)}, bf16[32,128,128]{2,1,0:T(8,128)(2,1)}, u32[]{:S(2)}, u32[]{:S(2)}) collective-permute-start(bf16[32,128,128]{2,1,0:T(8,128)(2,1)S(1)} %collective-permute-done.1), channel_id=1, source_target_pairs={{0,32},{32,0},{64,96},{96,64},{1,33},{33,1},{65,97},{97,65},{2,34}... | collective-permute-start | bytes 3145736 | tf_op jit(solution)/shard_map/ppermute | solution.py:86
  87.3 3.5 %copy-start.1 = (bf16[1,1,1,32,128,128]{5,4,3,2,1,0:T(8,128)(2,1)S(1)}, bf16[1,1,1,32,128,128]{5,4,3,2,1,0:T(8,128)(2,1)}, u32[]{:S(2)}) copy-start(bf16[1,1,1,32,128,128]{5,4,3,2,1,0:T(8,128)(2,1)} %param.7) | copy-start | bytes 3145732
  142.4 1.9 copy-start
  190.9 1.3 collective-permute-start.3
  192.2 3.7 %collective-permute-start.4 = (f32[16,128]{1,0:T(8,128)S(1)}, f32[16,128]{1,0:T(8,128)S(1)}, u32[]{:S(2)}, u32[]{:S(2)}) collective-permute-start(f32[16,128]{1,0:T(8,128)S(1)} %add.190), channel_id=1, source_target_pairs={{0,64},{32,96},{64,0},{96,32},{1,65},{33,97},{65,1},{97,33},{2,66}... | collective-permute-start | bytes 24584 | tf_op jit(solution)/shard_map/ppermute | solution.py:60
  195.9 3.7 %collective-permute-start.5 = (f32[16,128]{1,0:T(8,128)S(1)}, f32[16,128]{1,0:T(8,128)S(1)}, u32[]{:S(2)}, u32[]{:S(2)}) collective-permute-start(f32[16,128]{1,0:T(8,128)S(1)} %add.191), channel_id=1, source_target_pairs={{0,1},{1,0},{2,3},{3,2},{4,5},{5,4},{6,7},{7,6},{8,9},{9,8},{10,11... | collective-permute-start | bytes 24584 | tf_op jit(solution)/shard_map/ppermute | solution.py:60
  199.5 4.9 %collective-permute-start.6 = (f32[16,128]{1,0:T(8,128)S(1)}, f32[16,128]{1,0:T(8,128)S(1)}, u32[]{:S(2)}, u32[]{:S(2)}) collective-permute-start(f32[16,128]{1,0:T(8,128)S(1)} %add.192), channel_id=1, source_target_pairs={{0,3},{1,2},{2,1},{3,0},{4,7},{5,6},{6,5},{7,4},{8,11},{9,10},{10,... | collective-permute-start | bytes 24584 | tf_op jit(solution)/shard_map/ppermute | solution.py:60
Sparse Core Ops, SparseCore 0:
  9.7 120.1 all-gather.5
  144.5 44.4 reduce-scatter.1

commit v11 on v10

--- a/solution.py
+++ b/solution.py
@@ -10,19 +10,58 @@
 KA = 4
 
 
-def column_kernel(moff_ref, oidx_ref, flow_ref, graph_ref, out_ref, lhs_ref, *, n_q, n_g):
+def column_kernel(moff_ref, oidx_ref, flow_hbm, graph_hbm, out_ref, lhs_ref, rhs_ref, lhs_sem, rhs_sem, *, n_q, n_g):
     tile = out_ref.shape[-1]
     n_col = out_ref.shape[0] // n_q
-
-    def body(j, carry):
+    span = n_g * tile
+
+    def rhs_copy(j, slot):
+        src = graph_hbm.at[pl.ds(pl.multiple_of(j * span, span), span), :]
+        return pltpu.make_async_copy(src, rhs_ref.at[slot], rhs_sem.at[slot])
+
+    def lhs_copy(j, slot, q, g):
+        m_off = moff_ref[(j * n_q + q) * n_g + g]
+        src = flow_hbm.at[pl.ds(pl.multiple_of(jnp.maximum(m_off, 0), tile), tile), :]
+        dst = lhs_ref.at[slot, pl.ds(q * tile, tile), pl.ds(g * tile, tile)]
+        return m_off, pltpu.make_async_copy(src, dst, lhs_sem.at[slot, q * n_g + g])
+
+    def fetch(j, slot):
+        rhs_copy(j, slot).start()
         for q in range(n_q):
             for g in range(n_g):
-                m_off = moff_ref[(j * n_q + q) * n_g + g]
-                left = flow_ref[pl.ds(pl.multiple_of(jnp.maximum(m_off, 0), tile), tile), :]
-                left = jnp.where(m_off >= 0, left, jnp.zeros_like(left))
-                lhs_ref[pl.ds(q * tile, tile), pl.ds(g * tile, tile)] = left
-        right = graph_ref[pl.ds(pl.multiple_of(j * n_g * tile, n_g * tile), n_g * tile), :]
-        res = jnp.dot(lhs_ref[...], right, preferred_element_type=jnp.float32)
+                m_off, copy = lhs_copy(j, slot, q, g)
+
+                @pl.when(m_off >= 0)
+                def _():
+                    copy.start()
+
+                @pl.when(m_off < 0)
+                def _():
+                    lhs_ref[slot, pl.ds(q * tile, tile), pl.ds(g * tile, tile)] = jnp.zeros(
+                        (tile, tile), lhs_ref.dtype
+                    )
+
+    def wait(j, slot):
+        rhs_copy(j, slot).wait()
+        for q in range(n_q):
+            for g in range(n_g):
+                m_off, copy = lhs_copy(j, slot, q, g)
+
+                @pl.when(m_off >= 0)
+                def _():
+                    copy.wait()
+
+    fetch(0, 0)
+
+    def body(j, carry):
+        slot = j % 2
+
+        @pl.when(j + 1 < n_col)
+        def _():
+            fetch(j + 1, 1 - slot)
+
+        wait(j, slot)
+        res = jnp.dot(lhs_ref[slot], rhs_ref[slot], preferred_element_type=jnp.float32)
         for q in range(n_q):
             out_ref[oidx_ref[j * n_q + q]] = res[q * tile : (q + 1) * tile]
         return carry
@@ -39,12 +78,15 @@
         in_specs=[
             pl.BlockSpec(memory_space=pltpu.SMEM),
             pl.BlockSpec(memory_space=pltpu.SMEM),
-            pl.BlockSpec(memory_space=pltpu.VMEM),
-            pl.BlockSpec(memory_space=pltpu.VMEM),
+            pl.BlockSpec(memory_space=pl.ANY),
+            pl.BlockSpec(memory_space=pl.ANY),
         ],
         out_specs=pl.BlockSpec(memory_space=pltpu.VMEM),
         scratch_shapes=[
-            pltpu.VMEM((n_q * tile, n_g * tile), jnp.bfloat16),
+            pltpu.VMEM((2, n_q * tile, n_g * tile), jnp.bfloat16),
+            pltpu.VMEM((2, n_g * tile, tile), jnp.bfloat16),
+            pltpu.SemaphoreType.DMA((2, n_q * n_g)),
+            pltpu.SemaphoreType.DMA((2,)),
         ],
         compiler_params=pltpu.CompilerParams(vmem_limit_bytes=48 * 1024 * 1024),
         cost_estimate=pl.CostEstimate(

time: 214 us -> 219 us (1.023)
  Pallas kernels: 12.5 us -> 16.6 us
    pallas_call x1, Pallas kernels: 12.5 us -> 16.6 us  [kept_partials(): pl.pallas_call(kernel, out_shape=jax.ShapeDtypeStruct((n_out, tile, tile)...]
where the time goes in v11:
time: 219 us; the launch traced here: 218 us
  waiting for transfers between devices  86.5 us (39%)
  blocking collectives  67.4 us (31%)
  local copies, waits for them, and re-layouts  16.6 us (8%)
  Pallas kernels  16.6 us (8%)
  between operations  13.6 us (6%)
  other arithmetic  12.5 us (6%)
  starting transfers between devices  4.86 us (2%)
    reduce_scatter x1, waiting for transfers between devices, local(): lax.psum_scatter(partial_sum, 'layer', scatter_dimension=0, tiled=True)  44.5 us
    all_gather x1, blocking collectives, local(): lax.all_gather(b_coords[0, 0, 0][None], 'row', axis=0, tiled=True)  32.2 us
    all_gather x1, waiting for transfers between devices, local(): flow_tiles = lax.all_gather(a_tiles[0, 0, 0], 'col', axis=0, tiled=True)  30.6 us
    all_gather x1, blocking collectives, local(): lax.all_gather(a_coords[0, 0, 0][None], 'col', axis=0, tiled=True)  25.4 us
    pallas_call x1, Pallas kernels, kept_partials(): pl.pallas_call(kernel, out_shape=jax.ShapeDtypeStruct((n_out, tile, tile)...  16.6 us
    ppermute x4, waiting for transfers between devices, butterfly_sum(): x = x + lax.ppermute(x, axis, [(i, i ^ d) for i in range(n)])  10.7 us
    all_gather x1, blocking collectives, local(): lax.all_gather(out_coords[0, 0, 0][None], 'layer', axis=0, tiled=True)  9.78 us
    gather x1, local copies, waits for them, and re-layouts, local(): graph_flat = graph_tiles[g_tile.reshape(-1)].reshape(-1, tile)  5.23 us
  transfers between devices with their start and end apart: 9, of which 6 were waited for; matrix products, arithmetic and copies ran while one was open for 10% of the time, Pallas kernels for 0%

profile of v11, /device:TPU:0, one launch (start us, length us, event | category | flops | bytes accessed | tf_op | source)
XLA Modules:
  0.0 218.1 jit_solution(10857754641958972802)
XLA Ops:
  7.3 2.1 collective-permute-start.1
  9.4 32.2 %all-gather.1 = s32[4,1,1,32,2]{3,4,2,1,0:T(2,128)S(1)} all-gather(s32[1,1,1,32,2]{3,4,2,1,0:T(2,128)} %param.8), channel_id=3, replica_groups=mesh['row'=4,'col'=8,'layer'=4] {'row'}, dimensions={0}, use_global_device_ids=true | all-gather | bytes 1280 | tf_op jit(solution)/shard_map/all_gather | solution.py:131
  42.3 0.7 iota_reduce_fusion.2
  44.0 1.5 gather_fusion.5
  46.1 25.4 %all-gather = s32[8,1,1,32,2]{3,4,2,1,0:T(2,128)S(1)} all-gather(s32[1,1,1,32,2]{3,4,2,1,0:T(2,128)S(1)} %copy-done.2), channel_id=2, replica_groups=mesh['row'=4,'col'=8,'layer'=4] {'col'}, dimensions={0}, use_global_device_ids=true | all-gather | bytes 2304 | tf_op jit(solution)/shard_map/all_gather | solution.py:133
  71.5 9.8 %all-gather.2 = s32[4,1,1,16,2]{3,4,2,1,0:T(2,128)S(1)} all-gather(s32[1,1,1,16,2]{3,4,2,1,0:T(2,128)S(1)} %copy-done.3), channel_id=4, replica_groups=mesh['row'=4,'col'=8,'layer'=4] {'layer'}, dimensions={0}, use_global_device_ids=true | all-gather | bytes 640 | tf_op jit(solution)/shard_map/all_gather | solution.py:134
  81.3 0.7 iota_reduce_fusion.1
  82.1 0.9 gather_fusion.6
  83.9 3.0 %iota_reduce_fusion = (pred[16,4,8]{2,1,0:T(4,128)(4,1)}, s32[16,4,8]{2,1,0:T(4,128)S(1)}) fusion(s32[16,4]{1,0:T(8,128)S(1)} %copy.59, s32[16,8,32]{2,1,0:T(8,128)S(1)} %bitcast.71), kind=kLoop, calls=%fused_computation.11 | loop fusion | flops 127488 | bytes 19200 | tf_op jit(solution)/shard_map/local/reduce | solution.py:164
  87.3 2.6 %gather_fusion.2 = s32[512]{0:T(512)S(1)} fusion(s32[8,32]{1,0:T(8,128)S(1)} %get-tuple-element.13, s32[512]{0:T(512)S(1)} %reshape.389), kind=kCustom, calls=%fused_computation.2 | custom fusion | bytes 8192 | tf_op jit(solution)/shard_map/gather | solution.py:167
  90.8 3.3 %pad_maximum_fusion = bf16[128,128,128]{2,1,0:T(8,128)(2,1)} fusion(bf16[32,128,128]{2,1,0:T(8,128)(2,1)} %collective-permute-done.2, bf16[32,128,128]{2,1,0:T(8,128)(2,1)S(1)} %collective-permute-done.1, bf16[32,128,128]{2,1,0:T(8,128)(2,1)S(1)} %collective-permute-done, bf16[32,128,128]{2,1,0:T(8,128)(2,1)S(1)} %bitcast.70), kind=kLoop, calls=%fused_computation.8 | loop fusion | flops 6291456 | bytes 8388608 | tf_op jit(solution)/shard_map/concatenate | solution.py:130
  94.1 5.2 %gather_fusion.3 = bf16[128,128,128]{2,1,0:T(8,128)(2,1)} fusion(bf16[128,128,128]{2,1,0:T(8,128)(2,1)} %pad_maximum_fusion, s32[1024]{0:T(1024)S(1)} %pad_clamp_fusion.1), kind=kCustom, calls=%fused_computation.3 | custom fusion | bytes 8389120 | tf_op jit(solution)/shard_map/gather | solution.py:171
  99.3 30.6 %all-gather.6.cloned.1.call-done = bf16[1,1,1,256,128,128]{5,4,2,1,0,3:T(8,128)(2,1)} async-done(((bf16[1,1,1,32,128,128]{5,4,2,1,0,3:T(8,128)(2,1)}), bf16[1,1,1,256,128,128]{5,4,2,1,0,3:T(8,128)(2,1)}) %all-gather.6.cloned.1.call-update) | async-done | bytes 8388624 | tf_op jit(solution)/shard_map/all_gather | solution.py:132
  129.9 16.6 %shard_map.55 = f32[64,128,128]{2,1,0:T(8,128)S(1)} custom-call(s32[512]{0:T(512)S(1)} %reshape.368.moff_ref, s32[64]{0:T(128)S(1)} %reshape.369.oidx_ref, bf16[32768,128]{1,0:T(8,128)(2,1)} %bitcast.65, bf16[16384,128]{1,0:T(8,128)(2,1)} %bitcast.64), custom_call_target="tpu_custom_call" | custom-call | flops 2147483648 | bytes 16777216 | tf_op jit(solution)/shard_map/pallas_call | solution.py:75
  146.6 1.9 copy-done
  148.5 44.5 %reduce-scatter.2.cloned.1.call-done = f32[16,128,128]{2,1,0:T(8,128)} async-done(((f32[64,128,128]{2,1,0:T(8,128)}), f32[16,128,128]{2,1,0:T(8,128)}) %reduce-scatter.2.cloned.1.call-update) | async-done | bytes 1048592 | tf_op jit(solution)/shard_map/reduce_scatter | solution.py:181
  193.0 1.3 multiply_reduce_fusion
  195.1 1.2 collective-permute-done.3
  196.2 1.6 collective-permute-start.4
  197.8 2.1 collective-permute-done.4
  200.1 3.4 %collective-permute-done.5 = f32[16,128]{1,0:T(8,128)S(1)} collective-permute-done((f32[16,128]{1,0:T(8,128)S(1)}, f32[16,128]{1,0:T(8,128)S(1)}, u32[]{:S(2)}, u32[]{:S(2)}) %collective-permute-start.5) | collective-permute-done | bytes 8224 | tf_op jit(solution)/shard_map/ppermute | solution.py:102
  203.5 0.8 collective-permute-start.6
  204.4 4.0 %collective-permute-done.6 = f32[16,128]{1,0:T(8,128)S(1)} collective-permute-done((f32[16,128]{1,0:T(8,128)S(1)}, f32[16,128]{1,0:T(8,128)S(1)}, u32[]{:S(2)}, u32[]{:S(2)}) %collective-permute-start.6) | collective-permute-done | bytes 8224 | tf_op jit(solution)/shard_map/ppermute | solution.py:102
  209.0 2.3 %multiply_bitcast_fusion = f32[1,1,1,16,128,128]{5,4,3,2,1,0:T(8,128)} fusion(f32[16,128,128]{2,1,0:T(8,128)} %reduce-scatter.2.cloned.1.call-done, f32[16,128]{1,0:T(8,128)S(1)} %gather_fusion.4), kind=kLoop, calls=%fused_computation.9 | loop fusion | flops 524288 | bytes 2105344 | tf_op jit(solution)/shard_map/reshape | solution.py:192
  (75 shorter events, 6.6 us)
Async XLA Ops:
  6.5 123.4 %all-gather.6.cloned.1.call-start = ((), (), s32[]{:S(2)}) async-start(), calls=%async_computation.2 | async-start | bytes 9437184 | tf_op jit(solution)/shard_map/all_gather | solution.py:132
  7.3 185.8 %reduce-scatter.2.cloned.1.call-start = ((), (), s32[]{:S(2)}) async-start(), calls=%async_computation.1 | async-start | bytes 5242880 | tf_op jit(solution)/shard_map/reduce_scatter | solution.py:181
  7.3 79.6 %collective-permute-start.1 = (bf16[32,128,128]{2,1,0:T(8,128)(2,1)}, bf16[32,128,128]{2,1,0:T(8,128)(2,1)S(1)}, u32[]{:S(2)}, u32[]{:S(2)}) collective-permute-start(bf16[32,128,128]{2,1,0:T(8,128)(2,1)} %bitcast.68), channel_id=1, source_target_pairs={{0,64},{32,96},{64,0},{96,32},{1,65},{33,97},{65,1},{97,33},{2,66}... | collective-permute-start | bytes 3145736 | tf_op jit(solution)/shard_map/ppermute | solution.py:126
  9.4 81.4 %collective-permute-start = (bf16[32,128,128]{2,1,0:T(8,128)(2,1)}, bf16[32,128,128]{2,1,0:T(8,128)(2,1)S(1)}, u32[]{:S(2)}, u32[]{:S(2)}) collective-permute-start(bf16[32,128,128]{2,1,0:T(8,128)(2,1)} %bitcast.69), channel_id=1, source_target_pairs={{0,32},{32,0},{64,96},{96,64},{1,33},{33,1},{65,97},{97,65},{2,34}... | collective-permute-start | bytes 3145736 | tf_op jit(solution)/shard_map/ppermute | solution.py:127
  44.0 2.1 copy-start.2
  44.0 27.5 %copy-start.3 = (s32[1,1,1,16,2]{3,4,2,1,0:T(2,128)S(1)}, s32[1,1,1,16,2]{3,4,2,1,0:T(2,128)}, u32[]{:S(2)}) copy-start(s32[1,1,1,16,2]{3,4,2,1,0:T(2,128)} %param.9) | copy-start | bytes 388
  86.9 3.8 %collective-permute-start.2 = (bf16[32,128,128]{2,1,0:T(8,128)(2,1)S(1)}, bf16[32,128,128]{2,1,0:T(8,128)(2,1)}, u32[]{:S(2)}, u32[]{:S(2)}) collective-permute-start(bf16[32,128,128]{2,1,0:T(8,128)(2,1)S(1)} %collective-permute-done.1), channel_id=1, source_target_pairs={{0,32},{32,0},{64,96},{96,64},{1,33},{33,1},{65,97},{97,65},{2,34}... | collective-permute-start | bytes 3145736 | tf_op jit(solution)/shard_map/ppermute | solution.py:128
  87.3 3.5 %copy-start.1 = (bf16[1,1,1,32,128,128]{5,4,3,2,1,0:T(8,128)(2,1)S(1)}, bf16[1,1,1,32,128,128]{5,4,3,2,1,0:T(8,128)(2,1)}, u32[]{:S(2)}) copy-start(bf16[1,1,1,32,128,128]{5,4,3,2,1,0:T(8,128)(2,1)} %param.7) | copy-start | bytes 3145732
  146.6 1.9 copy-start
  195.0 1.3 collective-permute-start.3
  196.2 3.7 %collective-permute-start.4 = (f32[16,128]{1,0:T(8,128)S(1)}, f32[16,128]{1,0:T(8,128)S(1)}, u32[]{:S(2)}, u32[]{:S(2)}) collective-permute-start(f32[16,128]{1,0:T(8,128)S(1)} %add.190), channel_id=1, source_target_pairs={{0,64},{32,96},{64,0},{96,32},{1,65},{33,97},{65,1},{97,33},{2,66}... | collective-permute-start | bytes 24584 | tf_op jit(solution)/shard_map/ppermute | solution.py:102
  199.9 3.7 %collective-permute-start.5 = (f32[16,128]{1,0:T(8,128)S(1)}, f32[16,128]{1,0:T(8,128)S(1)}, u32[]{:S(2)}, u32[]{:S(2)}) collective-permute-start(f32[16,128]{1,0:T(8,128)S(1)} %add.191), channel_id=1, source_target_pairs={{0,1},{1,0},{2,3},{3,2},{4,5},{5,4},{6,7},{7,6},{8,9},{9,8},{10,11... | collective-permute-start | bytes 24584 | tf_op jit(solution)/shard_map/ppermute | solution.py:102
  203.5 4.9 %collective-permute-start.6 = (f32[16,128]{1,0:T(8,128)S(1)}, f32[16,128]{1,0:T(8,128)S(1)}, u32[]{:S(2)}, u32[]{:S(2)}) collective-permute-start(f32[16,128]{1,0:T(8,128)S(1)} %add.192), channel_id=1, source_target_pairs={{0,3},{1,2},{2,1},{3,0},{4,7},{5,6},{6,5},{7,4},{8,11},{9,10},{10,... | collective-permute-start | bytes 24584 | tf_op jit(solution)/shard_map/ppermute | solution.py:102
Sparse Core Ops, SparseCore 0:
  9.7 120.1 all-gather.5
  148.6 44.3 reduce-scatter.1

commit v12 on v10

--- a/solution.py
+++ b/solution.py
@@ -112,7 +112,7 @@
     kept_row0 = jnp.take_along_axis(kept_all[:, :, 0], kept_pos, axis=1)
     q_ids = jnp.arange(layer_count, dtype=jnp.int32)
     kept_row = q_ids[:, None] * quarter + kept_row0
-    oidx = (q_ids[:, None] * col_tiles + kept_pos).T
+    oidx = jnp.broadcast_to(q_ids[:, None] * col_tiles + col_ids[None, :], (layer_count, col_tiles)).T
 
     a_rows = flow_coords[:, :, 0]
     a_inner = flow_coords[:, :, 1]
@@ -140,13 +140,12 @@
 
     kept_cols = out_coords[0, 0, 0, :, 1]
     squared = kept_tiles * kept_tiles
-    column_part = jnp.sum(squared, axis=1)
-    local_mass = jnp.zeros_like(column_part).at[kept_cols].set(column_part)
+    local_mass = jnp.sum(squared, axis=1)
     column_total = butterfly_sum(
         butterfly_sum(local_mass, "row", row_count, (1, 2)), "layer", layer_count, (1, 3)
     )
     factor = jnp.float32(row_count * layer_count * tile) / column_total
-    flow = squared * factor[kept_cols][:, None, :]
+    flow = squared[kept_cols] * factor[kept_cols][:, None, :]
     return flow.reshape(1, 1, 1, col_tiles, tile, tile)
 
 

time: 214 us -> 213 us (level)
    reshape x1 -> x0, other arithmetic: 2.32 us -> none  [local(): return flow.reshape(1, 1, 1, col_tiles, tile, tile)]
  transfers between devices with their start and end apart: 9 -> 9, of which waited for: 6 -> 6; matrix products, arithmetic and copies ran while one was open for 10% -> 11% of each run, Pallas kernels for 0% -> 0%
where the time goes in v12:
time: 213 us; the launch traced here: 212 us
  waiting for transfers between devices  86.1 us (40%)
  blocking collectives  67.4 us (32%)
  local copies, waits for them, and re-layouts  16.5 us (8%)
  between operations  13.7 us (6%)
  Pallas kernels  12.5 us (6%)
  other arithmetic  11.3 us (5%)
  starting transfers between devices  4.89 us (2%)
    reduce_scatter x1, waiting for transfers between devices, local(): lax.psum_scatter(partial_sum, 'layer', scatter_dimension=0, tiled=True)  44.6 us
    all_gather x1, blocking collectives, local(): lax.all_gather(b_coords[0, 0, 0][None], 'row', axis=0, tiled=True)  32.2 us
    all_gather x1, waiting for transfers between devices, local(): flow_tiles = lax.all_gather(a_tiles[0, 0, 0], 'col', axis=0, tiled=True)  30.6 us
    all_gather x1, blocking collectives, local(): lax.all_gather(a_coords[0, 0, 0][None], 'col', axis=0, tiled=True)  25.6 us
    pallas_call x1, Pallas kernels, kept_partials(): pl.pallas_call(kernel, out_shape=jax.ShapeDtypeStruct((n_out, tile, tile)...  12.5 us
    ppermute x4, waiting for transfers between devices, butterfly_sum(): x = x + lax.ppermute(x, axis, [(i, i ^ d) for i in range(n)])  10.1 us
    all_gather x1, blocking collectives, local(): lax.all_gather(out_coords[0, 0, 0][None], 'layer', axis=0, tiled=True)  9.61 us
    gather x1, local copies, waits for them, and re-layouts, local(): graph_flat = graph_tiles[g_tile.reshape(-1)].reshape(-1, tile)  5.23 us
  transfers between devices with their start and end apart: 9, of which 6 were waited for; matrix products, arithmetic and copies ran while one was open for 11% of the time, Pallas kernels for 0%

profile of v12, /device:TPU:0, one launch (start us, length us, event | category | flops | bytes accessed | tf_op | source)
XLA Modules:
  0.0 212.3 jit_solution(8626136001375403659)
XLA Ops:
  7.3 2.1 collective-permute-start.1
  9.4 32.2 %all-gather.1 = s32[4,1,1,32,2]{3,4,2,1,0:T(2,128)S(1)} all-gather(s32[1,1,1,32,2]{3,4,2,1,0:T(2,128)} %param.8), channel_id=3, replica_groups=mesh['row'=4,'col'=8,'layer'=4] {'row'}, dimensions={0}, use_global_device_ids=true | all-gather | bytes 1280 | tf_op jit(solution)/shard_map/all_gather | solution.py:89
  42.3 0.7 iota_reduce_fusion.2
  44.0 1.5 gather_fusion.6
  45.9 9.6 %all-gather.2 = s32[4,1,1,16,2]{3,4,2,1,0:T(2,128)S(1)} all-gather(s32[1,1,1,16,2]{3,4,2,1,0:T(2,128)S(1)} %copy-done.3), channel_id=4, replica_groups=mesh['row'=4,'col'=8,'layer'=4] {'layer'}, dimensions={0}, use_global_device_ids=true | all-gather | bytes 640 | tf_op jit(solution)/shard_map/all_gather | solution.py:92
  55.5 0.7 iota_reduce_fusion.1
  56.4 0.9 gather_fusion.7
  57.6 25.6 %all-gather = s32[8,1,1,32,2]{3,4,2,1,0:T(2,128)S(1)} all-gather(s32[1,1,1,32,2]{3,4,2,1,0:T(2,128)S(1)} %copy-done.2), channel_id=2, replica_groups=mesh['row'=4,'col'=8,'layer'=4] {'col'}, dimensions={0}, use_global_device_ids=true | all-gather | bytes 2304 | tf_op jit(solution)/shard_map/all_gather | solution.py:91
  83.9 3.0 %iota_reduce_fusion = (pred[16,4,8]{2,1,0:T(4,128)(4,1)}, s32[16,4,8]{2,1,0:T(4,128)S(1)}) fusion(s32[16,4]{1,0:T(8,128)S(1)} %copy.56, s32[16,8,32]{2,1,0:T(8,128)S(1)} %bitcast.69), kind=kLoop, calls=%fused_computation.10 | loop fusion | flops 127488 | bytes 19200 | tf_op jit(solution)/shard_map/local/reduce | solution.py:122
  87.4 2.6 %gather_fusion.2 = s32[512]{0:T(512)S(1)} fusion(s32[8,32]{1,0:T(8,128)S(1)} %get-tuple-element.15, s32[512]{0:T(512)S(1)} %reshape.393), kind=kCustom, calls=%fused_computation.2 | custom fusion | bytes 8192 | tf_op jit(solution)/shard_map/gather | solution.py:125
  90.8 3.3 %pad_maximum_fusion = bf16[128,128,128]{2,1,0:T(8,128)(2,1)} fusion(bf16[32,128,128]{2,1,0:T(8,128)(2,1)} %collective-permute-done.2, bf16[32,128,128]{2,1,0:T(8,128)(2,1)S(1)} %collective-permute-done.1, bf16[32,128,128]{2,1,0:T(8,128)(2,1)S(1)} %collective-permute-done, bf16[32,128,128]{2,1,0:T(8,128)(2,1)S(1)} %bitcast.68), kind=kLoop, calls=%fused_computation.8 | loop fusion | flops 6291456 | bytes 8388608 | tf_op jit(solution)/shard_map/concatenate | solution.py:88
  94.2 5.2 %gather_fusion.3 = bf16[128,128,128]{2,1,0:T(8,128)(2,1)} fusion(bf16[128,128,128]{2,1,0:T(8,128)(2,1)} %pad_maximum_fusion, s32[1024]{0:T(1024)S(1)} %pad_clamp_fusion.1), kind=kCustom, calls=%fused_computation.3 | custom fusion | bytes 8389120 | tf_op jit(solution)/shard_map/gather | solution.py:129
  99.4 30.6 %all-gather.6.cloned.1.call-done = bf16[1,1,1,256,128,128]{5,4,2,1,0,3:T(8,128)(2,1)} async-done(((bf16[1,1,1,32,128,128]{5,4,2,1,0,3:T(8,128)(2,1)}), bf16[1,1,1,256,128,128]{5,4,2,1,0,3:T(8,128)(2,1)}) %all-gather.6.cloned.1.call-update) | async-done | bytes 8388624 | tf_op jit(solution)/shard_map/all_gather | solution.py:90
  130.0 12.5 %shard_map.55 = f32[64,128,128]{2,1,0:T(8,128)S(1)} custom-call(s32[512]{0:T(512)S(1)} %reshape.374.moff_ref, s32[64]{0:T(128)S(1)} %add.196.oidx_ref, bf16[32768,128]{1,0:T(8,128)(2,1)} %bitcast.63, bf16[16384,128]{1,0:T(8,128)(2,1)} %bitcast.62), custom_call_target="tpu_custom_call" | custom-call | flops 2147483648 | bytes 16777216 | tf_op jit(solution)/shard_map/pallas_call | solution.py:36
  142.5 1.9 copy-done
  144.4 44.6 %reduce-scatter.2.cloned.1.call-done = f32[16,128,128]{2,1,0:T(8,128)} async-done(((f32[64,128,128]{2,1,0:T(8,128)}), f32[16,128,128]{2,1,0:T(8,128)}) %reduce-scatter.2.cloned.1.call-update) | async-done | bytes 1048592 | tf_op jit(solution)/shard_map/reduce_scatter | solution.py:139
  189.1 1.3 multiply_reduce_fusion
  190.5 1.2 collective-permute-done.3
  191.7 1.5 collective-permute-start.4
  193.2 2.1 collective-permute-done.4
  195.6 3.4 %collective-permute-done.5 = f32[16,128]{1,0:T(8,128)S(1)} collective-permute-done((f32[16,128]{1,0:T(8,128)S(1)}, f32[16,128]{1,0:T(8,128)S(1)}, u32[]{:S(2)}, u32[]{:S(2)}) %collective-permute-start.5) | collective-permute-done | bytes 8224 | tf_op jit(solution)/shard_map/ppermute | solution.py:60
  199.0 0.8 collective-permute-start.6
  200.5 3.4 %collective-permute-done.6 = f32[16,128]{1,0:T(8,128)S(1)} collective-permute-done((f32[16,128]{1,0:T(8,128)S(1)}, f32[16,128]{1,0:T(8,128)S(1)}, u32[]{:S(2)}, u32[]{:S(2)}) %collective-permute-start.6) | collective-permute-done | bytes 8224 | tf_op jit(solution)/shard_map/ppermute | solution.py:60
  204.4 1.1 bitcast_multiply_fusion
  (76 shorter events, 6.6 us)
Async XLA Ops:
  6.5 123.4 %all-gather.6.cloned.1.call-start = ((), (), s32[]{:S(2)}) async-start(), calls=%async_computation.2 | async-start | bytes 9437184 | tf_op jit(solution)/shard_map/all_gather | solution.py:90
  7.3 181.8 %reduce-scatter.2.cloned.1.call-start = ((), (), s32[]{:S(2)}) async-start(), calls=%async_computation.1 | async-start | bytes 5242880 | tf_op jit(solution)/shard_map/reduce_scatter | solution.py:139
  7.3 79.8 %collective-permute-start.1 = (bf16[32,128,128]{2,1,0:T(8,128)(2,1)}, bf16[32,128,128]{2,1,0:T(8,128)(2,1)S(1)}, u32[]{:S(2)}, u32[]{:S(2)}) collective-permute-start(bf16[32,128,128]{2,1,0:T(8,128)(2,1)} %bitcast.66), channel_id=1, source_target_pairs={{0,64},{32,96},{64,0},{96,32},{1,65},{33,97},{65,1},{97,33},{2,66}... | collective-permute-start | bytes 3145736 | tf_op jit(solution)/shard_map/ppermute | solution.py:84
  9.4 81.4 %collective-permute-start = (bf16[32,128,128]{2,1,0:T(8,128)(2,1)}, bf16[32,128,128]{2,1,0:T(8,128)(2,1)S(1)}, u32[]{:S(2)}, u32[]{:S(2)}) collective-permute-start(bf16[32,128,128]{2,1,0:T(8,128)(2,1)} %bitcast.67), channel_id=1, source_target_pairs={{0,32},{32,0},{64,96},{96,64},{1,33},{33,1},{65,97},{97,65},{2,34}... | collective-permute-start | bytes 3145736 | tf_op jit(solution)/shard_map/ppermute | solution.py:85
  44.0 1.9 copy-start.3
  44.0 13.5 %copy-start.2 = (s32[1,1,1,32,2]{3,4,2,1,0:T(2,128)S(1)}, s32[1,1,1,32,2]{3,4,2,1,0:T(2,128)}, u32[]{:S(2)}) copy-start(s32[1,1,1,32,2]{3,4,2,1,0:T(2,128)} %param.6) | copy-start | bytes 772
  87.1 3.7 %collective-permute-start.2 = (bf16[32,128,128]{2,1,0:T(8,128)(2,1)S(1)}, bf16[32,128,128]{2,1,0:T(8,128)(2,1)}, u32[]{:S(2)}, u32[]{:S(2)}) collective-permute-start(bf16[32,128,128]{2,1,0:T(8,128)(2,1)S(1)} %collective-permute-done.1), channel_id=1, source_target_pairs={{0,32},{32,0},{64,96},{96,64},{1,33},{33,1},{65,97},{97,65},{2,34}... | collective-permute-start | bytes 3145736 | tf_op jit(solution)/shard_map/ppermute | solution.py:86
  87.4 3.5 %copy-start.1 = (bf16[1,1,1,32,128,128]{5,4,3,2,1,0:T(8,128)(2,1)S(1)}, bf16[1,1,1,32,128,128]{5,4,3,2,1,0:T(8,128)(2,1)}, u32[]{:S(2)}) copy-start(bf16[1,1,1,32,128,128]{5,4,3,2,1,0:T(8,128)(2,1)} %param.7) | copy-start | bytes 3145732
  142.5 1.9 copy-start
  190.4 1.3 collective-permute-start.3
  191.7 3.7 %collective-permute-start.4 = (f32[16,128]{1,0:T(8,128)S(1)}, f32[16,128]{1,0:T(8,128)S(1)}, u32[]{:S(2)}, u32[]{:S(2)}) collective-permute-start(f32[16,128]{1,0:T(8,128)S(1)} %add.202), channel_id=1, source_target_pairs={{0,64},{32,96},{64,0},{96,32},{1,65},{33,97},{65,1},{97,33},{2,66}... | collective-permute-start | bytes 24584 | tf_op jit(solution)/shard_map/ppermute | solution.py:60
  195.3 3.7 %collective-permute-start.5 = (f32[16,128]{1,0:T(8,128)S(1)}, f32[16,128]{1,0:T(8,128)S(1)}, u32[]{:S(2)}, u32[]{:S(2)}) collective-permute-start(f32[16,128]{1,0:T(8,128)S(1)} %add.203), channel_id=1, source_target_pairs={{0,1},{1,0},{2,3},{3,2},{4,5},{5,4},{6,7},{7,6},{8,9},{9,8},{10,11... | collective-permute-start | bytes 24584 | tf_op jit(solution)/shard_map/ppermute | solution.py:60
  199.0 4.9 %collective-permute-start.6 = (f32[16,128]{1,0:T(8,128)S(1)}, f32[16,128]{1,0:T(8,128)S(1)}, u32[]{:S(2)}, u32[]{:S(2)}) collective-permute-start(f32[16,128]{1,0:T(8,128)S(1)} %add.204), channel_id=1, source_target_pairs={{0,3},{1,2},{2,1},{3,0},{4,7},{5,6},{6,5},{7,4},{8,11},{9,10},{10,... | collective-permute-start | bytes 24584 | tf_op jit(solution)/shard_map/ppermute | solution.py:60
Sparse Core Ops, SparseCore 0:
  9.7 120.2 all-gather.5
  144.6 44.4 reduce-scatter.1

commit v13 on v12

--- a/solution.py
+++ b/solution.py
@@ -14,17 +14,31 @@
     tile = out_ref.shape[-1]
     n_col = out_ref.shape[0] // n_q
 
-    def body(j, carry):
+    lhs_ref[...] = jnp.zeros(lhs_ref.shape, lhs_ref.dtype)
+
+    def each_block(j, action):
         for q in range(n_q):
             for g in range(n_g):
                 m_off = moff_ref[(j * n_q + q) * n_g + g]
-                left = flow_ref[pl.ds(pl.multiple_of(jnp.maximum(m_off, 0), tile), tile), :]
-                left = jnp.where(m_off >= 0, left, jnp.zeros_like(left))
-                lhs_ref[pl.ds(q * tile, tile), pl.ds(g * tile, tile)] = left
+
+                @pl.when(m_off >= 0)
+                def _():
+                    action(q, g, m_off)
+
+    def put(q, g, m_off):
+        left = flow_ref[pl.ds(pl.multiple_of(m_off, tile), tile), :]
+        lhs_ref[pl.ds(q * tile, tile), pl.ds(g * tile, tile)] = left
+
+    def clear(q, g, m_off):
+        lhs_ref[pl.ds(q * tile, tile), pl.ds(g * tile, tile)] = jnp.zeros((tile, tile), lhs_ref.dtype)
+
+    def body(j, carry):
+        each_block(j, put)
         right = graph_ref[pl.ds(pl.multiple_of(j * n_g * tile, n_g * tile), n_g * tile), :]
         res = jnp.dot(lhs_ref[...], right, preferred_element_type=jnp.float32)
         for q in range(n_q):
             out_ref[oidx_ref[j * n_q + q]] = res[q * tile : (q + 1) * tile]
+        each_block(j, clear)
         return carry
 
     lax.fori_loop(0, n_col, body, 0)

time: 213 us -> 221 us (1.038)
  Pallas kernels: 12.5 us -> 20.8 us
    pallas_call x1, Pallas kernels: 12.5 us -> 20.8 us  [kept_partials(): pl.pallas_call(kernel, out_shape=jax.ShapeDtypeStruct((n_out, tile, tile)...]
  transfers between devices with their start and end apart: 9 -> 9, of which waited for: 6 -> 6; matrix products, arithmetic and copies ran while one was open for 11% -> 10% of each run, Pallas kernels for 0% -> 0%
where the time goes in v13:
time: 221 us
  waiting for transfers between devices  86.1 us (39%)
  blocking collectives  67.4 us (30%)
  Pallas kernels  20.8 us (9%)
  local copies, waits for them, and re-layouts  16.5 us (7%)
  between operations  13.7 us (6%)
  other arithmetic  11.3 us (5%)
  starting transfers between devices  4.92 us (2%)
    reduce_scatter x1, waiting for transfers between devices, local(): lax.psum_scatter(partial_sum, 'layer', scatter_dimension=0, tiled=True)  44.7 us
    all_gather x1, blocking collectives, local(): lax.all_gather(b_coords[0, 0, 0][None], 'row', axis=0, tiled=True)  32.2 us
    all_gather x1, waiting for transfers between devices, local(): flow_tiles = lax.all_gather(a_tiles[0, 0, 0], 'col', axis=0, tiled=True)  30.6 us
    all_gather x1, blocking collectives, local(): lax.all_gather(a_coords[0, 0, 0][None], 'col', axis=0, tiled=True)  25.6 us
    pallas_call x1, Pallas kernels, kept_partials(): pl.pallas_call(kernel, out_shape=jax.ShapeDtypeStruct((n_out, tile, tile)...  20.8 us
    ppermute x4, waiting for transfers between devices, butterfly_sum(): x = x + lax.ppermute(x, axis, [(i, i ^ d) for i in range(n)])  10.1 us
    all_gather x1, blocking collectives, local(): lax.all_gather(out_coords[0, 0, 0][None], 'layer', axis=0, tiled=True)  9.61 us
    gather x1, local copies, waits for them, and re-layouts, local(): graph_flat = graph_tiles[g_tile.reshape(-1)].reshape(-1, tile)  5.23 us
  transfers between devices with their start and end apart: 9, of which 6 were waited for; matrix products, arithmetic and copies ran while one was open for 10% of the time, Pallas kernels for 0%

profile of v13, /device:TPU:0, one launch (start us, length us, event | category | flops | bytes accessed | tf_op | source)
XLA Modules:
  0.0 220.7 jit_solution(4637024515994848142)
XLA Ops:
  7.3 2.1 collective-permute-start.1
  9.4 32.2 %all-gather.1 = s32[4,1,1,32,2]{3,4,2,1,0:T(2,128)S(1)} all-gather(s32[1,1,1,32,2]{3,4,2,1,0:T(2,128)} %param.8), channel_id=3, replica_groups=mesh['row'=4,'col'=8,'layer'=4] {'row'}, dimensions={0}, use_global_device_ids=true | all-gather | bytes 1280 | tf_op jit(solution)/shard_map/all_gather | solution.py:103
  42.3 0.7 iota_reduce_fusion.2
  44.0 1.5 gather_fusion.6
  45.9 9.6 %all-gather.2 = s32[4,1,1,16,2]{3,4,2,1,0:T(2,128)S(1)} all-gather(s32[1,1,1,16,2]{3,4,2,1,0:T(2,128)S(1)} %copy-done.3), channel_id=4, replica_groups=mesh['row'=4,'col'=8,'layer'=4] {'layer'}, dimensions={0}, use_global_device_ids=true | all-gather | bytes 640 | tf_op jit(solution)/shard_map/all_gather | solution.py:106
  55.5 0.7 iota_reduce_fusion.1
  56.4 0.9 gather_fusion.7
  57.6 25.6 %all-gather = s32[8,1,1,32,2]{3,4,2,1,0:T(2,128)S(1)} all-gather(s32[1,1,1,32,2]{3,4,2,1,0:T(2,128)S(1)} %copy-done.2), channel_id=2, replica_groups=mesh['row'=4,'col'=8,'layer'=4] {'col'}, dimensions={0}, use_global_device_ids=true | all-gather | bytes 2304 | tf_op jit(solution)/shard_map/all_gather | solution.py:105
  83.9 3.0 %iota_reduce_fusion = (pred[16,4,8]{2,1,0:T(4,128)(4,1)}, s32[16,4,8]{2,1,0:T(4,128)S(1)}) fusion(s32[16,4]{1,0:T(8,128)S(1)} %copy.56, s32[16,8,32]{2,1,0:T(8,128)S(1)} %bitcast.69), kind=kLoop, calls=%fused_computation.10 | loop fusion | flops 127488 | bytes 19200 | tf_op jit(solution)/shard_map/local/reduce | solution.py:136
  87.4 2.6 %gather_fusion.2 = s32[512]{0:T(512)S(1)} fusion(s32[8,32]{1,0:T(8,128)S(1)} %get-tuple-element.15, s32[512]{0:T(512)S(1)} %reshape.393), kind=kCustom, calls=%fused_computation.2 | custom fusion | bytes 8192 | tf_op jit(solution)/shard_map/gather | solution.py:139
  90.8 3.3 %pad_maximum_fusion = bf16[128,128,128]{2,1,0:T(8,128)(2,1)} fusion(bf16[32,128,128]{2,1,0:T(8,128)(2,1)} %collective-permute-done.2, bf16[32,128,128]{2,1,0:T(8,128)(2,1)S(1)} %collective-permute-done.1, bf16[32,128,128]{2,1,0:T(8,128)(2,1)S(1)} %collective-permute-done, bf16[32,128,128]{2,1,0:T(8,128)(2,1)S(1)} %bitcast.68), kind=kLoop, calls=%fused_computation.8 | loop fusion | flops 6291456 | bytes 8388608 | tf_op jit(solution)/shard_map/concatenate | solution.py:102
  94.2 5.2 %gather_fusion.3 = bf16[128,128,128]{2,1,0:T(8,128)(2,1)} fusion(bf16[128,128,128]{2,1,0:T(8,128)(2,1)} %pad_maximum_fusion, s32[1024]{0:T(1024)S(1)} %pad_clamp_fusion.1), kind=kCustom, calls=%fused_computation.3 | custom fusion | bytes 8389120 | tf_op jit(solution)/shard_map/gather | solution.py:143
  99.4 30.6 %all-gather.6.cloned.1.call-done = bf16[1,1,1,256,128,128]{5,4,2,1,0,3:T(8,128)(2,1)} async-done(((bf16[1,1,1,32,128,128]{5,4,2,1,0,3:T(8,128)(2,1)}), bf16[1,1,1,256,128,128]{5,4,2,1,0,3:T(8,128)(2,1)}) %all-gather.6.cloned.1.call-update) | async-done | bytes 8388624 | tf_op jit(solution)/shard_map/all_gather | solution.py:104
  130.0 20.8 %shard_map.55 = f32[64,128,128]{2,1,0:T(8,128)S(1)} custom-call(s32[512]{0:T(512)S(1)} %reshape.374.moff_ref, s32[64]{0:T(128)S(1)} %add.196.oidx_ref, bf16[32768,128]{1,0:T(8,128)(2,1)} %bitcast.63, bf16[16384,128]{1,0:T(8,128)(2,1)} %bitcast.62), custom_call_target="tpu_custom_call" | custom-call | flops 2147483648 | bytes 16777216 | tf_op jit(solution)/shard_map/pallas_call | solution.py:50
  150.8 1.9 copy-done
  152.7 44.7 %reduce-scatter.2.cloned.1.call-done = f32[16,128,128]{2,1,0:T(8,128)} async-done(((f32[64,128,128]{2,1,0:T(8,128)}), f32[16,128,128]{2,1,0:T(8,128)}) %reduce-scatter.2.cloned.1.call-update) | async-done | bytes 1048592 | tf_op jit(solution)/shard_map/reduce_scatter | solution.py:153
  197.4 1.3 multiply_reduce_fusion
  198.8 1.2 collective-permute-done.3
  200.0 1.5 collective-permute-start.4
  201.5 2.1 collective-permute-done.4
  203.9 3.4 %collective-permute-done.5 = f32[16,128]{1,0:T(8,128)S(1)} collective-permute-done((f32[16,128]{1,0:T(8,128)S(1)}, f32[16,128]{1,0:T(8,128)S(1)}, u32[]{:S(2)}, u32[]{:S(2)}) %collective-permute-start.5) | collective-permute-done | bytes 8224 | tf_op jit(solution)/shard_map/ppermute | solution.py:74
  207.3 0.8 collective-permute-start.6
  208.8 3.4 %collective-permute-done.6 = f32[16,128]{1,0:T(8,128)S(1)} collective-permute-done((f32[16,128]{1,0:T(8,128)S(1)}, f32[16,128]{1,0:T(8,128)S(1)}, u32[]{:S(2)}, u32[]{:S(2)}) %collective-permute-start.6) | collective-permute-done | bytes 8224 | tf_op jit(solution)/shard_map/ppermute | solution.py:74
  212.7 1.1 bitcast_multiply_fusion
  (76 shorter events, 6.6 us)
Async XLA Ops:
  6.5 123.4 %all-gather.6.cloned.1.call-start = ((), (), s32[]{:S(2)}) async-start(), calls=%async_computation.2 | async-start | bytes 9437184 | tf_op jit(solution)/shard_map/all_gather | solution.py:104
  7.3 190.1 %reduce-scatter.2.cloned.1.call-start = ((), (), s32[]{:S(2)}) async-start(), calls=%async_computation.1 | async-start | bytes 5242880 | tf_op jit(solution)/shard_map/reduce_scatter | solution.py:153
  7.3 79.8 %collective-permute-start.1 = (bf16[32,128,128]{2,1,0:T(8,128)(2,1)}, bf16[32,128,128]{2,1,0:T(8,128)(2,1)S(1)}, u32[]{:S(2)}, u32[]{:S(2)}) collective-permute-start(bf16[32,128,128]{2,1,0:T(8,128)(2,1)} %bitcast.66), channel_id=1, source_target_pairs={{0,64},{32,96},{64,0},{96,32},{1,65},{33,97},{65,1},{97,33},{2,66}... | collective-permute-start | bytes 3145736 | tf_op jit(solution)/shard_map/ppermute | solution.py:98
  9.4 81.4 %collective-permute-start = (bf16[32,128,128]{2,1,0:T(8,128)(2,1)}, bf16[32,128,128]{2,1,0:T(8,128)(2,1)S(1)}, u32[]{:S(2)}, u32[]{:S(2)}) collective-permute-start(bf16[32,128,128]{2,1,0:T(8,128)(2,1)} %bitcast.67), channel_id=1, source_target_pairs={{0,32},{32,0},{64,96},{96,64},{1,33},{33,1},{65,97},{97,65},{2,34}... | collective-permute-start | bytes 3145736 | tf_op jit(solution)/shard_map/ppermute | solution.py:99
  44.0 1.9 copy-start.3
  44.0 13.5 %copy-start.2 = (s32[1,1,1,32,2]{3,4,2,1,0:T(2,128)S(1)}, s32[1,1,1,32,2]{3,4,2,1,0:T(2,128)}, u32[]{:S(2)}) copy-start(s32[1,1,1,32,2]{3,4,2,1,0:T(2,128)} %param.6) | copy-start | bytes 772
  87.1 3.7 %collective-permute-start.2 = (bf16[32,128,128]{2,1,0:T(8,128)(2,1)S(1)}, bf16[32,128,128]{2,1,0:T(8,128)(2,1)}, u32[]{:S(2)}, u32[]{:S(2)}) collective-permute-start(bf16[32,128,128]{2,1,0:T(8,128)(2,1)S(1)} %collective-permute-done.1), channel_id=1, source_target_pairs={{0,32},{32,0},{64,96},{96,64},{1,33},{33,1},{65,97},{97,65},{2,34}... | collective-permute-start | bytes 3145736 | tf_op jit(solution)/shard_map/ppermute | solution.py:100
  87.4 3.5 %copy-start.1 = (bf16[1,1,1,32,128,128]{5,4,3,2,1,0:T(8,128)(2,1)S(1)}, bf16[1,1,1,32,128,128]{5,4,3,2,1,0:T(8,128)(2,1)}, u32[]{:S(2)}) copy-start(bf16[1,1,1,32,128,128]{5,4,3,2,1,0:T(8,128)(2,1)} %param.7) | copy-start | bytes 3145732
  150.8 1.9 copy-start
  198.7 1.3 collective-permute-start.3
  200.0 3.7 %collective-permute-start.4 = (f32[16,128]{1,0:T(8,128)S(1)}, f32[16,128]{1,0:T(8,128)S(1)}, u32[]{:S(2)}, u32[]{:S(2)}) collective-permute-start(f32[16,128]{1,0:T(8,128)S(1)} %add.202), channel_id=1, source_target_pairs={{0,64},{32,96},{64,0},{96,32},{1,65},{33,97},{65,1},{97,33},{2,66}... | collective-permute-start | bytes 24584 | tf_op jit(solution)/shard_map/ppermute | solution.py:74
  203.7 3.7 %collective-permute-start.5 = (f32[16,128]{1,0:T(8,128)S(1)}, f32[16,128]{1,0:T(8,128)S(1)}, u32[]{:S(2)}, u32[]{:S(2)}) collective-permute-start(f32[16,128]{1,0:T(8,128)S(1)} %add.203), channel_id=1, source_target_pairs={{0,1},{1,0},{2,3},{3,2},{4,5},{5,4},{6,7},{7,6},{8,9},{9,8},{10,11... | collective-permute-start | bytes 24584 | tf_op jit(solution)/shard_map/ppermute | solution.py:74
  207.3 4.9 %collective-permute-start.6 = (f32[16,128]{1,0:T(8,128)S(1)}, f32[16,128]{1,0:T(8,128)S(1)}, u32[]{:S(2)}, u32[]{:S(2)}) collective-permute-start(f32[16,128]{1,0:T(8,128)S(1)} %add.204), channel_id=1, source_target_pairs={{0,3},{1,2},{2,1},{3,0},{4,7},{5,6},{6,5},{7,4},{8,11},{9,10},{10,... | collective-permute-start | bytes 24584 | tf_op jit(solution)/shard_map/ppermute | solution.py:74
Sparse Core Ops, SparseCore 0:
  9.7 120.2 all-gather.5
  152.8 44.4 reduce-scatter.1

commit v14 on v12

--- a/solution.py
+++ b/solution.py
@@ -14,20 +14,24 @@
     tile = out_ref.shape[-1]
     n_col = out_ref.shape[0] // n_q
 
-    def body(j, carry):
+    def column(j, slot):
         for q in range(n_q):
             for g in range(n_g):
                 m_off = moff_ref[(j * n_q + q) * n_g + g]
                 left = flow_ref[pl.ds(pl.multiple_of(jnp.maximum(m_off, 0), tile), tile), :]
                 left = jnp.where(m_off >= 0, left, jnp.zeros_like(left))
-                lhs_ref[pl.ds(q * tile, tile), pl.ds(g * tile, tile)] = left
+                lhs_ref[slot, pl.ds(q * tile, tile), pl.ds(g * tile, tile)] = left
         right = graph_ref[pl.ds(pl.multiple_of(j * n_g * tile, n_g * tile), n_g * tile), :]
-        res = jnp.dot(lhs_ref[...], right, preferred_element_type=jnp.float32)
+        res = jnp.dot(lhs_ref[slot], right, preferred_element_type=jnp.float32)
         for q in range(n_q):
             out_ref[oidx_ref[j * n_q + q]] = res[q * tile : (q + 1) * tile]
+
+    def body(i, carry):
+        column(2 * i, 0)
+        column(2 * i + 1, 1)
         return carry
 
-    lax.fori_loop(0, n_col, body, 0)
+    lax.fori_loop(0, n_col // 2, body, 0)
 
 
 def kept_partials(moff, oidx, flow_flat, graph_flat, n_out, n_q, n_g):
@@ -44,7 +48,7 @@
         ],
         out_specs=pl.BlockSpec(memory_space=pltpu.VMEM),
         scratch_shapes=[
-            pltpu.VMEM((n_q * tile, n_g * tile), jnp.bfloat16),
+            pltpu.VMEM((2, n_q * tile, n_g * tile), jnp.bfloat16),
         ],
         compiler_params=pltpu.CompilerParams(vmem_limit_bytes=48 * 1024 * 1024),
         cost_estimate=pl.CostEstimate(

time: 213 us -> 211 us (level)
  no operation moved by 1% of the time
where the time goes in v14:
time: 211 us
  waiting for transfers between devices  86.1 us (41%)
  blocking collectives  67.4 us (32%)
  local copies, waits for them, and re-layouts  16.5 us (8%)
  between operations  13.7 us (6%)
  other arithmetic  11.3 us (5%)
  Pallas kernels  11 us (5%)
  starting transfers between devices  4.88 us (2%)
    reduce_scatter x1, waiting for transfers between devices, local(): lax.psum_scatter(partial_sum, 'layer', scatter_dimension=0, tiled=True)  44.6 us
    all_gather x1, blocking collectives, local(): lax.all_gather(b_coords[0, 0, 0][None], 'row', axis=0, tiled=True)  32.2 us
    all_gather x1, waiting for transfers between devices, local(): flow_tiles = lax.all_gather(a_tiles[0, 0, 0], 'col', axis=0, tiled=True)  30.6 us
    all_gather x1, blocking collectives, local(): lax.all_gather(a_coords[0, 0, 0][None], 'col', axis=0, tiled=True)  25.6 us
    pallas_call x1, Pallas kernels, kept_partials(): pl.pallas_call(kernel, out_shape=jax.ShapeDtypeStruct((n_out, tile, tile)...  11 us
    ppermute x4, waiting for transfers between devices, butterfly_sum(): x = x + lax.ppermute(x, axis, [(i, i ^ d) for i in range(n)])  10.1 us
    all_gather x1, blocking collectives, local(): lax.all_gather(out_coords[0, 0, 0][None], 'layer', axis=0, tiled=True)  9.61 us
    gather x1, local copies, waits for them, and re-layouts, local(): graph_flat = graph_tiles[g_tile.reshape(-1)].reshape(-1, tile)  5.23 us
  transfers between devices with their start and end apart: 9, of which 6 were waited for; matrix products, arithmetic and copies ran while one was open for 11% of the time, Pallas kernels for 0%

profile of v14, /device:TPU:0, one launch (start us, length us, event | category | flops | bytes accessed | tf_op | source)
XLA Modules:
  0.0 210.8 jit_solution(235131838540240499)
XLA Ops:
  7.3 2.1 collective-permute-start.1
  9.4 32.2 %all-gather.1 = s32[4,1,1,32,2]{3,4,2,1,0:T(2,128)S(1)} all-gather(s32[1,1,1,32,2]{3,4,2,1,0:T(2,128)} %param.8), channel_id=3, replica_groups=mesh['row'=4,'col'=8,'layer'=4] {'row'}, dimensions={0}, use_global_device_ids=true | all-gather | bytes 1280 | tf_op jit(solution)/shard_map/all_gather | solution.py:93
  42.3 0.7 iota_reduce_fusion.2
  44.0 1.5 gather_fusion.6
  45.9 9.6 %all-gather.2 = s32[4,1,1,16,2]{3,4,2,1,0:T(2,128)S(1)} all-gather(s32[1,1,1,16,2]{3,4,2,1,0:T(2,128)S(1)} %copy-done.3), channel_id=4, replica_groups=mesh['row'=4,'col'=8,'layer'=4] {'layer'}, dimensions={0}, use_global_device_ids=true | all-gather | bytes 640 | tf_op jit(solution)/shard_map/all_gather | solution.py:96
  55.5 0.7 iota_reduce_fusion.1
  56.4 0.9 gather_fusion.7
  57.6 25.6 %all-gather = s32[8,1,1,32,2]{3,4,2,1,0:T(2,128)S(1)} all-gather(s32[1,1,1,32,2]{3,4,2,1,0:T(2,128)S(1)} %copy-done.2), channel_id=2, replica_groups=mesh['row'=4,'col'=8,'layer'=4] {'col'}, dimensions={0}, use_global_device_ids=true | all-gather | bytes 2304 | tf_op jit(solution)/shard_map/all_gather | solution.py:95
  83.9 3.0 %iota_reduce_fusion = (pred[16,4,8]{2,1,0:T(4,128)(4,1)}, s32[16,4,8]{2,1,0:T(4,128)S(1)}) fusion(s32[16,4]{1,0:T(8,128)S(1)} %copy.56, s32[16,8,32]{2,1,0:T(8,128)S(1)} %bitcast.69), kind=kLoop, calls=%fused_computation.10 | loop fusion | flops 127488 | bytes 19200 | tf_op jit(solution)/shard_map/local/reduce | solution.py:126
  87.4 2.6 %gather_fusion.2 = s32[512]{0:T(512)S(1)} fusion(s32[8,32]{1,0:T(8,128)S(1)} %get-tuple-element.15, s32[512]{0:T(512)S(1)} %reshape.393), kind=kCustom, calls=%fused_computation.2 | custom fusion | bytes 8192 | tf_op jit(solution)/shard_map/gather | solution.py:129
  90.8 3.3 %pad_maximum_fusion = bf16[128,128,128]{2,1,0:T(8,128)(2,1)} fusion(bf16[32,128,128]{2,1,0:T(8,128)(2,1)} %collective-permute-done.2, bf16[32,128,128]{2,1,0:T(8,128)(2,1)S(1)} %collective-permute-done.1, bf16[32,128,128]{2,1,0:T(8,128)(2,1)S(1)} %collective-permute-done, bf16[32,128,128]{2,1,0:T(8,128)(2,1)S(1)} %bitcast.68), kind=kLoop, calls=%fused_computation.8 | loop fusion | flops 6291456 | bytes 8388608 | tf_op jit(solution)/shard_map/concatenate | solution.py:92
  94.2 5.2 %gather_fusion.3 = bf16[128,128,128]{2,1,0:T(8,128)(2,1)} fusion(bf16[128,128,128]{2,1,0:T(8,128)(2,1)} %pad_maximum_fusion, s32[1024]{0:T(1024)S(1)} %pad_clamp_fusion.1), kind=kCustom, calls=%fused_computation.3 | custom fusion | bytes 8389120 | tf_op jit(solution)/shard_map/gather | solution.py:133
  99.4 30.6 %all-gather.6.cloned.1.call-done = bf16[1,1,1,256,128,128]{5,4,2,1,0,3:T(8,128)(2,1)} async-done(((bf16[1,1,1,32,128,128]{5,4,2,1,0,3:T(8,128)(2,1)}), bf16[1,1,1,256,128,128]{5,4,2,1,0,3:T(8,128)(2,1)}) %all-gather.6.cloned.1.call-update) | async-done | bytes 8388624 | tf_op jit(solution)/shard_map/all_gather | solution.py:94
  130.0 11.0 %shard_map.55 = f32[64,128,128]{2,1,0:T(8,128)S(1)} custom-call(s32[512]{0:T(512)S(1)} %reshape.374.moff_ref, s32[64]{0:T(128)S(1)} %add.196.oidx_ref, bf16[32768,128]{1,0:T(8,128)(2,1)} %bitcast.63, bf16[16384,128]{1,0:T(8,128)(2,1)} %bitcast.62), custom_call_target="tpu_custom_call" | custom-call | flops 2147483648 | bytes 16777216 | tf_op jit(solution)/shard_map/pallas_call | solution.py:40
  141.0 1.9 copy-done
  142.9 44.6 %reduce-scatter.2.cloned.1.call-done = f32[16,128,128]{2,1,0:T(8,128)} async-done(((f32[64,128,128]{2,1,0:T(8,128)}), f32[16,128,128]{2,1,0:T(8,128)}) %reduce-scatter.2.cloned.1.call-update) | async-done | bytes 1048592 | tf_op jit(solution)/shard_map/reduce_scatter | solution.py:143
  187.6 1.3 multiply_reduce_fusion
  189.0 1.2 collective-permute-done.3
  190.2 1.5 collective-permute-start.4
  191.7 2.1 %collective-permute-done.4 = f32[16,128]{1,0:T(8,128)S(1)} collective-permute-done((f32[16,128]{1,0:T(8,128)S(1)}, f32[16,128]{1,0:T(8,128)S(1)}, u32[]{:S(2)}, u32[]{:S(2)}) %collective-permute-start.4) | collective-permute-done | bytes 8224 | tf_op jit(solution)/shard_map/ppermute | solution.py:64
  194.1 3.4 %collective-permute-done.5 = f32[16,128]{1,0:T(8,128)S(1)} collective-permute-done((f32[16,128]{1,0:T(8,128)S(1)}, f32[16,128]{1,0:T(8,128)S(1)}, u32[]{:S(2)}, u32[]{:S(2)}) %collective-permute-start.5) | collective-permute-done | bytes 8224 | tf_op jit(solution)/shard_map/ppermute | solution.py:64
  197.5 0.8 collective-permute-start.6
  199.0 3.4 %collective-permute-done.6 = f32[16,128]{1,0:T(8,128)S(1)} collective-permute-done((f32[16,128]{1,0:T(8,128)S(1)}, f32[16,128]{1,0:T(8,128)S(1)}, u32[]{:S(2)}, u32[]{:S(2)}) %collective-permute-start.6) | collective-permute-done | bytes 8224 | tf_op jit(solution)/shard_map/ppermute | solution.py:64
  202.9 1.1 bitcast_multiply_fusion
  (76 shorter events, 6.6 us)
Async XLA Ops:
  6.5 123.4 %all-gather.6.cloned.1.call-start = ((), (), s32[]{:S(2)}) async-start(), calls=%async_computation.2 | async-start | bytes 9437184 | tf_op jit(solution)/shard_map/all_gather | solution.py:94
  7.3 180.3 %reduce-scatter.2.cloned.1.call-start = ((), (), s32[]{:S(2)}) async-start(), calls=%async_computation.1 | async-start | bytes 5242880 | tf_op jit(solution)/shard_map/reduce_scatter | solution.py:143
  7.3 79.8 %collective-permute-start.1 = (bf16[32,128,128]{2,1,0:T(8,128)(2,1)}, bf16[32,128,128]{2,1,0:T(8,128)(2,1)S(1)}, u32[]{:S(2)}, u32[]{:S(2)}) collective-permute-start(bf16[32,128,128]{2,1,0:T(8,128)(2,1)} %bitcast.66), channel_id=1, source_target_pairs={{0,64},{32,96},{64,0},{96,32},{1,65},{33,97},{65,1},{97,33},{2,66}... | collective-permute-start | bytes 3145736 | tf_op jit(solution)/shard_map/ppermute | solution.py:88
  9.4 81.4 %collective-permute-start = (bf16[32,128,128]{2,1,0:T(8,128)(2,1)}, bf16[32,128,128]{2,1,0:T(8,128)(2,1)S(1)}, u32[]{:S(2)}, u32[]{:S(2)}) collective-permute-start(bf16[32,128,128]{2,1,0:T(8,128)(2,1)} %bitcast.67), channel_id=1, source_target_pairs={{0,32},{32,0},{64,96},{96,64},{1,33},{33,1},{65,97},{97,65},{2,34}... | collective-permute-start | bytes 3145736 | tf_op jit(solution)/shard_map/ppermute | solution.py:89
  44.0 1.9 copy-start.3
  44.0 13.5 %copy-start.2 = (s32[1,1,1,32,2]{3,4,2,1,0:T(2,128)S(1)}, s32[1,1,1,32,2]{3,4,2,1,0:T(2,128)}, u32[]{:S(2)}) copy-start(s32[1,1,1,32,2]{3,4,2,1,0:T(2,128)} %param.6) | copy-start | bytes 772
  87.1 3.7 %collective-permute-start.2 = (bf16[32,128,128]{2,1,0:T(8,128)(2,1)S(1)}, bf16[32,128,128]{2,1,0:T(8,128)(2,1)}, u32[]{:S(2)}, u32[]{:S(2)}) collective-permute-start(bf16[32,128,128]{2,1,0:T(8,128)(2,1)S(1)} %collective-permute-done.1), channel_id=1, source_target_pairs={{0,32},{32,0},{64,96},{96,64},{1,33},{33,1},{65,97},{97,65},{2,34}... | collective-permute-start | bytes 3145736 | tf_op jit(solution)/shard_map/ppermute | solution.py:90
  87.4 3.5 %copy-start.1 = (bf16[1,1,1,32,128,128]{5,4,3,2,1,0:T(8,128)(2,1)S(1)}, bf16[1,1,1,32,128,128]{5,4,3,2,1,0:T(8,128)(2,1)}, u32[]{:S(2)}) copy-start(bf16[1,1,1,32,128,128]{5,4,3,2,1,0:T(8,128)(2,1)} %param.7) | copy-start | bytes 3145732
  141.0 1.9 copy-start
  188.9 1.3 collective-permute-start.3
  190.2 3.7 %collective-permute-start.4 = (f32[16,128]{1,0:T(8,128)S(1)}, f32[16,128]{1,0:T(8,128)S(1)}, u32[]{:S(2)}, u32[]{:S(2)}) collective-permute-start(f32[16,128]{1,0:T(8,128)S(1)} %add.202), channel_id=1, source_target_pairs={{0,64},{32,96},{64,0},{96,32},{1,65},{33,97},{65,1},{97,33},{2,66}... | collective-permute-start | bytes 24584 | tf_op jit(solution)/shard_map/ppermute | solution.py:64
  193.8 3.7 %collective-permute-start.5 = (f32[16,128]{1,0:T(8,128)S(1)}, f32[16,128]{1,0:T(8,128)S(1)}, u32[]{:S(2)}, u32[]{:S(2)}) collective-permute-start(f32[16,128]{1,0:T(8,128)S(1)} %add.203), channel_id=1, source_target_pairs={{0,1},{1,0},{2,3},{3,2},{4,5},{5,4},{6,7},{7,6},{8,9},{9,8},{10,11... | collective-permute-start | bytes 24584 | tf_op jit(solution)/shard_map/ppermute | solution.py:64
  197.5 4.9 %collective-permute-start.6 = (f32[16,128]{1,0:T(8,128)S(1)}, f32[16,128]{1,0:T(8,128)S(1)}, u32[]{:S(2)}, u32[]{:S(2)}) collective-permute-start(f32[16,128]{1,0:T(8,128)S(1)} %add.204), channel_id=1, source_target_pairs={{0,3},{1,2},{2,1},{3,0},{4,7},{5,6},{6,5},{7,4},{8,11},{9,10},{10,... | collective-permute-start | bytes 24584 | tf_op jit(solution)/shard_map/ppermute | solution.py:64
Sparse Core Ops, SparseCore 0:
  9.7 120.2 all-gather.5
  143.1 44.4 reduce-scatter.1

commit v15 on v14

--- a/solution.py
+++ b/solution.py
@@ -8,6 +8,7 @@
 from jax.sharding import PartitionSpec as P
 
 KA = 4
+N_SLOT = 4
 
 
 def column_kernel(moff_ref, oidx_ref, flow_ref, graph_ref, out_ref, lhs_ref, *, n_q, n_g):
@@ -27,11 +28,11 @@
             out_ref[oidx_ref[j * n_q + q]] = res[q * tile : (q + 1) * tile]
 
     def body(i, carry):
-        column(2 * i, 0)
-        column(2 * i + 1, 1)
+        for k in range(N_SLOT):
+            column(N_SLOT * i + k, k)
         return carry
 
-    lax.fori_loop(0, n_col // 2, body, 0)
+    lax.fori_loop(0, n_col // N_SLOT, body, 0)
 
 
 def kept_partials(moff, oidx, flow_flat, graph_flat, n_out, n_q, n_g):
@@ -48,7 +49,7 @@
         ],
         out_specs=pl.BlockSpec(memory_space=pltpu.VMEM),
         scratch_shapes=[
-            pltpu.VMEM((2, n_q * tile, n_g * tile), jnp.bfloat16),
+            pltpu.VMEM((N_SLOT, n_q * tile, n_g * tile), jnp.bfloat16),
         ],
         compiler_params=pltpu.CompilerParams(vmem_limit_bytes=48 * 1024 * 1024),
         cost_estimate=pl.CostEstimate(

time: 211 us -> 210 us (level)
  no operation moved by 1% of the time
where the time goes in v15:
time: 210 us
  waiting for transfers between devices  86.1 us (41%)
  blocking collectives  67.4 us (32%)
  local copies, waits for them, and re-layouts  16.5 us (8%)
  between operations  13.7 us (7%)
  other arithmetic  11.3 us (5%)
  Pallas kernels  10.3 us (5%)
  starting transfers between devices  4.88 us (2%)
    reduce_scatter x1, waiting for transfers between devices, local(): lax.psum_scatter(partial_sum, 'layer', scatter_dimension=0, tiled=True)  44.6 us
    all_gather x1, blocking collectives, local(): lax.all_gather(b_coords[0, 0, 0][None], 'row', axis=0, tiled=True)  32.2 us
    all_gather x1, waiting for transfers between devices, local(): flow_tiles = lax.all_gather(a_tiles[0, 0, 0], 'col', axis=0, tiled=True)  30.6 us
    all_gather x1, blocking collectives, local(): lax.all_gather(a_coords[0, 0, 0][None], 'col', axis=0, tiled=True)  25.6 us
    pallas_call x1, Pallas kernels, kept_partials(): pl.pallas_call(kernel, out_shape=jax.ShapeDtypeStruct((n_out, tile, tile)...  10.3 us
    ppermute x4, waiting for transfers between devices, butterfly_sum(): x = x + lax.ppermute(x, axis, [(i, i ^ d) for i in range(n)])  10.1 us
    all_gather x1, blocking collectives, local(): lax.all_gather(out_coords[0, 0, 0][None], 'layer', axis=0, tiled=True)  9.61 us
    gather x1, local copies, waits for them, and re-layouts, local(): graph_flat = graph_tiles[g_tile.reshape(-1)].reshape(-1, tile)  5.23 us
  transfers between devices with their start and end apart: 9, of which 6 were waited for; matrix products, arithmetic and copies ran while one was open for 11% of the time, Pallas kernels for 0%

profile of v15, /device:TPU:0, one launch (start us, length us, event | category | flops | bytes accessed | tf_op | source)
XLA Modules:
  0.0 210.1 jit_solution(15211153961834705180)
XLA Ops:
  7.3 2.1 collective-permute-start.1
  9.4 32.2 %all-gather.1 = s32[4,1,1,32,2]{3,4,2,1,0:T(2,128)S(1)} all-gather(s32[1,1,1,32,2]{3,4,2,1,0:T(2,128)} %param.8), channel_id=3, replica_groups=mesh['row'=4,'col'=8,'layer'=4] {'row'}, dimensions={0}, use_global_device_ids=true | all-gather | bytes 1280 | tf_op jit(solution)/shard_map/all_gather | solution.py:94
  42.3 0.7 iota_reduce_fusion.2
  44.0 1.5 gather_fusion.6
  45.9 9.6 %all-gather.2 = s32[4,1,1,16,2]{3,4,2,1,0:T(2,128)S(1)} all-gather(s32[1,1,1,16,2]{3,4,2,1,0:T(2,128)S(1)} %copy-done.3), channel_id=4, replica_groups=mesh['row'=4,'col'=8,'layer'=4] {'layer'}, dimensions={0}, use_global_device_ids=true | all-gather | bytes 640 | tf_op jit(solution)/shard_map/all_gather | solution.py:97
  55.5 0.7 iota_reduce_fusion.1
  56.4 0.9 gather_fusion.7
  57.6 25.6 %all-gather = s32[8,1,1,32,2]{3,4,2,1,0:T(2,128)S(1)} all-gather(s32[1,1,1,32,2]{3,4,2,1,0:T(2,128)S(1)} %copy-done.2), channel_id=2, replica_groups=mesh['row'=4,'col'=8,'layer'=4] {'col'}, dimensions={0}, use_global_device_ids=true | all-gather | bytes 2304 | tf_op jit(solution)/shard_map/all_gather | solution.py:96
  83.9 3.0 %iota_reduce_fusion = (pred[16,4,8]{2,1,0:T(4,128)(4,1)}, s32[16,4,8]{2,1,0:T(4,128)S(1)}) fusion(s32[16,4]{1,0:T(8,128)S(1)} %copy.56, s32[16,8,32]{2,1,0:T(8,128)S(1)} %bitcast.69), kind=kLoop, calls=%fused_computation.10 | loop fusion | flops 127488 | bytes 19200 | tf_op jit(solution)/shard_map/local/reduce | solution.py:127
  87.4 2.6 %gather_fusion.2 = s32[512]{0:T(512)S(1)} fusion(s32[8,32]{1,0:T(8,128)S(1)} %get-tuple-element.15, s32[512]{0:T(512)S(1)} %reshape.393), kind=kCustom, calls=%fused_computation.2 | custom fusion | bytes 8192 | tf_op jit(solution)/shard_map/gather | solution.py:130
  90.8 3.3 %pad_maximum_fusion = bf16[128,128,128]{2,1,0:T(8,128)(2,1)} fusion(bf16[32,128,128]{2,1,0:T(8,128)(2,1)} %collective-permute-done.2, bf16[32,128,128]{2,1,0:T(8,128)(2,1)S(1)} %collective-permute-done.1, bf16[32,128,128]{2,1,0:T(8,128)(2,1)S(1)} %collective-permute-done, bf16[32,128,128]{2,1,0:T(8,128)(2,1)S(1)} %bitcast.68), kind=kLoop, calls=%fused_computation.8 | loop fusion | flops 6291456 | bytes 8388608 | tf_op jit(solution)/shard_map/concatenate | solution.py:93
  94.2 5.2 %gather_fusion.3 = bf16[128,128,128]{2,1,0:T(8,128)(2,1)} fusion(bf16[128,128,128]{2,1,0:T(8,128)(2,1)} %pad_maximum_fusion, s32[1024]{0:T(1024)S(1)} %pad_clamp_fusion.1), kind=kCustom, calls=%fused_computation.3 | custom fusion | bytes 8389120 | tf_op jit(solution)/shard_map/gather | solution.py:134
  99.4 30.6 %all-gather.6.cloned.1.call-done = bf16[1,1,1,256,128,128]{5,4,2,1,0,3:T(8,128)(2,1)} async-done(((bf16[1,1,1,32,128,128]{5,4,2,1,0,3:T(8,128)(2,1)}), bf16[1,1,1,256,128,128]{5,4,2,1,0,3:T(8,128)(2,1)}) %all-gather.6.cloned.1.call-update) | async-done | bytes 8388624 | tf_op jit(solution)/shard_map/all_gather | solution.py:95
  130.0 10.3 %shard_map.55 = f32[64,128,128]{2,1,0:T(8,128)S(1)} custom-call(s32[512]{0:T(512)S(1)} %reshape.374.moff_ref, s32[64]{0:T(128)S(1)} %add.196.oidx_ref, bf16[32768,128]{1,0:T(8,128)(2,1)} %bitcast.63, bf16[16384,128]{1,0:T(8,128)(2,1)} %bitcast.62), custom_call_target="tpu_custom_call" | custom-call | flops 2147483648 | bytes 16777216 | tf_op jit(solution)/shard_map/pallas_call | solution.py:41
  140.3 1.9 copy-done
  142.2 44.6 %reduce-scatter.2.cloned.1.call-done = f32[16,128,128]{2,1,0:T(8,128)} async-done(((f32[64,128,128]{2,1,0:T(8,128)}), f32[16,128,128]{2,1,0:T(8,128)}) %reduce-scatter.2.cloned.1.call-update) | async-done | bytes 1048592 | tf_op jit(solution)/shard_map/reduce_scatter | solution.py:144
  186.9 1.3 multiply_reduce_fusion
  188.3 1.2 collective-permute-done.3
  189.5 1.5 collective-permute-start.4
  191.0 2.1 %collective-permute-done.4 = f32[16,128]{1,0:T(8,128)S(1)} collective-permute-done((f32[16,128]{1,0:T(8,128)S(1)}, f32[16,128]{1,0:T(8,128)S(1)}, u32[]{:S(2)}, u32[]{:S(2)}) %collective-permute-start.4) | collective-permute-done | bytes 8224 | tf_op jit(solution)/shard_map/ppermute | solution.py:65
  193.4 3.4 %collective-permute-done.5 = f32[16,128]{1,0:T(8,128)S(1)} collective-permute-done((f32[16,128]{1,0:T(8,128)S(1)}, f32[16,128]{1,0:T(8,128)S(1)}, u32[]{:S(2)}, u32[]{:S(2)}) %collective-permute-start.5) | collective-permute-done | bytes 8224 | tf_op jit(solution)/shard_map/ppermute | solution.py:65
  196.8 0.8 collective-permute-start.6
  198.3 3.4 %collective-permute-done.6 = f32[16,128]{1,0:T(8,128)S(1)} collective-permute-done((f32[16,128]{1,0:T(8,128)S(1)}, f32[16,128]{1,0:T(8,128)S(1)}, u32[]{:S(2)}, u32[]{:S(2)}) %collective-permute-start.6) | collective-permute-done | bytes 8224 | tf_op jit(solution)/shard_map/ppermute | solution.py:65
  202.2 1.1 bitcast_multiply_fusion
  (76 shorter events, 6.6 us)
Async XLA Ops:
  6.5 123.4 %all-gather.6.cloned.1.call-start = ((), (), s32[]{:S(2)}) async-start(), calls=%async_computation.2 | async-start | bytes 9437184 | tf_op jit(solution)/shard_map/all_gather | solution.py:95
  7.3 179.6 %reduce-scatter.2.cloned.1.call-start = ((), (), s32[]{:S(2)}) async-start(), calls=%async_computation.1 | async-start | bytes 5242880 | tf_op jit(solution)/shard_map/reduce_scatter | solution.py:144
  7.3 79.8 %collective-permute-start.1 = (bf16[32,128,128]{2,1,0:T(8,128)(2,1)}, bf16[32,128,128]{2,1,0:T(8,128)(2,1)S(1)}, u32[]{:S(2)}, u32[]{:S(2)}) collective-permute-start(bf16[32,128,128]{2,1,0:T(8,128)(2,1)} %bitcast.66), channel_id=1, source_target_pairs={{0,64},{32,96},{64,0},{96,32},{1,65},{33,97},{65,1},{97,33},{2,66}... | collective-permute-start | bytes 3145736 | tf_op jit(solution)/shard_map/ppermute | solution.py:89
  9.4 81.4 %collective-permute-start = (bf16[32,128,128]{2,1,0:T(8,128)(2,1)}, bf16[32,128,128]{2,1,0:T(8,128)(2,1)S(1)}, u32[]{:S(2)}, u32[]{:S(2)}) collective-permute-start(bf16[32,128,128]{2,1,0:T(8,128)(2,1)} %bitcast.67), channel_id=1, source_target_pairs={{0,32},{32,0},{64,96},{96,64},{1,33},{33,1},{65,97},{97,65},{2,34}... | collective-permute-start | bytes 3145736 | tf_op jit(solution)/shard_map/ppermute | solution.py:90
  44.0 1.9 copy-start.3
  44.0 13.5 %copy-start.2 = (s32[1,1,1,32,2]{3,4,2,1,0:T(2,128)S(1)}, s32[1,1,1,32,2]{3,4,2,1,0:T(2,128)}, u32[]{:S(2)}) copy-start(s32[1,1,1,32,2]{3,4,2,1,0:T(2,128)} %param.6) | copy-start | bytes 772
  87.1 3.7 %collective-permute-start.2 = (bf16[32,128,128]{2,1,0:T(8,128)(2,1)S(1)}, bf16[32,128,128]{2,1,0:T(8,128)(2,1)}, u32[]{:S(2)}, u32[]{:S(2)}) collective-permute-start(bf16[32,128,128]{2,1,0:T(8,128)(2,1)S(1)} %collective-permute-done.1), channel_id=1, source_target_pairs={{0,32},{32,0},{64,96},{96,64},{1,33},{33,1},{65,97},{97,65},{2,34}... | collective-permute-start | bytes 3145736 | tf_op jit(solution)/shard_map/ppermute | solution.py:91
  87.4 3.5 %copy-start.1 = (bf16[1,1,1,32,128,128]{5,4,3,2,1,0:T(8,128)(2,1)S(1)}, bf16[1,1,1,32,128,128]{5,4,3,2,1,0:T(8,128)(2,1)}, u32[]{:S(2)}) copy-start(bf16[1,1,1,32,128,128]{5,4,3,2,1,0:T(8,128)(2,1)} %param.7) | copy-start | bytes 3145732
  140.3 1.9 copy-start
  188.2 1.3 collective-permute-start.3
  189.5 3.7 %collective-permute-start.4 = (f32[16,128]{1,0:T(8,128)S(1)}, f32[16,128]{1,0:T(8,128)S(1)}, u32[]{:S(2)}, u32[]{:S(2)}) collective-permute-start(f32[16,128]{1,0:T(8,128)S(1)} %add.202), channel_id=1, source_target_pairs={{0,64},{32,96},{64,0},{96,32},{1,65},{33,97},{65,1},{97,33},{2,66}... | collective-permute-start | bytes 24584 | tf_op jit(solution)/shard_map/ppermute | solution.py:65
  193.1 3.7 %collective-permute-start.5 = (f32[16,128]{1,0:T(8,128)S(1)}, f32[16,128]{1,0:T(8,128)S(1)}, u32[]{:S(2)}, u32[]{:S(2)}) collective-permute-start(f32[16,128]{1,0:T(8,128)S(1)} %add.203), channel_id=1, source_target_pairs={{0,1},{1,0},{2,3},{3,2},{4,5},{5,4},{6,7},{7,6},{8,9},{9,8},{10,11... | collective-permute-start | bytes 24584 | tf_op jit(solution)/shard_map/ppermute | solution.py:65
  196.8 4.9 %collective-permute-start.6 = (f32[16,128]{1,0:T(8,128)S(1)}, f32[16,128]{1,0:T(8,128)S(1)}, u32[]{:S(2)}, u32[]{:S(2)}) collective-permute-start(f32[16,128]{1,0:T(8,128)S(1)} %add.204), channel_id=1, source_target_pairs={{0,3},{1,2},{2,1},{3,0},{4,7},{5,6},{6,5},{7,4},{8,11},{9,10},{10,... | collective-permute-start | bytes 24584 | tf_op jit(solution)/shard_map/ppermute | solution.py:65
Sparse Core Ops, SparseCore 0:
  9.7 120.2 all-gather.5
  142.3 44.4 reduce-scatter.1

commit v16 on v15

--- a/solution.py
+++ b/solution.py
@@ -11,7 +11,7 @@
 N_SLOT = 4
 
 
-def column_kernel(moff_ref, oidx_ref, flow_ref, graph_ref, out_ref, lhs_ref, *, n_q, n_g):
+def column_kernel(moff_ref, oidx_ref, flow_ref, graph_hbm, out_ref, lhs_ref, graph_ref, graph_sem, *, n_q, n_g):
     tile = out_ref.shape[-1]
     n_col = out_ref.shape[0] // n_q
 
@@ -27,12 +27,25 @@
         for q in range(n_q):
             out_ref[oidx_ref[j * n_q + q]] = res[q * tile : (q + 1) * tile]
 
+    chunk = N_SLOT * n_g * tile
+    n_step = n_col // N_SLOT
+    copies = [
+        pltpu.make_async_copy(
+            graph_hbm.at[pl.ds(i * chunk, chunk), :], graph_ref.at[pl.ds(i * chunk, chunk), :], graph_sem.at[i]
+        )
+        for i in range(n_step)
+    ]
+    for copy in copies:
+        copy.start()
+
     def body(i, carry):
         for k in range(N_SLOT):
             column(N_SLOT * i + k, k)
         return carry
 
-    lax.fori_loop(0, n_col // N_SLOT, body, 0)
+    for i in range(n_step):
+        copies[i].wait()
+        body(i, 0)
 
 
 def kept_partials(moff, oidx, flow_flat, graph_flat, n_out, n_q, n_g):
@@ -45,11 +58,13 @@
             pl.BlockSpec(memory_space=pltpu.SMEM),
             pl.BlockSpec(memory_space=pltpu.SMEM),
             pl.BlockSpec(memory_space=pltpu.VMEM),
-            pl.BlockSpec(memory_space=pltpu.VMEM),
+            pl.BlockSpec(memory_space=pl.ANY),
         ],
         out_specs=pl.BlockSpec(memory_space=pltpu.VMEM),
         scratch_shapes=[
             pltpu.VMEM((N_SLOT, n_q * tile, n_g * tile), jnp.bfloat16),
+            pltpu.VMEM(graph_flat.shape, jnp.bfloat16),
+            pltpu.SemaphoreType.DMA((n_out // n_q // N_SLOT,)),
         ],
         compiler_params=pltpu.CompilerParams(vmem_limit_bytes=48 * 1024 * 1024),
         cost_estimate=pl.CostEstimate(

time: 210 us -> 210 us (level)
  no operation moved by 1% of the time
where the time goes in v16:
time: 210 us
  waiting for transfers between devices  85.9 us (41%)
  blocking collectives  67.4 us (32%)
  local copies, waits for them, and re-layouts  16.5 us (8%)
  between operations  13.7 us (7%)
  other arithmetic  11.3 us (5%)
  Pallas kernels  10.3 us (5%)
  starting transfers between devices  5.07 us (2%)
    reduce_scatter x1, waiting for transfers between devices, local(): lax.psum_scatter(partial_sum, 'layer', scatter_dimension=0, tiled=True)  44.6 us
    all_gather x1, blocking collectives, local(): lax.all_gather(b_coords[0, 0, 0][None], 'row', axis=0, tiled=True)  32.2 us
    all_gather x1, waiting for transfers between devices, local(): flow_tiles = lax.all_gather(a_tiles[0, 0, 0], 'col', axis=0, tiled=True)  30.4 us
    all_gather x1, blocking collectives, local(): lax.all_gather(a_coords[0, 0, 0][None], 'col', axis=0, tiled=True)  25.6 us
    pallas_call x1, Pallas kernels, kept_partials(): pl.pallas_call(kernel, out_shape=jax.ShapeDtypeStruct((n_out, tile, tile)...  10.3 us
    ppermute x4, waiting for transfers between devices, butterfly_sum(): x = x + lax.ppermute(x, axis, [(i, i ^ d) for i in range(n)])  10.1 us
    all_gather x1, blocking collectives, local(): lax.all_gather(out_coords[0, 0, 0][None], 'layer', axis=0, tiled=True)  9.61 us
    gather x1, local copies, waits for them, and re-layouts, local(): graph_flat = graph_tiles[g_tile.reshape(-1)].reshape(-1, tile)  5.23 us
  transfers between devices with their start and end apart: 9, of which 6 were waited for; matrix products, arithmetic and copies ran while one was open for 11% of the time, Pallas kernels for 0%

profile of v16, /device:TPU:0, one launch (start us, length us, event | category | flops | bytes accessed | tf_op | source)
XLA Modules:
  0.0 210.2 jit_solution(8003243692423123601)
XLA Ops:
  7.3 2.1 collective-permute-start.1
  9.4 32.2 %all-gather.1 = s32[4,1,1,32,2]{3,4,2,1,0:T(2,128)S(1)} all-gather(s32[1,1,1,32,2]{3,4,2,1,0:T(2,128)} %param.8), channel_id=3, replica_groups=mesh['row'=4,'col'=8,'layer'=4] {'row'}, dimensions={0}, use_global_device_ids=true | all-gather | bytes 1280 | tf_op jit(solution)/shard_map/all_gather | solution.py:109
  42.3 0.7 iota_reduce_fusion.2
  44.0 1.5 gather_fusion.6
  45.9 9.6 %all-gather.2 = s32[4,1,1,16,2]{3,4,2,1,0:T(2,128)S(1)} all-gather(s32[1,1,1,16,2]{3,4,2,1,0:T(2,128)S(1)} %copy-done.3), channel_id=4, replica_groups=mesh['row'=4,'col'=8,'layer'=4] {'layer'}, dimensions={0}, use_global_device_ids=true | all-gather | bytes 640 | tf_op jit(solution)/shard_map/all_gather | solution.py:112
  55.5 0.7 iota_reduce_fusion.1
  56.4 0.9 gather_fusion.7
  57.6 25.6 %all-gather = s32[8,1,1,32,2]{3,4,2,1,0:T(2,128)S(1)} all-gather(s32[1,1,1,32,2]{3,4,2,1,0:T(2,128)S(1)} %copy-done.2), channel_id=2, replica_groups=mesh['row'=4,'col'=8,'layer'=4] {'col'}, dimensions={0}, use_global_device_ids=true | all-gather | bytes 2304 | tf_op jit(solution)/shard_map/all_gather | solution.py:111
  83.9 3.0 %iota_reduce_fusion = (pred[16,4,8]{2,1,0:T(4,128)(4,1)}, s32[16,4,8]{2,1,0:T(4,128)S(1)}) fusion(s32[16,4]{1,0:T(8,128)S(1)} %copy.56, s32[16,8,32]{2,1,0:T(8,128)S(1)} %bitcast.69), kind=kLoop, calls=%fused_computation.10 | loop fusion | flops 127488 | bytes 19200 | tf_op jit(solution)/shard_map/local/reduce | solution.py:142
  87.6 2.6 %gather_fusion.2 = s32[512]{0:T(512)S(1)} fusion(s32[8,32]{1,0:T(8,128)S(1)} %get-tuple-element.15, s32[512]{0:T(512)S(1)} %reshape.393), kind=kCustom, calls=%fused_computation.2 | custom fusion | bytes 8192 | tf_op jit(solution)/shard_map/gather | solution.py:145
  91.0 3.3 %pad_maximum_fusion = bf16[128,128,128]{2,1,0:T(8,128)(2,1)} fusion(bf16[32,128,128]{2,1,0:T(8,128)(2,1)} %collective-permute-done.2, bf16[32,128,128]{2,1,0:T(8,128)(2,1)S(1)} %collective-permute-done.1, bf16[32,128,128]{2,1,0:T(8,128)(2,1)S(1)} %collective-permute-done, bf16[32,128,128]{2,1,0:T(8,128)(2,1)S(1)} %bitcast.68), kind=kLoop, calls=%fused_computation.8 | loop fusion | flops 6291456 | bytes 8388608 | tf_op jit(solution)/shard_map/concatenate | solution.py:108
  94.3 5.2 %gather_fusion.3 = bf16[128,128,128]{2,1,0:T(8,128)(2,1)} fusion(bf16[128,128,128]{2,1,0:T(8,128)(2,1)} %pad_maximum_fusion, s32[1024]{0:T(1024)S(1)} %pad_clamp_fusion.1), kind=kCustom, calls=%fused_computation.3 | custom fusion | bytes 8389120 | tf_op jit(solution)/shard_map/gather | solution.py:149
  99.6 30.4 %all-gather.6.cloned.1.call-done = bf16[1,1,1,256,128,128]{5,4,2,1,0,3:T(8,128)(2,1)} async-done(((bf16[1,1,1,32,128,128]{5,4,2,1,0,3:T(8,128)(2,1)}), bf16[1,1,1,256,128,128]{5,4,2,1,0,3:T(8,128)(2,1)}) %all-gather.6.cloned.1.call-update) | async-done | bytes 8388624 | tf_op jit(solution)/shard_map/all_gather | solution.py:110
  130.0 10.3 %shard_map.55 = f32[64,128,128]{2,1,0:T(8,128)S(1)} custom-call(s32[512]{0:T(512)S(1)} %reshape.374.moff_ref, s32[64]{0:T(128)S(1)} %add.196.oidx_ref, bf16[32768,128]{1,0:T(8,128)(2,1)} %bitcast.63, bf16[16384,128]{1,0:T(8,128)(2,1)} %bitcast.62), custom_call_target="tpu_custom_call" | custom-call | flops 2147483648 | bytes 16777216 | tf_op jit(solution)/shard_map/pallas_call | solution.py:54
  140.3 1.9 copy-done
  142.3 44.6 %reduce-scatter.2.cloned.1.call-done = f32[16,128,128]{2,1,0:T(8,128)} async-done(((f32[64,128,128]{2,1,0:T(8,128)}), f32[16,128,128]{2,1,0:T(8,128)}) %reduce-scatter.2.cloned.1.call-update) | async-done | bytes 1048592 | tf_op jit(solution)/shard_map/reduce_scatter | solution.py:159
  186.9 1.3 multiply_reduce_fusion
  188.4 1.2 collective-permute-done.3
  189.5 1.5 collective-permute-start.4
  191.1 2.1 %collective-permute-done.4 = f32[16,128]{1,0:T(8,128)S(1)} collective-permute-done((f32[16,128]{1,0:T(8,128)S(1)}, f32[16,128]{1,0:T(8,128)S(1)}, u32[]{:S(2)}, u32[]{:S(2)}) %collective-permute-start.4) | collective-permute-done | bytes 8224 | tf_op jit(solution)/shard_map/ppermute | solution.py:80
  193.4 3.4 %collective-permute-done.5 = f32[16,128]{1,0:T(8,128)S(1)} collective-permute-done((f32[16,128]{1,0:T(8,128)S(1)}, f32[16,128]{1,0:T(8,128)S(1)}, u32[]{:S(2)}, u32[]{:S(2)}) %collective-permute-start.5) | collective-permute-done | bytes 8224 | tf_op jit(solution)/shard_map/ppermute | solution.py:80
  196.8 0.8 collective-permute-start.6
  198.3 3.4 %collective-permute-done.6 = f32[16,128]{1,0:T(8,128)S(1)} collective-permute-done((f32[16,128]{1,0:T(8,128)S(1)}, f32[16,128]{1,0:T(8,128)S(1)}, u32[]{:S(2)}, u32[]{:S(2)}) %collective-permute-start.6) | collective-permute-done | bytes 8224 | tf_op jit(solution)/shard_map/ppermute | solution.py:80
  202.3 1.1 bitcast_multiply_fusion
  (76 shorter events, 6.8 us)
Async XLA Ops:
  6.5 123.4 %all-gather.6.cloned.1.call-start = ((), (), s32[]{:S(2)}) async-start(), calls=%async_computation.2 | async-start | bytes 9437184 | tf_op jit(solution)/shard_map/all_gather | solution.py:110
  7.3 179.7 %reduce-scatter.2.cloned.1.call-start = ((), (), s32[]{:S(2)}) async-start(), calls=%async_computation.1 | async-start | bytes 5242880 | tf_op jit(solution)/shard_map/reduce_scatter | solution.py:159
  7.3 79.8 %collective-permute-start.1 = (bf16[32,128,128]{2,1,0:T(8,128)(2,1)}, bf16[32,128,128]{2,1,0:T(8,128)(2,1)S(1)}, u32[]{:S(2)}, u32[]{:S(2)}) collective-permute-start(bf16[32,128,128]{2,1,0:T(8,128)(2,1)} %bitcast.66), channel_id=1, source_target_pairs={{0,64},{32,96},{64,0},{96,32},{1,65},{33,97},{65,1},{97,33},{2,66}... | collective-permute-start | bytes 3145736 | tf_op jit(solution)/shard_map/ppermute | solution.py:104
  9.4 81.6 %collective-permute-start = (bf16[32,128,128]{2,1,0:T(8,128)(2,1)}, bf16[32,128,128]{2,1,0:T(8,128)(2,1)S(1)}, u32[]{:S(2)}, u32[]{:S(2)}) collective-permute-start(bf16[32,128,128]{2,1,0:T(8,128)(2,1)} %bitcast.67), channel_id=1, source_target_pairs={{0,32},{32,0},{64,96},{96,64},{1,33},{33,1},{65,97},{97,65},{2,34}... | collective-permute-start | bytes 3145736 | tf_op jit(solution)/shard_map/ppermute | solution.py:105
  44.0 1.9 copy-start.3
  44.0 13.5 %copy-start.2 = (s32[1,1,1,32,2]{3,4,2,1,0:T(2,128)S(1)}, s32[1,1,1,32,2]{3,4,2,1,0:T(2,128)}, u32[]{:S(2)}) copy-start(s32[1,1,1,32,2]{3,4,2,1,0:T(2,128)} %param.6) | copy-start | bytes 772
  87.1 3.9 %collective-permute-start.2 = (bf16[32,128,128]{2,1,0:T(8,128)(2,1)S(1)}, bf16[32,128,128]{2,1,0:T(8,128)(2,1)}, u32[]{:S(2)}, u32[]{:S(2)}) collective-permute-start(bf16[32,128,128]{2,1,0:T(8,128)(2,1)S(1)} %collective-permute-done.1), channel_id=1, source_target_pairs={{0,32},{32,0},{64,96},{96,64},{1,33},{33,1},{65,97},{97,65},{2,34}... | collective-permute-start | bytes 3145736 | tf_op jit(solution)/shard_map/ppermute | solution.py:106
  87.5 3.5 %copy-start.1 = (bf16[1,1,1,32,128,128]{5,4,3,2,1,0:T(8,128)(2,1)S(1)}, bf16[1,1,1,32,128,128]{5,4,3,2,1,0:T(8,128)(2,1)}, u32[]{:S(2)}) copy-start(bf16[1,1,1,32,128,128]{5,4,3,2,1,0:T(8,128)(2,1)} %param.7) | copy-start | bytes 3145732
  140.3 1.9 copy-start
  188.3 1.3 collective-permute-start.3
  189.5 3.7 %collective-permute-start.4 = (f32[16,128]{1,0:T(8,128)S(1)}, f32[16,128]{1,0:T(8,128)S(1)}, u32[]{:S(2)}, u32[]{:S(2)}) collective-permute-start(f32[16,128]{1,0:T(8,128)S(1)} %add.202), channel_id=1, source_target_pairs={{0,64},{32,96},{64,0},{96,32},{1,65},{33,97},{65,1},{97,33},{2,66}... | collective-permute-start | bytes 24584 | tf_op jit(solution)/shard_map/ppermute | solution.py:80
  193.2 3.7 %collective-permute-start.5 = (f32[16,128]{1,0:T(8,128)S(1)}, f32[16,128]{1,0:T(8,128)S(1)}, u32[]{:S(2)}, u32[]{:S(2)}) collective-permute-start(f32[16,128]{1,0:T(8,128)S(1)} %add.203), channel_id=1, source_target_pairs={{0,1},{1,0},{2,3},{3,2},{4,5},{5,4},{6,7},{7,6},{8,9},{9,8},{10,11... | collective-permute-start | bytes 24584 | tf_op jit(solution)/shard_map/ppermute | solution.py:80
  196.8 4.9 %collective-permute-start.6 = (f32[16,128]{1,0:T(8,128)S(1)}, f32[16,128]{1,0:T(8,128)S(1)}, u32[]{:S(2)}, u32[]{:S(2)}) collective-permute-start(f32[16,128]{1,0:T(8,128)S(1)} %add.204), channel_id=1, source_target_pairs={{0,3},{1,2},{2,1},{3,0},{4,7},{5,6},{6,5},{7,4},{8,11},{9,10},{10,... | collective-permute-start | bytes 24584 | tf_op jit(solution)/shard_map/ppermute | solution.py:80
Sparse Core Ops, SparseCore 0:
  9.7 120.2 all-gather.5
  142.4 44.4 reduce-scatter.1

commit v17 on v15

--- a/solution.py
+++ b/solution.py
@@ -146,9 +146,9 @@
     kept_cols = out_coords[0, 0, 0, :, 1]
     squared = kept_tiles * kept_tiles
     local_mass = jnp.sum(squared, axis=1)
-    column_total = butterfly_sum(
-        butterfly_sum(local_mass, "row", row_count, (1, 2)), "layer", layer_count, (1, 3)
-    )
+    row_parts = [lax.ppermute(local_mass, "row", [(i, i ^ d) for i in range(row_count)]) for d in range(1, row_count)]
+    row_total = local_mass + sum(row_parts[1:], row_parts[0])
+    column_total = butterfly_sum(row_total, "layer", layer_count, (1, 3))
     factor = jnp.float32(row_count * layer_count * tile) / column_total
     flow = squared[kept_cols] * factor[kept_cols][:, None, :]
     return flow.reshape(1, 1, 1, col_tiles, tile, tile)

time: 210 us -> 210 us (level)
    ppermute x4 -> x2, waiting for transfers between devices: 10.1 us -> 6.77 us  [butterfly_sum(): x = x + lax.ppermute(x, axis, [(i, i ^ d) for i in range(n)])]
    ppermute x0 -> x3, waiting for transfers between devices: none -> 2.83 us  [local(): lax.ppermute(local_mass, 'row', [(i, i ^ d) for i in range(row_count)])]
  transfers between devices with their start and end apart: 9 -> 10, of which waited for: 6 -> 6; matrix products, arithmetic and copies ran while one was open for 11% -> 11% of each run, Pallas kernels for 0% -> 0%
where the time goes in v17:
time: 210 us
  waiting for transfers between devices  85.6 us (41%)
  blocking collectives  67.4 us (32%)
  local copies, waits for them, and re-layouts  16.5 us (8%)
  between operations  13.7 us (7%)
  other arithmetic  11.3 us (5%)
  Pallas kernels  10.3 us (5%)
  starting transfers between devices  5.27 us (3%)
    reduce_scatter x1, waiting for transfers between devices, local(): lax.psum_scatter(partial_sum, 'layer', scatter_dimension=0, tiled=True)  44.6 us
    all_gather x1, blocking collectives, local(): lax.all_gather(b_coords[0, 0, 0][None], 'row', axis=0, tiled=True)  32.2 us
    all_gather x1, waiting for transfers between devices, local(): flow_tiles = lax.all_gather(a_tiles[0, 0, 0], 'col', axis=0, tiled=True)  30.6 us
    all_gather x1, blocking collectives, local(): lax.all_gather(a_coords[0, 0, 0][None], 'col', axis=0, tiled=True)  25.6 us
    pallas_call x1, Pallas kernels, kept_partials(): pl.pallas_call(kernel, out_shape=jax.ShapeDtypeStruct((n_out, tile, tile)...  10.3 us
    all_gather x1, blocking collectives, local(): lax.all_gather(out_coords[0, 0, 0][None], 'layer', axis=0, tiled=True)  9.61 us
    ppermute x2, waiting for transfers between devices, butterfly_sum(): x = x + lax.ppermute(x, axis, [(i, i ^ d) for i in range(n)])  6.77 us
    gather x1, local copies, waits for them, and re-layouts, local(): graph_flat = graph_tiles[g_tile.reshape(-1)].reshape(-1, tile)  5.23 us
  transfers between devices with their start and end apart: 10, of which 6 were waited for; matrix products, arithmetic and copies ran while one was open for 11% of the time, Pallas kernels for 0%

profile of v17, /device:TPU:0, one launch (start us, length us, event | category | flops | bytes accessed | tf_op | source)
XLA Modules:
  0.0 210.0 jit_solution(12851073153860132523)
XLA Ops:
  7.3 2.1 collective-permute-start.1
  9.4 32.2 %all-gather.1 = s32[4,1,1,32,2]{3,4,2,1,0:T(2,128)S(1)} all-gather(s32[1,1,1,32,2]{3,4,2,1,0:T(2,128)} %param.8), channel_id=3, replica_groups=mesh['row'=4,'col'=8,'layer'=4] {'row'}, dimensions={0}, use_global_device_ids=true | all-gather | bytes 1280 | tf_op jit(solution)/shard_map/all_gather | solution.py:94
  42.3 0.7 iota_reduce_fusion.2
  44.0 1.5 gather_fusion.6
  45.9 9.6 %all-gather.2 = s32[4,1,1,16,2]{3,4,2,1,0:T(2,128)S(1)} all-gather(s32[1,1,1,16,2]{3,4,2,1,0:T(2,128)S(1)} %copy-done.3), channel_id=4, replica_groups=mesh['row'=4,'col'=8,'layer'=4] {'layer'}, dimensions={0}, use_global_device_ids=true | all-gather | bytes 640 | tf_op jit(solution)/shard_map/all_gather | solution.py:97
  55.5 0.7 iota_reduce_fusion.1
  56.4 0.9 gather_fusion.7
  57.6 25.6 %all-gather = s32[8,1,1,32,2]{3,4,2,1,0:T(2,128)S(1)} all-gather(s32[1,1,1,32,2]{3,4,2,1,0:T(2,128)S(1)} %copy-done.2), channel_id=2, replica_groups=mesh['row'=4,'col'=8,'layer'=4] {'col'}, dimensions={0}, use_global_device_ids=true | all-gather | bytes 2304 | tf_op jit(solution)/shard_map/all_gather | solution.py:96
  83.9 3.0 %iota_reduce_fusion = (pred[16,4,8]{2,1,0:T(4,128)(4,1)}, s32[16,4,8]{2,1,0:T(4,128)S(1)}) fusion(s32[16,4]{1,0:T(8,128)S(1)} %copy.56, s32[16,8,32]{2,1,0:T(8,128)S(1)} %bitcast.69), kind=kLoop, calls=%fused_computation.10 | loop fusion | flops 127488 | bytes 19200 | tf_op jit(solution)/shard_map/local/reduce | solution.py:127
  87.4 2.6 %gather_fusion.2 = s32[512]{0:T(512)S(1)} fusion(s32[8,32]{1,0:T(8,128)S(1)} %get-tuple-element.15, s32[512]{0:T(512)S(1)} %reshape.393), kind=kCustom, calls=%fused_computation.2 | custom fusion | bytes 8192 | tf_op jit(solution)/shard_map/gather | solution.py:130
  90.8 3.3 %pad_maximum_fusion = bf16[128,128,128]{2,1,0:T(8,128)(2,1)} fusion(bf16[32,128,128]{2,1,0:T(8,128)(2,1)} %collective-permute-done.2, bf16[32,128,128]{2,1,0:T(8,128)(2,1)S(1)} %collective-permute-done.1, bf16[32,128,128]{2,1,0:T(8,128)(2,1)S(1)} %collective-permute-done, bf16[32,128,128]{2,1,0:T(8,128)(2,1)S(1)} %bitcast.68), kind=kLoop, calls=%fused_computation.8 | loop fusion | flops 6291456 | bytes 8388608 | tf_op jit(solution)/shard_map/concatenate | solution.py:93
  94.2 5.2 %gather_fusion.3 = bf16[128,128,128]{2,1,0:T(8,128)(2,1)} fusion(bf16[128,128,128]{2,1,0:T(8,128)(2,1)} %pad_maximum_fusion, s32[1024]{0:T(1024)S(1)} %pad_clamp_fusion.1), kind=kCustom, calls=%fused_computation.3 | custom fusion | bytes 8389120 | tf_op jit(solution)/shard_map/gather | solution.py:134
  99.4 30.6 %all-gather.6.cloned.1.call-done = bf16[1,1,1,256,128,128]{5,4,2,1,0,3:T(8,128)(2,1)} async-done(((bf16[1,1,1,32,128,128]{5,4,2,1,0,3:T(8,128)(2,1)}), bf16[1,1,1,256,128,128]{5,4,2,1,0,3:T(8,128)(2,1)}) %all-gather.6.cloned.1.call-update) | async-done | bytes 8388624 | tf_op jit(solution)/shard_map/all_gather | solution.py:95
  130.0 10.3 %shard_map.55 = f32[64,128,128]{2,1,0:T(8,128)S(1)} custom-call(s32[512]{0:T(512)S(1)} %reshape.374.moff_ref, s32[64]{0:T(128)S(1)} %add.199.oidx_ref, bf16[32768,128]{1,0:T(8,128)(2,1)} %bitcast.63, bf16[16384,128]{1,0:T(8,128)(2,1)} %bitcast.62), custom_call_target="tpu_custom_call" | custom-call | flops 2147483648 | bytes 16777216 | tf_op jit(solution)/shard_map/pallas_call | solution.py:41
  140.3 1.9 copy-done
  142.2 44.6 %reduce-scatter.2.cloned.1.call-done = f32[16,128,128]{2,1,0:T(8,128)} async-done(((f32[64,128,128]{2,1,0:T(8,128)}), f32[16,128,128]{2,1,0:T(8,128)}) %reduce-scatter.2.cloned.1.call-update) | async-done | bytes 1048592 | tf_op jit(solution)/shard_map/reduce_scatter | solution.py:144
  186.9 1.3 multiply_reduce_fusion
  188.3 1.6 collective-permute-start.4
  190.2 1.9 collective-permute-done.4
  192.0 1.0 collective-permute-done.5
  193.3 3.4 %collective-permute-done.6 = f32[16,128]{1,0:T(8,128)S(1)} collective-permute-done((f32[16,128]{1,0:T(8,128)S(1)}, f32[16,128]{1,0:T(8,128)S(1)}, u32[]{:S(2)}, u32[]{:S(2)}) %collective-permute-start.6) | collective-permute-done | bytes 8224 | tf_op jit(solution)/shard_map/ppermute | solution.py:65
  196.7 0.8 collective-permute-start.7
  198.1 3.4 %collective-permute-done.7 = f32[16,128]{1,0:T(8,128)S(1)} collective-permute-done((f32[16,128]{1,0:T(8,128)S(1)}, f32[16,128]{1,0:T(8,128)S(1)}, u32[]{:S(2)}, u32[]{:S(2)}) %collective-permute-start.7) | collective-permute-done | bytes 8224 | tf_op jit(solution)/shard_map/ppermute | solution.py:65
  202.1 1.1 bitcast_multiply_fusion
  (77 shorter events, 6.9 us)
Async XLA Ops:
  6.5 123.4 %all-gather.6.cloned.1.call-start = ((), (), s32[]{:S(2)}) async-start(), calls=%async_computation.2 | async-start | bytes 9437184 | tf_op jit(solution)/shard_map/all_gather | solution.py:95
  7.3 179.6 %reduce-scatter.2.cloned.1.call-start = ((), (), s32[]{:S(2)}) async-start(), calls=%async_computation.1 | async-start | bytes 5242880 | tf_op jit(solution)/shard_map/reduce_scatter | solution.py:144
  7.3 79.8 %collective-permute-start.1 = (bf16[32,128,128]{2,1,0:T(8,128)(2,1)}, bf16[32,128,128]{2,1,0:T(8,128)(2,1)S(1)}, u32[]{:S(2)}, u32[]{:S(2)}) collective-permute-start(bf16[32,128,128]{2,1,0:T(8,128)(2,1)} %bitcast.66), channel_id=1, source_target_pairs={{0,64},{32,96},{64,0},{96,32},{1,65},{33,97},{65,1},{97,33},{2,66}... | collective-permute-start | bytes 3145736 | tf_op jit(solution)/shard_map/ppermute | solution.py:89
  9.4 81.4 %collective-permute-start = (bf16[32,128,128]{2,1,0:T(8,128)(2,1)}, bf16[32,128,128]{2,1,0:T(8,128)(2,1)S(1)}, u32[]{:S(2)}, u32[]{:S(2)}) collective-permute-start(bf16[32,128,128]{2,1,0:T(8,128)(2,1)} %bitcast.67), channel_id=1, source_target_pairs={{0,32},{32,0},{64,96},{96,64},{1,33},{33,1},{65,97},{97,65},{2,34}... | collective-permute-start | bytes 3145736 | tf_op jit(solution)/shard_map/ppermute | solution.py:90
  44.0 1.9 copy-start.3
  44.0 13.5 %copy-start.2 = (s32[1,1,1,32,2]{3,4,2,1,0:T(2,128)S(1)}, s32[1,1,1,32,2]{3,4,2,1,0:T(2,128)}, u32[]{:S(2)}) copy-start(s32[1,1,1,32,2]{3,4,2,1,0:T(2,128)} %param.6) | copy-start | bytes 772
  87.1 3.7 %collective-permute-start.2 = (bf16[32,128,128]{2,1,0:T(8,128)(2,1)S(1)}, bf16[32,128,128]{2,1,0:T(8,128)(2,1)}, u32[]{:S(2)}, u32[]{:S(2)}) collective-permute-start(bf16[32,128,128]{2,1,0:T(8,128)(2,1)S(1)} %collective-permute-done.1), channel_id=1, source_target_pairs={{0,32},{32,0},{64,96},{96,64},{1,33},{33,1},{65,97},{97,65},{2,34}... | collective-permute-start | bytes 3145736 | tf_op jit(solution)/shard_map/ppermute | solution.py:91
  87.4 3.5 %copy-start.1 = (bf16[1,1,1,32,128,128]{5,4,3,2,1,0:T(8,128)(2,1)S(1)}, bf16[1,1,1,32,128,128]{5,4,3,2,1,0:T(8,128)(2,1)}, u32[]{:S(2)}) copy-start(bf16[1,1,1,32,128,128]{5,4,3,2,1,0:T(8,128)(2,1)} %param.7) | copy-start | bytes 3145732
  140.3 1.9 copy-start
  188.2 2.0 collective-permute-start.3
  188.3 3.7 %collective-permute-start.4 = (f32[16,128]{1,0:T(8,128)S(1)}, f32[16,128]{1,0:T(8,128)S(1)}, u32[]{:S(2)}, u32[]{:S(2)}) collective-permute-start(f32[16,128]{1,0:T(8,128)S(1)} %get-tuple-element.13), channel_id=1, source_target_pairs={{0,64},{32,96},{64,0},{96,32},{1,65},{33,97},{65,1},{97,33},{2,66}... | collective-permute-start | bytes 24584 | tf_op jit(solution)/shard_map/ppermute | solution.py:149
  189.9 3.1 %collective-permute-start.5 = (f32[16,128]{1,0:T(8,128)S(1)}, f32[16,128]{1,0:T(8,128)S(1)}, u32[]{:S(2)}, u32[]{:S(2)}) collective-permute-start(f32[16,128]{1,0:T(8,128)S(1)} %get-tuple-element.13), channel_id=1, source_target_pairs={{0,96},{32,64},{64,32},{96,0},{1,97},{33,65},{65,33},{97,1},{2,98}... | collective-permute-start | bytes 24584 | tf_op jit(solution)/shard_map/ppermute | solution.py:149
  193.0 3.7 %collective-permute-start.6 = (f32[16,128]{1,0:T(8,128)S(1)}, f32[16,128]{1,0:T(8,128)S(1)}, u32[]{:S(2)}, u32[]{:S(2)}) collective-permute-start(f32[16,128]{1,0:T(8,128)S(1)} %add_add_fusion), channel_id=1, source_target_pairs={{0,1},{1,0},{2,3},{3,2},{4,5},{5,4},{6,7},{7,6},{8,9},{9,8},{10,11... | collective-permute-start | bytes 24584 | tf_op jit(solution)/shard_map/ppermute | solution.py:65
  196.7 4.9 %collective-permute-start.7 = (f32[16,128]{1,0:T(8,128)S(1)}, f32[16,128]{1,0:T(8,128)S(1)}, u32[]{:S(2)}, u32[]{:S(2)}) collective-permute-start(f32[16,128]{1,0:T(8,128)S(1)} %add.208), channel_id=1, source_target_pairs={{0,3},{1,2},{2,1},{3,0},{4,7},{5,6},{6,5},{7,4},{8,11},{9,10},{10,... | collective-permute-start | bytes 24584 | tf_op jit(solution)/shard_map/ppermute | solution.py:65
Sparse Core Ops, SparseCore 0:
  9.7 120.2 all-gather.5
  142.3 44.4 reduce-scatter.1

commit v18 on v17

--- a/solution.py
+++ b/solution.py
@@ -60,10 +60,9 @@
     )(moff, oidx, flow_flat, graph_flat)
 
 
-def butterfly_sum(x, axis, n, masks):
-    for d in masks:
-        x = x + lax.ppermute(x, axis, [(i, i ^ d) for i in range(n)])
-    return x
+def round_sum(x, axis, n):
+    parts = [lax.ppermute(x, axis, [(i, i ^ d) for i in range(n)]) for d in range(1, n)]
+    return x + sum(parts[1:], parts[0])
 
 
 def first_two(mask):
@@ -146,9 +145,7 @@
     kept_cols = out_coords[0, 0, 0, :, 1]
     squared = kept_tiles * kept_tiles
     local_mass = jnp.sum(squared, axis=1)
-    row_parts = [lax.ppermute(local_mass, "row", [(i, i ^ d) for i in range(row_count)]) for d in range(1, row_count)]
-    row_total = local_mass + sum(row_parts[1:], row_parts[0])
-    column_total = butterfly_sum(row_total, "layer", layer_count, (1, 3))
+    column_total = round_sum(round_sum(local_mass, "row", row_count), "layer", layer_count)
     factor = jnp.float32(row_count * layer_count * tile) / column_total
     flow = squared[kept_cols] * factor[kept_cols][:, None, :]
     return flow.reshape(1, 1, 1, col_tiles, tile, tile)

time: 210 us -> 209 us (level)
  waiting for transfers between devices: 85.6 us -> 80.6 us
  starting transfers between devices: 5.27 us -> 8.85 us
    ppermute x5 -> x6, waiting for transfers between devices: 9.59 us -> 4.66 us  [round_sum(): lax.ppermute(x, axis, [(i, i ^ d) for i in range(n)])]
    ppermute x5 -> x6, starting transfers between devices: 3.06 us -> 6.65 us  [round_sum(): lax.ppermute(x, axis, [(i, i ^ d) for i in range(n)])]
  transfers between devices with their start and end apart: 10 -> 11, of which waited for: 6 -> 6; matrix products, arithmetic and copies ran while one was open for 11% -> 11% of each run, Pallas kernels for 0% -> 0%
where the time goes in v18:
time: 209 us
  waiting for transfers between devices  80.6 us (39%)
  blocking collectives  67.4 us (32%)
  local copies, waits for them, and re-layouts  16.5 us (8%)
  between operations  13.7 us (7%)
  other arithmetic  11.3 us (5%)
  Pallas kernels  10.3 us (5%)
  starting transfers between devices  8.85 us (4%)
    reduce_scatter x1, waiting for transfers between devices, local(): lax.psum_scatter(partial_sum, 'layer', scatter_dimension=0, tiled=True)  44.6 us
    all_gather x1, blocking collectives, local(): lax.all_gather(b_coords[0, 0, 0][None], 'row', axis=0, tiled=True)  32.2 us
    all_gather x1, waiting for transfers between devices, local(): flow_tiles = lax.all_gather(a_tiles[0, 0, 0], 'col', axis=0, tiled=True)  30.6 us
    all_gather x1, blocking collectives, local(): lax.all_gather(a_coords[0, 0, 0][None], 'col', axis=0, tiled=True)  25.6 us
    pallas_call x1, Pallas kernels, kept_partials(): pl.pallas_call(kernel, out_shape=jax.ShapeDtypeStruct((n_out, tile, tile)...  10.3 us
    all_gather x1, blocking collectives, local(): lax.all_gather(out_coords[0, 0, 0][None], 'layer', axis=0, tiled=True)  9.61 us
    ppermute x6, starting transfers between devices, round_sum(): lax.ppermute(x, axis, [(i, i ^ d) for i in range(n)])  6.65 us
    gather x1, local copies, waits for them, and re-layouts, local(): graph_flat = graph_tiles[g_tile.reshape(-1)].reshape(-1, tile)  5.23 us
  transfers between devices with their start and end apart: 11, of which 6 were waited for; matrix products, arithmetic and copies ran while one was open for 11% of the time, Pallas kernels for 0%

profile of v18, /device:TPU:0, one launch (start us, length us, event | category | flops | bytes accessed | tf_op | source)
XLA Modules:
  0.0 208.7 jit_solution(10143421124483406588)
XLA Ops:
  7.3 2.1 collective-permute-start.1
  9.4 32.2 %all-gather.1 = s32[4,1,1,32,2]{3,4,2,1,0:T(2,128)S(1)} all-gather(s32[1,1,1,32,2]{3,4,2,1,0:T(2,128)} %param.8), channel_id=3, replica_groups=mesh['row'=4,'col'=8,'layer'=4] {'row'}, dimensions={0}, use_global_device_ids=true | all-gather | bytes 1280 | tf_op jit(solution)/shard_map/all_gather | solution.py:93
  42.3 0.7 iota_reduce_fusion.2
  44.0 1.5 gather_fusion.6
  45.9 9.6 %all-gather.2 = s32[4,1,1,16,2]{3,4,2,1,0:T(2,128)S(1)} all-gather(s32[1,1,1,16,2]{3,4,2,1,0:T(2,128)S(1)} %copy-done.3), channel_id=4, replica_groups=mesh['row'=4,'col'=8,'layer'=4] {'layer'}, dimensions={0}, use_global_device_ids=true | all-gather | bytes 640 | tf_op jit(solution)/shard_map/all_gather | solution.py:96
  55.5 0.7 iota_reduce_fusion.1
  56.4 0.9 gather_fusion.7
  57.6 25.6 %all-gather = s32[8,1,1,32,2]{3,4,2,1,0:T(2,128)S(1)} all-gather(s32[1,1,1,32,2]{3,4,2,1,0:T(2,128)S(1)} %copy-done.2), channel_id=2, replica_groups=mesh['row'=4,'col'=8,'layer'=4] {'col'}, dimensions={0}, use_global_device_ids=true | all-gather | bytes 2304 | tf_op jit(solution)/shard_map/all_gather | solution.py:95
  83.9 3.0 %iota_reduce_fusion = (pred[16,4,8]{2,1,0:T(4,128)(4,1)}, s32[16,4,8]{2,1,0:T(4,128)S(1)}) fusion(s32[16,4]{1,0:T(8,128)S(1)} %copy.56, s32[16,8,32]{2,1,0:T(8,128)S(1)} %bitcast.69), kind=kLoop, calls=%fused_computation.10 | loop fusion | flops 127488 | bytes 19200 | tf_op jit(solution)/shard_map/local/reduce | solution.py:126
  87.4 2.6 %gather_fusion.2 = s32[512]{0:T(512)S(1)} fusion(s32[8,32]{1,0:T(8,128)S(1)} %get-tuple-element.15, s32[512]{0:T(512)S(1)} %reshape.393), kind=kCustom, calls=%fused_computation.2 | custom fusion | bytes 8192 | tf_op jit(solution)/shard_map/gather | solution.py:129
  90.8 3.3 %pad_maximum_fusion = bf16[128,128,128]{2,1,0:T(8,128)(2,1)} fusion(bf16[32,128,128]{2,1,0:T(8,128)(2,1)} %collective-permute-done.2, bf16[32,128,128]{2,1,0:T(8,128)(2,1)S(1)} %collective-permute-done.1, bf16[32,128,128]{2,1,0:T(8,128)(2,1)S(1)} %collective-permute-done, bf16[32,128,128]{2,1,0:T(8,128)(2,1)S(1)} %bitcast.68), kind=kLoop, calls=%fused_computation.8 | loop fusion | flops 6291456 | bytes 8388608 | tf_op jit(solution)/shard_map/concatenate | solution.py:92
  94.2 5.2 %gather_fusion.3 = bf16[128,128,128]{2,1,0:T(8,128)(2,1)} fusion(bf16[128,128,128]{2,1,0:T(8,128)(2,1)} %pad_maximum_fusion, s32[1024]{0:T(1024)S(1)} %pad_clamp_fusion.1), kind=kCustom, calls=%fused_computation.3 | custom fusion | bytes 8389120 | tf_op jit(solution)/shard_map/gather | solution.py:133
  99.4 30.6 %all-gather.6.cloned.1.call-done = bf16[1,1,1,256,128,128]{5,4,2,1,0,3:T(8,128)(2,1)} async-done(((bf16[1,1,1,32,128,128]{5,4,2,1,0,3:T(8,128)(2,1)}), bf16[1,1,1,256,128,128]{5,4,2,1,0,3:T(8,128)(2,1)}) %all-gather.6.cloned.1.call-update) | async-done | bytes 8388624 | tf_op jit(solution)/shard_map/all_gather | solution.py:94
  130.0 10.3 %shard_map.55 = f32[64,128,128]{2,1,0:T(8,128)S(1)} custom-call(s32[512]{0:T(512)S(1)} %reshape.374.moff_ref, s32[64]{0:T(128)S(1)} %add.202.oidx_ref, bf16[32768,128]{1,0:T(8,128)(2,1)} %bitcast.63, bf16[16384,128]{1,0:T(8,128)(2,1)} %bitcast.62), custom_call_target="tpu_custom_call" | custom-call | flops 2147483648 | bytes 16777216 | tf_op jit(solution)/shard_map/pallas_call | solution.py:41
  140.3 1.9 copy-done
  142.2 44.6 %reduce-scatter.2.cloned.1.call-done = f32[16,128,128]{2,1,0:T(8,128)} async-done(((f32[64,128,128]{2,1,0:T(8,128)}), f32[16,128,128]{2,1,0:T(8,128)}) %reduce-scatter.2.cloned.1.call-update) | async-done | bytes 1048592 | tf_op jit(solution)/shard_map/reduce_scatter | solution.py:143
  186.9 1.3 multiply_reduce_fusion
  188.3 1.6 collective-permute-start.4
  190.2 1.9 collective-permute-done.4
  192.0 1.0 collective-permute-done.5
  193.3 2.1 collective-permute-start.7
  195.3 2.4 %collective-permute-start.8 = (f32[16,128]{1,0:T(8,128)S(1)}, f32[16,128]{1,0:T(8,128)S(1)}, u32[]{:S(2)}, u32[]{:S(2)}) collective-permute-start(f32[16,128]{1,0:T(8,128)S(1)} %add_add_fusion), channel_id=1, source_target_pairs={{0,3},{1,2},{2,1},{3,0},{4,7},{5,6},{6,5},{7,4},{8,11},{9,10},{10,... | collective-permute-start | bytes 24584 | tf_op jit(solution)/shard_map/ppermute | solution.py:64
  198.4 1.8 collective-permute-done.8
  200.8 1.1 bitcast_multiply_fusion
  (78 shorter events, 6.9 us)
Async XLA Ops:
  6.5 123.4 %all-gather.6.cloned.1.call-start = ((), (), s32[]{:S(2)}) async-start(), calls=%async_computation.2 | async-start | bytes 9437184 | tf_op jit(solution)/shard_map/all_gather | solution.py:94
  7.3 179.6 %reduce-scatter.2.cloned.1.call-start = ((), (), s32[]{:S(2)}) async-start(), calls=%async_computation.1 | async-start | bytes 5242880 | tf_op jit(solution)/shard_map/reduce_scatter | solution.py:143
  7.3 79.8 %collective-permute-start.1 = (bf16[32,128,128]{2,1,0:T(8,128)(2,1)}, bf16[32,128,128]{2,1,0:T(8,128)(2,1)S(1)}, u32[]{:S(2)}, u32[]{:S(2)}) collective-permute-start(bf16[32,128,128]{2,1,0:T(8,128)(2,1)} %bitcast.66), channel_id=1, source_target_pairs={{0,64},{32,96},{64,0},{96,32},{1,65},{33,97},{65,1},{97,33},{2,66}... | collective-permute-start | bytes 3145736 | tf_op jit(solution)/shard_map/ppermute | solution.py:88
  9.4 81.4 %collective-permute-start = (bf16[32,128,128]{2,1,0:T(8,128)(2,1)}, bf16[32,128,128]{2,1,0:T(8,128)(2,1)S(1)}, u32[]{:S(2)}, u32[]{:S(2)}) collective-permute-start(bf16[32,128,128]{2,1,0:T(8,128)(2,1)} %bitcast.67), channel_id=1, source_target_pairs={{0,32},{32,0},{64,96},{96,64},{1,33},{33,1},{65,97},{97,65},{2,34}... | collective-permute-start | bytes 3145736 | tf_op jit(solution)/shard_map/ppermute | solution.py:89
  44.0 1.9 copy-start.3
  44.0 13.5 %copy-start.2 = (s32[1,1,1,32,2]{3,4,2,1,0:T(2,128)S(1)}, s32[1,1,1,32,2]{3,4,2,1,0:T(2,128)}, u32[]{:S(2)}) copy-start(s32[1,1,1,32,2]{3,4,2,1,0:T(2,128)} %param.6) | copy-start | bytes 772
  87.1 3.7 %collective-permute-start.2 = (bf16[32,128,128]{2,1,0:T(8,128)(2,1)S(1)}, bf16[32,128,128]{2,1,0:T(8,128)(2,1)}, u32[]{:S(2)}, u32[]{:S(2)}) collective-permute-start(bf16[32,128,128]{2,1,0:T(8,128)(2,1)S(1)} %collective-permute-done.1), channel_id=1, source_target_pairs={{0,32},{32,0},{64,96},{96,64},{1,33},{33,1},{65,97},{97,65},{2,34}... | collective-permute-start | bytes 3145736 | tf_op jit(solution)/shard_map/ppermute | solution.py:90
  87.4 3.5 %copy-start.1 = (bf16[1,1,1,32,128,128]{5,4,3,2,1,0:T(8,128)(2,1)S(1)}, bf16[1,1,1,32,128,128]{5,4,3,2,1,0:T(8,128)(2,1)}, u32[]{:S(2)}) copy-start(bf16[1,1,1,32,128,128]{5,4,3,2,1,0:T(8,128)(2,1)} %param.7) | copy-start | bytes 3145732
  140.3 1.9 copy-start
  188.2 2.0 collective-permute-start.3
  188.3 3.7 %collective-permute-start.4 = (f32[16,128]{1,0:T(8,128)S(1)}, f32[16,128]{1,0:T(8,128)S(1)}, u32[]{:S(2)}, u32[]{:S(2)}) collective-permute-start(f32[16,128]{1,0:T(8,128)S(1)} %get-tuple-element.13), channel_id=1, source_target_pairs={{0,64},{32,96},{64,0},{96,32},{1,65},{33,97},{65,1},{97,33},{2,66}... | collective-permute-start | bytes 24584 | tf_op jit(solution)/shard_map/ppermute | solution.py:64
  189.9 3.1 %collective-permute-start.5 = (f32[16,128]{1,0:T(8,128)S(1)}, f32[16,128]{1,0:T(8,128)S(1)}, u32[]{:S(2)}, u32[]{:S(2)}) collective-permute-start(f32[16,128]{1,0:T(8,128)S(1)} %get-tuple-element.13), channel_id=1, source_target_pairs={{0,96},{32,64},{64,32},{96,0},{1,97},{33,65},{65,33},{97,1},{2,98}... | collective-permute-start | bytes 24584 | tf_op jit(solution)/shard_map/ppermute | solution.py:64
  193.0 5.3 %collective-permute-start.6 = (f32[16,128]{1,0:T(8,128)S(1)}, f32[16,128]{1,0:T(8,128)S(1)}, u32[]{:S(2)}, u32[]{:S(2)}) collective-permute-start(f32[16,128]{1,0:T(8,128)S(1)} %add_add_fusion), channel_id=1, source_target_pairs={{0,1},{1,0},{2,3},{3,2},{4,5},{5,4},{6,7},{7,6},{8,9},{9,8},{10,11... | collective-permute-start | bytes 24584 | tf_op jit(solution)/shard_map/ppermute | solution.py:64
  193.3 5.2 %collective-permute-start.7 = (f32[16,128]{1,0:T(8,128)S(1)}, f32[16,128]{1,0:T(8,128)S(1)}, u32[]{:S(2)}, u32[]{:S(2)}) collective-permute-start(f32[16,128]{1,0:T(8,128)S(1)} %add_add_fusion), channel_id=1, source_target_pairs={{0,2},{1,3},{2,0},{3,1},{4,6},{5,7},{6,4},{7,5},{8,10},{9,11},{10,... | collective-permute-start | bytes 24584 | tf_op jit(solution)/shard_map/ppermute | solution.py:64
  195.3 4.9 %collective-permute-start.8 = (f32[16,128]{1,0:T(8,128)S(1)}, f32[16,128]{1,0:T(8,128)S(1)}, u32[]{:S(2)}, u32[]{:S(2)}) collective-permute-start(f32[16,128]{1,0:T(8,128)S(1)} %add_add_fusion), channel_id=1, source_target_pairs={{0,3},{1,2},{2,1},{3,0},{4,7},{5,6},{6,5},{7,4},{8,11},{9,10},{10,... | collective-permute-start | bytes 24584 | tf_op jit(solution)/shard_map/ppermute | solution.py:64
Sparse Core Ops, SparseCore 0:
  9.7 120.2 all-gather.5
  142.3 44.4 reduce-scatter.1

commit v19 on v18

--- a/solution.py
+++ b/solution.py
@@ -8,7 +8,7 @@
 from jax.sharding import PartitionSpec as P
 
 KA = 4
-N_SLOT = 4
+N_SLOT = 8
 
 
 def column_kernel(moff_ref, oidx_ref, flow_ref, graph_ref, out_ref, lhs_ref, *, n_q, n_g):

time: 209 us -> 209 us (level)
  no operation moved by 1% of the time
where the time goes in v19:
time: 209 us; the launch traced here: 208 us
  waiting for transfers between devices  80.6 us (39%)
  blocking collectives  67.4 us (32%)
  local copies, waits for them, and re-layouts  16.5 us (8%)
  between operations  13.7 us (7%)
  other arithmetic  11.3 us (5%)
  Pallas kernels  9.96 us (5%)
  starting transfers between devices  8.85 us (4%)
    reduce_scatter x1, waiting for transfers between devices, local(): lax.psum_scatter(partial_sum, 'layer', scatter_dimension=0, tiled=True)  44.6 us
    all_gather x1, blocking collectives, local(): lax.all_gather(b_coords[0, 0, 0][None], 'row', axis=0, tiled=True)  32.2 us
    all_gather x1, waiting for transfers between devices, local(): flow_tiles = lax.all_gather(a_tiles[0, 0, 0], 'col', axis=0, tiled=True)  30.6 us
    all_gather x1, blocking collectives, local(): lax.all_gather(a_coords[0, 0, 0][None], 'col', axis=0, tiled=True)  25.6 us
    pallas_call x1, Pallas kernels, kept_partials(): pl.pallas_call(kernel, out_shape=jax.ShapeDtypeStruct((n_out, tile, tile)...  9.96 us
    all_gather x1, blocking collectives, local(): lax.all_gather(out_coords[0, 0, 0][None], 'layer', axis=0, tiled=True)  9.61 us
    ppermute x6, starting transfers between devices, round_sum(): lax.ppermute(x, axis, [(i, i ^ d) for i in range(n)])  6.65 us
    gather x1, local copies, waits for them, and re-layouts, local(): graph_flat = graph_tiles[g_tile.reshape(-1)].reshape(-1, tile)  5.23 us
  transfers between devices with their start and end apart: 11, of which 6 were waited for; matrix products, arithmetic and copies ran while one was open for 11% of the time, Pallas kernels for 0%

profile of v19, /device:TPU:0, one launch (start us, length us, event | category | flops | bytes accessed | tf_op | source)
XLA Modules:
  0.0 208.3 jit_solution(7499995454459382820)
XLA Ops:
  7.3 2.1 collective-permute-start.1
  9.4 32.2 %all-gather.1 = s32[4,1,1,32,2]{3,4,2,1,0:T(2,128)S(1)} all-gather(s32[1,1,1,32,2]{3,4,2,1,0:T(2,128)} %param.8), channel_id=3, replica_groups=mesh['row'=4,'col'=8,'layer'=4] {'row'}, dimensions={0}, use_global_device_ids=true | all-gather | bytes 1280 | tf_op jit(solution)/shard_map/all_gather | solution.py:93
  42.3 0.7 iota_reduce_fusion.2
  44.0 1.5 gather_fusion.6
  45.9 9.6 %all-gather.2 = s32[4,1,1,16,2]{3,4,2,1,0:T(2,128)S(1)} all-gather(s32[1,1,1,16,2]{3,4,2,1,0:T(2,128)S(1)} %copy-done.3), channel_id=4, replica_groups=mesh['row'=4,'col'=8,'layer'=4] {'layer'}, dimensions={0}, use_global_device_ids=true | all-gather | bytes 640 | tf_op jit(solution)/shard_map/all_gather | solution.py:96
  55.5 0.7 iota_reduce_fusion.1
  56.4 0.9 gather_fusion.7
  57.6 25.6 %all-gather = s32[8,1,1,32,2]{3,4,2,1,0:T(2,128)S(1)} all-gather(s32[1,1,1,32,2]{3,4,2,1,0:T(2,128)S(1)} %copy-done.2), channel_id=2, replica_groups=mesh['row'=4,'col'=8,'layer'=4] {'col'}, dimensions={0}, use_global_device_ids=true | all-gather | bytes 2304 | tf_op jit(solution)/shard_map/all_gather | solution.py:95
  83.9 3.0 %iota_reduce_fusion = (pred[16,4,8]{2,1,0:T(4,128)(4,1)}, s32[16,4,8]{2,1,0:T(4,128)S(1)}) fusion(s32[16,4]{1,0:T(8,128)S(1)} %copy.56, s32[16,8,32]{2,1,0:T(8,128)S(1)} %bitcast.69), kind=kLoop, calls=%fused_computation.10 | loop fusion | flops 127488 | bytes 19200 | tf_op jit(solution)/shard_map/local/reduce | solution.py:126
  87.4 2.6 %gather_fusion.2 = s32[512]{0:T(512)S(1)} fusion(s32[8,32]{1,0:T(8,128)S(1)} %get-tuple-element.15, s32[512]{0:T(512)S(1)} %reshape.393), kind=kCustom, calls=%fused_computation.2 | custom fusion | bytes 8192 | tf_op jit(solution)/shard_map/gather | solution.py:129
  90.8 3.3 %pad_maximum_fusion = bf16[128,128,128]{2,1,0:T(8,128)(2,1)} fusion(bf16[32,128,128]{2,1,0:T(8,128)(2,1)} %collective-permute-done.2, bf16[32,128,128]{2,1,0:T(8,128)(2,1)S(1)} %collective-permute-done.1, bf16[32,128,128]{2,1,0:T(8,128)(2,1)S(1)} %collective-permute-done, bf16[32,128,128]{2,1,0:T(8,128)(2,1)S(1)} %bitcast.68), kind=kLoop, calls=%fused_computation.8 | loop fusion | flops 6291456 | bytes 8388608 | tf_op jit(solution)/shard_map/concatenate | solution.py:92
  94.2 5.2 %gather_fusion.3 = bf16[128,128,128]{2,1,0:T(8,128)(2,1)} fusion(bf16[128,128,128]{2,1,0:T(8,128)(2,1)} %pad_maximum_fusion, s32[1024]{0:T(1024)S(1)} %pad_clamp_fusion.1), kind=kCustom, calls=%fused_computation.3 | custom fusion | bytes 8389120 | tf_op jit(solution)/shard_map/gather | solution.py:133
  99.4 30.6 %all-gather.6.cloned.1.call-done = bf16[1,1,1,256,128,128]{5,4,2,1,0,3:T(8,128)(2,1)} async-done(((bf16[1,1,1,32,128,128]{5,4,2,1,0,3:T(8,128)(2,1)}), bf16[1,1,1,256,128,128]{5,4,2,1,0,3:T(8,128)(2,1)}) %all-gather.6.cloned.1.call-update) | async-done | bytes 8388624 | tf_op jit(solution)/shard_map/all_gather | solution.py:94
  130.0 10.0 %shard_map.55 = f32[64,128,128]{2,1,0:T(8,128)S(1)} custom-call(s32[512]{0:T(512)S(1)} %reshape.374.moff_ref, s32[64]{0:T(128)S(1)} %add.202.oidx_ref, bf16[32768,128]{1,0:T(8,128)(2,1)} %bitcast.63, bf16[16384,128]{1,0:T(8,128)(2,1)} %bitcast.62), custom_call_target="tpu_custom_call" | custom-call | flops 2147483648 | bytes 16777216 | tf_op jit(solution)/shard_map/pallas_call | solution.py:41
  140.0 1.9 copy-done
  141.9 44.6 %reduce-scatter.2.cloned.1.call-done = f32[16,128,128]{2,1,0:T(8,128)} async-done(((f32[64,128,128]{2,1,0:T(8,128)}), f32[16,128,128]{2,1,0:T(8,128)}) %reduce-scatter.2.cloned.1.call-update) | async-done | bytes 1048592 | tf_op jit(solution)/shard_map/reduce_scatter | solution.py:143
  186.5 1.3 multiply_reduce_fusion
  188.0 1.6 collective-permute-start.4
  189.9 1.9 collective-permute-done.4
  191.7 1.0 collective-permute-done.5
  192.9 2.0 collective-permute-start.7
  195.0 2.4 %collective-permute-start.8 = (f32[16,128]{1,0:T(8,128)S(1)}, f32[16,128]{1,0:T(8,128)S(1)}, u32[]{:S(2)}, u32[]{:S(2)}) collective-permute-start(f32[16,128]{1,0:T(8,128)S(1)} %add_add_fusion), channel_id=1, source_target_pairs={{0,3},{1,2},{2,1},{3,0},{4,7},{5,6},{6,5},{7,4},{8,11},{9,10},{10,... | collective-permute-start | bytes 24584 | tf_op jit(solution)/shard_map/ppermute | solution.py:64
  198.1 1.8 collective-permute-done.8
  200.4 1.1 bitcast_multiply_fusion
  (78 shorter events, 6.9 us)
Async XLA Ops:
  6.5 123.4 %all-gather.6.cloned.1.call-start = ((), (), s32[]{:S(2)}) async-start(), calls=%async_computation.2 | async-start | bytes 9437184 | tf_op jit(solution)/shard_map/all_gather | solution.py:94
  7.3 179.3 %reduce-scatter.2.cloned.1.call-start = ((), (), s32[]{:S(2)}) async-start(), calls=%async_computation.1 | async-start | bytes 5242880 | tf_op jit(solution)/shard_map/reduce_scatter | solution.py:143
  7.3 79.8 %collective-permute-start.1 = (bf16[32,128,128]{2,1,0:T(8,128)(2,1)}, bf16[32,128,128]{2,1,0:T(8,128)(2,1)S(1)}, u32[]{:S(2)}, u32[]{:S(2)}) collective-permute-start(bf16[32,128,128]{2,1,0:T(8,128)(2,1)} %bitcast.66), channel_id=1, source_target_pairs={{0,64},{32,96},{64,0},{96,32},{1,65},{33,97},{65,1},{97,33},{2,66}... | collective-permute-start | bytes 3145736 | tf_op jit(solution)/shard_map/ppermute | solution.py:88
  9.4 81.4 %collective-permute-start = (bf16[32,128,128]{2,1,0:T(8,128)(2,1)}, bf16[32,128,128]{2,1,0:T(8,128)(2,1)S(1)}, u32[]{:S(2)}, u32[]{:S(2)}) collective-permute-start(bf16[32,128,128]{2,1,0:T(8,128)(2,1)} %bitcast.67), channel_id=1, source_target_pairs={{0,32},{32,0},{64,96},{96,64},{1,33},{33,1},{65,97},{97,65},{2,34}... | collective-permute-start | bytes 3145736 | tf_op jit(solution)/shard_map/ppermute | solution.py:89
  44.0 1.9 copy-start.3
  44.0 13.5 %copy-start.2 = (s32[1,1,1,32,2]{3,4,2,1,0:T(2,128)S(1)}, s32[1,1,1,32,2]{3,4,2,1,0:T(2,128)}, u32[]{:S(2)}) copy-start(s32[1,1,1,32,2]{3,4,2,1,0:T(2,128)} %param.6) | copy-start | bytes 772
  87.1 3.7 %collective-permute-start.2 = (bf16[32,128,128]{2,1,0:T(8,128)(2,1)S(1)}, bf16[32,128,128]{2,1,0:T(8,128)(2,1)}, u32[]{:S(2)}, u32[]{:S(2)}) collective-permute-start(bf16[32,128,128]{2,1,0:T(8,128)(2,1)S(1)} %collective-permute-done.1), channel_id=1, source_target_pairs={{0,32},{32,0},{64,96},{96,64},{1,33},{33,1},{65,97},{97,65},{2,34}... | collective-permute-start | bytes 3145736 | tf_op jit(solution)/shard_map/ppermute | solution.py:90
  87.4 3.5 %copy-start.1 = (bf16[1,1,1,32,128,128]{5,4,3,2,1,0:T(8,128)(2,1)S(1)}, bf16[1,1,1,32,128,128]{5,4,3,2,1,0:T(8,128)(2,1)}, u32[]{:S(2)}) copy-start(bf16[1,1,1,32,128,128]{5,4,3,2,1,0:T(8,128)(2,1)} %param.7) | copy-start | bytes 3145732
  139.9 1.9 copy-start
  187.9 2.0 collective-permute-start.3
  188.0 3.7 %collective-permute-start.4 = (f32[16,128]{1,0:T(8,128)S(1)}, f32[16,128]{1,0:T(8,128)S(1)}, u32[]{:S(2)}, u32[]{:S(2)}) collective-permute-start(f32[16,128]{1,0:T(8,128)S(1)} %get-tuple-element.13), channel_id=1, source_target_pairs={{0,64},{32,96},{64,0},{96,32},{1,65},{33,97},{65,1},{97,33},{2,66}... | collective-permute-start | bytes 24584 | tf_op jit(solution)/shard_map/ppermute | solution.py:64
  189.6 3.1 %collective-permute-start.5 = (f32[16,128]{1,0:T(8,128)S(1)}, f32[16,128]{1,0:T(8,128)S(1)}, u32[]{:S(2)}, u32[]{:S(2)}) collective-permute-start(f32[16,128]{1,0:T(8,128)S(1)} %get-tuple-element.13), channel_id=1, source_target_pairs={{0,96},{32,64},{64,32},{96,0},{1,97},{33,65},{65,33},{97,1},{2,98}... | collective-permute-start | bytes 24584 | tf_op jit(solution)/shard_map/ppermute | solution.py:64
  192.7 5.3 %collective-permute-start.6 = (f32[16,128]{1,0:T(8,128)S(1)}, f32[16,128]{1,0:T(8,128)S(1)}, u32[]{:S(2)}, u32[]{:S(2)}) collective-permute-start(f32[16,128]{1,0:T(8,128)S(1)} %add_add_fusion), channel_id=1, source_target_pairs={{0,1},{1,0},{2,3},{3,2},{4,5},{5,4},{6,7},{7,6},{8,9},{9,8},{10,11... | collective-permute-start | bytes 24584 | tf_op jit(solution)/shard_map/ppermute | solution.py:64
  192.9 5.2 %collective-permute-start.7 = (f32[16,128]{1,0:T(8,128)S(1)}, f32[16,128]{1,0:T(8,128)S(1)}, u32[]{:S(2)}, u32[]{:S(2)}) collective-permute-start(f32[16,128]{1,0:T(8,128)S(1)} %add_add_fusion), channel_id=1, source_target_pairs={{0,2},{1,3},{2,0},{3,1},{4,6},{5,7},{6,4},{7,5},{8,10},{9,11},{10,... | collective-permute-start | bytes 24584 | tf_op jit(solution)/shard_map/ppermute | solution.py:64
  195.0 4.9 %collective-permute-start.8 = (f32[16,128]{1,0:T(8,128)S(1)}, f32[16,128]{1,0:T(8,128)S(1)}, u32[]{:S(2)}, u32[]{:S(2)}) collective-permute-start(f32[16,128]{1,0:T(8,128)S(1)} %add_add_fusion), channel_id=1, source_target_pairs={{0,3},{1,2},{2,1},{3,0},{4,7},{5,6},{6,5},{7,4},{8,11},{9,10},{10,... | collective-permute-start | bytes 24584 | tf_op jit(solution)/shard_map/ppermute | solution.py:64
Sparse Core Ops, SparseCore 0:
  9.7 120.2 all-gather.5
  142.0 44.4 reduce-scatter.1

commit v20 on v19

--- a/solution.py
+++ b/solution.py
@@ -8,7 +8,7 @@
 from jax.sharding import PartitionSpec as P
 
 KA = 4
-N_SLOT = 8
+N_SLOT = 16
 
 
 def column_kernel(moff_ref, oidx_ref, flow_ref, graph_ref, out_ref, lhs_ref, *, n_q, n_g):

time: 209 us -> 208 us (level)
  transfers between devices with their start and end apart: 11 -> 11, of which waited for: 6 -> 5; matrix products, arithmetic and copies ran while one was open for 11% -> 11% of each run, Pallas kernels for 0% -> 0%
where the time goes in v20:
time: 208 us
  waiting for transfers between devices  80.5 us (39%)
  blocking collectives  67.4 us (32%)
  local copies, waits for them, and re-layouts  16.5 us (8%)
  between operations  13.7 us (7%)
  other arithmetic  11.3 us (5%)
  Pallas kernels  9.72 us (5%)
  starting transfers between devices  9.03 us (4%)
    reduce_scatter x1, waiting for transfers between devices, local(): lax.psum_scatter(partial_sum, 'layer', scatter_dimension=0, tiled=True)  44.6 us
    all_gather x1, blocking collectives, local(): lax.all_gather(b_coords[0, 0, 0][None], 'row', axis=0, tiled=True)  32.2 us
    all_gather x1, waiting for transfers between devices, local(): flow_tiles = lax.all_gather(a_tiles[0, 0, 0], 'col', axis=0, tiled=True)  30.4 us
    all_gather x1, blocking collectives, local(): lax.all_gather(a_coords[0, 0, 0][None], 'col', axis=0, tiled=True)  25.6 us
    pallas_call x1, Pallas kernels, kept_partials(): pl.pallas_call(kernel, out_shape=jax.ShapeDtypeStruct((n_out, tile, tile)...  9.72 us
    all_gather x1, blocking collectives, local(): lax.all_gather(out_coords[0, 0, 0][None], 'layer', axis=0, tiled=True)  9.61 us
    ppermute x6, starting transfers between devices, round_sum(): lax.ppermute(x, axis, [(i, i ^ d) for i in range(n)])  6.65 us
    gather x1, local copies, waits for them, and re-layouts, local(): graph_flat = graph_tiles[g_tile.reshape(-1)].reshape(-1, tile)  5.23 us
  transfers between devices with their start and end apart: 11, of which 5 were waited for; matrix products, arithmetic and copies ran while one was open for 11% of the time, Pallas kernels for 0%

profile of v20, /device:TPU:0, one launch (start us, length us, event | category | flops | bytes accessed | tf_op | source)
XLA Modules:
  0.0 208.1 jit_solution(17989739291684801470)
XLA Ops:
  7.3 2.1 collective-permute-start.1
  9.4 32.2 %all-gather.1 = s32[4,1,1,32,2]{3,4,2,1,0:T(2,128)S(1)} all-gather(s32[1,1,1,32,2]{3,4,2,1,0:T(2,128)} %param.8), channel_id=3, replica_groups=mesh['row'=4,'col'=8,'layer'=4] {'row'}, dimensions={0}, use_global_device_ids=true | all-gather | bytes 1280 | tf_op jit(solution)/shard_map/all_gather | solution.py:93
  42.3 0.7 iota_reduce_fusion.2
  44.0 1.5 gather_fusion.6
  45.9 9.6 %all-gather.2 = s32[4,1,1,16,2]{3,4,2,1,0:T(2,128)S(1)} all-gather(s32[1,1,1,16,2]{3,4,2,1,0:T(2,128)S(1)} %copy-done.3), channel_id=4, replica_groups=mesh['row'=4,'col'=8,'layer'=4] {'layer'}, dimensions={0}, use_global_device_ids=true | all-gather | bytes 640 | tf_op jit(solution)/shard_map/all_gather | solution.py:96
  55.5 0.7 iota_reduce_fusion.1
  56.4 0.9 gather_fusion.7
  57.6 25.6 %all-gather = s32[8,1,1,32,2]{3,4,2,1,0:T(2,128)S(1)} all-gather(s32[1,1,1,32,2]{3,4,2,1,0:T(2,128)S(1)} %copy-done.2), channel_id=2, replica_groups=mesh['row'=4,'col'=8,'layer'=4] {'col'}, dimensions={0}, use_global_device_ids=true | all-gather | bytes 2304 | tf_op jit(solution)/shard_map/all_gather | solution.py:95
  83.9 3.0 %iota_reduce_fusion = (pred[16,4,8]{2,1,0:T(4,128)(4,1)}, s32[16,4,8]{2,1,0:T(4,128)S(1)}) fusion(s32[16,4]{1,0:T(8,128)S(1)} %copy.56, s32[16,8,32]{2,1,0:T(8,128)S(1)} %bitcast.69), kind=kLoop, calls=%fused_computation.10 | loop fusion | flops 127488 | bytes 19200 | tf_op jit(solution)/shard_map/local/reduce | solution.py:126
  87.6 2.6 %gather_fusion.2 = s32[512]{0:T(512)S(1)} fusion(s32[8,32]{1,0:T(8,128)S(1)} %get-tuple-element.15, s32[512]{0:T(512)S(1)} %reshape.393), kind=kCustom, calls=%fused_computation.2 | custom fusion | bytes 8192 | tf_op jit(solution)/shard_map/gather | solution.py:129
  91.0 3.3 %pad_maximum_fusion = bf16[128,128,128]{2,1,0:T(8,128)(2,1)} fusion(bf16[32,128,128]{2,1,0:T(8,128)(2,1)} %collective-permute-done.2, bf16[32,128,128]{2,1,0:T(8,128)(2,1)S(1)} %collective-permute-done.1, bf16[32,128,128]{2,1,0:T(8,128)(2,1)S(1)} %collective-permute-done, bf16[32,128,128]{2,1,0:T(8,128)(2,1)S(1)} %bitcast.68), kind=kLoop, calls=%fused_computation.8 | loop fusion | flops 6291456 | bytes 8388608 | tf_op jit(solution)/shard_map/concatenate | solution.py:92
  94.3 5.2 %gather_fusion.3 = bf16[128,128,128]{2,1,0:T(8,128)(2,1)} fusion(bf16[128,128,128]{2,1,0:T(8,128)(2,1)} %pad_maximum_fusion, s32[1024]{0:T(1024)S(1)} %pad_clamp_fusion.1), kind=kCustom, calls=%fused_computation.3 | custom fusion | bytes 8389120 | tf_op jit(solution)/shard_map/gather | solution.py:133
  99.6 30.4 %all-gather.6.cloned.1.call-done = bf16[1,1,1,256,128,128]{5,4,2,1,0,3:T(8,128)(2,1)} async-done(((bf16[1,1,1,32,128,128]{5,4,2,1,0,3:T(8,128)(2,1)}), bf16[1,1,1,256,128,128]{5,4,2,1,0,3:T(8,128)(2,1)}) %all-gather.6.cloned.1.call-update) | async-done | bytes 8388624 | tf_op jit(solution)/shard_map/all_gather | solution.py:94
  130.0 9.7 %shard_map.55 = f32[64,128,128]{2,1,0:T(8,128)S(1)} custom-call(s32[512]{0:T(512)S(1)} %reshape.374.moff_ref, s32[64]{0:T(128)S(1)} %add.202.oidx_ref, bf16[32768,128]{1,0:T(8,128)(2,1)} %bitcast.63, bf16[16384,128]{1,0:T(8,128)(2,1)} %bitcast.62), custom_call_target="tpu_custom_call" | custom-call | flops 2147483648 | bytes 16777216 | tf_op jit(solution)/shard_map/pallas_call | solution.py:41
  139.7 1.9 copy-done
  141.7 44.6 %reduce-scatter.2.cloned.1.call-done = f32[16,128,128]{2,1,0:T(8,128)} async-done(((f32[64,128,128]{2,1,0:T(8,128)}), f32[16,128,128]{2,1,0:T(8,128)}) %reduce-scatter.2.cloned.1.call-update) | async-done | bytes 1048592 | tf_op jit(solution)/shard_map/reduce_scatter | solution.py:143
  186.3 1.3 multiply_reduce_fusion
  187.7 1.6 collective-permute-start.4
  189.6 1.9 collective-permute-done.4
  191.5 1.0 collective-permute-done.5
  192.7 2.1 collective-permute-start.7
  194.8 2.4 %collective-permute-start.8 = (f32[16,128]{1,0:T(8,128)S(1)}, f32[16,128]{1,0:T(8,128)S(1)}, u32[]{:S(2)}, u32[]{:S(2)}) collective-permute-start(f32[16,128]{1,0:T(8,128)S(1)} %add_add_fusion), channel_id=1, source_target_pairs={{0,3},{1,2},{2,1},{3,0},{4,7},{5,6},{6,5},{7,4},{8,11},{9,10},{10,... | collective-permute-start | bytes 24584 | tf_op jit(solution)/shard_map/ppermute | solution.py:64
  197.8 1.8 collective-permute-done.8
  200.2 1.1 bitcast_multiply_fusion
  (78 shorter events, 7.0 us)
Async XLA Ops:
  6.5 123.4 %all-gather.6.cloned.1.call-start = ((), (), s32[]{:S(2)}) async-start(), calls=%async_computation.2 | async-start | bytes 9437184 | tf_op jit(solution)/shard_map/all_gather | solution.py:94
  7.3 179.0 %reduce-scatter.2.cloned.1.call-start = ((), (), s32[]{:S(2)}) async-start(), calls=%async_computation.1 | async-start | bytes 5242880 | tf_op jit(solution)/shard_map/reduce_scatter | solution.py:143
  7.3 79.8 %collective-permute-start.1 = (bf16[32,128,128]{2,1,0:T(8,128)(2,1)}, bf16[32,128,128]{2,1,0:T(8,128)(2,1)S(1)}, u32[]{:S(2)}, u32[]{:S(2)}) collective-permute-start(bf16[32,128,128]{2,1,0:T(8,128)(2,1)} %bitcast.66), channel_id=1, source_target_pairs={{0,64},{32,96},{64,0},{96,32},{1,65},{33,97},{65,1},{97,33},{2,66}... | collective-permute-start | bytes 3145736 | tf_op jit(solution)/shard_map/ppermute | solution.py:88
  9.4 81.6 %collective-permute-start = (bf16[32,128,128]{2,1,0:T(8,128)(2,1)}, bf16[32,128,128]{2,1,0:T(8,128)(2,1)S(1)}, u32[]{:S(2)}, u32[]{:S(2)}) collective-permute-start(bf16[32,128,128]{2,1,0:T(8,128)(2,1)} %bitcast.67), channel_id=1, source_target_pairs={{0,32},{32,0},{64,96},{96,64},{1,33},{33,1},{65,97},{97,65},{2,34}... | collective-permute-start | bytes 3145736 | tf_op jit(solution)/shard_map/ppermute | solution.py:89
  44.0 1.9 copy-start.3
  44.0 13.5 %copy-start.2 = (s32[1,1,1,32,2]{3,4,2,1,0:T(2,128)S(1)}, s32[1,1,1,32,2]{3,4,2,1,0:T(2,128)}, u32[]{:S(2)}) copy-start(s32[1,1,1,32,2]{3,4,2,1,0:T(2,128)} %param.6) | copy-start | bytes 772
  87.1 3.9 %collective-permute-start.2 = (bf16[32,128,128]{2,1,0:T(8,128)(2,1)S(1)}, bf16[32,128,128]{2,1,0:T(8,128)(2,1)}, u32[]{:S(2)}, u32[]{:S(2)}) collective-permute-start(bf16[32,128,128]{2,1,0:T(8,128)(2,1)S(1)} %collective-permute-done.1), channel_id=1, source_target_pairs={{0,32},{32,0},{64,96},{96,64},{1,33},{33,1},{65,97},{97,65},{2,34}... | collective-permute-start | bytes 3145736 | tf_op jit(solution)/shard_map/ppermute | solution.py:90
  87.5 3.5 %copy-start.1 = (bf16[1,1,1,32,128,128]{5,4,3,2,1,0:T(8,128)(2,1)S(1)}, bf16[1,1,1,32,128,128]{5,4,3,2,1,0:T(8,128)(2,1)}, u32[]{:S(2)}) copy-start(bf16[1,1,1,32,128,128]{5,4,3,2,1,0:T(8,128)(2,1)} %param.7) | copy-start | bytes 3145732
  139.7 1.9 copy-start
  187.7 2.0 collective-permute-start.3
  187.7 3.7 %collective-permute-start.4 = (f32[16,128]{1,0:T(8,128)S(1)}, f32[16,128]{1,0:T(8,128)S(1)}, u32[]{:S(2)}, u32[]{:S(2)}) collective-permute-start(f32[16,128]{1,0:T(8,128)S(1)} %get-tuple-element.13), channel_id=1, source_target_pairs={{0,64},{32,96},{64,0},{96,32},{1,65},{33,97},{65,1},{97,33},{2,66}... | collective-permute-start | bytes 24584 | tf_op jit(solution)/shard_map/ppermute | solution.py:64
  189.4 3.1 %collective-permute-start.5 = (f32[16,128]{1,0:T(8,128)S(1)}, f32[16,128]{1,0:T(8,128)S(1)}, u32[]{:S(2)}, u32[]{:S(2)}) collective-permute-start(f32[16,128]{1,0:T(8,128)S(1)} %get-tuple-element.13), channel_id=1, source_target_pairs={{0,96},{32,64},{64,32},{96,0},{1,97},{33,65},{65,33},{97,1},{2,98}... | collective-permute-start | bytes 24584 | tf_op jit(solution)/shard_map/ppermute | solution.py:64
  192.5 5.3 %collective-permute-start.6 = (f32[16,128]{1,0:T(8,128)S(1)}, f32[16,128]{1,0:T(8,128)S(1)}, u32[]{:S(2)}, u32[]{:S(2)}) collective-permute-start(f32[16,128]{1,0:T(8,128)S(1)} %add_add_fusion), channel_id=1, source_target_pairs={{0,1},{1,0},{2,3},{3,2},{4,5},{5,4},{6,7},{7,6},{8,9},{9,8},{10,11... | collective-permute-start | bytes 24584 | tf_op jit(solution)/shard_map/ppermute | solution.py:64
  192.7 5.2 %collective-permute-start.7 = (f32[16,128]{1,0:T(8,128)S(1)}, f32[16,128]{1,0:T(8,128)S(1)}, u32[]{:S(2)}, u32[]{:S(2)}) collective-permute-start(f32[16,128]{1,0:T(8,128)S(1)} %add_add_fusion), channel_id=1, source_target_pairs={{0,2},{1,3},{2,0},{3,1},{4,6},{5,7},{6,4},{7,5},{8,10},{9,11},{10,... | collective-permute-start | bytes 24584 | tf_op jit(solution)/shard_map/ppermute | solution.py:64
  194.8 4.9 %collective-permute-start.8 = (f32[16,128]{1,0:T(8,128)S(1)}, f32[16,128]{1,0:T(8,128)S(1)}, u32[]{:S(2)}, u32[]{:S(2)}) collective-permute-start(f32[16,128]{1,0:T(8,128)S(1)} %add_add_fusion), channel_id=1, source_target_pairs={{0,3},{1,2},{2,1},{3,0},{4,7},{5,6},{6,5},{7,4},{8,11},{9,10},{10,... | collective-permute-start | bytes 24584 | tf_op jit(solution)/shard_map/ppermute | solution.py:64
Sparse Core Ops, SparseCore 0:
  9.7 120.2 all-gather.5
  141.8 44.4 reduce-scatter.1

commit v21 on v19

--- a/solution.py
+++ b/solution.py
@@ -11,7 +11,7 @@
 N_SLOT = 8
 
 
-def column_kernel(moff_ref, oidx_ref, flow_ref, graph_ref, out_ref, lhs_ref, *, n_q, n_g):
+def column_kernel(moff_ref, flow_ref, graph_ref, out_ref, lhs_ref, *, n_q, n_g):
     tile = out_ref.shape[-1]
     n_col = out_ref.shape[0] // n_q
 
@@ -25,7 +25,7 @@
         right = graph_ref[pl.ds(pl.multiple_of(j * n_g * tile, n_g * tile), n_g * tile), :]
         res = jnp.dot(lhs_ref[slot], right, preferred_element_type=jnp.float32)
         for q in range(n_q):
-            out_ref[oidx_ref[j * n_q + q]] = res[q * tile : (q + 1) * tile]
+            out_ref[q * n_col + j] = res[q * tile : (q + 1) * tile]
 
     def body(i, carry):
         for k in range(N_SLOT):
@@ -35,14 +35,13 @@
     lax.fori_loop(0, n_col // N_SLOT, body, 0)
 
 
-def kept_partials(moff, oidx, flow_flat, graph_flat, n_out, n_q, n_g):
+def kept_partials(moff, flow_flat, graph_flat, n_out, n_q, n_g):
     tile = flow_flat.shape[-1]
     kernel = functools.partial(column_kernel, n_q=n_q, n_g=n_g)
     return pl.pallas_call(
         kernel,
         out_shape=jax.ShapeDtypeStruct((n_out, tile, tile), jnp.float32),
         in_specs=[
-            pl.BlockSpec(memory_space=pltpu.SMEM),
             pl.BlockSpec(memory_space=pltpu.SMEM),
             pl.BlockSpec(memory_space=pltpu.VMEM),
             pl.BlockSpec(memory_space=pltpu.VMEM),
@@ -57,7 +56,7 @@
             transcendentals=0,
             bytes_accessed=2 * (flow_flat.size + graph_flat.size) + 4 * n_out * tile * tile,
         ),
-    )(moff, oidx, flow_flat, graph_flat)
+    )(moff, flow_flat, graph_flat)
 
 
 def round_sum(x, axis, n):
@@ -116,7 +115,6 @@
     kept_row0 = jnp.take_along_axis(kept_all[:, :, 0], kept_pos, axis=1)
     q_ids = jnp.arange(layer_count, dtype=jnp.int32)
     kept_row = q_ids[:, None] * quarter + kept_row0
-    oidx = jnp.broadcast_to(q_ids[:, None] * col_tiles + col_ids[None, :], (layer_count, col_tiles)).T
 
     a_rows = flow_coords[:, :, 0]
     a_inner = flow_coords[:, :, 1]
@@ -133,7 +131,6 @@
     graph_flat = graph_tiles[g_tile.reshape(-1)].reshape(-1, tile)
     partial_sum = kept_partials(
         moff.reshape(-1).astype(jnp.int32),
-        oidx.reshape(-1).astype(jnp.int32),
         flow_flat,
         graph_flat,
         n_out,

time: 209 us -> 208 us (level)
  no operation moved by 1% of the time
where the time goes in v21:
time: 208 us
  waiting for transfers between devices  80.8 us (39%)
  blocking collectives  67.4 us (32%)
  local copies, waits for them, and re-layouts  16.5 us (8%)
  between operations  13.6 us (7%)
  other arithmetic  11.3 us (5%)
  Pallas kernels  9.77 us (5%)
  starting transfers between devices  8.77 us (4%)
    reduce_scatter x1, waiting for transfers between devices, local(): lax.psum_scatter(partial_sum, 'layer', scatter_dimension=0, tiled=True)  44.6 us
    all_gather x1, blocking collectives, local(): lax.all_gather(b_coords[0, 0, 0][None], 'row', axis=0, tiled=True)  32.2 us
    all_gather x1, waiting for transfers between devices, local(): flow_tiles = lax.all_gather(a_tiles[0, 0, 0], 'col', axis=0, tiled=True)  30.7 us
    all_gather x1, blocking collectives, local(): lax.all_gather(a_coords[0, 0, 0][None], 'col', axis=0, tiled=True)  25.4 us
    all_gather x1, blocking collectives, local(): lax.all_gather(out_coords[0, 0, 0][None], 'layer', axis=0, tiled=True)  9.78 us
    pallas_call x1, Pallas kernels, kept_partials(): pl.pallas_call(kernel, out_shape=jax.ShapeDtypeStruct((n_out, tile, tile)...  9.77 us
    ppermute x6, starting transfers between devices, round_sum(): lax.ppermute(x, axis, [(i, i ^ d) for i in range(n)])  6.65 us
    gather x1, local copies, waits for them, and re-layouts, local(): graph_flat = graph_tiles[g_tile.reshape(-1)].reshape(-1, tile)  5.23 us
  transfers between devices with their start and end apart: 11, of which 6 were waited for; matrix products, arithmetic and copies ran while one was open for 11% of the time, Pallas kernels for 0%

profile of v21, /device:TPU:0, one launch (start us, length us, event | category | flops | bytes accessed | tf_op | source)
XLA Modules:
  0.0 208.1 jit_solution(11617969036250496543)
XLA Ops:
  7.3 2.1 collective-permute-start.1
  9.4 32.2 %all-gather.1 = s32[4,1,1,32,2]{3,4,2,1,0:T(2,128)S(1)} all-gather(s32[1,1,1,32,2]{3,4,2,1,0:T(2,128)} %param.8), channel_id=3, replica_groups=mesh['row'=4,'col'=8,'layer'=4] {'row'}, dimensions={0}, use_global_device_ids=true | all-gather | bytes 1280 | tf_op jit(solution)/shard_map/all_gather | solution.py:92
  42.3 0.7 iota_reduce_fusion.2
  44.0 1.5 gather_fusion.6
  46.1 25.4 %all-gather = s32[8,1,1,32,2]{3,4,2,1,0:T(2,128)S(1)} all-gather(s32[1,1,1,32,2]{3,4,2,1,0:T(2,128)S(1)} %copy-done.2), channel_id=2, replica_groups=mesh['row'=4,'col'=8,'layer'=4] {'col'}, dimensions={0}, use_global_device_ids=true | all-gather | bytes 2304 | tf_op jit(solution)/shard_map/all_gather | solution.py:94
  71.5 9.8 %all-gather.2 = s32[4,1,1,16,2]{3,4,2,1,0:T(2,128)S(1)} all-gather(s32[1,1,1,16,2]{3,4,2,1,0:T(2,128)S(1)} %copy-done.3), channel_id=4, replica_groups=mesh['row'=4,'col'=8,'layer'=4] {'layer'}, dimensions={0}, use_global_device_ids=true | all-gather | bytes 640 | tf_op jit(solution)/shard_map/all_gather | solution.py:95
  81.3 0.7 iota_reduce_fusion.1
  82.1 0.9 gather_fusion.7
  83.9 3.0 %iota_reduce_fusion = (pred[16,4,8]{2,1,0:T(4,128)(4,1)}, s32[16,4,8]{2,1,0:T(4,128)S(1)}) fusion(s32[16,4]{1,0:T(8,128)S(1)} %copy.56, s32[16,8,32]{2,1,0:T(8,128)S(1)} %bitcast.69), kind=kLoop, calls=%fused_computation.10 | loop fusion | flops 127488 | bytes 19200 | tf_op jit(solution)/shard_map/local/reduce | solution.py:124
  87.3 2.6 %gather_fusion.2 = s32[512]{0:T(512)S(1)} fusion(s32[8,32]{1,0:T(8,128)S(1)} %get-tuple-element.15, s32[512]{0:T(512)S(1)} %reshape.384), kind=kCustom, calls=%fused_computation.2 | custom fusion | bytes 8192 | tf_op jit(solution)/shard_map/gather | solution.py:127
  90.6 3.3 %pad_maximum_fusion = bf16[128,128,128]{2,1,0:T(8,128)(2,1)} fusion(bf16[32,128,128]{2,1,0:T(8,128)(2,1)} %collective-permute-done.2, bf16[32,128,128]{2,1,0:T(8,128)(2,1)S(1)} %collective-permute-done.1, bf16[32,128,128]{2,1,0:T(8,128)(2,1)S(1)} %collective-permute-done, bf16[32,128,128]{2,1,0:T(8,128)(2,1)S(1)} %bitcast.68), kind=kLoop, calls=%fused_computation.8 | loop fusion | flops 6291456 | bytes 8388608 | tf_op jit(solution)/shard_map/concatenate | solution.py:91
  93.9 5.2 %gather_fusion.3 = bf16[128,128,128]{2,1,0:T(8,128)(2,1)} fusion(bf16[128,128,128]{2,1,0:T(8,128)(2,1)} %pad_maximum_fusion, s32[1024]{0:T(1024)S(1)} %pad_clamp_fusion.1), kind=kCustom, calls=%fused_computation.3 | custom fusion | bytes 8389120 | tf_op jit(solution)/shard_map/gather | solution.py:131
  99.2 30.7 %all-gather.6.cloned.1.call-done = bf16[1,1,1,256,128,128]{5,4,2,1,0,3:T(8,128)(2,1)} async-done(((bf16[1,1,1,32,128,128]{5,4,2,1,0,3:T(8,128)(2,1)}), bf16[1,1,1,256,128,128]{5,4,2,1,0,3:T(8,128)(2,1)}) %all-gather.6.cloned.1.call-update) | async-done | bytes 8388624 | tf_op jit(solution)/shard_map/all_gather | solution.py:93
  129.9 9.8 %shard_map.55 = f32[64,128,128]{2,1,0:T(8,128)S(1)} custom-call(s32[512]{0:T(512)S(1)} %reshape.365.moff_ref, bf16[32768,128]{1,0:T(8,128)(2,1)} %bitcast.63, bf16[16384,128]{1,0:T(8,128)(2,1)} %bitcast.62), custom_call_target="tpu_custom_call" | custom-call | flops 2147483648 | bytes 16777216 | tf_op jit(solution)/shard_map/pallas_call | solution.py:41
  139.7 1.9 copy-done
  141.6 44.6 %reduce-scatter.2.cloned.1.call-done = f32[16,128,128]{2,1,0:T(8,128)} async-done(((f32[64,128,128]{2,1,0:T(8,128)}), f32[16,128,128]{2,1,0:T(8,128)}) %reduce-scatter.2.cloned.1.call-update) | async-done | bytes 1048592 | tf_op jit(solution)/shard_map/reduce_scatter | solution.py:140
  186.3 1.3 multiply_reduce_fusion
  187.7 1.6 collective-permute-start.4
  189.6 1.9 collective-permute-done.4
  191.5 1.0 collective-permute-done.5
  192.7 2.1 collective-permute-start.7
  194.8 2.4 %collective-permute-start.8 = (f32[16,128]{1,0:T(8,128)S(1)}, f32[16,128]{1,0:T(8,128)S(1)}, u32[]{:S(2)}, u32[]{:S(2)}) collective-permute-start(f32[16,128]{1,0:T(8,128)S(1)} %add_add_fusion), channel_id=1, source_target_pairs={{0,3},{1,2},{2,1},{3,0},{4,7},{5,6},{6,5},{7,4},{8,11},{9,10},{10,... | collective-permute-start | bytes 24584 | tf_op jit(solution)/shard_map/ppermute | solution.py:63
  197.8 1.8 collective-permute-done.8
  200.2 1.1 bitcast_multiply_fusion
  (75 shorter events, 6.7 us)
Async XLA Ops:
  6.5 123.4 %all-gather.6.cloned.1.call-start = ((), (), s32[]{:S(2)}) async-start(), calls=%async_computation.2 | async-start | bytes 9437184 | tf_op jit(solution)/shard_map/all_gather | solution.py:93
  7.3 179.0 %reduce-scatter.2.cloned.1.call-start = ((), (), s32[]{:S(2)}) async-start(), calls=%async_computation.1 | async-start | bytes 5242880 | tf_op jit(solution)/shard_map/reduce_scatter | solution.py:140
  7.3 79.6 %collective-permute-start.1 = (bf16[32,128,128]{2,1,0:T(8,128)(2,1)}, bf16[32,128,128]{2,1,0:T(8,128)(2,1)S(1)}, u32[]{:S(2)}, u32[]{:S(2)}) collective-permute-start(bf16[32,128,128]{2,1,0:T(8,128)(2,1)} %bitcast.66), channel_id=1, source_target_pairs={{0,64},{32,96},{64,0},{96,32},{1,65},{33,97},{65,1},{97,33},{2,66}... | collective-permute-start | bytes 3145736 | tf_op jit(solution)/shard_map/ppermute | solution.py:87
  9.4 81.2 %collective-permute-start = (bf16[32,128,128]{2,1,0:T(8,128)(2,1)}, bf16[32,128,128]{2,1,0:T(8,128)(2,1)S(1)}, u32[]{:S(2)}, u32[]{:S(2)}) collective-permute-start(bf16[32,128,128]{2,1,0:T(8,128)(2,1)} %bitcast.67), channel_id=1, source_target_pairs={{0,32},{32,0},{64,96},{96,64},{1,33},{33,1},{65,97},{97,65},{2,34}... | collective-permute-start | bytes 3145736 | tf_op jit(solution)/shard_map/ppermute | solution.py:88
  44.0 2.1 copy-start.2
  44.0 27.5 %copy-start.3 = (s32[1,1,1,16,2]{3,4,2,1,0:T(2,128)S(1)}, s32[1,1,1,16,2]{3,4,2,1,0:T(2,128)}, u32[]{:S(2)}) copy-start(s32[1,1,1,16,2]{3,4,2,1,0:T(2,128)} %param.9) | copy-start | bytes 388
  86.9 3.7 %collective-permute-start.2 = (bf16[32,128,128]{2,1,0:T(8,128)(2,1)S(1)}, bf16[32,128,128]{2,1,0:T(8,128)(2,1)}, u32[]{:S(2)}, u32[]{:S(2)}) collective-permute-start(bf16[32,128,128]{2,1,0:T(8,128)(2,1)S(1)} %collective-permute-done.1), channel_id=1, source_target_pairs={{0,32},{32,0},{64,96},{96,64},{1,33},{33,1},{65,97},{97,65},{2,34}... | collective-permute-start | bytes 3145736 | tf_op jit(solution)/shard_map/ppermute | solution.py:89
  87.3 3.3 %copy-start.1 = (bf16[1,1,1,32,128,128]{5,4,3,2,1,0:T(8,128)(2,1)S(1)}, bf16[1,1,1,32,128,128]{5,4,3,2,1,0:T(8,128)(2,1)}, u32[]{:S(2)}) copy-start(bf16[1,1,1,32,128,128]{5,4,3,2,1,0:T(8,128)(2,1)} %param.7) | copy-start | bytes 3145732
  139.7 1.9 copy-start
  187.6 2.0 collective-permute-start.3
  187.7 3.7 %collective-permute-start.4 = (f32[16,128]{1,0:T(8,128)S(1)}, f32[16,128]{1,0:T(8,128)S(1)}, u32[]{:S(2)}, u32[]{:S(2)}) collective-permute-start(f32[16,128]{1,0:T(8,128)S(1)} %get-tuple-element.13), channel_id=1, source_target_pairs={{0,64},{32,96},{64,0},{96,32},{1,65},{33,97},{65,1},{97,33},{2,66}... | collective-permute-start | bytes 24584 | tf_op jit(solution)/shard_map/ppermute | solution.py:63
  189.4 3.1 %collective-permute-start.5 = (f32[16,128]{1,0:T(8,128)S(1)}, f32[16,128]{1,0:T(8,128)S(1)}, u32[]{:S(2)}, u32[]{:S(2)}) collective-permute-start(f32[16,128]{1,0:T(8,128)S(1)} %get-tuple-element.13), channel_id=1, source_target_pairs={{0,96},{32,64},{64,32},{96,0},{1,97},{33,65},{65,33},{97,1},{2,98}... | collective-permute-start | bytes 24584 | tf_op jit(solution)/shard_map/ppermute | solution.py:63
  192.5 5.3 %collective-permute-start.6 = (f32[16,128]{1,0:T(8,128)S(1)}, f32[16,128]{1,0:T(8,128)S(1)}, u32[]{:S(2)}, u32[]{:S(2)}) collective-permute-start(f32[16,128]{1,0:T(8,128)S(1)} %add_add_fusion), channel_id=1, source_target_pairs={{0,1},{1,0},{2,3},{3,2},{4,5},{5,4},{6,7},{7,6},{8,9},{9,8},{10,11... | collective-permute-start | bytes 24584 | tf_op jit(solution)/shard_map/ppermute | solution.py:63
  192.7 5.2 %collective-permute-start.7 = (f32[16,128]{1,0:T(8,128)S(1)}, f32[16,128]{1,0:T(8,128)S(1)}, u32[]{:S(2)}, u32[]{:S(2)}) collective-permute-start(f32[16,128]{1,0:T(8,128)S(1)} %add_add_fusion), channel_id=1, source_target_pairs={{0,2},{1,3},{2,0},{3,1},{4,6},{5,7},{6,4},{7,5},{8,10},{9,11},{10,... | collective-permute-start | bytes 24584 | tf_op jit(solution)/shard_map/ppermute | solution.py:63
  194.8 4.9 %collective-permute-start.8 = (f32[16,128]{1,0:T(8,128)S(1)}, f32[16,128]{1,0:T(8,128)S(1)}, u32[]{:S(2)}, u32[]{:S(2)}) collective-permute-start(f32[16,128]{1,0:T(8,128)S(1)} %add_add_fusion), channel_id=1, source_target_pairs={{0,3},{1,2},{2,1},{3,0},{4,7},{5,6},{6,5},{7,4},{8,11},{9,10},{10,... | collective-permute-start | bytes 24584 | tf_op jit(solution)/shard_map/ppermute | solution.py:63
Sparse Core Ops, SparseCore 0:
  9.7 120.1 all-gather.5
  141.8 44.4 reduce-scatter.1
